TPU v7x, 512 devices: a whole 4x8x8 slice. The times are simulated.
512 devices in a mesh: freq: 128 (over y, z, core), tm: 4 (over x).
Axes of the slice: x: 4, y: 8, z: 8, core: 2. Of those that a mesh axis runs over, the one named last changes fastest.
Arguments:
- spectrogram: bfloat16 [65536, 2048], P('freq', 'tm'), may hold values from -6 to 6
- low_share: int32 [2047], replicated, may hold values from 24 to 44
- jitter: int32 [4094], replicated, may hold values from 0 to 63
Outputs:
- best: float32 [9, 2048], P(None, 'tm')
All inputs are finite; a program needn't handle non-finite values.
Results may differ from a plain program's by a relative error of at most 0.0003.
Values sent between devices are 32-bit elements; how exact they have to be, the bound alone decides.
No kernel may reach another device: no remote copies, remote signals or barrier semaphores. Data moves between devices by JAX's collectives and lax.ppermute only.
A program may use at most 64 MiB of HBM per device.

v0:
```python
import math

import jax
import jax.numpy as jnp
from jax import lax
from jax.sharding import PartitionSpec as P

SUMMED = 32
WIDTHS = 9


def passed_along(block, axis, distance):
    devices = range(lax.axis_size(axis))
    route = [(i - distance, i) for i in devices if i - distance in devices]
    return lax.ppermute(block, axis, route)


def swapped(block, axis, apart):
    count = lax.axis_size(axis)
    route = []
    for low in range(count):
        high = low | 1 << apart
        if high != low and high < count:
            route += [(low, high), (high, low)]
    return lax.ppermute(block, axis, route)


def widen(trial_rows, fetch_width):
    if fetch_width == 0:
        return trial_rows
    span_time = trial_rows.shape[-1]
    hop_count = min(-(-fetch_width // span_time), lax.axis_size("tm") - 1)
    pieces = [trial_rows]
    fetched = 0
    for hop_index in range(1, hop_count + 1):
        taken_cols = min(span_time, fetch_width - fetched)
        arrived = passed_along(trial_rows[..., span_time - taken_cols :], "tm", hop_index)
        pieces.insert(0, arrived)
        fetched = fetched + taken_cols
    if fetched < fetch_width:
        pieces.insert(
            0, jnp.zeros(trial_rows.shape[:-1] + (fetch_width - fetched,), trial_rows.dtype)
        )
    return jnp.concatenate(pieces, axis=-1)


def align_pair(low_set, high_set, need_now, fetch_width):
    high_set = widen(high_set, fetch_width)
    low_set = widen(low_set, fetch_width - need_now)
    return (low_set, high_set, fetch_width - need_now)


def delay_of(trial_ids, subband_ids, trial_count, low_share, jitter):
    all_trials = low_share.shape[0] + 1
    rate_rows = jnp.take(low_share, all_trials // trial_count - 1 + subband_ids)
    return (trial_ids * rate_rows + jnp.take(jitter, trial_count - 2 + trial_ids)) // 64


def merge_rows(low_rows, high_rows, shifts, need_now):
    offsets = need_now - shifts
    bit_count = max(need_now.bit_length(), 1)
    moved = high_rows
    for bit_index in range(bit_count):
        step_size = 2**bit_index
        cols = moved.shape[-1]
        selected = (offsets >> bit_index & 1)[:, None] == 1
        moved = jnp.where(selected, moved[:, step_size:], moved[:, : cols - step_size])
    return low_rows + moved


def shards(spectrogram, low_share, jitter):
    trial_dev = spectrogram.shape[0] // SUMMED
    span_time = spectrogram.shape[1]
    all_trials = low_share.shape[0] + 1
    freq_bits = lax.axis_size("freq").bit_length() - 1
    device = lax.axis_index("freq")
    local_counts = []
    trial_count = 2
    while trial_count <= trial_dev:
        local_counts.append(trial_count)
        trial_count = trial_count * 2
    cross_counts = [trial_dev * 2 ** (bit_index + 1) for bit_index in range(freq_bits)]
    need_list = [count_now - 1 for count_now in local_counts + cross_counts] + [
        2 ** (WIDTHS - 1) - 1
    ]
    fetch_plan = []
    for position in range(len(need_list)):
        need_now = need_list[position]
        fetch_plan.append(need_now)
    states = jnp.sum(spectrogram.reshape(trial_dev, SUMMED, span_time), axis=1, dtype=jnp.float32)[
        :, None, :
    ]
    section_index = 0
    for trial_count in local_counts:
        need_now = trial_count - 1
        groups = states.shape[0] // 2
        low_set, high_set, margin = align_pair(
            states[0::2], states[1::2], need_now, fetch_plan[section_index]
        )
        low_rows = jnp.repeat(low_set, 2, axis=1).reshape(groups * trial_count, -1)
        high_rows = jnp.repeat(high_set, 2, axis=1).reshape(groups * trial_count, -1)
        trial_ids = jnp.tile(jnp.arange(trial_count, dtype=jnp.int32), groups)
        subband_ids = device * (trial_dev // trial_count) + jnp.repeat(
            jnp.arange(groups, dtype=jnp.int32), trial_count
        )
        shifts = delay_of(trial_ids, subband_ids, trial_count, low_share, jitter)
        states = merge_rows(low_rows, high_rows, shifts, need_now).reshape(groups, trial_count, -1)
        section_index = section_index + 1
    trial_rows = states[0]
    trial_ids = jnp.arange(trial_dev, dtype=jnp.int32)
    for bit_index in range(freq_bits):
        trial_count = cross_counts[bit_index]
        need_now = trial_count - 1
        partner = swapped(trial_rows, "freq", bit_index)
        upper_half = device >> bit_index & 1
        low_rows = jnp.where(upper_half == 1, partner, trial_rows)
        high_rows = jnp.where(upper_half == 1, trial_rows, partner)
        low_rows, high_rows, margin = align_pair(
            low_rows, high_rows, need_now, fetch_plan[section_index]
        )
        trial_ids = 2 * trial_ids + upper_half
        shifts = delay_of(trial_ids, device >> bit_index + 1, trial_count, low_share, jitter)
        trial_rows = merge_rows(low_rows, high_rows, shifts, need_now)
        section_index = section_index + 1
    trial_rows = widen(trial_rows, fetch_plan[section_index])
    signal = trial_rows / math.sqrt(all_trials * SUMMED)
    peak_rows = []
    window_sum = signal
    width_now = 1
    for level_index in range(WIDTHS):
        length = window_sum.shape[1]
        peak_rows.append(
            jnp.max(window_sum[:, length - span_time :], axis=0) / math.sqrt(width_now)
        )
        if level_index + 1 < WIDTHS:
            window_sum = window_sum[:, width_now:] + window_sum[:, : length - width_now]
            width_now = width_now * 2
    local_best = jnp.stack(peak_rows)
    return lax.pmax(local_best, "freq")


def solution(mesh):
    placed = (P("freq", "tm"), P(), P())
    return jax.shard_map(
        shards, mesh=mesh, in_specs=placed, out_specs=P(None, "tm"), check_vma=False
    )
```

profile of v0, /device:TPU:6, one launch (start us, length us, event | category | flops | bytes accessed | tf_op | source)
XLA Modules:
  0.0 640.6 jit_solution(10059896096188159181)
XLA Ops:
  15.2 4.8 collective-permute-done.1
  21.8 4.1 collective-permute-done.2
  27.8 4.1 collective-permute-done.3
  32.4 1.9 collective-permute-start.4
  37.0 4.2 collective-permute-done.5
  41.6 4.3 collective-permute-start.6
  45.9 1.9 collective-permute-done.6
  49.2 4.2 collective-permute-done.7
  54.0 6.1 collective-permute-start.8
  63.3 4.2 collective-permute-done.9
  68.2 9.3 %collective-permute-start.10 = (f32[16,512]{1,0:T(8,128)S(1)}, f32[16,512]{1,0:T(8,128)S(1)}, u32[]{:S(2)}, u32[]{:S(2)}) collective-permute-start(f32[16,512]{1,0:T(8,128)S(1)} %fusion.10), channel_id=1, source_target_pairs={{0,32},{32,0},{4,36},{36,4},{8,40},{40,8},{12,44},{44,12},{16,48},... | collective-permute-start | bytes 98312 | tf_op jit(solution)/shard_map/ppermute | solution.py:25
  77.5 1.9 collective-permute-done.10
  80.8 4.3 collective-permute-done.11
  85.8 3.5 collective-permute-start.12
  89.3 2.3 collective-permute-done.12
  91.7 1.3 collective-permute-start.13
  95.6 1.9 collective-permute-done.13
  98.3 4.5 collective-permute-start.14
  102.8 2.2 collective-permute-done.14
  105.1 1.3 collective-permute-start.16
  106.4 1.3 collective-permute-start.15
  107.7 6.5 %collective-permute-done.15 = f32[16,511]{1,0:T(8,128)S(1)} collective-permute-done((f32[16,511]{1,0:T(8,128)S(1)}, f32[16,511]{1,0:T(8,128)S(1)}, u32[]{:S(2)}, u32[]{:S(2)}) %collective-permute-start.15) | collective-permute-done | bytes 32736 | tf_op jit(solution)/shard_map/ppermute | solution.py:15
  115.3 8.1 %collective-permute-start.17 = (f32[16,512]{1,0:T(8,128)S(1)}, f32[16,512]{1,0:T(8,128)S(1)}, u32[]{:S(2)}, u32[]{:S(2)}) collective-permute-start(f32[16,512]{1,0:T(8,128)S(1)} %fusion.7), channel_id=1, source_target_pairs={{0,256},{256,0},{4,260},{260,4},{8,264},{264,8},{12,268},{268,12},... | collective-permute-start | bytes 98312 | tf_op jit(solution)/shard_map/ppermute | solution.py:25
  123.4 2.0 collective-permute-done.17
  126.6 1.3 collective-permute-start.19
  127.9 1.3 collective-permute-start.18
  129.3 2.0 collective-permute-done.20
  131.2 3.4 collective-permute-done.19
  134.6 2.5 collective-permute-done.18
  138.4 1.3 collective-permute-start.21
  139.7 4.3 collective-permute-done.21
  145.6 495.1 %pmax.7 = f32[9,512]{1,0:T(8,128)} all-reduce(f32[9,512]{1,0:T(8,128)S(1)} %stack.5), channel_id=1, replica_groups=mesh['freq'=128,'tm'=4] {'freq'}, use_global_device_ids=true, to_apply=%region_10.13 | all-reduce | flops 4608 | bytes 36864 | tf_op jit(solution)/shard_map/pmax | solution.py:139
  (231 shorter events, 33.6 us)
Async XLA Ops:
  0.0 3.1 copy-start
  1.3 12.3 %collective-permute-start = (f32[8,1,1]{2,0,1:T(8,128)S(1)}, f32[8,1,1]{2,0,1:T(8,128)S(1)}, u32[]{:S(2)}, u32[]{:S(2)}) collective-permute-start(f32[8,1,1]{2,0,1:T(8,128)S(1)} %slice.773), channel_id=1, source_target_pairs={{0,1},{1,2},{2,3},{4,5},{5,6},{6,7},{8,9},{9,10},{10,11},{12,13},{... | collective-permute-start | bytes 104 | tf_op jit(solution)/shard_map/ppermute | solution.py:15
  3.1 0.7 copy-start.1
  13.9 6.1 collective-permute-start.1
  20.4 5.5 collective-permute-start.2
  26.4 5.5 collective-permute-start.3
  32.4 3.2 collective-permute-start.4
  35.7 5.5 collective-permute-start.5
  41.6 6.2 collective-permute-start.6
  47.9 5.5 collective-permute-start.7
  54.0 8.0 %collective-permute-start.8 = (f32[16,512]{1,0:T(8,128)S(1)}, f32[16,512]{1,0:T(8,128)S(1)}, u32[]{:S(2)}, u32[]{:S(2)}) collective-permute-start(f32[16,512]{1,0:T(8,128)S(1)} %fusion.11), channel_id=1, source_target_pairs={{0,16},{16,0},{4,20},{20,4},{8,24},{24,8},{12,28},{28,12},{32,48},... | collective-permute-start | bytes 98312 | tf_op jit(solution)/shard_map/ppermute | solution.py:25
  62.0 5.5 collective-permute-start.9
  68.2 11.2 %collective-permute-start.10 = (f32[16,512]{1,0:T(8,128)S(1)}, f32[16,512]{1,0:T(8,128)S(1)}, u32[]{:S(2)}, u32[]{:S(2)}) collective-permute-start(f32[16,512]{1,0:T(8,128)S(1)} %fusion.10), channel_id=1, source_target_pairs={{0,32},{32,0},{4,36},{36,4},{8,40},{40,8},{12,44},{44,12},{16,48},... | collective-permute-start | bytes 98312 | tf_op jit(solution)/shard_map/ppermute | solution.py:25
  79.5 5.6 collective-permute-start.11
  85.8 5.8 collective-permute-start.12
  91.7 5.8 collective-permute-start.13
  98.3 6.7 %collective-permute-start.14 = (f32[16,512]{1,0:T(8,128)S(1)}, f32[16,512]{1,0:T(8,128)S(1)}, u32[]{:S(2)}, u32[]{:S(2)}) collective-permute-start(f32[16,512]{1,0:T(8,128)S(1)} %fusion.8), channel_id=1, source_target_pairs={{0,128},{128,0},{4,132},{132,4},{8,136},{136,8},{12,140},{140,12},... | collective-permute-start | bytes 98312 | tf_op jit(solution)/shard_map/ppermute | solution.py:25
  105.1 9.2 %collective-permute-start.16 = (f32[16,512]{1,0:T(8,128)S(1)}, f32[16,512]{1,0:T(8,128)S(1)}, u32[]{:S(2)}, u32[]{:S(2)}) collective-permute-start(f32[16,512]{1,0:T(8,128)S(1)} %broadcast_select_fusion.5), channel_id=1, source_target_pairs={{0,1},{1,2},{2,3},{4,5},{5,6},{6,7},{8,9},{9,10},{10,11},{12,13},{... | collective-permute-start | bytes 98312 | tf_op jit(solution)/shard_map/ppermute | solution.py:15
  106.4 7.9 %collective-permute-start.15 = (f32[16,511]{1,0:T(8,128)S(1)}, f32[16,511]{1,0:T(8,128)S(1)}, u32[]{:S(2)}, u32[]{:S(2)}) collective-permute-start(f32[16,511]{1,0:T(8,128)S(1)} %slice.874), channel_id=1, source_target_pairs={{0,2},{1,3},{4,6},{5,7},{8,10},{9,11},{12,14},{13,15},{16,18},{17,... | collective-permute-start | bytes 98120 | tf_op jit(solution)/shard_map/ppermute | solution.py:15
  115.3 10.1 %collective-permute-start.17 = (f32[16,512]{1,0:T(8,128)S(1)}, f32[16,512]{1,0:T(8,128)S(1)}, u32[]{:S(2)}, u32[]{:S(2)}) collective-permute-start(f32[16,512]{1,0:T(8,128)S(1)} %fusion.7), channel_id=1, source_target_pairs={{0,256},{256,0},{4,260},{260,4},{8,264},{264,8},{12,268},{268,12},... | collective-permute-start | bytes 98312 | tf_op jit(solution)/shard_map/ppermute | solution.py:25
  125.3 5.9 collective-permute-start.20
  126.6 7.9 %collective-permute-start.19 = (f32[16,512]{1,0:T(8,128)S(1)}, f32[16,512]{1,0:T(8,128)S(1)}, u32[]{:S(2)}, u32[]{:S(2)}) collective-permute-start(f32[16,512]{1,0:T(8,128)S(1)} %broadcast_select_fusion.6), channel_id=1, source_target_pairs={{0,2},{1,3},{4,6},{5,7},{8,10},{9,11},{12,14},{13,15},{16,18},{17,... | collective-permute-start | bytes 98312 | tf_op jit(solution)/shard_map/ppermute | solution.py:15
  127.9 9.2 %collective-permute-start.18 = (f32[16,512]{1,0:T(8,128)S(1)}, f32[16,512]{1,0:T(8,128)S(1)}, u32[]{:S(2)}, u32[]{:S(2)}) collective-permute-start(f32[16,512]{1,0:T(8,128)S(1)} %broadcast_select_fusion.6), channel_id=1, source_target_pairs={{0,3},{4,7},{8,11},{12,15},{16,19},{20,23},{24,27},{28,31},{32,35}... | collective-permute-start | bytes 98312 | tf_op jit(solution)/shard_map/ppermute | solution.py:15
  138.4 5.6 collective-permute-start.21
where the time goes:
time: 641 us
  blocking collectives  495 us (77%)
  waiting for transfers between devices  61.4 us (10%)
  starting transfers between devices  56.9 us (9%)
  local copies, waits for them, and re-layouts  12.6 us (2%)
  other arithmetic  8.99 us (1%)
    pmax x1, blocking collectives, shards(): return lax.pmax(local_best, 'freq')  495 us
    ppermute x15, waiting for transfers between devices, passed_along(): return lax.ppermute(block, axis, route)  50.7 us
    ppermute x7, starting transfers between devices, swapped(): return lax.ppermute(block, axis, route)  37.6 us
    ppermute x15, starting transfers between devices, passed_along(): return lax.ppermute(block, axis, route)  19.3 us
  transfers between devices with their start and end apart: 22, of which 19 were waited for; matrix products, arithmetic and copies ran while one was open for 2% of the time, Pallas kernels for 0%

commit v1 on v0

--- a/solution.py
+++ b/solution.py
@@ -136,7 +136,9 @@
             window_sum = window_sum[:, width_now:] + window_sum[:, : length - width_now]
             width_now = width_now * 2
     local_best = jnp.stack(peak_rows)
-    return lax.pmax(local_best, "freq")
+    for bit_index in range(freq_bits):
+        local_best = jnp.maximum(local_best, swapped(local_best, "freq", bit_index))
+    return local_best
 
 
 def solution(mesh):

time: 641 us -> 196 us (0.31)
  the two profiles are of different devices: /device:TPU:6 before, /device:TPU:38 now
where the time goes in v1:
time: 196 us; the launch traced here: 195 us
  waiting for transfers between devices  93.9 us (48%)
  starting transfers between devices  72.5 us (37%)
  local copies, waits for them, and re-layouts  12.6 us (6%)
  other arithmetic  9.64 us (5%)
  between operations  5.94 us (3%)
    ppermute x14, starting transfers between devices, swapped(): return lax.ppermute(block, axis, route)  53.2 us
    ppermute x15, waiting for transfers between devices, passed_along(): return lax.ppermute(block, axis, route)  50.5 us
    ppermute x14, waiting for transfers between devices, swapped(): return lax.ppermute(block, axis, route)  43.4 us
    ppermute x15, starting transfers between devices, passed_along(): return lax.ppermute(block, axis, route)  19.3 us
    gather x11, local copies, waits for them, and re-layouts, delay_of(): jnp.take(jitter, trial_count - 2 + trial_ids)  7.21 us
    select_n x55, other arithmetic, merge_rows(): jnp.where(selected, moved[:, step_size:], moved[:, :cols - step_size])  4.78 us
  transfers between devices with their start and end apart: 29, of which 26 were waited for; matrix products, arithmetic and copies ran while one was open for 6% of the time, Pallas kernels for 0%

profile of v1, /device:TPU:38, one launch (start us, length us, event | category | flops | bytes accessed | tf_op | source)
XLA Modules:
  0.0 194.6 jit_solution(15536152071409607525)
XLA Ops:
  15.3 4.8 %collective-permute-done.1 = f32[4,2,3]{2,1,0:T(2,128)S(1)} collective-permute-done((f32[4,2,3]{2,1,0:T(2,128)S(1)}, f32[4,2,3]{2,1,0:T(2,128)S(1)}, u32[]{:S(2)}, u32[]{:S(2)}) %collective-permute-start.1) | collective-permute-done | bytes 128 | tf_op jit(solution)/shard_map/ppermute | solution.py:15
  21.8 4.1 %collective-permute-done.2 = f32[2,4,7]{2,1,0:T(4,128)S(1)} collective-permute-done((f32[2,4,7]{2,1,0:T(4,128)S(1)}, f32[2,4,7]{2,1,0:T(4,128)S(1)}, u32[]{:S(2)}, u32[]{:S(2)}) %collective-permute-start.2) | collective-permute-done | bytes 256 | tf_op jit(solution)/shard_map/ppermute | solution.py:15
  27.8 4.1 %collective-permute-done.3 = f32[1,8,15]{2,1,0:T(8,128)S(1)} collective-permute-done((f32[1,8,15]{2,1,0:T(8,128)S(1)}, f32[1,8,15]{2,1,0:T(8,128)S(1)}, u32[]{:S(2)}, u32[]{:S(2)}) %collective-permute-start.3) | collective-permute-done | bytes 512 | tf_op jit(solution)/shard_map/ppermute | solution.py:15
  32.4 1.9 collective-permute-start.4
  37.0 4.2 %collective-permute-done.5 = f32[16,31]{1,0:T(8,128)S(1)} collective-permute-done((f32[16,31]{1,0:T(8,128)S(1)}, f32[16,31]{1,0:T(8,128)S(1)}, u32[]{:S(2)}, u32[]{:S(2)}) %collective-permute-start.5) | collective-permute-done | bytes 2016 | tf_op jit(solution)/shard_map/ppermute | solution.py:15
  41.7 4.3 %collective-permute-start.6 = (f32[16,512]{1,0:T(8,128)S(1)}, f32[16,512]{1,0:T(8,128)S(1)}, u32[]{:S(2)}, u32[]{:S(2)}) collective-permute-start(f32[16,512]{1,0:T(8,128)S(1)} %fusion.12), channel_id=1, source_target_pairs={{0,8},{8,0},{4,12},{12,4},{16,24},{24,16},{20,28},{28,20},{32,40},... | collective-permute-start | bytes 98312 | tf_op jit(solution)/shard_map/ppermute | solution.py:25
  49.3 4.2 %collective-permute-done.7 = f32[16,63]{1,0:T(8,128)S(1)} collective-permute-done((f32[16,63]{1,0:T(8,128)S(1)}, f32[16,63]{1,0:T(8,128)S(1)}, u32[]{:S(2)}, u32[]{:S(2)}) %collective-permute-start.7) | collective-permute-done | bytes 4064 | tf_op jit(solution)/shard_map/ppermute | solution.py:15
  54.0 6.1 %collective-permute-start.8 = (f32[16,512]{1,0:T(8,128)S(1)}, f32[16,512]{1,0:T(8,128)S(1)}, u32[]{:S(2)}, u32[]{:S(2)}) collective-permute-start(f32[16,512]{1,0:T(8,128)S(1)} %fusion.11), channel_id=1, source_target_pairs={{0,16},{16,0},{4,20},{20,4},{8,24},{24,8},{12,28},{28,12},{32,48},... | collective-permute-start | bytes 98312 | tf_op jit(solution)/shard_map/ppermute | solution.py:25
  63.4 4.2 %collective-permute-done.9 = f32[16,127]{1,0:T(8,128)S(1)} collective-permute-done((f32[16,127]{1,0:T(8,128)S(1)}, f32[16,127]{1,0:T(8,128)S(1)}, u32[]{:S(2)}, u32[]{:S(2)}) %collective-permute-start.9) | collective-permute-done | bytes 8160 | tf_op jit(solution)/shard_map/ppermute | solution.py:15
  68.2 9.3 %collective-permute-start.10 = (f32[16,512]{1,0:T(8,128)S(1)}, f32[16,512]{1,0:T(8,128)S(1)}, u32[]{:S(2)}, u32[]{:S(2)}) collective-permute-start(f32[16,512]{1,0:T(8,128)S(1)} %fusion.10), channel_id=1, source_target_pairs={{0,32},{32,0},{4,36},{36,4},{8,40},{40,8},{12,44},{44,12},{16,48},... | collective-permute-start | bytes 98312 | tf_op jit(solution)/shard_map/ppermute | solution.py:25
  80.8 4.3 %collective-permute-done.11 = f32[16,255]{1,0:T(8,128)S(1)} collective-permute-done((f32[16,255]{1,0:T(8,128)S(1)}, f32[16,255]{1,0:T(8,128)S(1)}, u32[]{:S(2)}, u32[]{:S(2)}) %collective-permute-start.11) | collective-permute-done | bytes 16352 | tf_op jit(solution)/shard_map/ppermute | solution.py:15
  85.9 2.6 %collective-permute-start.12 = (f32[16,512]{1,0:T(8,128)S(1)}, f32[16,512]{1,0:T(8,128)S(1)}, u32[]{:S(2)}, u32[]{:S(2)}) collective-permute-start(f32[16,512]{1,0:T(8,128)S(1)} %fusion.9), channel_id=1, source_target_pairs={{0,64},{64,0},{4,68},{68,4},{8,72},{72,8},{12,76},{76,12},{16,80},... | collective-permute-start | bytes 98312 | tf_op jit(solution)/shard_map/ppermute | solution.py:25
  88.5 3.2 %collective-permute-done.12 = f32[16,512]{1,0:T(8,128)S(1)} collective-permute-done((f32[16,512]{1,0:T(8,128)S(1)}, f32[16,512]{1,0:T(8,128)S(1)}, u32[]{:S(2)}, u32[]{:S(2)}) %collective-permute-start.12) | collective-permute-done | bytes 32800 | tf_op jit(solution)/shard_map/ppermute | solution.py:25
  98.4 2.7 %collective-permute-start.14 = (f32[16,512]{1,0:T(8,128)S(1)}, f32[16,512]{1,0:T(8,128)S(1)}, u32[]{:S(2)}, u32[]{:S(2)}) collective-permute-start(f32[16,512]{1,0:T(8,128)S(1)} %fusion.8), channel_id=1, source_target_pairs={{0,128},{128,0},{4,132},{132,4},{8,136},{136,8},{12,140},{140,12},... | collective-permute-start | bytes 98312 | tf_op jit(solution)/shard_map/ppermute | solution.py:25
  101.1 4.3 %collective-permute-done.14 = f32[16,512]{1,0:T(8,128)S(1)} collective-permute-done((f32[16,512]{1,0:T(8,128)S(1)}, f32[16,512]{1,0:T(8,128)S(1)}, u32[]{:S(2)}, u32[]{:S(2)}) %collective-permute-start.14) | collective-permute-done | bytes 32800 | tf_op jit(solution)/shard_map/ppermute | solution.py:25
  108.1 6.5 %collective-permute-done.15 = f32[16,511]{1,0:T(8,128)S(1)} collective-permute-done((f32[16,511]{1,0:T(8,128)S(1)}, f32[16,511]{1,0:T(8,128)S(1)}, u32[]{:S(2)}, u32[]{:S(2)}) %collective-permute-start.15) | collective-permute-done | bytes 32736 | tf_op jit(solution)/shard_map/ppermute | solution.py:15
  117.6 7.9 %collective-permute-done.17 = f32[16,512]{1,0:T(8,128)S(1)} collective-permute-done((f32[16,512]{1,0:T(8,128)S(1)}, f32[16,512]{1,0:T(8,128)S(1)}, u32[]{:S(2)}, u32[]{:S(2)}) %collective-permute-start.17) | collective-permute-done | bytes 32800 | tf_op jit(solution)/shard_map/ppermute | solution.py:25
  129.5 2.0 %collective-permute-done.20 = f32[16,512]{1,0:T(8,128)S(1)} collective-permute-done((f32[16,512]{1,0:T(8,128)S(1)}, f32[16,512]{1,0:T(8,128)S(1)}, u32[]{:S(2)}, u32[]{:S(2)}) %collective-permute-start.20) | collective-permute-done | bytes 32800 | tf_op jit(solution)/shard_map/ppermute | solution.py:15
  131.4 3.4 %collective-permute-done.19 = f32[16,512]{1,0:T(8,128)S(1)} collective-permute-done((f32[16,512]{1,0:T(8,128)S(1)}, f32[16,512]{1,0:T(8,128)S(1)}, u32[]{:S(2)}, u32[]{:S(2)}) %collective-permute-start.19) | collective-permute-done | bytes 32800 | tf_op jit(solution)/shard_map/ppermute | solution.py:15
  134.8 2.5 %collective-permute-done.18 = f32[16,512]{1,0:T(8,128)S(1)} collective-permute-done((f32[16,512]{1,0:T(8,128)S(1)}, f32[16,512]{1,0:T(8,128)S(1)}, u32[]{:S(2)}, u32[]{:S(2)}) %collective-permute-start.18) | collective-permute-done | bytes 32800 | tf_op jit(solution)/shard_map/ppermute | solution.py:15
  139.9 4.3 %collective-permute-done.21 = f32[16,255]{1,0:T(8,128)S(1)} collective-permute-done((f32[16,255]{1,0:T(8,128)S(1)}, f32[16,255]{1,0:T(8,128)S(1)}, u32[]{:S(2)}, u32[]{:S(2)}) %collective-permute-start.21) | collective-permute-done | bytes 16352 | tf_op jit(solution)/shard_map/ppermute | solution.py:15
  145.8 1.9 collective-permute-start.22
  148.9 3.3 %collective-permute-start.23 = (f32[9,512]{1,0:T(8,128)S(1)}, f32[9,512]{1,0:T(8,128)S(1)}, u32[]{:S(2)}, u32[]{:S(2)}) collective-permute-start(f32[9,512]{1,0:T(8,128)S(1)} %max.21), channel_id=1, source_target_pairs={{0,8},{8,0},{4,12},{12,4},{16,24},{24,16},{20,28},{28,20},{32,40},... | collective-permute-start | bytes 55304 | tf_op jit(solution)/shard_map/ppermute | solution.py:25
  152.2 2.5 %collective-permute-done.23 = f32[9,512]{1,0:T(8,128)S(1)} collective-permute-done((f32[9,512]{1,0:T(8,128)S(1)}, f32[9,512]{1,0:T(8,128)S(1)}, u32[]{:S(2)}, u32[]{:S(2)}) %collective-permute-start.23) | collective-permute-done | bytes 18464 | tf_op jit(solution)/shard_map/ppermute | solution.py:25
  154.7 4.6 %collective-permute-start.24 = (f32[9,512]{1,0:T(8,128)S(1)}, f32[9,512]{1,0:T(8,128)S(1)}, u32[]{:S(2)}, u32[]{:S(2)}) collective-permute-start(f32[9,512]{1,0:T(8,128)S(1)} %max.22), channel_id=1, source_target_pairs={{0,16},{16,0},{4,20},{20,4},{8,24},{24,8},{12,28},{28,12},{32,48},... | collective-permute-start | bytes 55304 | tf_op jit(solution)/shard_map/ppermute | solution.py:25
  159.3 2.1 %collective-permute-done.24 = f32[9,512]{1,0:T(8,128)S(1)} collective-permute-done((f32[9,512]{1,0:T(8,128)S(1)}, f32[9,512]{1,0:T(8,128)S(1)}, u32[]{:S(2)}, u32[]{:S(2)}) %collective-permute-start.24) | collective-permute-done | bytes 18464 | tf_op jit(solution)/shard_map/ppermute | solution.py:25
  161.4 8.0 %collective-permute-start.25 = (f32[9,512]{1,0:T(8,128)S(1)}, f32[9,512]{1,0:T(8,128)S(1)}, u32[]{:S(2)}, u32[]{:S(2)}) collective-permute-start(f32[9,512]{1,0:T(8,128)S(1)} %max.23), channel_id=1, source_target_pairs={{0,32},{32,0},{4,36},{36,4},{8,40},{40,8},{12,44},{44,12},{16,48},... | collective-permute-start | bytes 55304 | tf_op jit(solution)/shard_map/ppermute | solution.py:25
  171.3 2.5 %collective-permute-start.26 = (f32[9,512]{1,0:T(8,128)S(1)}, f32[9,512]{1,0:T(8,128)S(1)}, u32[]{:S(2)}, u32[]{:S(2)}) collective-permute-start(f32[9,512]{1,0:T(8,128)S(1)} %max.24), channel_id=1, source_target_pairs={{0,64},{64,0},{4,68},{68,4},{8,72},{72,8},{12,76},{76,12},{16,80},... | collective-permute-start | bytes 55304 | tf_op jit(solution)/shard_map/ppermute | solution.py:25
  173.8 3.3 %collective-permute-done.26 = f32[9,512]{1,0:T(8,128)S(1)} collective-permute-done((f32[9,512]{1,0:T(8,128)S(1)}, f32[9,512]{1,0:T(8,128)S(1)}, u32[]{:S(2)}, u32[]{:S(2)}) %collective-permute-start.26) | collective-permute-done | bytes 18464 | tf_op jit(solution)/shard_map/ppermute | solution.py:25
  177.1 2.2 %collective-permute-start.27 = (f32[9,512]{1,0:T(8,128)S(1)}, f32[9,512]{1,0:T(8,128)S(1)}, u32[]{:S(2)}, u32[]{:S(2)}) collective-permute-start(f32[9,512]{1,0:T(8,128)S(1)} %max.25), channel_id=1, source_target_pairs={{0,128},{128,0},{4,132},{132,4},{8,136},{136,8},{12,140},{140,12},... | collective-permute-start | bytes 55304 | tf_op jit(solution)/shard_map/ppermute | solution.py:25
  179.3 4.8 %collective-permute-done.27 = f32[9,512]{1,0:T(8,128)S(1)} collective-permute-done((f32[9,512]{1,0:T(8,128)S(1)}, f32[9,512]{1,0:T(8,128)S(1)}, u32[]{:S(2)}, u32[]{:S(2)}) %collective-permute-start.27) | collective-permute-done | bytes 18464 | tf_op jit(solution)/shard_map/ppermute | solution.py:25
  186.1 7.9 %collective-permute-done.28 = f32[9,512]{1,0:T(8,128)S(1)} collective-permute-done((f32[9,512]{1,0:T(8,128)S(1)}, f32[9,512]{1,0:T(8,128)S(1)}, u32[]{:S(2)}, u32[]{:S(2)}) %collective-permute-start.28) | collective-permute-done | bytes 18464 | tf_op jit(solution)/shard_map/ppermute | solution.py:25
  (251 shorter events, 54.5 us)
Async XLA Ops:
  0.0 3.1 %copy-start = (s32[4094]{0:T(1024)S(1)}, s32[4094]{0:T(1024)}, u32[]{:S(2)}) copy-start(s32[4094]{0:T(1024)} %param.9) | copy-start | bytes 49132
  1.3 12.3 %collective-permute-start = (f32[8,1,1]{2,0,1:T(8,128)S(1)}, f32[8,1,1]{2,0,1:T(8,128)S(1)}, u32[]{:S(2)}, u32[]{:S(2)}) collective-permute-start(f32[8,1,1]{2,0,1:T(8,128)S(1)} %slice.773), channel_id=1, source_target_pairs={{0,1},{1,2},{2,3},{4,5},{5,6},{6,7},{8,9},{9,10},{10,11},{12,13},{... | collective-permute-start | bytes 104 | tf_op jit(solution)/shard_map/ppermute | solution.py:15
  3.1 0.7 copy-start.1
  13.9 6.1 %collective-permute-start.1 = (f32[4,2,3]{2,1,0:T(2,128)S(1)}, f32[4,2,3]{2,1,0:T(2,128)S(1)}, u32[]{:S(2)}, u32[]{:S(2)}) collective-permute-start(f32[4,2,3]{2,1,0:T(2,128)S(1)} %slice.776), channel_id=1, source_target_pairs={{0,1},{1,2},{2,3},{4,5},{5,6},{6,7},{8,9},{9,10},{10,11},{12,13},{... | collective-permute-start | bytes 296 | tf_op jit(solution)/shard_map/ppermute | solution.py:15
  20.5 5.5 %collective-permute-start.2 = (f32[2,4,7]{2,1,0:T(4,128)S(1)}, f32[2,4,7]{2,1,0:T(4,128)S(1)}, u32[]{:S(2)}, u32[]{:S(2)}) collective-permute-start(f32[2,4,7]{2,1,0:T(4,128)S(1)} %slice.781), channel_id=1, source_target_pairs={{0,1},{1,2},{2,3},{4,5},{5,6},{6,7},{8,9},{9,10},{10,11},{12,13},{... | collective-permute-start | bytes 680 | tf_op jit(solution)/shard_map/ppermute | solution.py:15
  26.4 5.5 %collective-permute-start.3 = (f32[1,8,15]{2,1,0:T(8,128)S(1)}, f32[1,8,15]{2,1,0:T(8,128)S(1)}, u32[]{:S(2)}, u32[]{:S(2)}) collective-permute-start(f32[1,8,15]{2,1,0:T(8,128)S(1)} %slice.789), channel_id=1, source_target_pairs={{0,1},{1,2},{2,3},{4,5},{5,6},{6,7},{8,9},{9,10},{10,11},{12,13},{... | collective-permute-start | bytes 1448 | tf_op jit(solution)/shard_map/ppermute | solution.py:15
  32.4 3.2 %collective-permute-start.4 = (f32[16,512]{1,0:T(8,128)S(1)}, f32[16,512]{1,0:T(8,128)S(1)}, u32[]{:S(2)}, u32[]{:S(2)}) collective-permute-start(f32[16,512]{1,0:T(8,128)S(1)} %fusion.13), channel_id=1, source_target_pairs={{0,4},{4,0},{8,12},{12,8},{16,20},{20,16},{24,28},{28,24},{32,36},... | collective-permute-start | bytes 98312 | tf_op jit(solution)/shard_map/ppermute | solution.py:25
  35.7 5.5 %collective-permute-start.5 = (f32[16,31]{1,0:T(8,128)S(1)}, f32[16,31]{1,0:T(8,128)S(1)}, u32[]{:S(2)}, u32[]{:S(2)}) collective-permute-start(f32[16,31]{1,0:T(8,128)S(1)} %slice.799), channel_id=1, source_target_pairs={{0,1},{1,2},{2,3},{4,5},{5,6},{6,7},{8,9},{9,10},{10,11},{12,13},{... | collective-permute-start | bytes 5960 | tf_op jit(solution)/shard_map/ppermute | solution.py:15
  41.7 6.2 %collective-permute-start.6 = (f32[16,512]{1,0:T(8,128)S(1)}, f32[16,512]{1,0:T(8,128)S(1)}, u32[]{:S(2)}, u32[]{:S(2)}) collective-permute-start(f32[16,512]{1,0:T(8,128)S(1)} %fusion.12), channel_id=1, source_target_pairs={{0,8},{8,0},{4,12},{12,4},{16,24},{24,16},{20,28},{28,20},{32,40},... | collective-permute-start | bytes 98312 | tf_op jit(solution)/shard_map/ppermute | solution.py:25
  48.0 5.5 %collective-permute-start.7 = (f32[16,63]{1,0:T(8,128)S(1)}, f32[16,63]{1,0:T(8,128)S(1)}, u32[]{:S(2)}, u32[]{:S(2)}) collective-permute-start(f32[16,63]{1,0:T(8,128)S(1)} %slice.810), channel_id=1, source_target_pairs={{0,1},{1,2},{2,3},{4,5},{5,6},{6,7},{8,9},{9,10},{10,11},{12,13},{... | collective-permute-start | bytes 12104 | tf_op jit(solution)/shard_map/ppermute | solution.py:15
  54.0 8.0 %collective-permute-start.8 = (f32[16,512]{1,0:T(8,128)S(1)}, f32[16,512]{1,0:T(8,128)S(1)}, u32[]{:S(2)}, u32[]{:S(2)}) collective-permute-start(f32[16,512]{1,0:T(8,128)S(1)} %fusion.11), channel_id=1, source_target_pairs={{0,16},{16,0},{4,20},{20,4},{8,24},{24,8},{12,28},{28,12},{32,48},... | collective-permute-start | bytes 98312 | tf_op jit(solution)/shard_map/ppermute | solution.py:25
  62.1 5.5 %collective-permute-start.9 = (f32[16,127]{1,0:T(8,128)S(1)}, f32[16,127]{1,0:T(8,128)S(1)}, u32[]{:S(2)}, u32[]{:S(2)}) collective-permute-start(f32[16,127]{1,0:T(8,128)S(1)} %slice.823), channel_id=1, source_target_pairs={{0,1},{1,2},{2,3},{4,5},{5,6},{6,7},{8,9},{9,10},{10,11},{12,13},{... | collective-permute-start | bytes 24392 | tf_op jit(solution)/shard_map/ppermute | solution.py:15
  68.2 11.2 %collective-permute-start.10 = (f32[16,512]{1,0:T(8,128)S(1)}, f32[16,512]{1,0:T(8,128)S(1)}, u32[]{:S(2)}, u32[]{:S(2)}) collective-permute-start(f32[16,512]{1,0:T(8,128)S(1)} %fusion.10), channel_id=1, source_target_pairs={{0,32},{32,0},{4,36},{36,4},{8,40},{40,8},{12,44},{44,12},{16,48},... | collective-permute-start | bytes 98312 | tf_op jit(solution)/shard_map/ppermute | solution.py:25
  79.5 5.6 %collective-permute-start.11 = (f32[16,255]{1,0:T(8,128)S(1)}, f32[16,255]{1,0:T(8,128)S(1)}, u32[]{:S(2)}, u32[]{:S(2)}) collective-permute-start(f32[16,255]{1,0:T(8,128)S(1)} %slice.838), channel_id=1, source_target_pairs={{0,1},{1,2},{2,3},{4,5},{5,6},{6,7},{8,9},{9,10},{10,11},{12,13},{... | collective-permute-start | bytes 48968 | tf_op jit(solution)/shard_map/ppermute | solution.py:15
  85.9 5.8 %collective-permute-start.12 = (f32[16,512]{1,0:T(8,128)S(1)}, f32[16,512]{1,0:T(8,128)S(1)}, u32[]{:S(2)}, u32[]{:S(2)}) collective-permute-start(f32[16,512]{1,0:T(8,128)S(1)} %fusion.9), channel_id=1, source_target_pairs={{0,64},{64,0},{4,68},{68,4},{8,72},{72,8},{12,76},{76,12},{16,80},... | collective-permute-start | bytes 98312 | tf_op jit(solution)/shard_map/ppermute | solution.py:25
  91.8 5.8 %collective-permute-start.13 = (f32[16,511]{1,0:T(8,128)S(1)}, f32[16,511]{1,0:T(8,128)S(1)}, u32[]{:S(2)}, u32[]{:S(2)}) collective-permute-start(f32[16,511]{1,0:T(8,128)S(1)} %slice.855), channel_id=1, source_target_pairs={{0,1},{1,2},{2,3},{4,5},{5,6},{6,7},{8,9},{9,10},{10,11},{12,13},{... | collective-permute-start | bytes 98120 | tf_op jit(solution)/shard_map/ppermute | solution.py:15
  98.4 7.0 %collective-permute-start.14 = (f32[16,512]{1,0:T(8,128)S(1)}, f32[16,512]{1,0:T(8,128)S(1)}, u32[]{:S(2)}, u32[]{:S(2)}) collective-permute-start(f32[16,512]{1,0:T(8,128)S(1)} %fusion.8), channel_id=1, source_target_pairs={{0,128},{128,0},{4,132},{132,4},{8,136},{136,8},{12,140},{140,12},... | collective-permute-start | bytes 98312 | tf_op jit(solution)/shard_map/ppermute | solution.py:25
  105.5 9.2 %collective-permute-start.16 = (f32[16,512]{1,0:T(8,128)S(1)}, f32[16,512]{1,0:T(8,128)S(1)}, u32[]{:S(2)}, u32[]{:S(2)}) collective-permute-start(f32[16,512]{1,0:T(8,128)S(1)} %broadcast_select_fusion.5), channel_id=1, source_target_pairs={{0,1},{1,2},{2,3},{4,5},{5,6},{6,7},{8,9},{9,10},{10,11},{12,13},{... | collective-permute-start | bytes 98312 | tf_op jit(solution)/shard_map/ppermute | solution.py:15
  106.8 7.9 %collective-permute-start.15 = (f32[16,511]{1,0:T(8,128)S(1)}, f32[16,511]{1,0:T(8,128)S(1)}, u32[]{:S(2)}, u32[]{:S(2)}) collective-permute-start(f32[16,511]{1,0:T(8,128)S(1)} %slice.874), channel_id=1, source_target_pairs={{0,2},{1,3},{4,6},{5,7},{8,10},{9,11},{12,14},{13,15},{16,18},{17,... | collective-permute-start | bytes 98120 | tf_op jit(solution)/shard_map/ppermute | solution.py:15
  115.7 9.8 %collective-permute-start.17 = (f32[16,512]{1,0:T(8,128)S(1)}, f32[16,512]{1,0:T(8,128)S(1)}, u32[]{:S(2)}, u32[]{:S(2)}) collective-permute-start(f32[16,512]{1,0:T(8,128)S(1)} %fusion.7), channel_id=1, source_target_pairs={{0,256},{256,0},{4,260},{260,4},{8,264},{264,8},{12,268},{268,12},... | collective-permute-start | bytes 98312 | tf_op jit(solution)/shard_map/ppermute | solution.py:25
  125.6 5.9 %collective-permute-start.20 = (f32[16,512]{1,0:T(8,128)S(1)}, f32[16,512]{1,0:T(8,128)S(1)}, u32[]{:S(2)}, u32[]{:S(2)}) collective-permute-start(f32[16,512]{1,0:T(8,128)S(1)} %broadcast_select_fusion.6), channel_id=1, source_target_pairs={{0,1},{1,2},{2,3},{4,5},{5,6},{6,7},{8,9},{9,10},{10,11},{12,13},{... | collective-permute-start | bytes 98312 | tf_op jit(solution)/shard_map/ppermute | solution.py:15
  126.8 7.9 %collective-permute-start.19 = (f32[16,512]{1,0:T(8,128)S(1)}, f32[16,512]{1,0:T(8,128)S(1)}, u32[]{:S(2)}, u32[]{:S(2)}) collective-permute-start(f32[16,512]{1,0:T(8,128)S(1)} %broadcast_select_fusion.6), channel_id=1, source_target_pairs={{0,2},{1,3},{4,6},{5,7},{8,10},{9,11},{12,14},{13,15},{16,18},{17,... | collective-permute-start | bytes 98312 | tf_op jit(solution)/shard_map/ppermute | solution.py:15
  128.1 9.2 %collective-permute-start.18 = (f32[16,512]{1,0:T(8,128)S(1)}, f32[16,512]{1,0:T(8,128)S(1)}, u32[]{:S(2)}, u32[]{:S(2)}) collective-permute-start(f32[16,512]{1,0:T(8,128)S(1)} %broadcast_select_fusion.6), channel_id=1, source_target_pairs={{0,3},{4,7},{8,11},{12,15},{16,19},{20,23},{24,27},{28,31},{32,35}... | collective-permute-start | bytes 98312 | tf_op jit(solution)/shard_map/ppermute | solution.py:15
  138.7 5.6 %collective-permute-start.21 = (f32[16,255]{1,0:T(8,128)S(1)}, f32[16,255]{1,0:T(8,128)S(1)}, u32[]{:S(2)}, u32[]{:S(2)}) collective-permute-start(f32[16,255]{1,0:T(8,128)S(1)} %slice.917), channel_id=1, source_target_pairs={{0,1},{1,2},{2,3},{4,5},{5,6},{6,7},{8,9},{9,10},{10,11},{12,13},{... | collective-permute-start | bytes 48968 | tf_op jit(solution)/shard_map/ppermute | solution.py:15
  145.8 3.1 %collective-permute-start.22 = (f32[9,512]{1,0:T(8,128)S(1)}, f32[9,512]{1,0:T(8,128)S(1)}, u32[]{:S(2)}, u32[]{:S(2)}) collective-permute-start(f32[9,512]{1,0:T(8,128)S(1)} %stack.5), channel_id=1, source_target_pairs={{0,4},{4,0},{8,12},{12,8},{16,20},{20,16},{24,28},{28,24},{32,36},... | collective-permute-start | bytes 55304 | tf_op jit(solution)/shard_map/ppermute | solution.py:25
  148.9 5.8 %collective-permute-start.23 = (f32[9,512]{1,0:T(8,128)S(1)}, f32[9,512]{1,0:T(8,128)S(1)}, u32[]{:S(2)}, u32[]{:S(2)}) collective-permute-start(f32[9,512]{1,0:T(8,128)S(1)} %max.21), channel_id=1, source_target_pairs={{0,8},{8,0},{4,12},{12,4},{16,24},{24,16},{20,28},{28,20},{32,40},... | collective-permute-start | bytes 55304 | tf_op jit(solution)/shard_map/ppermute | solution.py:25
  154.7 6.7 %collective-permute-start.24 = (f32[9,512]{1,0:T(8,128)S(1)}, f32[9,512]{1,0:T(8,128)S(1)}, u32[]{:S(2)}, u32[]{:S(2)}) collective-permute-start(f32[9,512]{1,0:T(8,128)S(1)} %max.22), channel_id=1, source_target_pairs={{0,16},{16,0},{4,20},{20,4},{8,24},{24,8},{12,28},{28,12},{32,48},... | collective-permute-start | bytes 55304 | tf_op jit(solution)/shard_map/ppermute | solution.py:25
  161.4 9.9 %collective-permute-start.25 = (f32[9,512]{1,0:T(8,128)S(1)}, f32[9,512]{1,0:T(8,128)S(1)}, u32[]{:S(2)}, u32[]{:S(2)}) collective-permute-start(f32[9,512]{1,0:T(8,128)S(1)} %max.23), channel_id=1, source_target_pairs={{0,32},{32,0},{4,36},{36,4},{8,40},{40,8},{12,44},{44,12},{16,48},... | collective-permute-start | bytes 55304 | tf_op jit(solution)/shard_map/ppermute | solution.py:25
  171.3 5.8 %collective-permute-start.26 = (f32[9,512]{1,0:T(8,128)S(1)}, f32[9,512]{1,0:T(8,128)S(1)}, u32[]{:S(2)}, u32[]{:S(2)}) collective-permute-start(f32[9,512]{1,0:T(8,128)S(1)} %max.24), channel_id=1, source_target_pairs={{0,64},{64,0},{4,68},{68,4},{8,72},{72,8},{12,76},{76,12},{16,80},... | collective-permute-start | bytes 55304 | tf_op jit(solution)/shard_map/ppermute | solution.py:25
  177.1 7.0 %collective-permute-start.27 = (f32[9,512]{1,0:T(8,128)S(1)}, f32[9,512]{1,0:T(8,128)S(1)}, u32[]{:S(2)}, u32[]{:S(2)}) collective-permute-start(f32[9,512]{1,0:T(8,128)S(1)} %max.25), channel_id=1, source_target_pairs={{0,128},{128,0},{4,132},{132,4},{8,136},{136,8},{12,140},{140,12},... | collective-permute-start | bytes 55304 | tf_op jit(solution)/shard_map/ppermute | solution.py:25
  184.2 9.8 %collective-permute-start.28 = (f32[9,512]{1,0:T(8,128)S(1)}, f32[9,512]{1,0:T(8,128)S(1)}, u32[]{:S(2)}, u32[]{:S(2)}) collective-permute-start(f32[9,512]{1,0:T(8,128)S(1)} %max.26), channel_id=1, source_target_pairs={{0,256},{256,0},{4,260},{260,4},{8,264},{264,8},{12,268},{268,12},... | collective-permute-start | bytes 55304 | tf_op jit(solution)/shard_map/ppermute | solution.py:25

commit v2 on v1

v2 whole, which is shorter than its diff:
```python
import math

import jax
import jax.numpy as jnp
from jax import lax
from jax.sharding import PartitionSpec as P

SUMMED = 32
WIDTHS = 9


def swapped(block, axis, apart):
    count = lax.axis_size(axis)
    route = []
    for low in range(count):
        high = low | 1 << apart
        if high != low and high < count:
            route += [(low, high), (high, low)]
    return lax.ppermute(block, axis, route)


def delay_of(trial_ids, subband_ids, trial_count, low_share, jitter):
    all_trials = low_share.shape[0] + 1
    rate_rows = jnp.take(low_share, all_trials // trial_count - 1 + subband_ids)
    return (trial_ids * rate_rows + jnp.take(jitter, trial_count - 2 + trial_ids)) // 64


def zero_front(rows, width):
    return jnp.pad(rows, [(0, 0)] * (rows.ndim - 1) + [(width, 0)])


def merge_rows(low_rows, high_rows, shifts, need_now):
    offsets = need_now - shifts
    bit_count = max(need_now.bit_length(), 1)
    moved = high_rows
    for bit_index in range(bit_count):
        step_size = 2**bit_index
        cols = moved.shape[-1]
        selected = (offsets >> bit_index & 1)[:, None] == 1
        moved = jnp.where(selected, moved[:, step_size:], moved[:, : cols - step_size])
    return low_rows + moved


def halved_max(block, axis, apart, keep_bit):
    parts = block.shape[-2] // 2
    split = block.reshape(block.shape[:-2] + (2, parts) + block.shape[-1:])
    kept = jnp.where(keep_bit == 1, split[..., 1, :, :], split[..., 0, :, :])
    given = jnp.where(keep_bit == 1, split[..., 0, :, :], split[..., 1, :, :])
    return jnp.maximum(kept, swapped(given, axis, apart))


def shards(spectrogram, low_share, jitter):
    sub_dev = spectrogram.shape[0] // SUMMED
    span_time = spectrogram.shape[1]
    all_trials = low_share.shape[0] + 1
    freq_bits = lax.axis_size("freq").bit_length() - 1
    tm_count = lax.axis_size("tm")
    tm_bits = tm_count.bit_length() - 1
    device = lax.axis_index("freq")
    place = lax.axis_index("tm")
    base = jnp.sum(spectrogram.reshape(sub_dev, SUMMED, span_time), axis=1, dtype=jnp.float32)
    base = lax.all_gather(base, "tm", axis=1, tiled=True)
    full_time = base.shape[1]
    states = base[:, None, :]
    trial_count = 2
    while trial_count <= sub_dev:
        need_now = trial_count - 1
        groups = states.shape[0] // 2
        low_rows = jnp.repeat(states[0::2], 2, axis=1).reshape(groups * trial_count, -1)
        high_rows = jnp.repeat(zero_front(states[1::2], need_now), 2, axis=1).reshape(
            groups * trial_count, -1
        )
        trial_ids = jnp.tile(jnp.arange(trial_count, dtype=jnp.int32), groups)
        subband_ids = device * (sub_dev // trial_count) + jnp.repeat(
            jnp.arange(groups, dtype=jnp.int32), trial_count
        )
        shifts = delay_of(trial_ids, subband_ids, trial_count, low_share, jitter)
        states = merge_rows(low_rows, high_rows, shifts, need_now).reshape(
            groups, trial_count, -1
        )
        trial_count = trial_count * 2
    held = sub_dev // tm_count
    trial_rows = lax.dynamic_slice_in_dim(states[0], place * held, held, axis=0)
    trial_ids = place * held + jnp.arange(held, dtype=jnp.int32)
    for bit_index in range(freq_bits):
        trial_count = sub_dev * 2 ** (bit_index + 1)
        need_now = trial_count - 1
        partner = swapped(trial_rows, "freq", bit_index)
        upper_half = device >> bit_index & 1
        low_rows = jnp.where(upper_half == 1, partner, trial_rows)
        high_rows = jnp.where(upper_half == 1, trial_rows, partner)
        trial_ids = 2 * trial_ids + upper_half
        shifts = delay_of(trial_ids, device >> bit_index + 1, trial_count, low_share, jitter)
        trial_rows = merge_rows(low_rows, zero_front(high_rows, need_now), shifts, need_now)
    signal = trial_rows / math.sqrt(all_trials * SUMMED)
    peak_rows = []
    window_sum = signal
    width_now = 1
    for level_index in range(WIDTHS):
        peak_rows.append(jnp.max(window_sum, axis=0) / math.sqrt(width_now))
        if level_index + 1 < WIDTHS:
            window_sum = window_sum + zero_front(window_sum, width_now)[:, :full_time]
            width_now = width_now * 2
    best = jnp.stack(peak_rows).reshape(WIDTHS, tm_count, span_time)
    for bit_index in reversed(range(tm_bits)):
        best = halved_max(best, "tm", bit_index, place >> bit_index & 1)
    best = best.reshape(WIDTHS, span_time)
    for bit_index in range(freq_bits):
        best = jnp.maximum(best, swapped(best, "freq", bit_index))
    return best


def solution(mesh):
    placed = (P("freq", "tm"), P(), P())
    return jax.shard_map(
        shards, mesh=mesh, in_specs=placed, out_specs=P(None, "tm"), check_vma=False
    )
```

time: 196 us -> 150 us (0.77)
  the two profiles are of different devices: /device:TPU:38 before, /device:TPU:56 now
where the time goes in v2:
time: 150 us
  starting transfers between devices  68 us (45%)
  waiting for transfers between devices  41.3 us (28%)
  local copies, waits for them, and re-layouts  12.9 us (9%)
  blocking collectives  12.3 us (8%)
  other arithmetic  9.19 us (6%)
  between operations  5.86 us (4%)
    ppermute x16, starting transfers between devices, swapped(): return lax.ppermute(block, axis, route)  68 us
    ppermute x16, waiting for transfers between devices, swapped(): return lax.ppermute(block, axis, route)  41.3 us
    all_gather x1, blocking collectives, shards(): base = lax.all_gather(base, 'tm', axis=1, tiled=True)  12.3 us
    gather x11, local copies, waits for them, and re-layouts, delay_of(): jnp.take(jitter, trial_count - 2 + trial_ids)  7.05 us
    select_n x55, other arithmetic, merge_rows(): jnp.where(selected, moved[:, step_size:], moved[:, :cols - step_size])  5.03 us
  transfers between devices with their start and end apart: 16, of which 14 were waited for; matrix products, arithmetic and copies ran while one was open for 4% of the time, Pallas kernels for 0%

profile of v2, /device:TPU:56, one launch (start us, length us, event | category | flops | bytes accessed | tf_op | source)
XLA Modules:
  0.0 149.7 jit_solution(13755305790766001285)
XLA Ops:
  0.0 1.2 convert_reduce_fusion
  1.2 12.3 %all_gather.3 = f32[16,2048]{1,0:T(8,128)S(1)} all-gather(f32[16,512]{1,0:T(8,128)S(1)} %convert_reduce_fusion), channel_id=1, replica_groups=mesh['freq'=128,'tm'=4] {'tm'}, dimensions={1}, use_global_device_ids=true | all-gather | bytes 163840 | tf_op jit(solution)/shard_map/all_gather | solution.py:62
  22.9 1.9 %collective-permute-start = (f32[4,2048]{1,0:T(4,128)S(1)}, f32[4,2048]{1,0:T(4,128)S(1)}, u32[]{:S(2)}, u32[]{:S(2)}) collective-permute-start(f32[4,2048]{1,0:T(4,128)S(1)} %dynamic-slice_add_fusion), channel_id=1, source_target_pairs={{0,4},{4,0},{8,12},{12,8},{16,20},{20,16},{24,28},{28,24},{32,36},... | collective-permute-start | bytes 98312 | tf_op jit(solution)/shard_map/ppermute | solution.py:19
  32.7 4.3 %collective-permute-start.1 = (f32[4,2048]{1,0:T(4,128)S(1)}, f32[4,2048]{1,0:T(4,128)S(1)}, u32[]{:S(2)}, u32[]{:S(2)}) collective-permute-start(f32[4,2048]{1,0:T(4,128)S(1)} %fusion.22), channel_id=1, source_target_pairs={{0,8},{8,0},{4,12},{12,4},{16,24},{24,16},{20,28},{28,20},{32,40},... | collective-permute-start | bytes 98312 | tf_op jit(solution)/shard_map/ppermute | solution.py:19
  37.0 2.0 %collective-permute-done.1 = f32[4,2048]{1,0:T(4,128)S(1)} collective-permute-done((f32[4,2048]{1,0:T(4,128)S(1)}, f32[4,2048]{1,0:T(4,128)S(1)}, u32[]{:S(2)}, u32[]{:S(2)}) %collective-permute-start.1) | collective-permute-done | bytes 32800 | tf_op jit(solution)/shard_map/ppermute | solution.py:19
  39.7 6.1 %collective-permute-start.2 = (f32[4,2048]{1,0:T(4,128)S(1)}, f32[4,2048]{1,0:T(4,128)S(1)}, u32[]{:S(2)}, u32[]{:S(2)}) collective-permute-start(f32[4,2048]{1,0:T(4,128)S(1)} %fusion.21), channel_id=1, source_target_pairs={{0,16},{16,0},{4,20},{20,4},{8,24},{24,8},{12,28},{28,12},{32,48},... | collective-permute-start | bytes 98312 | tf_op jit(solution)/shard_map/ppermute | solution.py:19
  45.8 2.2 %collective-permute-done.2 = f32[4,2048]{1,0:T(4,128)S(1)} collective-permute-done((f32[4,2048]{1,0:T(4,128)S(1)}, f32[4,2048]{1,0:T(4,128)S(1)}, u32[]{:S(2)}, u32[]{:S(2)}) %collective-permute-start.2) | collective-permute-done | bytes 32800 | tf_op jit(solution)/shard_map/ppermute | solution.py:19
  48.6 8.8 %collective-permute-start.3 = (f32[4,2048]{1,0:T(4,128)S(1)}, f32[4,2048]{1,0:T(4,128)S(1)}, u32[]{:S(2)}, u32[]{:S(2)}) collective-permute-start(f32[4,2048]{1,0:T(4,128)S(1)} %fusion.20), channel_id=1, source_target_pairs={{0,32},{32,0},{4,36},{36,4},{8,40},{40,8},{12,44},{44,12},{16,48},... | collective-permute-start | bytes 98312 | tf_op jit(solution)/shard_map/ppermute | solution.py:19
  60.8 3.2 %collective-permute-start.4 = (f32[4,2048]{1,0:T(4,128)S(1)}, f32[4,2048]{1,0:T(4,128)S(1)}, u32[]{:S(2)}, u32[]{:S(2)}) collective-permute-start(f32[4,2048]{1,0:T(4,128)S(1)} %fusion.19), channel_id=1, source_target_pairs={{0,64},{64,0},{4,68},{68,4},{8,72},{72,8},{12,76},{76,12},{16,80},... | collective-permute-start | bytes 98312 | tf_op jit(solution)/shard_map/ppermute | solution.py:19
  64.1 2.5 %collective-permute-done.4 = f32[4,2048]{1,0:T(4,128)S(1)} collective-permute-done((f32[4,2048]{1,0:T(4,128)S(1)}, f32[4,2048]{1,0:T(4,128)S(1)}, u32[]{:S(2)}, u32[]{:S(2)}) %collective-permute-start.4) | collective-permute-done | bytes 32800 | tf_op jit(solution)/shard_map/ppermute | solution.py:19
  67.5 4.0 %collective-permute-start.5 = (f32[4,2048]{1,0:T(4,128)S(1)}, f32[4,2048]{1,0:T(4,128)S(1)}, u32[]{:S(2)}, u32[]{:S(2)}) collective-permute-start(f32[4,2048]{1,0:T(4,128)S(1)} %fusion.18), channel_id=1, source_target_pairs={{0,128},{128,0},{4,132},{132,4},{8,136},{136,8},{12,140},{140,12},... | collective-permute-start | bytes 98312 | tf_op jit(solution)/shard_map/ppermute | solution.py:19
  71.5 2.6 %collective-permute-done.5 = f32[4,2048]{1,0:T(4,128)S(1)} collective-permute-done((f32[4,2048]{1,0:T(4,128)S(1)}, f32[4,2048]{1,0:T(4,128)S(1)}, u32[]{:S(2)}, u32[]{:S(2)}) %collective-permute-start.5) | collective-permute-done | bytes 32800 | tf_op jit(solution)/shard_map/ppermute | solution.py:19
  75.1 4.9 %collective-permute-start.6 = (f32[4,2048]{1,0:T(4,128)S(1)}, f32[4,2048]{1,0:T(4,128)S(1)}, u32[]{:S(2)}, u32[]{:S(2)}) collective-permute-start(f32[4,2048]{1,0:T(4,128)S(1)} %fusion.17), channel_id=1, source_target_pairs={{0,256},{256,0},{4,260},{260,4},{8,264},{264,8},{12,268},{268,12},... | collective-permute-start | bytes 98312 | tf_op jit(solution)/shard_map/ppermute | solution.py:19
  80.1 5.1 %collective-permute-done.6 = f32[4,2048]{1,0:T(4,128)S(1)} collective-permute-done((f32[4,2048]{1,0:T(4,128)S(1)}, f32[4,2048]{1,0:T(4,128)S(1)}, u32[]{:S(2)}, u32[]{:S(2)}) %collective-permute-start.6) | collective-permute-done | bytes 32800 | tf_op jit(solution)/shard_map/ppermute | solution.py:19
  87.3 3.4 %collective-permute-start.7 = (f32[9,2,512]{2,0,1:T(8,128)S(1)}, f32[9,2,512]{2,0,1:T(8,128)S(1)}, u32[]{:S(2)}, u32[]{:S(2)}) collective-permute-start(f32[9,2,512]{2,0,1:T(8,128)S(1)} %select_bitcast_fusion), channel_id=1, source_target_pairs={{0,2},{2,0},{1,3},{3,1},{4,6},{6,4},{5,7},{7,5},{8,10},{10,8},{9,1... | collective-permute-start | bytes 110600 | tf_op jit(solution)/shard_map/ppermute | solution.py:19
  90.7 4.6 %collective-permute-done.7 = f32[9,2,512]{2,0,1:T(8,128)S(1)} collective-permute-done((f32[9,2,512]{2,0,1:T(8,128)S(1)}, f32[9,2,512]{2,0,1:T(8,128)S(1)}, u32[]{:S(2)}, u32[]{:S(2)}) %collective-permute-start.7) | collective-permute-done | bytes 36896 | tf_op jit(solution)/shard_map/ppermute | solution.py:19
  95.3 2.8 %collective-permute-start.8 = (f32[9,1,512]{2,0,1:T(8,128)S(1)}, f32[9,1,512]{2,0,1:T(8,128)S(1)}, u32[]{:S(2)}, u32[]{:S(2)}) collective-permute-start(f32[9,1,512]{2,0,1:T(8,128)S(1)} %select_bitcast_fusion.1), channel_id=1, source_target_pairs={{0,1},{1,0},{2,3},{3,2},{4,5},{5,4},{6,7},{7,6},{8,9},{9,8},{10,11... | collective-permute-start | bytes 55304 | tf_op jit(solution)/shard_map/ppermute | solution.py:19
  98.1 3.0 %collective-permute-done.8 = f32[9,1,512]{2,0,1:T(8,128)S(1)} collective-permute-done((f32[9,1,512]{2,0,1:T(8,128)S(1)}, f32[9,1,512]{2,0,1:T(8,128)S(1)}, u32[]{:S(2)}, u32[]{:S(2)}) %collective-permute-start.8) | collective-permute-done | bytes 18464 | tf_op jit(solution)/shard_map/ppermute | solution.py:19
  101.1 1.9 %collective-permute-start.9 = (f32[9,512]{1,0:T(8,128)S(1)}, f32[9,512]{1,0:T(8,128)S(1)}, u32[]{:S(2)}, u32[]{:S(2)}) collective-permute-start(f32[9,512]{1,0:T(8,128)S(1)} %fusion.23), channel_id=1, source_target_pairs={{0,4},{4,0},{8,12},{12,8},{16,20},{20,16},{24,28},{28,24},{32,36},... | collective-permute-start | bytes 55304 | tf_op jit(solution)/shard_map/ppermute | solution.py:19
  103.1 1.2 collective-permute-done.9
  104.2 3.4 %collective-permute-start.10 = (f32[9,512]{1,0:T(8,128)S(1)}, f32[9,512]{1,0:T(8,128)S(1)}, u32[]{:S(2)}, u32[]{:S(2)}) collective-permute-start(f32[9,512]{1,0:T(8,128)S(1)} %max.29), channel_id=1, source_target_pairs={{0,8},{8,0},{4,12},{12,4},{16,24},{24,16},{20,28},{28,20},{32,40},... | collective-permute-start | bytes 55304 | tf_op jit(solution)/shard_map/ppermute | solution.py:19
  107.6 2.4 %collective-permute-done.10 = f32[9,512]{1,0:T(8,128)S(1)} collective-permute-done((f32[9,512]{1,0:T(8,128)S(1)}, f32[9,512]{1,0:T(8,128)S(1)}, u32[]{:S(2)}, u32[]{:S(2)}) %collective-permute-start.10) | collective-permute-done | bytes 18464 | tf_op jit(solution)/shard_map/ppermute | solution.py:19
  110.0 4.3 %collective-permute-start.11 = (f32[9,512]{1,0:T(8,128)S(1)}, f32[9,512]{1,0:T(8,128)S(1)}, u32[]{:S(2)}, u32[]{:S(2)}) collective-permute-start(f32[9,512]{1,0:T(8,128)S(1)} %max.30), channel_id=1, source_target_pairs={{0,16},{16,0},{4,20},{20,4},{8,24},{24,8},{12,28},{28,12},{32,48},... | collective-permute-start | bytes 55304 | tf_op jit(solution)/shard_map/ppermute | solution.py:19
  114.4 2.4 %collective-permute-done.11 = f32[9,512]{1,0:T(8,128)S(1)} collective-permute-done((f32[9,512]{1,0:T(8,128)S(1)}, f32[9,512]{1,0:T(8,128)S(1)}, u32[]{:S(2)}, u32[]{:S(2)}) %collective-permute-start.11) | collective-permute-done | bytes 18464 | tf_op jit(solution)/shard_map/ppermute | solution.py:19
  116.7 7.1 %collective-permute-start.12 = (f32[9,512]{1,0:T(8,128)S(1)}, f32[9,512]{1,0:T(8,128)S(1)}, u32[]{:S(2)}, u32[]{:S(2)}) collective-permute-start(f32[9,512]{1,0:T(8,128)S(1)} %max.31), channel_id=1, source_target_pairs={{0,32},{32,0},{4,36},{36,4},{8,40},{40,8},{12,44},{44,12},{16,48},... | collective-permute-start | bytes 55304 | tf_op jit(solution)/shard_map/ppermute | solution.py:19
  123.8 2.7 %collective-permute-done.12 = f32[9,512]{1,0:T(8,128)S(1)} collective-permute-done((f32[9,512]{1,0:T(8,128)S(1)}, f32[9,512]{1,0:T(8,128)S(1)}, u32[]{:S(2)}, u32[]{:S(2)}) %collective-permute-start.12) | collective-permute-done | bytes 18464 | tf_op jit(solution)/shard_map/ppermute | solution.py:19
  126.5 2.9 %collective-permute-start.13 = (f32[9,512]{1,0:T(8,128)S(1)}, f32[9,512]{1,0:T(8,128)S(1)}, u32[]{:S(2)}, u32[]{:S(2)}) collective-permute-start(f32[9,512]{1,0:T(8,128)S(1)} %max.32), channel_id=1, source_target_pairs={{0,64},{64,0},{4,68},{68,4},{8,72},{72,8},{12,76},{76,12},{16,80},... | collective-permute-start | bytes 55304 | tf_op jit(solution)/shard_map/ppermute | solution.py:19
  129.4 2.9 %collective-permute-done.13 = f32[9,512]{1,0:T(8,128)S(1)} collective-permute-done((f32[9,512]{1,0:T(8,128)S(1)}, f32[9,512]{1,0:T(8,128)S(1)}, u32[]{:S(2)}, u32[]{:S(2)}) %collective-permute-start.13) | collective-permute-done | bytes 18464 | tf_op jit(solution)/shard_map/ppermute | solution.py:19
  132.3 4.4 %collective-permute-start.14 = (f32[9,512]{1,0:T(8,128)S(1)}, f32[9,512]{1,0:T(8,128)S(1)}, u32[]{:S(2)}, u32[]{:S(2)}) collective-permute-start(f32[9,512]{1,0:T(8,128)S(1)} %max.33), channel_id=1, source_target_pairs={{0,128},{128,0},{4,132},{132,4},{8,136},{136,8},{12,140},{140,12},... | collective-permute-start | bytes 55304 | tf_op jit(solution)/shard_map/ppermute | solution.py:19
  136.7 2.3 %collective-permute-done.14 = f32[9,512]{1,0:T(8,128)S(1)} collective-permute-done((f32[9,512]{1,0:T(8,128)S(1)}, f32[9,512]{1,0:T(8,128)S(1)}, u32[]{:S(2)}, u32[]{:S(2)}) %collective-permute-start.14) | collective-permute-done | bytes 18464 | tf_op jit(solution)/shard_map/ppermute | solution.py:19
  139.0 4.6 %collective-permute-start.15 = (f32[9,512]{1,0:T(8,128)S(1)}, f32[9,512]{1,0:T(8,128)S(1)}, u32[]{:S(2)}, u32[]{:S(2)}) collective-permute-start(f32[9,512]{1,0:T(8,128)S(1)} %max.34), channel_id=1, source_target_pairs={{0,256},{256,0},{4,260},{260,4},{8,264},{264,8},{12,268},{268,12},... | collective-permute-start | bytes 55304 | tf_op jit(solution)/shard_map/ppermute | solution.py:19
  143.6 5.5 %collective-permute-done.15 = f32[9,512]{1,0:T(8,128)S(1)} collective-permute-done((f32[9,512]{1,0:T(8,128)S(1)}, f32[9,512]{1,0:T(8,128)S(1)}, u32[]{:S(2)}, u32[]{:S(2)}) %collective-permute-start.15) | collective-permute-done | bytes 18464 | tf_op jit(solution)/shard_map/ppermute | solution.py:19
  (205 shorter events, 21.0 us)
Async XLA Ops:
  0.0 14.3 %copy-start = (s32[4094]{0:T(1024)S(1)}, s32[4094]{0:T(1024)}, u32[]{:S(2)}) copy-start(s32[4094]{0:T(1024)} %param.11) | copy-start | bytes 49132
  14.3 0.7 copy-start.1
  22.9 9.4 %collective-permute-start = (f32[4,2048]{1,0:T(4,128)S(1)}, f32[4,2048]{1,0:T(4,128)S(1)}, u32[]{:S(2)}, u32[]{:S(2)}) collective-permute-start(f32[4,2048]{1,0:T(4,128)S(1)} %dynamic-slice_add_fusion), channel_id=1, source_target_pairs={{0,4},{4,0},{8,12},{12,8},{16,20},{20,16},{24,28},{28,24},{32,36},... | collective-permute-start | bytes 98312 | tf_op jit(solution)/shard_map/ppermute | solution.py:19
  32.7 6.3 %collective-permute-start.1 = (f32[4,2048]{1,0:T(4,128)S(1)}, f32[4,2048]{1,0:T(4,128)S(1)}, u32[]{:S(2)}, u32[]{:S(2)}) collective-permute-start(f32[4,2048]{1,0:T(4,128)S(1)} %fusion.22), channel_id=1, source_target_pairs={{0,8},{8,0},{4,12},{12,4},{16,24},{24,16},{20,28},{28,20},{32,40},... | collective-permute-start | bytes 98312 | tf_op jit(solution)/shard_map/ppermute | solution.py:19
  39.7 8.3 %collective-permute-start.2 = (f32[4,2048]{1,0:T(4,128)S(1)}, f32[4,2048]{1,0:T(4,128)S(1)}, u32[]{:S(2)}, u32[]{:S(2)}) collective-permute-start(f32[4,2048]{1,0:T(4,128)S(1)} %fusion.21), channel_id=1, source_target_pairs={{0,16},{16,0},{4,20},{20,4},{8,24},{24,8},{12,28},{28,12},{32,48},... | collective-permute-start | bytes 98312 | tf_op jit(solution)/shard_map/ppermute | solution.py:19
  48.6 11.4 %collective-permute-start.3 = (f32[4,2048]{1,0:T(4,128)S(1)}, f32[4,2048]{1,0:T(4,128)S(1)}, u32[]{:S(2)}, u32[]{:S(2)}) collective-permute-start(f32[4,2048]{1,0:T(4,128)S(1)} %fusion.20), channel_id=1, source_target_pairs={{0,32},{32,0},{4,36},{36,4},{8,40},{40,8},{12,44},{44,12},{16,48},... | collective-permute-start | bytes 98312 | tf_op jit(solution)/shard_map/ppermute | solution.py:19
  60.8 5.8 %collective-permute-start.4 = (f32[4,2048]{1,0:T(4,128)S(1)}, f32[4,2048]{1,0:T(4,128)S(1)}, u32[]{:S(2)}, u32[]{:S(2)}) collective-permute-start(f32[4,2048]{1,0:T(4,128)S(1)} %fusion.19), channel_id=1, source_target_pairs={{0,64},{64,0},{4,68},{68,4},{8,72},{72,8},{12,76},{76,12},{16,80},... | collective-permute-start | bytes 98312 | tf_op jit(solution)/shard_map/ppermute | solution.py:19
  67.5 6.7 %collective-permute-start.5 = (f32[4,2048]{1,0:T(4,128)S(1)}, f32[4,2048]{1,0:T(4,128)S(1)}, u32[]{:S(2)}, u32[]{:S(2)}) collective-permute-start(f32[4,2048]{1,0:T(4,128)S(1)} %fusion.18), channel_id=1, source_target_pairs={{0,128},{128,0},{4,132},{132,4},{8,136},{136,8},{12,140},{140,12},... | collective-permute-start | bytes 98312 | tf_op jit(solution)/shard_map/ppermute | solution.py:19
  75.1 10.1 %collective-permute-start.6 = (f32[4,2048]{1,0:T(4,128)S(1)}, f32[4,2048]{1,0:T(4,128)S(1)}, u32[]{:S(2)}, u32[]{:S(2)}) collective-permute-start(f32[4,2048]{1,0:T(4,128)S(1)} %fusion.17), channel_id=1, source_target_pairs={{0,256},{256,0},{4,260},{260,4},{8,264},{264,8},{12,268},{268,12},... | collective-permute-start | bytes 98312 | tf_op jit(solution)/shard_map/ppermute | solution.py:19
  87.3 8.0 %collective-permute-start.7 = (f32[9,2,512]{2,0,1:T(8,128)S(1)}, f32[9,2,512]{2,0,1:T(8,128)S(1)}, u32[]{:S(2)}, u32[]{:S(2)}) collective-permute-start(f32[9,2,512]{2,0,1:T(8,128)S(1)} %select_bitcast_fusion), channel_id=1, source_target_pairs={{0,2},{2,0},{1,3},{3,1},{4,6},{6,4},{5,7},{7,5},{8,10},{10,8},{9,1... | collective-permute-start | bytes 110600 | tf_op jit(solution)/shard_map/ppermute | solution.py:19
  95.3 5.8 %collective-permute-start.8 = (f32[9,1,512]{2,0,1:T(8,128)S(1)}, f32[9,1,512]{2,0,1:T(8,128)S(1)}, u32[]{:S(2)}, u32[]{:S(2)}) collective-permute-start(f32[9,1,512]{2,0,1:T(8,128)S(1)} %select_bitcast_fusion.1), channel_id=1, source_target_pairs={{0,1},{1,0},{2,3},{3,2},{4,5},{5,4},{6,7},{7,6},{8,9},{9,8},{10,11... | collective-permute-start | bytes 55304 | tf_op jit(solution)/shard_map/ppermute | solution.py:19
  101.1 3.1 %collective-permute-start.9 = (f32[9,512]{1,0:T(8,128)S(1)}, f32[9,512]{1,0:T(8,128)S(1)}, u32[]{:S(2)}, u32[]{:S(2)}) collective-permute-start(f32[9,512]{1,0:T(8,128)S(1)} %fusion.23), channel_id=1, source_target_pairs={{0,4},{4,0},{8,12},{12,8},{16,20},{20,16},{24,28},{28,24},{32,36},... | collective-permute-start | bytes 55304 | tf_op jit(solution)/shard_map/ppermute | solution.py:19
  104.2 5.8 %collective-permute-start.10 = (f32[9,512]{1,0:T(8,128)S(1)}, f32[9,512]{1,0:T(8,128)S(1)}, u32[]{:S(2)}, u32[]{:S(2)}) collective-permute-start(f32[9,512]{1,0:T(8,128)S(1)} %max.29), channel_id=1, source_target_pairs={{0,8},{8,0},{4,12},{12,4},{16,24},{24,16},{20,28},{28,20},{32,40},... | collective-permute-start | bytes 55304 | tf_op jit(solution)/shard_map/ppermute | solution.py:19
  110.0 6.7 %collective-permute-start.11 = (f32[9,512]{1,0:T(8,128)S(1)}, f32[9,512]{1,0:T(8,128)S(1)}, u32[]{:S(2)}, u32[]{:S(2)}) collective-permute-start(f32[9,512]{1,0:T(8,128)S(1)} %max.30), channel_id=1, source_target_pairs={{0,16},{16,0},{4,20},{20,4},{8,24},{24,8},{12,28},{28,12},{32,48},... | collective-permute-start | bytes 55304 | tf_op jit(solution)/shard_map/ppermute | solution.py:19
  116.7 9.7 %collective-permute-start.12 = (f32[9,512]{1,0:T(8,128)S(1)}, f32[9,512]{1,0:T(8,128)S(1)}, u32[]{:S(2)}, u32[]{:S(2)}) collective-permute-start(f32[9,512]{1,0:T(8,128)S(1)} %max.31), channel_id=1, source_target_pairs={{0,32},{32,0},{4,36},{36,4},{8,40},{40,8},{12,44},{44,12},{16,48},... | collective-permute-start | bytes 55304 | tf_op jit(solution)/shard_map/ppermute | solution.py:19
  126.5 5.8 %collective-permute-start.13 = (f32[9,512]{1,0:T(8,128)S(1)}, f32[9,512]{1,0:T(8,128)S(1)}, u32[]{:S(2)}, u32[]{:S(2)}) collective-permute-start(f32[9,512]{1,0:T(8,128)S(1)} %max.32), channel_id=1, source_target_pairs={{0,64},{64,0},{4,68},{68,4},{8,72},{72,8},{12,76},{76,12},{16,80},... | collective-permute-start | bytes 55304 | tf_op jit(solution)/shard_map/ppermute | solution.py:19
  132.3 6.7 %collective-permute-start.14 = (f32[9,512]{1,0:T(8,128)S(1)}, f32[9,512]{1,0:T(8,128)S(1)}, u32[]{:S(2)}, u32[]{:S(2)}) collective-permute-start(f32[9,512]{1,0:T(8,128)S(1)} %max.33), channel_id=1, source_target_pairs={{0,128},{128,0},{4,132},{132,4},{8,136},{136,8},{12,140},{140,12},... | collective-permute-start | bytes 55304 | tf_op jit(solution)/shard_map/ppermute | solution.py:19
  139.0 10.1 %collective-permute-start.15 = (f32[9,512]{1,0:T(8,128)S(1)}, f32[9,512]{1,0:T(8,128)S(1)}, u32[]{:S(2)}, u32[]{:S(2)}) collective-permute-start(f32[9,512]{1,0:T(8,128)S(1)} %max.34), channel_id=1, source_target_pairs={{0,256},{256,0},{4,260},{260,4},{8,264},{264,8},{12,268},{268,12},... | collective-permute-start | bytes 55304 | tf_op jit(solution)/shard_map/ppermute | solution.py:19

commit v3 on v2

v3 whole, which is shorter than its diff:
```python
import math

import jax
import jax.numpy as jnp
from jax import lax
from jax.sharding import PartitionSpec as P

SUMMED = 32
WIDTHS = 9
SHARED_LEVELS = 3


def swapped(block, axis, apart):
    count = lax.axis_size(axis)
    route = []
    for low in range(count):
        high = low | 1 << apart
        if high != low and high < count:
            route += [(low, high), (high, low)]
    return lax.ppermute(block, axis, route)


def zero_front(rows, width):
    return jnp.pad(rows, [(0, 0)] * (rows.ndim - 1) + [(width, 0)])


def merge_rows(low_rows, high_rows, shifts, need_now):
    offsets = need_now - shifts
    bit_count = max(need_now.bit_length(), 1)
    moved = high_rows
    for bit_index in range(bit_count):
        step_size = 2**bit_index
        cols = moved.shape[-1]
        selected = (offsets >> bit_index & 1)[:, None] == 1
        moved = jnp.where(selected, moved[:, step_size:], moved[:, : cols - step_size])
    return low_rows + moved


def shards(spectrogram, low_share, jitter):
    sub_dev = spectrogram.shape[0] // SUMMED
    span_time = spectrogram.shape[1]
    all_trials = low_share.shape[0] + 1
    freq_bits = lax.axis_size("freq").bit_length() - 1
    tm_count = lax.axis_size("tm")
    shared = min(SHARED_LEVELS, freq_bits)
    device = lax.axis_index("freq")
    place = lax.axis_index("tm")
    held = sub_dev // tm_count

    rate_index, jitter_index, level_rows = [], [], []
    trial_count = 2
    while trial_count <= sub_dev:
        groups = sub_dev // trial_count
        trial_ids = jnp.tile(jnp.arange(trial_count, dtype=jnp.int32), groups)
        subband_ids = device * groups + jnp.repeat(jnp.arange(groups, dtype=jnp.int32), trial_count)
        rate_index.append(all_trials // trial_count - 1 + subband_ids)
        jitter_index.append(trial_count - 2 + trial_ids)
        level_rows.append(trial_ids)
        trial_count = trial_count * 2
    trial_ids = place * held + jnp.arange(held, dtype=jnp.int32)
    for bit_index in range(freq_bits):
        trial_count = sub_dev * 2 ** (bit_index + 1)
        if bit_index >= freq_bits - shared:
            trial_ids = (2 * trial_ids[:, None] + jnp.arange(2, dtype=jnp.int32)).reshape(-1)
        else:
            trial_ids = 2 * trial_ids + (device >> bit_index & 1)
        subband_ids = jnp.broadcast_to(device >> bit_index + 1, trial_ids.shape)
        rate_index.append(all_trials // trial_count - 1 + subband_ids)
        jitter_index.append(trial_count - 2 + trial_ids)
        level_rows.append(trial_ids)
    rates = jnp.take(low_share, jnp.concatenate(rate_index))
    jitters = jnp.take(jitter, jnp.concatenate(jitter_index))
    ids_all = jnp.concatenate(level_rows)
    shift_table = (ids_all * rates + jitters) // 64
    level_shifts = []
    start = 0
    for rows in level_rows:
        level_shifts.append(shift_table[start : start + rows.shape[0]])
        start = start + rows.shape[0]

    base = jnp.sum(spectrogram.reshape(sub_dev, SUMMED, span_time), axis=1, dtype=jnp.float32)
    spread = jnp.broadcast_to(base[None], (tm_count,) + base.shape)
    gathered = lax.all_to_all(spread, "tm", 0, 0, tiled=True)
    base = jnp.transpose(gathered, (1, 0, 2)).reshape(sub_dev, tm_count * span_time)
    full_time = base.shape[1]
    states = base[:, None, :]
    level = 0
    trial_count = 2
    while trial_count <= sub_dev:
        need_now = trial_count - 1
        groups = states.shape[0] // 2
        low_rows = jnp.repeat(states[0::2], 2, axis=1).reshape(groups * trial_count, -1)
        high_rows = jnp.repeat(zero_front(states[1::2], need_now), 2, axis=1).reshape(
            groups * trial_count, -1
        )
        states = merge_rows(low_rows, high_rows, level_shifts[level], need_now).reshape(
            groups, trial_count, -1
        )
        level = level + 1
        trial_count = trial_count * 2
    trial_rows = lax.dynamic_slice_in_dim(states[0], place * held, held, axis=0)
    for bit_index in range(freq_bits):
        need_now = sub_dev * 2 ** (bit_index + 1) - 1
        partner = swapped(trial_rows, "freq", bit_index)
        upper_half = device >> bit_index & 1
        low_rows = jnp.where(upper_half == 1, partner, trial_rows)
        high_rows = jnp.where(upper_half == 1, trial_rows, partner)
        if bit_index >= freq_bits - shared:
            low_rows = jnp.repeat(low_rows, 2, axis=0)
            high_rows = jnp.repeat(high_rows, 2, axis=0)
        trial_rows = merge_rows(
            low_rows, zero_front(high_rows, need_now), level_shifts[level], need_now
        )
        level = level + 1
    signal = trial_rows / math.sqrt(all_trials * SUMMED)
    peak_rows = []
    window_sum = signal
    width_now = 1
    for level_index in range(WIDTHS):
        peak_rows.append(jnp.max(window_sum, axis=0) / math.sqrt(width_now))
        if level_index + 1 < WIDTHS:
            window_sum = window_sum + zero_front(window_sum, width_now)[:, :full_time]
            width_now = width_now * 2
    best = jnp.stack(peak_rows).reshape(WIDTHS, tm_count, span_time)
    best = jnp.max(lax.all_to_all(best, "tm", 1, 1, tiled=True), axis=1)
    for bit_index in range(freq_bits - shared):
        best = jnp.maximum(best, swapped(best, "freq", bit_index))
    return best


def solution(mesh):
    placed = (P("freq", "tm"), P(), P())
    return jax.shard_map(
        shards, mesh=mesh, in_specs=placed, out_specs=P(None, "tm"), check_vma=False
    )
```

time: 150 us -> 116 us (0.77)
  the two profiles are of different devices: /device:TPU:56 before, /device:TPU:32 now
where the time goes in v3:
time: 116 us; the launch traced here: 115 us
  starting transfers between devices  53 us (46%)
  waiting for transfers between devices  30.1 us (26%)
  other arithmetic  10.8 us (9%)
  blocking collectives  10.6 us (9%)
  local copies, waits for them, and re-layouts  9.15 us (8%)
  between operations  1.27 us (1%)
    ppermute x11, starting transfers between devices, swapped(): return lax.ppermute(block, axis, route)  48.7 us
    ppermute x11, waiting for transfers between devices, swapped(): return lax.ppermute(block, axis, route)  30.1 us
    all_to_all x1, blocking collectives, shards(): best = jnp.max(lax.all_to_all(best, 'tm', 1, 1, tiled=True), axis=1)  10.6 us
    select_n x55, other arithmetic, merge_rows(): jnp.where(selected, moved[:, step_size:], moved[:, :cols - step_size])  6.01 us
    all_to_all x1, starting transfers between devices, shards(): gathered = lax.all_to_all(spread, 'tm', 0, 0, tiled=True)  4.29 us
  transfers between devices with their start and end apart: 12, of which 11 were waited for; matrix products, arithmetic and copies ran while one was open for 5% of the time, Pallas kernels for 0%

profile of v3, /device:TPU:32, one launch (start us, length us, event | category | flops | bytes accessed | tf_op | source)
XLA Modules:
  0.0 114.9 jit_solution(15293913375291359807)
XLA Ops:
  0.0 1.2 %convert_reduce_fusion = f32[16,512]{1,0:T(8,128)S(1)} fusion(bf16[512,512]{1,0:T(8,128)(2,1)} %param.3), kind=kLoop, calls=%fused_computation.2 | loop fusion | flops 516096 | bytes 557056 | tf_op jit(solution)/shard_map/reduce_sum | solution.py:81
  1.2 0.7 broadcast_in_dim.679
  1.9 4.3 %all-to-all-start = ((f32[4,16,512]{2,1,0:T(8,128)}), f32[4,16,512]{2,1,0:T(8,128)S(1)}, u32[]{:S(2)}, u32[]{:S(2)}) async-start(f32[4,16,512]{2,1,0:T(8,128)} %broadcast_in_dim.679), calls=%async_computation | async-start | bytes 262144 | tf_op jit(solution)/shard_map/all_to_all | solution.py:83
  8.1 0.7 copy-done.1
  8.7 1.4 %gather_fusion = s32[136]{0:T(256)S(1)} fusion(s32[2047]{0:T(1024)S(1)} %copy-done.1, s32[1024]{0:T(1024)S(1)} %pad_clamp_fusion.1), kind=kCustom, calls=%fused_computation | custom fusion | bytes 1632 | tf_op jit(solution)/shard_map/jit(_take)/gather | solution.py:71
  10.2 1.4 %gather_fusion.1 = s32[136]{0:T(256)S(1)} fusion(s32[4094]{0:T(1024)S(1)} %copy-done, s32[1024]{0:T(1024)S(1)} %pad_clamp_fusion), kind=kCustom, calls=%fused_computation.1 | custom fusion | bytes 1632 | tf_op jit(solution)/shard_map/jit(_take)/gather | solution.py:72
  15.4 1.9 %collective-permute-start = (f32[4,2048]{1,0:T(4,128)S(1)}, f32[4,2048]{1,0:T(4,128)S(1)}, u32[]{:S(2)}, u32[]{:S(2)}) collective-permute-start(f32[4,2048]{1,0:T(4,128)S(1)} %dynamic-slice_add_fusion), channel_id=1, source_target_pairs={{0,4},{4,0},{8,12},{12,8},{16,20},{20,16},{24,28},{28,24},{32,36},... | collective-permute-start | bytes 98312 | tf_op jit(solution)/shard_map/ppermute | solution.py:20
  17.4 1.1 collective-permute-done
  19.0 4.3 %collective-permute-start.1 = (f32[4,2048]{1,0:T(4,128)S(1)}, f32[4,2048]{1,0:T(4,128)S(1)}, u32[]{:S(2)}, u32[]{:S(2)}) collective-permute-start(f32[4,2048]{1,0:T(4,128)S(1)} %fusion.22), channel_id=1, source_target_pairs={{0,8},{8,0},{4,12},{12,4},{16,24},{24,16},{20,28},{28,20},{32,40},... | collective-permute-start | bytes 98312 | tf_op jit(solution)/shard_map/ppermute | solution.py:20
  23.4 1.8 %collective-permute-done.1 = f32[4,2048]{1,0:T(4,128)S(1)} collective-permute-done((f32[4,2048]{1,0:T(4,128)S(1)}, f32[4,2048]{1,0:T(4,128)S(1)}, u32[]{:S(2)}, u32[]{:S(2)}) %collective-permute-start.1) | collective-permute-done | bytes 32800 | tf_op jit(solution)/shard_map/ppermute | solution.py:20
  25.8 6.1 %collective-permute-start.2 = (f32[4,2048]{1,0:T(4,128)S(1)}, f32[4,2048]{1,0:T(4,128)S(1)}, u32[]{:S(2)}, u32[]{:S(2)}) collective-permute-start(f32[4,2048]{1,0:T(4,128)S(1)} %fusion.21), channel_id=1, source_target_pairs={{0,16},{16,0},{4,20},{20,4},{8,24},{24,8},{12,28},{28,12},{32,48},... | collective-permute-start | bytes 98312 | tf_op jit(solution)/shard_map/ppermute | solution.py:20
  31.9 2.0 %collective-permute-done.2 = f32[4,2048]{1,0:T(4,128)S(1)} collective-permute-done((f32[4,2048]{1,0:T(4,128)S(1)}, f32[4,2048]{1,0:T(4,128)S(1)}, u32[]{:S(2)}, u32[]{:S(2)}) %collective-permute-start.2) | collective-permute-done | bytes 32800 | tf_op jit(solution)/shard_map/ppermute | solution.py:20
  34.6 9.2 %collective-permute-start.3 = (f32[4,2048]{1,0:T(4,128)S(1)}, f32[4,2048]{1,0:T(4,128)S(1)}, u32[]{:S(2)}, u32[]{:S(2)}) collective-permute-start(f32[4,2048]{1,0:T(4,128)S(1)} %fusion.20), channel_id=1, source_target_pairs={{0,32},{32,0},{4,36},{36,4},{8,40},{40,8},{12,44},{44,12},{16,48},... | collective-permute-start | bytes 98312 | tf_op jit(solution)/shard_map/ppermute | solution.py:20
  43.8 1.9 %collective-permute-done.3 = f32[4,2048]{1,0:T(4,128)S(1)} collective-permute-done((f32[4,2048]{1,0:T(4,128)S(1)}, f32[4,2048]{1,0:T(4,128)S(1)}, u32[]{:S(2)}, u32[]{:S(2)}) %collective-permute-start.3) | collective-permute-done | bytes 32800 | tf_op jit(solution)/shard_map/ppermute | solution.py:20
  46.4 2.6 %collective-permute-start.4 = (f32[4,2048]{1,0:T(4,128)S(1)}, f32[4,2048]{1,0:T(4,128)S(1)}, u32[]{:S(2)}, u32[]{:S(2)}) collective-permute-start(f32[4,2048]{1,0:T(4,128)S(1)} %fusion.19), channel_id=1, source_target_pairs={{0,64},{64,0},{4,68},{68,4},{8,72},{72,8},{12,76},{76,12},{16,80},... | collective-permute-start | bytes 98312 | tf_op jit(solution)/shard_map/ppermute | solution.py:20
  49.1 3.1 %collective-permute-done.4 = f32[4,2048]{1,0:T(4,128)S(1)} collective-permute-done((f32[4,2048]{1,0:T(4,128)S(1)}, f32[4,2048]{1,0:T(4,128)S(1)}, u32[]{:S(2)}, u32[]{:S(2)}) %collective-permute-start.4) | collective-permute-done | bytes 32800 | tf_op jit(solution)/shard_map/ppermute | solution.py:20
  53.3 2.7 %collective-permute-start.5 = (f32[8,2048]{1,0:T(8,128)S(1)}, f32[8,2048]{1,0:T(8,128)S(1)}, u32[]{:S(2)}, u32[]{:S(2)}) collective-permute-start(f32[8,2048]{1,0:T(8,128)S(1)} %fusion.18), channel_id=1, source_target_pairs={{0,128},{128,0},{4,132},{132,4},{8,136},{136,8},{12,140},{140,12},... | collective-permute-start | bytes 196616 | tf_op jit(solution)/shard_map/ppermute | solution.py:20
  56.0 5.1 %collective-permute-done.5 = f32[8,2048]{1,0:T(8,128)S(1)} collective-permute-done((f32[8,2048]{1,0:T(8,128)S(1)}, f32[8,2048]{1,0:T(8,128)S(1)}, u32[]{:S(2)}, u32[]{:S(2)}) %collective-permute-start.5) | collective-permute-done | bytes 65568 | tf_op jit(solution)/shard_map/ppermute | solution.py:20
  62.5 3.0 %collective-permute-start.6 = (f32[16,2048]{1,0:T(8,128)S(1)}, f32[16,2048]{1,0:T(8,128)S(1)}, u32[]{:S(2)}, u32[]{:S(2)}) collective-permute-start(f32[16,2048]{1,0:T(8,128)S(1)} %fusion.13), channel_id=1, source_target_pairs={{0,256},{256,0},{4,260},{260,4},{8,264},{264,8},{12,268},{268,12},... | collective-permute-start | bytes 393224 | tf_op jit(solution)/shard_map/ppermute | solution.py:20
  65.6 8.2 %collective-permute-done.6 = f32[16,2048]{1,0:T(8,128)S(1)} collective-permute-done((f32[16,2048]{1,0:T(8,128)S(1)}, f32[16,2048]{1,0:T(8,128)S(1)}, u32[]{:S(2)}, u32[]{:S(2)}) %collective-permute-start.6) | collective-permute-done | bytes 131104 | tf_op jit(solution)/shard_map/ppermute | solution.py:20
  74.5 0.2 fusion
  75.1 0.2 slice_select_fusion.2
  77.7 10.6 %all_to_all.10 = f32[9,4,512]{2,0,1:T(8,128)S(1)} all-to-all(f32[9,4,512]{2,0,1:T(8,128)S(1)} %stack.5), channel_id=1, replica_groups=mesh['freq'=128,'tm'=4] {'tm'}, dimensions={1} | all-to-all | bytes 147456 | tf_op jit(solution)/shard_map/all_to_all | solution.py:125
  88.3 1.9 %collective-permute-start.7 = (f32[9,512]{1,0:T(8,128)S(1)}, f32[9,512]{1,0:T(8,128)S(1)}, u32[]{:S(2)}, u32[]{:S(2)}) collective-permute-start(f32[9,512]{1,0:T(8,128)S(1)} %reduce_max.99), channel_id=1, source_target_pairs={{0,4},{4,0},{8,12},{12,8},{16,20},{20,16},{24,28},{28,24},{32,36},... | collective-permute-start | bytes 55304 | tf_op jit(solution)/shard_map/ppermute | solution.py:20
  90.2 1.2 %collective-permute-done.7 = f32[9,512]{1,0:T(8,128)S(1)} collective-permute-done((f32[9,512]{1,0:T(8,128)S(1)}, f32[9,512]{1,0:T(8,128)S(1)}, u32[]{:S(2)}, u32[]{:S(2)}) %collective-permute-start.7) | collective-permute-done | bytes 18464 | tf_op jit(solution)/shard_map/ppermute | solution.py:20
  91.4 3.8 %collective-permute-start.8 = (f32[9,512]{1,0:T(8,128)S(1)}, f32[9,512]{1,0:T(8,128)S(1)}, u32[]{:S(2)}, u32[]{:S(2)}) collective-permute-start(f32[9,512]{1,0:T(8,128)S(1)} %max.12), channel_id=1, source_target_pairs={{0,8},{8,0},{4,12},{12,4},{16,24},{24,16},{20,28},{28,20},{32,40},... | collective-permute-start | bytes 55304 | tf_op jit(solution)/shard_map/ppermute | solution.py:20
  95.2 2.0 %collective-permute-done.8 = f32[9,512]{1,0:T(8,128)S(1)} collective-permute-done((f32[9,512]{1,0:T(8,128)S(1)}, f32[9,512]{1,0:T(8,128)S(1)}, u32[]{:S(2)}, u32[]{:S(2)}) %collective-permute-start.8) | collective-permute-done | bytes 18464 | tf_op jit(solution)/shard_map/ppermute | solution.py:20
  97.2 5.0 %collective-permute-start.9 = (f32[9,512]{1,0:T(8,128)S(1)}, f32[9,512]{1,0:T(8,128)S(1)}, u32[]{:S(2)}, u32[]{:S(2)}) collective-permute-start(f32[9,512]{1,0:T(8,128)S(1)} %max.13), channel_id=1, source_target_pairs={{0,16},{16,0},{4,20},{20,4},{8,24},{24,8},{12,28},{28,12},{32,48},... | collective-permute-start | bytes 55304 | tf_op jit(solution)/shard_map/ppermute | solution.py:20
  102.3 1.9 %collective-permute-done.9 = f32[9,512]{1,0:T(8,128)S(1)} collective-permute-done((f32[9,512]{1,0:T(8,128)S(1)}, f32[9,512]{1,0:T(8,128)S(1)}, u32[]{:S(2)}, u32[]{:S(2)}) %collective-permute-start.9) | collective-permute-done | bytes 18464 | tf_op jit(solution)/shard_map/ppermute | solution.py:20
  104.2 8.3 %collective-permute-start.10 = (f32[9,512]{1,0:T(8,128)S(1)}, f32[9,512]{1,0:T(8,128)S(1)}, u32[]{:S(2)}, u32[]{:S(2)}) collective-permute-start(f32[9,512]{1,0:T(8,128)S(1)} %max.14), channel_id=1, source_target_pairs={{0,32},{32,0},{4,36},{36,4},{8,40},{40,8},{12,44},{44,12},{16,48},... | collective-permute-start | bytes 55304 | tf_op jit(solution)/shard_map/ppermute | solution.py:20
  112.4 1.9 %collective-permute-done.10 = f32[9,512]{1,0:T(8,128)S(1)} collective-permute-done((f32[9,512]{1,0:T(8,128)S(1)}, f32[9,512]{1,0:T(8,128)S(1)}, u32[]{:S(2)}, u32[]{:S(2)}) %collective-permute-start.10) | collective-permute-done | bytes 18464 | tf_op jit(solution)/shard_map/ppermute | solution.py:20
  114.3 0.6 max.15
  (207 shorter events, 13.6 us)
Async XLA Ops:
  0.0 10.2 %copy-start = (s32[4094]{0:T(1024)S(1)}, s32[4094]{0:T(1024)}, u32[]{:S(2)}) copy-start(s32[4094]{0:T(1024)} %param.5) | copy-start | bytes 49132
  1.9 10.3 %all-to-all-start = ((f32[4,16,512]{2,1,0:T(8,128)}), f32[4,16,512]{2,1,0:T(8,128)S(1)}, u32[]{:S(2)}, u32[]{:S(2)}) async-start(f32[4,16,512]{2,1,0:T(8,128)} %broadcast_in_dim.679), calls=%async_computation | async-start | bytes 262144 | tf_op jit(solution)/shard_map/all_to_all | solution.py:83
  8.0 0.7 copy-start.1
  15.4 3.1 %collective-permute-start = (f32[4,2048]{1,0:T(4,128)S(1)}, f32[4,2048]{1,0:T(4,128)S(1)}, u32[]{:S(2)}, u32[]{:S(2)}) collective-permute-start(f32[4,2048]{1,0:T(4,128)S(1)} %dynamic-slice_add_fusion), channel_id=1, source_target_pairs={{0,4},{4,0},{8,12},{12,8},{16,20},{20,16},{24,28},{28,24},{32,36},... | collective-permute-start | bytes 98312 | tf_op jit(solution)/shard_map/ppermute | solution.py:20
  19.0 6.2 %collective-permute-start.1 = (f32[4,2048]{1,0:T(4,128)S(1)}, f32[4,2048]{1,0:T(4,128)S(1)}, u32[]{:S(2)}, u32[]{:S(2)}) collective-permute-start(f32[4,2048]{1,0:T(4,128)S(1)} %fusion.22), channel_id=1, source_target_pairs={{0,8},{8,0},{4,12},{12,4},{16,24},{24,16},{20,28},{28,20},{32,40},... | collective-permute-start | bytes 98312 | tf_op jit(solution)/shard_map/ppermute | solution.py:20
  25.8 8.1 %collective-permute-start.2 = (f32[4,2048]{1,0:T(4,128)S(1)}, f32[4,2048]{1,0:T(4,128)S(1)}, u32[]{:S(2)}, u32[]{:S(2)}) collective-permute-start(f32[4,2048]{1,0:T(4,128)S(1)} %fusion.21), channel_id=1, source_target_pairs={{0,16},{16,0},{4,20},{20,4},{8,24},{24,8},{12,28},{28,12},{32,48},... | collective-permute-start | bytes 98312 | tf_op jit(solution)/shard_map/ppermute | solution.py:20
  34.6 11.1 %collective-permute-start.3 = (f32[4,2048]{1,0:T(4,128)S(1)}, f32[4,2048]{1,0:T(4,128)S(1)}, u32[]{:S(2)}, u32[]{:S(2)}) collective-permute-start(f32[4,2048]{1,0:T(4,128)S(1)} %fusion.20), channel_id=1, source_target_pairs={{0,32},{32,0},{4,36},{36,4},{8,40},{40,8},{12,44},{44,12},{16,48},... | collective-permute-start | bytes 98312 | tf_op jit(solution)/shard_map/ppermute | solution.py:20
  46.4 5.8 %collective-permute-start.4 = (f32[4,2048]{1,0:T(4,128)S(1)}, f32[4,2048]{1,0:T(4,128)S(1)}, u32[]{:S(2)}, u32[]{:S(2)}) collective-permute-start(f32[4,2048]{1,0:T(4,128)S(1)} %fusion.19), channel_id=1, source_target_pairs={{0,64},{64,0},{4,68},{68,4},{8,72},{72,8},{12,76},{76,12},{16,80},... | collective-permute-start | bytes 98312 | tf_op jit(solution)/shard_map/ppermute | solution.py:20
  53.3 7.8 %collective-permute-start.5 = (f32[8,2048]{1,0:T(8,128)S(1)}, f32[8,2048]{1,0:T(8,128)S(1)}, u32[]{:S(2)}, u32[]{:S(2)}) collective-permute-start(f32[8,2048]{1,0:T(8,128)S(1)} %fusion.18), channel_id=1, source_target_pairs={{0,128},{128,0},{4,132},{132,4},{8,136},{136,8},{12,140},{140,12},... | collective-permute-start | bytes 196616 | tf_op jit(solution)/shard_map/ppermute | solution.py:20
  62.5 11.3 %collective-permute-start.6 = (f32[16,2048]{1,0:T(8,128)S(1)}, f32[16,2048]{1,0:T(8,128)S(1)}, u32[]{:S(2)}, u32[]{:S(2)}) collective-permute-start(f32[16,2048]{1,0:T(8,128)S(1)} %fusion.13), channel_id=1, source_target_pairs={{0,256},{256,0},{4,260},{260,4},{8,264},{264,8},{12,268},{268,12},... | collective-permute-start | bytes 393224 | tf_op jit(solution)/shard_map/ppermute | solution.py:20
  88.3 3.1 %collective-permute-start.7 = (f32[9,512]{1,0:T(8,128)S(1)}, f32[9,512]{1,0:T(8,128)S(1)}, u32[]{:S(2)}, u32[]{:S(2)}) collective-permute-start(f32[9,512]{1,0:T(8,128)S(1)} %reduce_max.99), channel_id=1, source_target_pairs={{0,4},{4,0},{8,12},{12,8},{16,20},{20,16},{24,28},{28,24},{32,36},... | collective-permute-start | bytes 55304 | tf_op jit(solution)/shard_map/ppermute | solution.py:20
  91.4 5.8 %collective-permute-start.8 = (f32[9,512]{1,0:T(8,128)S(1)}, f32[9,512]{1,0:T(8,128)S(1)}, u32[]{:S(2)}, u32[]{:S(2)}) collective-permute-start(f32[9,512]{1,0:T(8,128)S(1)} %max.12), channel_id=1, source_target_pairs={{0,8},{8,0},{4,12},{12,4},{16,24},{24,16},{20,28},{28,20},{32,40},... | collective-permute-start | bytes 55304 | tf_op jit(solution)/shard_map/ppermute | solution.py:20
  97.2 6.9 %collective-permute-start.9 = (f32[9,512]{1,0:T(8,128)S(1)}, f32[9,512]{1,0:T(8,128)S(1)}, u32[]{:S(2)}, u32[]{:S(2)}) collective-permute-start(f32[9,512]{1,0:T(8,128)S(1)} %max.13), channel_id=1, source_target_pairs={{0,16},{16,0},{4,20},{20,4},{8,24},{24,8},{12,28},{28,12},{32,48},... | collective-permute-start | bytes 55304 | tf_op jit(solution)/shard_map/ppermute | solution.py:20
  104.2 10.2 %collective-permute-start.10 = (f32[9,512]{1,0:T(8,128)S(1)}, f32[9,512]{1,0:T(8,128)S(1)}, u32[]{:S(2)}, u32[]{:S(2)}) collective-permute-start(f32[9,512]{1,0:T(8,128)S(1)} %max.14), channel_id=1, source_target_pairs={{0,32},{32,0},{4,36},{36,4},{8,40},{40,8},{12,44},{44,12},{16,48},... | collective-permute-start | bytes 55304 | tf_op jit(solution)/shard_map/ppermute | solution.py:20

commit v4 on v3

--- a/solution.py
+++ b/solution.py
@@ -1,5 +1,6 @@
 import math
 
+import numpy as np
 import jax
 import jax.numpy as jnp
 from jax import lax
@@ -8,6 +9,7 @@
 SUMMED = 32
 WIDTHS = 9
 SHARED_LEVELS = 3
+NEAR_HALF = (6, 7, 4, 5, 2, 3, 0, 1)
 
 
 def swapped(block, axis, apart):
@@ -18,6 +20,18 @@
         if high != low and high < count:
             route += [(low, high), (high, low)]
     return lax.ppermute(block, axis, route)
+
+
+def paired(block, axis, partner_of):
+    return lax.ppermute(block, axis, [(partner_of(i), i) for i in range(lax.axis_size(axis))])
+
+
+def near_half(bit_index, ring_bits):
+    def partner_of(i):
+        ring = i >> ring_bits & 7
+        return i - (ring << ring_bits) + (NEAR_HALF[ring] << ring_bits)
+
+    return partner_of
 
 
 def zero_front(rows, width):
@@ -36,6 +50,56 @@
     return low_rows + moved
 
 
+def delay_plan(sub_dev, held, freq_bits, shared, all_trials):
+    terms = 2 + freq_bits
+    ids, rates, jits, level_rows = [], [], [], []
+    trial_count = 2
+    while trial_count <= sub_dev:
+        groups = sub_dev // trial_count
+        rows = groups * trial_count
+        trial = np.tile(np.arange(trial_count), groups)
+        group = np.repeat(np.arange(groups), trial_count)
+        one_id = np.zeros((terms, rows), np.int64)
+        one_id[0] = trial
+        one_rate = np.zeros((terms, rows), np.int64)
+        one_rate[0] = all_trials // trial_count - 1 + group
+        for bit in range(freq_bits):
+            one_rate[2 + bit] = groups << bit
+        ids.append(one_id)
+        rates.append(one_rate)
+        level_rows.append(rows)
+        trial_count = trial_count * 2
+    now = np.zeros((terms, held), np.int64)
+    now[0] = np.arange(held)
+    now[1] = held
+    for bit_index in range(freq_bits):
+        trial_count = sub_dev * 2 ** (bit_index + 1)
+        if bit_index >= freq_bits - shared:
+            now = 2 * np.repeat(now, 2, axis=1)
+            now[0] = now[0] + np.tile(np.arange(2), now.shape[1] // 2)
+        else:
+            now = 2 * now
+            now[2 + bit_index] = now[2 + bit_index] + 1
+        one_rate = np.zeros_like(now)
+        one_rate[0] = all_trials // trial_count - 1
+        for bit in range(bit_index + 1, freq_bits):
+            one_rate[2 + bit] = 1 << (bit - bit_index - 1)
+        ids.append(now.copy())
+        rates.append(one_rate)
+        level_rows.append(now.shape[1])
+    counts = []
+    trial_count = 2
+    while trial_count <= sub_dev:
+        counts.append(trial_count)
+        trial_count = trial_count * 2
+    counts += [sub_dev * 2 ** (bit_index + 1) for bit_index in range(freq_bits)]
+    jit_rows = [one_id.copy() for one_id in ids]
+    for one_jit, trial_count in zip(jit_rows, counts):
+        one_jit[0] = one_jit[0] + trial_count - 2
+    pack = lambda parts: np.concatenate(parts, axis=1).astype(np.int32)
+    return pack(ids), pack(rates), pack(jit_rows), level_rows
+
+
 def shards(spectrogram, low_share, jitter):
     sub_dev = spectrogram.shape[0] // SUMMED
     span_time = spectrogram.shape[1]
@@ -47,36 +111,22 @@
     place = lax.axis_index("tm")
     held = sub_dev // tm_count
 
-    rate_index, jitter_index, level_rows = [], [], []
-    trial_count = 2
-    while trial_count <= sub_dev:
-        groups = sub_dev // trial_count
-        trial_ids = jnp.tile(jnp.arange(trial_count, dtype=jnp.int32), groups)
-        subband_ids = device * groups + jnp.repeat(jnp.arange(groups, dtype=jnp.int32), trial_count)
-        rate_index.append(all_trials // trial_count - 1 + subband_ids)
-        jitter_index.append(trial_count - 2 + trial_ids)
-        level_rows.append(trial_ids)
-        trial_count = trial_count * 2
-    trial_ids = place * held + jnp.arange(held, dtype=jnp.int32)
-    for bit_index in range(freq_bits):
-        trial_count = sub_dev * 2 ** (bit_index + 1)
-        if bit_index >= freq_bits - shared:
-            trial_ids = (2 * trial_ids[:, None] + jnp.arange(2, dtype=jnp.int32)).reshape(-1)
-        else:
-            trial_ids = 2 * trial_ids + (device >> bit_index & 1)
-        subband_ids = jnp.broadcast_to(device >> bit_index + 1, trial_ids.shape)
-        rate_index.append(all_trials // trial_count - 1 + subband_ids)
-        jitter_index.append(trial_count - 2 + trial_ids)
-        level_rows.append(trial_ids)
-    rates = jnp.take(low_share, jnp.concatenate(rate_index))
-    jitters = jnp.take(jitter, jnp.concatenate(jitter_index))
-    ids_all = jnp.concatenate(level_rows)
+    id_terms, rate_terms, jitter_terms, level_rows = delay_plan(
+        sub_dev, held, freq_bits, shared, all_trials
+    )
+    factors = jnp.concatenate(
+        [jnp.ones((1,), jnp.int32), place[None].astype(jnp.int32),
+         (device >> jnp.arange(freq_bits, dtype=jnp.int32) & 1).astype(jnp.int32)]
+    )[:, None]
+    ids_all = jnp.sum(factors * id_terms, axis=0)
+    rates = jnp.take(low_share, jnp.sum(factors * rate_terms, axis=0))
+    jitters = jnp.take(jitter, jnp.sum(factors * jitter_terms, axis=0))
     shift_table = (ids_all * rates + jitters) // 64
     level_shifts = []
     start = 0
     for rows in level_rows:
-        level_shifts.append(shift_table[start : start + rows.shape[0]])
-        start = start + rows.shape[0]
+        level_shifts.append(shift_table[start : start + rows])
+        start = start + rows
 
     base = jnp.sum(spectrogram.reshape(sub_dev, SUMMED, span_time), axis=1, dtype=jnp.float32)
     spread = jnp.broadcast_to(base[None], (tm_count,) + base.shape)
@@ -101,7 +151,10 @@
     trial_rows = lax.dynamic_slice_in_dim(states[0], place * held, held, axis=0)
     for bit_index in range(freq_bits):
         need_now = sub_dev * 2 ** (bit_index + 1) - 1
-        partner = swapped(trial_rows, "freq", bit_index)
+        if bit_index == freq_bits - 1 and shared >= 3 and bit_index >= 2:
+            partner = paired(trial_rows, "freq", near_half(bit_index, bit_index - 2))
+        else:
+            partner = swapped(trial_rows, "freq", bit_index)
         upper_half = device >> bit_index & 1
         low_rows = jnp.where(upper_half == 1, partner, trial_rows)
         high_rows = jnp.where(upper_half == 1, trial_rows, partner)
@@ -124,7 +177,10 @@
     best = jnp.stack(peak_rows).reshape(WIDTHS, tm_count, span_time)
     best = jnp.max(lax.all_to_all(best, "tm", 1, 1, tiled=True), axis=1)
     for bit_index in range(freq_bits - shared):
-        best = jnp.maximum(best, swapped(best, "freq", bit_index))
+        if bit_index == 3:
+            best = jnp.maximum(best, paired(best, "freq", near_half(bit_index, 1)))
+        else:
+            best = jnp.maximum(best, swapped(best, "freq", bit_index))
     return best
 
 

time: 116 us -> 113 us (0.974)
  the two profiles are of different devices: /device:TPU:32 before, /device:TPU:16 now
where the time goes in v4:
time: 113 us; the launch traced here: 112 us
  starting transfers between devices  57.3 us (51%)
  waiting for transfers between devices  25.7 us (23%)
  other arithmetic  10.8 us (10%)
  blocking collectives  9.3 us (8%)
  local copies, waits for them, and re-layouts  8.08 us (7%)
    ppermute x9, starting transfers between devices, swapped(): return lax.ppermute(block, axis, route)  38.2 us
    ppermute x9, waiting for transfers between devices, swapped(): return lax.ppermute(block, axis, route)  18.3 us
    ppermute x2, starting transfers between devices, paired(): lax.ppermute(block, axis, [(partner_of(i), i) for i in range(lax.axis_siz...  14.6 us
    all_to_all x1, blocking collectives, shards(): best = jnp.max(lax.all_to_all(best, 'tm', 1, 1, tiled=True), axis=1)  9.3 us
    ppermute x2, waiting for transfers between devices, paired(): lax.ppermute(block, axis, [(partner_of(i), i) for i in range(lax.axis_siz...  6.14 us
    select_n x55, other arithmetic, merge_rows(): jnp.where(selected, moved[:, step_size:], moved[:, :cols - step_size])  6.01 us
    all_to_all x1, starting transfers between devices, shards(): gathered = lax.all_to_all(spread, 'tm', 0, 0, tiled=True)  4.42 us
  transfers between devices with their start and end apart: 12, of which 12 were waited for; matrix products, arithmetic and copies ran while one was open for 3% of the time, Pallas kernels for 0%

profile of v4, /device:TPU:16, one launch (start us, length us, event | category | flops | bytes accessed | tf_op | source)
XLA Modules:
  0.0 112.3 jit_solution(5312839576611575569)
XLA Ops:
  0.0 1.2 %convert_reduce_fusion = f32[16,512]{1,0:T(8,128)S(1)} fusion(bf16[512,512]{1,0:T(8,128)(2,1)} %param.6), kind=kLoop, calls=%fused_computation.2 | loop fusion | flops 516096 | bytes 557056 | tf_op jit(solution)/shard_map/reduce_sum | solution.py:131
  1.2 0.6 broadcast_in_dim.639
  1.8 4.4 %all-to-all-start = ((f32[4,16,512]{2,1,0:T(8,128)}), f32[4,16,512]{2,1,0:T(8,128)S(1)}, u32[]{:S(2)}, u32[]{:S(2)}) async-start(f32[4,16,512]{2,1,0:T(8,128)} %broadcast_in_dim.639), calls=%async_computation | async-start | bytes 262144 | tf_op jit(solution)/shard_map/all_to_all | solution.py:133
  6.4 0.6 copy-done.2
  7.1 0.7 copy-done.1
  7.8 1.4 %gather_fusion = s32[136]{0:T(256)S(1)} fusion(s32[2047]{0:T(1024)S(1)} %copy-done.1, s32[1024]{0:T(1024)S(1)} %pad_clamp_fusion.1), kind=kCustom, calls=%fused_computation | custom fusion | bytes 1632 | tf_op jit(solution)/shard_map/jit(_take)/gather | solution.py:122
  9.2 1.4 %gather_fusion.1 = s32[136]{0:T(256)S(1)} fusion(s32[4094]{0:T(1024)S(1)} %copy-done, s32[1024]{0:T(1024)S(1)} %pad_clamp_fusion), kind=kCustom, calls=%fused_computation.1 | custom fusion | bytes 1632 | tf_op jit(solution)/shard_map/jit(_take)/gather | solution.py:123
  11.0 1.3 %all-to-all-done = f32[4,16,512]{2,1,0:T(8,128)S(1)} async-done(((f32[4,16,512]{2,1,0:T(8,128)}), f32[4,16,512]{2,1,0:T(8,128)S(1)}, u32[]{:S(2)}, u32[]{:S(2)}) %all-to-all-start) | async-done | bytes 131104 | tf_op jit(solution)/shard_map/all_to_all | solution.py:133
  15.5 1.9 %collective-permute-start = (f32[4,2048]{1,0:T(4,128)S(1)}, f32[4,2048]{1,0:T(4,128)S(1)}, u32[]{:S(2)}, u32[]{:S(2)}) collective-permute-start(f32[4,2048]{1,0:T(4,128)S(1)} %dynamic-slice_add_fusion), channel_id=1, source_target_pairs={{0,4},{4,0},{8,12},{12,8},{16,20},{20,16},{24,28},{28,24},{32,36},... | collective-permute-start | bytes 98312 | tf_op jit(solution)/shard_map/ppermute | solution.py:22
  17.5 1.1 collective-permute-done
  19.1 4.3 %collective-permute-start.1 = (f32[4,2048]{1,0:T(4,128)S(1)}, f32[4,2048]{1,0:T(4,128)S(1)}, u32[]{:S(2)}, u32[]{:S(2)}) collective-permute-start(f32[4,2048]{1,0:T(4,128)S(1)} %fusion.22), channel_id=1, source_target_pairs={{0,8},{8,0},{4,12},{12,4},{16,24},{24,16},{20,28},{28,20},{32,40},... | collective-permute-start | bytes 98312 | tf_op jit(solution)/shard_map/ppermute | solution.py:22
  23.5 1.8 %collective-permute-done.1 = f32[4,2048]{1,0:T(4,128)S(1)} collective-permute-done((f32[4,2048]{1,0:T(4,128)S(1)}, f32[4,2048]{1,0:T(4,128)S(1)}, u32[]{:S(2)}, u32[]{:S(2)}) %collective-permute-start.1) | collective-permute-done | bytes 32800 | tf_op jit(solution)/shard_map/ppermute | solution.py:22
  25.9 6.1 %collective-permute-start.2 = (f32[4,2048]{1,0:T(4,128)S(1)}, f32[4,2048]{1,0:T(4,128)S(1)}, u32[]{:S(2)}, u32[]{:S(2)}) collective-permute-start(f32[4,2048]{1,0:T(4,128)S(1)} %fusion.21), channel_id=1, source_target_pairs={{0,16},{16,0},{4,20},{20,4},{8,24},{24,8},{12,28},{28,12},{32,48},... | collective-permute-start | bytes 98312 | tf_op jit(solution)/shard_map/ppermute | solution.py:22
  32.0 2.0 %collective-permute-done.2 = f32[4,2048]{1,0:T(4,128)S(1)} collective-permute-done((f32[4,2048]{1,0:T(4,128)S(1)}, f32[4,2048]{1,0:T(4,128)S(1)}, u32[]{:S(2)}, u32[]{:S(2)}) %collective-permute-start.2) | collective-permute-done | bytes 32800 | tf_op jit(solution)/shard_map/ppermute | solution.py:22
  34.7 9.2 %collective-permute-start.3 = (f32[4,2048]{1,0:T(4,128)S(1)}, f32[4,2048]{1,0:T(4,128)S(1)}, u32[]{:S(2)}, u32[]{:S(2)}) collective-permute-start(f32[4,2048]{1,0:T(4,128)S(1)} %fusion.20), channel_id=1, source_target_pairs={{0,32},{32,0},{4,36},{36,4},{8,40},{40,8},{12,44},{44,12},{16,48},... | collective-permute-start | bytes 98312 | tf_op jit(solution)/shard_map/ppermute | solution.py:22
  43.9 1.9 %collective-permute-done.3 = f32[4,2048]{1,0:T(4,128)S(1)} collective-permute-done((f32[4,2048]{1,0:T(4,128)S(1)}, f32[4,2048]{1,0:T(4,128)S(1)}, u32[]{:S(2)}, u32[]{:S(2)}) %collective-permute-start.3) | collective-permute-done | bytes 32800 | tf_op jit(solution)/shard_map/ppermute | solution.py:22
  46.5 3.5 %collective-permute-start.4 = (f32[4,2048]{1,0:T(4,128)S(1)}, f32[4,2048]{1,0:T(4,128)S(1)}, u32[]{:S(2)}, u32[]{:S(2)}) collective-permute-start(f32[4,2048]{1,0:T(4,128)S(1)} %fusion.19), channel_id=1, source_target_pairs={{0,64},{64,0},{4,68},{68,4},{8,72},{72,8},{12,76},{76,12},{16,80},... | collective-permute-start | bytes 98312 | tf_op jit(solution)/shard_map/ppermute | solution.py:22
  50.1 2.2 %collective-permute-done.4 = f32[4,2048]{1,0:T(4,128)S(1)} collective-permute-done((f32[4,2048]{1,0:T(4,128)S(1)}, f32[4,2048]{1,0:T(4,128)S(1)}, u32[]{:S(2)}, u32[]{:S(2)}) %collective-permute-start.4) | collective-permute-done | bytes 32800 | tf_op jit(solution)/shard_map/ppermute | solution.py:22
  53.4 3.5 %collective-permute-start.5 = (f32[8,2048]{1,0:T(8,128)S(1)}, f32[8,2048]{1,0:T(8,128)S(1)}, u32[]{:S(2)}, u32[]{:S(2)}) collective-permute-start(f32[8,2048]{1,0:T(8,128)S(1)} %fusion.18), channel_id=1, source_target_pairs={{0,128},{128,0},{4,132},{132,4},{8,136},{136,8},{12,140},{140,12},... | collective-permute-start | bytes 196616 | tf_op jit(solution)/shard_map/ppermute | solution.py:22
  56.8 3.6 %collective-permute-done.5 = f32[8,2048]{1,0:T(8,128)S(1)} collective-permute-done((f32[8,2048]{1,0:T(8,128)S(1)}, f32[8,2048]{1,0:T(8,128)S(1)}, u32[]{:S(2)}, u32[]{:S(2)}) %collective-permute-start.5) | collective-permute-done | bytes 65568 | tf_op jit(solution)/shard_map/ppermute | solution.py:22
  61.9 6.3 %collective-permute-start.6 = (f32[16,2048]{1,0:T(8,128)S(1)}, f32[16,2048]{1,0:T(8,128)S(1)}, u32[]{:S(2)}, u32[]{:S(2)}) collective-permute-start(f32[16,2048]{1,0:T(8,128)S(1)} %fusion.13), channel_id=1, source_target_pairs={{384,0},{388,4},{392,8},{396,12},{400,16},{404,20},{408,24},{412,2... | collective-permute-start | bytes 393224 | tf_op jit(solution)/shard_map/ppermute | solution.py:26
  68.4 4.2 %collective-permute-done.6 = f32[16,2048]{1,0:T(8,128)S(1)} collective-permute-done((f32[16,2048]{1,0:T(8,128)S(1)}, f32[16,2048]{1,0:T(8,128)S(1)}, u32[]{:S(2)}, u32[]{:S(2)}) %collective-permute-start.6) | collective-permute-done | bytes 131104 | tf_op jit(solution)/shard_map/ppermute | solution.py:26
  76.6 9.3 %all_to_all.10 = f32[9,4,512]{2,0,1:T(8,128)S(1)} all-to-all(f32[9,4,512]{2,0,1:T(8,128)S(1)} %stack.5), channel_id=1, replica_groups=mesh['freq'=128,'tm'=4] {'tm'}, dimensions={1} | all-to-all | bytes 147456 | tf_op jit(solution)/shard_map/all_to_all | solution.py:178
  85.9 1.9 %collective-permute-start.7 = (f32[9,512]{1,0:T(8,128)S(1)}, f32[9,512]{1,0:T(8,128)S(1)}, u32[]{:S(2)}, u32[]{:S(2)}) collective-permute-start(f32[9,512]{1,0:T(8,128)S(1)} %reduce_max.99), channel_id=1, source_target_pairs={{0,4},{4,0},{8,12},{12,8},{16,20},{20,16},{24,28},{28,24},{32,36},... | collective-permute-start | bytes 55304 | tf_op jit(solution)/shard_map/ppermute | solution.py:22
  87.8 1.2 %collective-permute-done.7 = f32[9,512]{1,0:T(8,128)S(1)} collective-permute-done((f32[9,512]{1,0:T(8,128)S(1)}, f32[9,512]{1,0:T(8,128)S(1)}, u32[]{:S(2)}, u32[]{:S(2)}) %collective-permute-start.7) | collective-permute-done | bytes 18464 | tf_op jit(solution)/shard_map/ppermute | solution.py:22
  89.0 3.3 %collective-permute-start.8 = (f32[9,512]{1,0:T(8,128)S(1)}, f32[9,512]{1,0:T(8,128)S(1)}, u32[]{:S(2)}, u32[]{:S(2)}) collective-permute-start(f32[9,512]{1,0:T(8,128)S(1)} %max.12), channel_id=1, source_target_pairs={{0,8},{8,0},{4,12},{12,4},{16,24},{24,16},{20,28},{28,20},{32,40},... | collective-permute-start | bytes 55304 | tf_op jit(solution)/shard_map/ppermute | solution.py:22
  92.3 2.4 %collective-permute-done.8 = f32[9,512]{1,0:T(8,128)S(1)} collective-permute-done((f32[9,512]{1,0:T(8,128)S(1)}, f32[9,512]{1,0:T(8,128)S(1)}, u32[]{:S(2)}, u32[]{:S(2)}) %collective-permute-start.8) | collective-permute-done | bytes 18464 | tf_op jit(solution)/shard_map/ppermute | solution.py:22
  94.8 4.6 %collective-permute-start.9 = (f32[9,512]{1,0:T(8,128)S(1)}, f32[9,512]{1,0:T(8,128)S(1)}, u32[]{:S(2)}, u32[]{:S(2)}) collective-permute-start(f32[9,512]{1,0:T(8,128)S(1)} %max.13), channel_id=1, source_target_pairs={{0,16},{16,0},{4,20},{20,4},{8,24},{24,8},{12,28},{28,12},{32,48},... | collective-permute-start | bytes 55304 | tf_op jit(solution)/shard_map/ppermute | solution.py:22
  99.4 2.1 %collective-permute-done.9 = f32[9,512]{1,0:T(8,128)S(1)} collective-permute-done((f32[9,512]{1,0:T(8,128)S(1)}, f32[9,512]{1,0:T(8,128)S(1)}, u32[]{:S(2)}, u32[]{:S(2)}) %collective-permute-start.9) | collective-permute-done | bytes 18464 | tf_op jit(solution)/shard_map/ppermute | solution.py:22
  101.5 8.3 %collective-permute-start.10 = (f32[9,512]{1,0:T(8,128)S(1)}, f32[9,512]{1,0:T(8,128)S(1)}, u32[]{:S(2)}, u32[]{:S(2)}) collective-permute-start(f32[9,512]{1,0:T(8,128)S(1)} %max.14), channel_id=1, source_target_pairs={{48,0},{52,4},{56,8},{60,12},{32,16},{36,20},{40,24},{44,28},{16,3... | collective-permute-start | bytes 55304 | tf_op jit(solution)/shard_map/ppermute | solution.py:26
  109.8 1.9 %collective-permute-done.10 = f32[9,512]{1,0:T(8,128)S(1)} collective-permute-done((f32[9,512]{1,0:T(8,128)S(1)}, f32[9,512]{1,0:T(8,128)S(1)}, u32[]{:S(2)}, u32[]{:S(2)}) %collective-permute-start.10) | collective-permute-done | bytes 18464 | tf_op jit(solution)/shard_map/ppermute | solution.py:26
  111.7 0.6 max.15
  (158 shorter events, 12.2 us)
Async XLA Ops:
  0.0 9.2 %copy-start = (s32[4094]{0:T(1024)S(1)}, s32[4094]{0:T(1024)}, u32[]{:S(2)}) copy-start(s32[4094]{0:T(1024)} %param.8) | copy-start | bytes 49132
  1.8 4.5 %copy-start.3 = (s32[9,136]{1,0:T(8,128)S(1)}, s32[9,136]{1,0:T(8,128)}, u32[]{:S(2)}) copy-start(s32[9,136]{1,0:T(8,128)} %constant.84.clone) | copy-start | bytes 14692
  1.8 4.5 %copy-start.4 = (s32[9,136]{1,0:T(8,128)S(1)}, s32[9,136]{1,0:T(8,128)}, u32[]{:S(2)}) copy-start(s32[9,136]{1,0:T(8,128)} %constant.83.clone) | copy-start | bytes 14692
  1.8 10.4 %all-to-all-start = ((f32[4,16,512]{2,1,0:T(8,128)}), f32[4,16,512]{2,1,0:T(8,128)S(1)}, u32[]{:S(2)}, u32[]{:S(2)}) async-start(f32[4,16,512]{2,1,0:T(8,128)} %broadcast_in_dim.639), calls=%async_computation | async-start | bytes 262144 | tf_op jit(solution)/shard_map/all_to_all | solution.py:133
  6.3 0.7 copy-start.2
  7.1 0.7 copy-start.1
  15.5 3.1 %collective-permute-start = (f32[4,2048]{1,0:T(4,128)S(1)}, f32[4,2048]{1,0:T(4,128)S(1)}, u32[]{:S(2)}, u32[]{:S(2)}) collective-permute-start(f32[4,2048]{1,0:T(4,128)S(1)} %dynamic-slice_add_fusion), channel_id=1, source_target_pairs={{0,4},{4,0},{8,12},{12,8},{16,20},{20,16},{24,28},{28,24},{32,36},... | collective-permute-start | bytes 98312 | tf_op jit(solution)/shard_map/ppermute | solution.py:22
  19.1 6.2 %collective-permute-start.1 = (f32[4,2048]{1,0:T(4,128)S(1)}, f32[4,2048]{1,0:T(4,128)S(1)}, u32[]{:S(2)}, u32[]{:S(2)}) collective-permute-start(f32[4,2048]{1,0:T(4,128)S(1)} %fusion.22), channel_id=1, source_target_pairs={{0,8},{8,0},{4,12},{12,4},{16,24},{24,16},{20,28},{28,20},{32,40},... | collective-permute-start | bytes 98312 | tf_op jit(solution)/shard_map/ppermute | solution.py:22
  25.9 8.1 %collective-permute-start.2 = (f32[4,2048]{1,0:T(4,128)S(1)}, f32[4,2048]{1,0:T(4,128)S(1)}, u32[]{:S(2)}, u32[]{:S(2)}) collective-permute-start(f32[4,2048]{1,0:T(4,128)S(1)} %fusion.21), channel_id=1, source_target_pairs={{0,16},{16,0},{4,20},{20,4},{8,24},{24,8},{12,28},{28,12},{32,48},... | collective-permute-start | bytes 98312 | tf_op jit(solution)/shard_map/ppermute | solution.py:22
  34.7 11.1 %collective-permute-start.3 = (f32[4,2048]{1,0:T(4,128)S(1)}, f32[4,2048]{1,0:T(4,128)S(1)}, u32[]{:S(2)}, u32[]{:S(2)}) collective-permute-start(f32[4,2048]{1,0:T(4,128)S(1)} %fusion.20), channel_id=1, source_target_pairs={{0,32},{32,0},{4,36},{36,4},{8,40},{40,8},{12,44},{44,12},{16,48},... | collective-permute-start | bytes 98312 | tf_op jit(solution)/shard_map/ppermute | solution.py:22
  46.5 5.8 %collective-permute-start.4 = (f32[4,2048]{1,0:T(4,128)S(1)}, f32[4,2048]{1,0:T(4,128)S(1)}, u32[]{:S(2)}, u32[]{:S(2)}) collective-permute-start(f32[4,2048]{1,0:T(4,128)S(1)} %fusion.19), channel_id=1, source_target_pairs={{0,64},{64,0},{4,68},{68,4},{8,72},{72,8},{12,76},{76,12},{16,80},... | collective-permute-start | bytes 98312 | tf_op jit(solution)/shard_map/ppermute | solution.py:22
  53.4 7.1 %collective-permute-start.5 = (f32[8,2048]{1,0:T(8,128)S(1)}, f32[8,2048]{1,0:T(8,128)S(1)}, u32[]{:S(2)}, u32[]{:S(2)}) collective-permute-start(f32[8,2048]{1,0:T(8,128)S(1)} %fusion.18), channel_id=1, source_target_pairs={{0,128},{128,0},{4,132},{132,4},{8,136},{136,8},{12,140},{140,12},... | collective-permute-start | bytes 196616 | tf_op jit(solution)/shard_map/ppermute | solution.py:22
  61.9 10.7 %collective-permute-start.6 = (f32[16,2048]{1,0:T(8,128)S(1)}, f32[16,2048]{1,0:T(8,128)S(1)}, u32[]{:S(2)}, u32[]{:S(2)}) collective-permute-start(f32[16,2048]{1,0:T(8,128)S(1)} %fusion.13), channel_id=1, source_target_pairs={{384,0},{388,4},{392,8},{396,12},{400,16},{404,20},{408,24},{412,2... | collective-permute-start | bytes 393224 | tf_op jit(solution)/shard_map/ppermute | solution.py:26
  85.9 3.1 %collective-permute-start.7 = (f32[9,512]{1,0:T(8,128)S(1)}, f32[9,512]{1,0:T(8,128)S(1)}, u32[]{:S(2)}, u32[]{:S(2)}) collective-permute-start(f32[9,512]{1,0:T(8,128)S(1)} %reduce_max.99), channel_id=1, source_target_pairs={{0,4},{4,0},{8,12},{12,8},{16,20},{20,16},{24,28},{28,24},{32,36},... | collective-permute-start | bytes 55304 | tf_op jit(solution)/shard_map/ppermute | solution.py:22
  89.0 5.8 %collective-permute-start.8 = (f32[9,512]{1,0:T(8,128)S(1)}, f32[9,512]{1,0:T(8,128)S(1)}, u32[]{:S(2)}, u32[]{:S(2)}) collective-permute-start(f32[9,512]{1,0:T(8,128)S(1)} %max.12), channel_id=1, source_target_pairs={{0,8},{8,0},{4,12},{12,4},{16,24},{24,16},{20,28},{28,20},{32,40},... | collective-permute-start | bytes 55304 | tf_op jit(solution)/shard_map/ppermute | solution.py:22
  94.8 6.7 %collective-permute-start.9 = (f32[9,512]{1,0:T(8,128)S(1)}, f32[9,512]{1,0:T(8,128)S(1)}, u32[]{:S(2)}, u32[]{:S(2)}) collective-permute-start(f32[9,512]{1,0:T(8,128)S(1)} %max.13), channel_id=1, source_target_pairs={{0,16},{16,0},{4,20},{20,4},{8,24},{24,8},{12,28},{28,12},{32,48},... | collective-permute-start | bytes 55304 | tf_op jit(solution)/shard_map/ppermute | solution.py:22
  101.5 10.2 %collective-permute-start.10 = (f32[9,512]{1,0:T(8,128)S(1)}, f32[9,512]{1,0:T(8,128)S(1)}, u32[]{:S(2)}, u32[]{:S(2)}) collective-permute-start(f32[9,512]{1,0:T(8,128)S(1)} %max.14), channel_id=1, source_target_pairs={{48,0},{52,4},{56,8},{60,12},{32,16},{36,20},{40,24},{44,28},{16,3... | collective-permute-start | bytes 55304 | tf_op jit(solution)/shard_map/ppermute | solution.py:26

commit v5 on v4

--- a/solution.py
+++ b/solution.py
@@ -1,9 +1,12 @@
+import functools
 import math
 
 import numpy as np
 import jax
 import jax.numpy as jnp
 from jax import lax
+from jax.experimental import pallas as pl
+from jax.experimental.pallas import tpu as pltpu
 from jax.sharding import PartitionSpec as P
 
 SUMMED = 32
@@ -38,16 +41,25 @@
     return jnp.pad(rows, [(0, 0)] * (rows.ndim - 1) + [(width, 0)])
 
 
+def merge_kernel(bit_count, shift_ref, low_ref, high_ref, out_ref):
+    shifts = shift_ref[...]
+    moved = high_ref[...]
+    for bit_index in range(bit_count):
+        rolled = pltpu.roll(moved, 1 << bit_index, 1)
+        moved = jnp.where((shifts >> bit_index & 1) == 1, rolled, moved)
+    col = lax.broadcasted_iota(jnp.int32, moved.shape, 1)
+    out_ref[...] = low_ref[...] + jnp.where(col >= shifts, moved, 0.0)
+
+
 def merge_rows(low_rows, high_rows, shifts, need_now):
-    offsets = need_now - shifts
-    bit_count = max(need_now.bit_length(), 1)
-    moved = high_rows
-    for bit_index in range(bit_count):
-        step_size = 2**bit_index
-        cols = moved.shape[-1]
-        selected = (offsets >> bit_index & 1)[:, None] == 1
-        moved = jnp.where(selected, moved[:, step_size:], moved[:, : cols - step_size])
-    return low_rows + moved
+    rows, cols = low_rows.shape
+    return pl.pallas_call(
+        functools.partial(merge_kernel, max(need_now.bit_length(), 1)),
+        out_shape=jax.ShapeDtypeStruct((rows, cols), jnp.float32),
+        cost_estimate=pl.CostEstimate(
+            flops=rows * cols * 24, transcendentals=0, bytes_accessed=rows * cols * 12
+        ),
+    )(shifts[:, None].astype(jnp.int32), low_rows, high_rows)
 
 
 def delay_plan(sub_dev, held, freq_bits, shared, all_trials):
@@ -140,7 +152,7 @@
         need_now = trial_count - 1
         groups = states.shape[0] // 2
         low_rows = jnp.repeat(states[0::2], 2, axis=1).reshape(groups * trial_count, -1)
-        high_rows = jnp.repeat(zero_front(states[1::2], need_now), 2, axis=1).reshape(
+        high_rows = jnp.repeat(states[1::2], 2, axis=1).reshape(
             groups * trial_count, -1
         )
         states = merge_rows(low_rows, high_rows, level_shifts[level], need_now).reshape(
@@ -161,9 +173,7 @@
         if bit_index >= freq_bits - shared:
             low_rows = jnp.repeat(low_rows, 2, axis=0)
             high_rows = jnp.repeat(high_rows, 2, axis=0)
-        trial_rows = merge_rows(
-            low_rows, zero_front(high_rows, need_now), level_shifts[level], need_now
-        )
+        trial_rows = merge_rows(low_rows, high_rows, level_shifts[level], need_now)
         level = level + 1
     signal = trial_rows / math.sqrt(all_trials * SUMMED)
     peak_rows = []

time: 113 us -> 154 us (1.36)
  Pallas kernels: 0 us -> 22.6 us
  local copies, waits for them, and re-layouts: 8.08 us -> 27.7 us
  waiting for transfers between devices: 25.7 us -> 21.2 us
    pallas_call x0 -> x11, Pallas kernels: none -> 22.6 us  [merge_rows(): pl.pallas_call(functools.partial(merge_kernel, max(need_now.bit_length(),...]
    broadcast_in_dim x5 -> x20, local copies, waits for them, and re-layouts: 0.3 us -> 8.6 us  [the longest x15 7.66 us: merge_rows(): shifts[:, None].astype(jnp.int32)]
    select_n x7, other arithmetic: 0.08 us -> 8.17 us  [shards(): high_rows = jnp.where(upper_half == 1, trial_rows, partner)]
    select_n x55 -> x1, other arithmetic: 6.01 us -> 0.01 us  [shards(): rates = jnp.take(low_share, jnp.sum(factors * rate_terms, axis=0))]
    ppermute x9, waiting for transfers between devices: 18.3 us -> 15.5 us  [swapped(): return lax.ppermute(block, axis, route)]
    reshape x3, local copies, waits for them, and re-layouts: 0.32 us -> 2.29 us  [shards(): high_rows = jnp.repeat(high_rows, 2, axis=0)]
    reshape x3, local copies, waits for them, and re-layouts: 0.32 us -> 2.27 us  [shards(): low_rows = jnp.repeat(low_rows, 2, axis=0)]
    another operation x3, local copies, waits for them, and re-layouts: 0.29 us -> 2.23 us  [shards(): jnp.repeat(states[1::2], 2, axis=1).reshape(groups * trial_count, -1)]
  transfers between devices with their start and end apart: 12 -> 12, of which waited for: 12 -> 11; matrix products, arithmetic and copies ran while one was open for 3% -> 7% of each run, Pallas kernels for 0% -> 0%
where the time goes in v5:
time: 154 us; the launch traced here: 152 us
  starting transfers between devices  57.3 us (37%)
  local copies, waits for them, and re-layouts  27.7 us (18%)
  Pallas kernels  22.6 us (15%)
  waiting for transfers between devices  21.2 us (14%)
  other arithmetic  12.3 us (8%)
  blocking collectives  10.6 us (7%)
    ppermute x9, starting transfers between devices, swapped(): return lax.ppermute(block, axis, route)  38.2 us
    pallas_call x11, Pallas kernels, merge_rows(): pl.pallas_call(functools.partial(merge_kernel, max(need_now.bit_length(),...  22.6 us
    ppermute x9, waiting for transfers between devices, swapped(): return lax.ppermute(block, axis, route)  15.5 us
    ppermute x2, starting transfers between devices, paired(): lax.ppermute(block, axis, [(partner_of(i), i) for i in range(lax.axis_siz...  14.6 us
    all_to_all x1, blocking collectives, shards(): best = jnp.max(lax.all_to_all(best, 'tm', 1, 1, tiled=True), axis=1)  10.6 us
    select_n x7, other arithmetic, shards(): high_rows = jnp.where(upper_half == 1, trial_rows, partner)  8.17 us
    broadcast_in_dim x15, local copies, waits for them, and re-layouts, merge_rows(): shifts[:, None].astype(jnp.int32)  7.66 us
    ppermute x2, waiting for transfers between devices, paired(): lax.ppermute(block, axis, [(partner_of(i), i) for i in range(lax.axis_siz...  5.67 us
  transfers between devices with their start and end apart: 12, of which 11 were waited for; matrix products, arithmetic and copies ran while one was open for 7% of the time, Pallas kernels for 0%

profile of v5, /device:TPU:16, one launch (start us, length us, event | category | flops | bytes accessed | tf_op | source)
XLA Modules:
  0.0 152.2 jit_solution(8051368287815520262)
XLA Ops:
  1.8 4.4 %all-to-all-start = ((f32[4,16,512]{2,1,0:T(8,128)}), f32[4,16,512]{2,1,0:T(8,128)S(1)}, u32[]{:S(2)}, u32[]{:S(2)}) async-start(f32[4,16,512]{2,1,0:T(8,128)} %broadcast_in_dim.112), calls=%async_computation | async-start | bytes 262144 | tf_op jit(solution)/shard_map/all_to_all | solution.py:145
  15.3 1.8 %shard_map.64 = f32[16,2048]{1,0:T(8,128)} custom-call(s32[16,1]{1,0:T(8,128)} %copy.53.shift_ref, f32[16,2048]{1,0:T(8,128)} %reshape_reshape.20.low_ref, f32[16,2048]{1,0:T(8,128)} %reshape_reshape.21.high_ref), custom_call_target="tpu_custom_call" | custom-call | flops 786432 | bytes 393216 | tf_op jit(solution)/shard_map/pallas_call | solution.py:56
  19.7 1.9 %shard_map.65 = f32[16,2048]{1,0:T(8,128)} custom-call(s32[16,1]{1,0:T(8,128)} %copy.54.shift_ref, f32[16,2048]{1,0:T(8,128)} %reshape_reshape.22.low_ref, f32[16,2048]{1,0:T(8,128)} %reshape_reshape.23.high_ref), custom_call_target="tpu_custom_call" | custom-call | flops 786432 | bytes 393216 | tf_op jit(solution)/shard_map/pallas_call | solution.py:56
  24.1 2.0 %shard_map.66 = f32[16,2048]{1,0:T(8,128)} custom-call(s32[16,1]{1,0:T(8,128)} %copy.55.shift_ref, f32[16,2048]{1,0:T(8,128)} %reshape_reshape.24.low_ref, f32[16,2048]{1,0:T(8,128)} %reshape_reshape.25.high_ref), custom_call_target="tpu_custom_call" | custom-call | flops 786432 | bytes 393216 | tf_op jit(solution)/shard_map/pallas_call | solution.py:56
  28.5 2.0 %shard_map.67 = f32[16,2048]{1,0:T(8,128)} custom-call(s32[16,1]{1,0:T(8,128)} %copy.56.shift_ref, f32[16,2048]{1,0:T(8,128)} %broadcast_in_dim.120.low_ref, f32[16,2048]{1,0:T(8,128)} %broadcast_in_dim.122.high_ref), custom_call_target="tpu_custom_call" | custom-call | flops 786432 | bytes 393216 | tf_op jit(solution)/shard_map/pallas_call | solution.py:56
  31.4 1.9 %collective-permute-start = (f32[4,2048]{1,0:T(4,128)S(1)}, f32[4,2048]{1,0:T(4,128)S(1)}, u32[]{:S(2)}, u32[]{:S(2)}) collective-permute-start(f32[4,2048]{1,0:T(4,128)S(1)} %constant_dynamic-slice_fusion), channel_id=1, source_target_pairs={{0,4},{4,0},{8,12},{12,8},{16,20},{20,16},{24,28},{28,24},{32,36},... | collective-permute-start | bytes 98312 | tf_op jit(solution)/shard_map/ppermute | solution.py:25
  34.5 1.5 broadcast_select_fusion.4
  36.0 1.8 %shard_map.68 = f32[4,2048]{1,0:T(4,128)} custom-call(s32[4,1]{1,0:T(4,128)} %copy.57.shift_ref, f32[4,2048]{1,0:T(4,128)} %get-tuple-element.43.low_ref, f32[4,2048]{1,0:T(4,128)} %get-tuple-element.42.high_ref), custom_call_target="tpu_custom_call" | custom-call | flops 196608 | bytes 98304 | tf_op jit(solution)/shard_map/pallas_call | solution.py:56
  37.8 4.3 %collective-permute-start.1 = (f32[4,2048]{1,0:T(4,128)}, f32[4,2048]{1,0:T(4,128)S(1)}, u32[]{:S(2)}, u32[]{:S(2)}) collective-permute-start(f32[4,2048]{1,0:T(4,128)} %shard_map.68), channel_id=1, source_target_pairs={{0,8},{8,0},{4,12},{12,4},{16,24},{24,16},{20,28},{28,20},{32,40},... | collective-permute-start | bytes 98312 | tf_op jit(solution)/shard_map/ppermute | solution.py:25
  45.6 1.9 %shard_map.69 = f32[4,2048]{1,0:T(4,128)} custom-call(s32[4,1]{1,0:T(4,128)} %copy.58.shift_ref, f32[4,2048]{1,0:T(4,128)} %get-tuple-element.41.low_ref, f32[4,2048]{1,0:T(4,128)} %get-tuple-element.40.high_ref), custom_call_target="tpu_custom_call" | custom-call | flops 196608 | bytes 98304 | tf_op jit(solution)/shard_map/pallas_call | solution.py:56
  47.5 6.1 %collective-permute-start.2 = (f32[4,2048]{1,0:T(4,128)}, f32[4,2048]{1,0:T(4,128)S(1)}, u32[]{:S(2)}, u32[]{:S(2)}) collective-permute-start(f32[4,2048]{1,0:T(4,128)} %shard_map.69), channel_id=1, source_target_pairs={{0,16},{16,0},{4,20},{20,4},{8,24},{24,8},{12,28},{28,12},{32,48},... | collective-permute-start | bytes 98312 | tf_op jit(solution)/shard_map/ppermute | solution.py:25
  54.2 1.6 %collective-permute-done.2 = f32[4,2048]{1,0:T(4,128)S(1)} collective-permute-done((f32[4,2048]{1,0:T(4,128)}, f32[4,2048]{1,0:T(4,128)S(1)}, u32[]{:S(2)}, u32[]{:S(2)}) %collective-permute-start.2) | collective-permute-done | bytes 32800 | tf_op jit(solution)/shard_map/ppermute | solution.py:25
  57.1 2.0 %shard_map.70 = f32[4,2048]{1,0:T(4,128)} custom-call(s32[4,1]{1,0:T(4,128)} %copy.59.shift_ref, f32[4,2048]{1,0:T(4,128)} %get-tuple-element.39.low_ref, f32[4,2048]{1,0:T(4,128)} %get-tuple-element.38.high_ref), custom_call_target="tpu_custom_call" | custom-call | flops 196608 | bytes 98304 | tf_op jit(solution)/shard_map/pallas_call | solution.py:56
  59.1 9.2 %collective-permute-start.3 = (f32[4,2048]{1,0:T(4,128)}, f32[4,2048]{1,0:T(4,128)S(1)}, u32[]{:S(2)}, u32[]{:S(2)}) collective-permute-start(f32[4,2048]{1,0:T(4,128)} %shard_map.70), channel_id=1, source_target_pairs={{0,32},{32,0},{4,36},{36,4},{8,40},{40,8},{12,44},{44,12},{16,48},... | collective-permute-start | bytes 98312 | tf_op jit(solution)/shard_map/ppermute | solution.py:25
  71.8 2.0 %shard_map.71 = f32[4,2048]{1,0:T(4,128)} custom-call(s32[4,1]{1,0:T(4,128)} %copy.60.shift_ref, f32[4,2048]{1,0:T(4,128)} %get-tuple-element.37.low_ref, f32[4,2048]{1,0:T(4,128)} %get-tuple-element.36.high_ref), custom_call_target="tpu_custom_call" | custom-call | flops 196608 | bytes 98304 | tf_op jit(solution)/shard_map/pallas_call | solution.py:56
  73.8 3.5 %collective-permute-start.4 = (f32[4,2048]{1,0:T(4,128)}, f32[4,2048]{1,0:T(4,128)S(1)}, u32[]{:S(2)}, u32[]{:S(2)}) collective-permute-start(f32[4,2048]{1,0:T(4,128)} %shard_map.71), channel_id=1, source_target_pairs={{0,64},{64,0},{4,68},{68,4},{8,72},{72,8},{12,76},{76,12},{16,80},... | collective-permute-start | bytes 98312 | tf_op jit(solution)/shard_map/ppermute | solution.py:25
  78.0 1.8 %collective-permute-done.4 = f32[4,2048]{1,0:T(4,128)S(1)} collective-permute-done((f32[4,2048]{1,0:T(4,128)}, f32[4,2048]{1,0:T(4,128)S(1)}, u32[]{:S(2)}, u32[]{:S(2)}) %collective-permute-start.4) | collective-permute-done | bytes 32800 | tf_op jit(solution)/shard_map/ppermute | solution.py:25
  82.0 2.1 %shard_map.72 = f32[8,2048]{1,0:T(8,128)} custom-call(s32[8,1]{1,0:T(8,128)} %copy.61.shift_ref, f32[8,2048]{1,0:T(8,128)} %reshape.193.low_ref, f32[8,2048]{1,0:T(8,128)} %reshape.194.high_ref), custom_call_target="tpu_custom_call" | custom-call | flops 393216 | bytes 196608 | tf_op jit(solution)/shard_map/pallas_call | solution.py:56
  84.1 3.5 %collective-permute-start.5 = (f32[8,2048]{1,0:T(8,128)}, f32[8,2048]{1,0:T(8,128)S(1)}, u32[]{:S(2)}, u32[]{:S(2)}) collective-permute-start(f32[8,2048]{1,0:T(8,128)} %shard_map.72), channel_id=1, source_target_pairs={{0,128},{128,0},{4,132},{132,4},{8,136},{136,8},{12,140},{140,12},... | collective-permute-start | bytes 196616 | tf_op jit(solution)/shard_map/ppermute | solution.py:25
  88.3 3.1 %collective-permute-done.5 = f32[8,2048]{1,0:T(8,128)S(1)} collective-permute-done((f32[8,2048]{1,0:T(8,128)}, f32[8,2048]{1,0:T(8,128)S(1)}, u32[]{:S(2)}, u32[]{:S(2)}) %collective-permute-start.5) | collective-permute-done | bytes 65568 | tf_op jit(solution)/shard_map/ppermute | solution.py:25
  93.8 2.4 %shard_map.73 = f32[16,2048]{1,0:T(8,128)} custom-call(s32[16,1]{1,0:T(8,128)} %copy.62.shift_ref, f32[16,2048]{1,0:T(8,128)} %reshape.195.low_ref, f32[16,2048]{1,0:T(8,128)} %reshape.196.high_ref), custom_call_target="tpu_custom_call" | custom-call | flops 786432 | bytes 393216 | tf_op jit(solution)/shard_map/pallas_call | solution.py:56
  96.2 6.3 %collective-permute-start.6 = (f32[16,2048]{1,0:T(8,128)}, f32[16,2048]{1,0:T(8,128)S(1)}, u32[]{:S(2)}, u32[]{:S(2)}) collective-permute-start(f32[16,2048]{1,0:T(8,128)} %shard_map.73), channel_id=1, source_target_pairs={{384,0},{388,4},{392,8},{396,12},{400,16},{404,20},{408,24},{412,2... | collective-permute-start | bytes 393224 | tf_op jit(solution)/shard_map/ppermute | solution.py:29
  103.3 3.8 %collective-permute-done.6 = f32[16,2048]{1,0:T(8,128)S(1)} collective-permute-done((f32[16,2048]{1,0:T(8,128)}, f32[16,2048]{1,0:T(8,128)S(1)}, u32[]{:S(2)}, u32[]{:S(2)}) %collective-permute-start.6) | collective-permute-done | bytes 131104 | tf_op jit(solution)/shard_map/ppermute | solution.py:29
  110.0 2.8 %shard_map.74 = f32[32,2048]{1,0:T(8,128)} custom-call(s32[32,1]{1,0:T(8,128)} %copy.63.shift_ref, f32[32,2048]{1,0:T(8,128)} %reshape.197.low_ref, f32[32,2048]{1,0:T(8,128)} %reshape.198.high_ref), custom_call_target="tpu_custom_call" | custom-call | flops 1572864 | bytes 786432 | tf_op jit(solution)/shard_map/pallas_call | solution.py:56
  115.2 10.6 %all_to_all.10 = f32[9,4,512]{2,0,1:T(8,128)S(1)} all-to-all(f32[9,4,512]{2,0,1:T(8,128)S(1)} %stack.5), channel_id=1, replica_groups=mesh['freq'=128,'tm'=4] {'tm'}, dimensions={1} | all-to-all | bytes 147456 | tf_op jit(solution)/shard_map/all_to_all | solution.py:188
  125.7 1.9 %collective-permute-start.7 = (f32[9,512]{1,0:T(8,128)S(1)}, f32[9,512]{1,0:T(8,128)S(1)}, u32[]{:S(2)}, u32[]{:S(2)}) collective-permute-start(f32[9,512]{1,0:T(8,128)S(1)} %reduce_max.99), channel_id=1, source_target_pairs={{0,4},{4,0},{8,12},{12,8},{16,20},{20,16},{24,28},{28,24},{32,36},... | collective-permute-start | bytes 55304 | tf_op jit(solution)/shard_map/ppermute | solution.py:25
  128.9 3.3 %collective-permute-start.8 = (f32[9,512]{1,0:T(8,128)S(1)}, f32[9,512]{1,0:T(8,128)S(1)}, u32[]{:S(2)}, u32[]{:S(2)}) collective-permute-start(f32[9,512]{1,0:T(8,128)S(1)} %max.12), channel_id=1, source_target_pairs={{0,8},{8,0},{4,12},{12,4},{16,24},{24,16},{20,28},{28,20},{32,40},... | collective-permute-start | bytes 55304 | tf_op jit(solution)/shard_map/ppermute | solution.py:25
  132.2 2.4 %collective-permute-done.8 = f32[9,512]{1,0:T(8,128)S(1)} collective-permute-done((f32[9,512]{1,0:T(8,128)S(1)}, f32[9,512]{1,0:T(8,128)S(1)}, u32[]{:S(2)}, u32[]{:S(2)}) %collective-permute-start.8) | collective-permute-done | bytes 18464 | tf_op jit(solution)/shard_map/ppermute | solution.py:25
  134.7 4.6 %collective-permute-start.9 = (f32[9,512]{1,0:T(8,128)S(1)}, f32[9,512]{1,0:T(8,128)S(1)}, u32[]{:S(2)}, u32[]{:S(2)}) collective-permute-start(f32[9,512]{1,0:T(8,128)S(1)} %max.13), channel_id=1, source_target_pairs={{0,16},{16,0},{4,20},{20,4},{8,24},{24,8},{12,28},{28,12},{32,48},... | collective-permute-start | bytes 55304 | tf_op jit(solution)/shard_map/ppermute | solution.py:25
  139.3 2.1 %collective-permute-done.9 = f32[9,512]{1,0:T(8,128)S(1)} collective-permute-done((f32[9,512]{1,0:T(8,128)S(1)}, f32[9,512]{1,0:T(8,128)S(1)}, u32[]{:S(2)}, u32[]{:S(2)}) %collective-permute-start.9) | collective-permute-done | bytes 18464 | tf_op jit(solution)/shard_map/ppermute | solution.py:25
  141.4 8.3 %collective-permute-start.10 = (f32[9,512]{1,0:T(8,128)S(1)}, f32[9,512]{1,0:T(8,128)S(1)}, u32[]{:S(2)}, u32[]{:S(2)}) collective-permute-start(f32[9,512]{1,0:T(8,128)S(1)} %max.14), channel_id=1, source_target_pairs={{48,0},{52,4},{56,8},{60,12},{32,16},{36,20},{40,24},{44,28},{16,3... | collective-permute-start | bytes 55304 | tf_op jit(solution)/shard_map/ppermute | solution.py:29
  149.7 1.9 %collective-permute-done.10 = f32[9,512]{1,0:T(8,128)S(1)} collective-permute-done((f32[9,512]{1,0:T(8,128)S(1)}, f32[9,512]{1,0:T(8,128)S(1)}, u32[]{:S(2)}, u32[]{:S(2)}) %collective-permute-start.10) | collective-permute-done | bytes 18464 | tf_op jit(solution)/shard_map/ppermute | solution.py:29
  (108 shorter events, 43.1 us)
Async XLA Ops:
  0.0 9.2 %copy-start = (s32[4094]{0:T(1024)S(1)}, s32[4094]{0:T(1024)}, u32[]{:S(2)}) copy-start(s32[4094]{0:T(1024)} %param.8) | copy-start | bytes 49132
  1.8 4.5 %copy-start.3 = (s32[9,136]{1,0:T(8,128)S(1)}, s32[9,136]{1,0:T(8,128)}, u32[]{:S(2)}) copy-start(s32[9,136]{1,0:T(8,128)} %constant.110.clone) | copy-start | bytes 14692
  1.8 4.5 %copy-start.4 = (s32[9,136]{1,0:T(8,128)S(1)}, s32[9,136]{1,0:T(8,128)}, u32[]{:S(2)}) copy-start(s32[9,136]{1,0:T(8,128)} %constant.109.clone) | copy-start | bytes 14692
  1.8 11.7 %all-to-all-start = ((f32[4,16,512]{2,1,0:T(8,128)}), f32[4,16,512]{2,1,0:T(8,128)S(1)}, u32[]{:S(2)}, u32[]{:S(2)}) async-start(f32[4,16,512]{2,1,0:T(8,128)} %broadcast_in_dim.112), calls=%async_computation | async-start | bytes 262144 | tf_op jit(solution)/shard_map/all_to_all | solution.py:145
  6.3 0.7 copy-start.2
  7.1 0.7 copy-start.1
  31.4 3.1 %collective-permute-start = (f32[4,2048]{1,0:T(4,128)S(1)}, f32[4,2048]{1,0:T(4,128)S(1)}, u32[]{:S(2)}, u32[]{:S(2)}) collective-permute-start(f32[4,2048]{1,0:T(4,128)S(1)} %constant_dynamic-slice_fusion), channel_id=1, source_target_pairs={{0,4},{4,0},{8,12},{12,8},{16,20},{20,16},{24,28},{28,24},{32,36},... | collective-permute-start | bytes 98312 | tf_op jit(solution)/shard_map/ppermute | solution.py:25
  37.8 6.4 %collective-permute-start.1 = (f32[4,2048]{1,0:T(4,128)}, f32[4,2048]{1,0:T(4,128)S(1)}, u32[]{:S(2)}, u32[]{:S(2)}) collective-permute-start(f32[4,2048]{1,0:T(4,128)} %shard_map.68), channel_id=1, source_target_pairs={{0,8},{8,0},{4,12},{12,4},{16,24},{24,16},{20,28},{28,20},{32,40},... | collective-permute-start | bytes 98312 | tf_op jit(solution)/shard_map/ppermute | solution.py:25
  47.5 8.3 %collective-permute-start.2 = (f32[4,2048]{1,0:T(4,128)}, f32[4,2048]{1,0:T(4,128)S(1)}, u32[]{:S(2)}, u32[]{:S(2)}) collective-permute-start(f32[4,2048]{1,0:T(4,128)} %shard_map.69), channel_id=1, source_target_pairs={{0,16},{16,0},{4,20},{20,4},{8,24},{24,8},{12,28},{28,12},{32,48},... | collective-permute-start | bytes 98312 | tf_op jit(solution)/shard_map/ppermute | solution.py:25
  59.1 11.3 %collective-permute-start.3 = (f32[4,2048]{1,0:T(4,128)}, f32[4,2048]{1,0:T(4,128)S(1)}, u32[]{:S(2)}, u32[]{:S(2)}) collective-permute-start(f32[4,2048]{1,0:T(4,128)} %shard_map.70), channel_id=1, source_target_pairs={{0,32},{32,0},{4,36},{36,4},{8,40},{40,8},{12,44},{44,12},{16,48},... | collective-permute-start | bytes 98312 | tf_op jit(solution)/shard_map/ppermute | solution.py:25
  73.8 6.0 %collective-permute-start.4 = (f32[4,2048]{1,0:T(4,128)}, f32[4,2048]{1,0:T(4,128)S(1)}, u32[]{:S(2)}, u32[]{:S(2)}) collective-permute-start(f32[4,2048]{1,0:T(4,128)} %shard_map.71), channel_id=1, source_target_pairs={{0,64},{64,0},{4,68},{68,4},{8,72},{72,8},{12,76},{76,12},{16,80},... | collective-permute-start | bytes 98312 | tf_op jit(solution)/shard_map/ppermute | solution.py:25
  84.1 7.3 %collective-permute-start.5 = (f32[8,2048]{1,0:T(8,128)}, f32[8,2048]{1,0:T(8,128)S(1)}, u32[]{:S(2)}, u32[]{:S(2)}) collective-permute-start(f32[8,2048]{1,0:T(8,128)} %shard_map.72), channel_id=1, source_target_pairs={{0,128},{128,0},{4,132},{132,4},{8,136},{136,8},{12,140},{140,12},... | collective-permute-start | bytes 196616 | tf_op jit(solution)/shard_map/ppermute | solution.py:25
  96.2 10.9 %collective-permute-start.6 = (f32[16,2048]{1,0:T(8,128)}, f32[16,2048]{1,0:T(8,128)S(1)}, u32[]{:S(2)}, u32[]{:S(2)}) collective-permute-start(f32[16,2048]{1,0:T(8,128)} %shard_map.73), channel_id=1, source_target_pairs={{384,0},{388,4},{392,8},{396,12},{400,16},{404,20},{408,24},{412,2... | collective-permute-start | bytes 393224 | tf_op jit(solution)/shard_map/ppermute | solution.py:29
  125.7 3.1 %collective-permute-start.7 = (f32[9,512]{1,0:T(8,128)S(1)}, f32[9,512]{1,0:T(8,128)S(1)}, u32[]{:S(2)}, u32[]{:S(2)}) collective-permute-start(f32[9,512]{1,0:T(8,128)S(1)} %reduce_max.99), channel_id=1, source_target_pairs={{0,4},{4,0},{8,12},{12,8},{16,20},{20,16},{24,28},{28,24},{32,36},... | collective-permute-start | bytes 55304 | tf_op jit(solution)/shard_map/ppermute | solution.py:25
  128.9 5.8 %collective-permute-start.8 = (f32[9,512]{1,0:T(8,128)S(1)}, f32[9,512]{1,0:T(8,128)S(1)}, u32[]{:S(2)}, u32[]{:S(2)}) collective-permute-start(f32[9,512]{1,0:T(8,128)S(1)} %max.12), channel_id=1, source_target_pairs={{0,8},{8,0},{4,12},{12,4},{16,24},{24,16},{20,28},{28,20},{32,40},... | collective-permute-start | bytes 55304 | tf_op jit(solution)/shard_map/ppermute | solution.py:25
  134.7 6.7 %collective-permute-start.9 = (f32[9,512]{1,0:T(8,128)S(1)}, f32[9,512]{1,0:T(8,128)S(1)}, u32[]{:S(2)}, u32[]{:S(2)}) collective-permute-start(f32[9,512]{1,0:T(8,128)S(1)} %max.13), channel_id=1, source_target_pairs={{0,16},{16,0},{4,20},{20,4},{8,24},{24,8},{12,28},{28,12},{32,48},... | collective-permute-start | bytes 55304 | tf_op jit(solution)/shard_map/ppermute | solution.py:25
  141.4 10.2 %collective-permute-start.10 = (f32[9,512]{1,0:T(8,128)S(1)}, f32[9,512]{1,0:T(8,128)S(1)}, u32[]{:S(2)}, u32[]{:S(2)}) collective-permute-start(f32[9,512]{1,0:T(8,128)S(1)} %max.14), channel_id=1, source_target_pairs={{48,0},{52,4},{56,8},{60,12},{32,16},{36,20},{40,24},{44,28},{16,3... | collective-permute-start | bytes 55304 | tf_op jit(solution)/shard_map/ppermute | solution.py:29

commit v6 on v4

--- a/solution.py
+++ b/solution.py
@@ -8,8 +8,9 @@
 
 SUMMED = 32
 WIDTHS = 9
-SHARED_LEVELS = 3
+SHARED_LEVELS = 4
 NEAR_HALF = (6, 7, 4, 5, 2, 3, 0, 1)
+NEXT_PAIR = (7, 2, 1, 4, 3, 6, 5, 0)
 
 
 def swapped(block, axis, apart):
@@ -26,10 +27,10 @@
     return lax.ppermute(block, axis, [(partner_of(i), i) for i in range(lax.axis_size(axis))])
 
 
-def near_half(bit_index, ring_bits):
+def ring_partner(table, ring_bits):
     def partner_of(i):
         ring = i >> ring_bits & 7
-        return i - (ring << ring_bits) + (NEAR_HALF[ring] << ring_bits)
+        return i - (ring << ring_bits) + (table[ring] << ring_bits)
 
     return partner_of
 
@@ -152,7 +153,7 @@
     for bit_index in range(freq_bits):
         need_now = sub_dev * 2 ** (bit_index + 1) - 1
         if bit_index == freq_bits - 1 and shared >= 3 and bit_index >= 2:
-            partner = paired(trial_rows, "freq", near_half(bit_index, bit_index - 2))
+            partner = paired(trial_rows, "freq", ring_partner(NEAR_HALF, bit_index - 2))
         else:
             partner = swapped(trial_rows, "freq", bit_index)
         upper_half = device >> bit_index & 1
@@ -178,7 +179,9 @@
     best = jnp.max(lax.all_to_all(best, "tm", 1, 1, tiled=True), axis=1)
     for bit_index in range(freq_bits - shared):
         if bit_index == 3:
-            best = jnp.maximum(best, paired(best, "freq", near_half(bit_index, 1)))
+            best = jnp.maximum(best, paired(best, "freq", ring_partner(NEAR_HALF, 1)))
+        elif bit_index == 2 and freq_bits - shared == 3:
+            best = jnp.maximum(best, paired(best, "freq", ring_partner(NEXT_PAIR, 1)))
         else:
             best = jnp.maximum(best, swapped(best, "freq", bit_index))
     return best

time: 113 us -> 115 us (1.018)
  starting transfers between devices: 57.3 us -> 53.4 us
  other arithmetic: 10.8 us -> 12.9 us
  local copies, waits for them, and re-layouts: 8.08 us -> 9.93 us
  waiting for transfers between devices: 25.7 us -> 26.9 us
    ppermute x9 -> x8, starting transfers between devices: 38.2 us -> 33.7 us  [swapped(): return lax.ppermute(block, axis, route)]
    ppermute x2, waiting for transfers between devices: 6.14 us -> 8.75 us  [paired(): lax.ppermute(block, axis, [(partner_of(i), i) for i in range(lax.axis_siz...]
    select_n x55, other arithmetic: 6.01 us -> 7.66 us  [merge_rows(): jnp.where(selected, moved[:, step_size:], moved[:, :cols - step_size])]
    ppermute x9 -> x8, waiting for transfers between devices: 18.3 us -> 17.3 us  [swapped(): return lax.ppermute(block, axis, route)]
  transfers between devices with their start and end apart: 12 -> 11, of which waited for: 12 -> 11; matrix products, arithmetic and copies ran while one was open for 3% -> 4% of each run, Pallas kernels for 0% -> 0%
where the time goes in v6:
time: 115 us; the launch traced here: 114 us
  starting transfers between devices  53.4 us (46%)
  waiting for transfers between devices  26.9 us (23%)
  other arithmetic  12.9 us (11%)
  local copies, waits for them, and re-layouts  9.93 us (9%)
  blocking collectives  9.8 us (9%)
    ppermute x8, starting transfers between devices, swapped(): return lax.ppermute(block, axis, route)  33.7 us
    ppermute x8, waiting for transfers between devices, swapped(): return lax.ppermute(block, axis, route)  17.3 us
    ppermute x2, starting transfers between devices, paired(): lax.ppermute(block, axis, [(partner_of(i), i) for i in range(lax.axis_siz...  15.4 us
    all_to_all x1, blocking collectives, shards(): best = jnp.max(lax.all_to_all(best, 'tm', 1, 1, tiled=True), axis=1)  9.8 us
    ppermute x2, waiting for transfers between devices, paired(): lax.ppermute(block, axis, [(partner_of(i), i) for i in range(lax.axis_siz...  8.75 us
    select_n x55, other arithmetic, merge_rows(): jnp.where(selected, moved[:, step_size:], moved[:, :cols - step_size])  7.66 us
    all_to_all x1, starting transfers between devices, shards(): gathered = lax.all_to_all(spread, 'tm', 0, 0, tiled=True)  4.42 us
  transfers between devices with their start and end apart: 11, of which 11 were waited for; matrix products, arithmetic and copies ran while one was open for 4% of the time, Pallas kernels for 0%

profile of v6, /device:TPU:16, one launch (start us, length us, event | category | flops | bytes accessed | tf_op | source)
XLA Modules:
  0.0 114.1 jit_solution(575983808272267463)
XLA Ops:
  0.0 1.2 %convert_reduce_fusion = f32[16,512]{1,0:T(8,128)S(1)} fusion(bf16[512,512]{1,0:T(8,128)(2,1)} %param.6), kind=kLoop, calls=%fused_computation.10 | loop fusion | flops 516096 | bytes 557056 | tf_op jit(solution)/shard_map/reduce_sum | solution.py:132
  1.2 0.6 broadcast_in_dim.648
  1.8 4.4 %all-to-all-start = ((f32[4,16,512]{2,1,0:T(8,128)}), f32[4,16,512]{2,1,0:T(8,128)S(1)}, u32[]{:S(2)}, u32[]{:S(2)}) async-start(f32[4,16,512]{2,1,0:T(8,128)} %broadcast_in_dim.648), calls=%async_computation | async-start | bytes 262144 | tf_op jit(solution)/shard_map/all_to_all | solution.py:134
  6.4 0.6 copy-done.2
  7.1 0.7 copy-done.1
  7.8 1.7 %gather_fusion = s32[196]{0:T(256)S(1)} fusion(s32[2047]{0:T(1024)S(1)} %copy-done.1, s32[1024]{0:T(1024)S(1)} %pad_clamp_fusion.1), kind=kCustom, calls=%fused_computation | custom fusion | bytes 2352 | tf_op jit(solution)/shard_map/jit(_take)/gather | solution.py:123
  9.5 1.7 %gather_fusion.1 = s32[196]{0:T(256)S(1)} fusion(s32[4094]{0:T(1024)S(1)} %copy-done, s32[1024]{0:T(1024)S(1)} %pad_clamp_fusion), kind=kCustom, calls=%fused_computation.1 | custom fusion | bytes 2352 | tf_op jit(solution)/shard_map/jit(_take)/gather | solution.py:124
  11.5 0.8 all-to-all-done
  15.5 1.9 %collective-permute-start = (f32[4,2048]{1,0:T(4,128)S(1)}, f32[4,2048]{1,0:T(4,128)S(1)}, u32[]{:S(2)}, u32[]{:S(2)}) collective-permute-start(f32[4,2048]{1,0:T(4,128)S(1)} %dynamic-slice_add_fusion), channel_id=1, source_target_pairs={{0,4},{4,0},{8,12},{12,8},{16,20},{20,16},{24,28},{28,24},{32,36},... | collective-permute-start | bytes 98312 | tf_op jit(solution)/shard_map/ppermute | solution.py:23
  17.5 1.1 collective-permute-done
  19.1 4.3 %collective-permute-start.1 = (f32[4,2048]{1,0:T(4,128)S(1)}, f32[4,2048]{1,0:T(4,128)S(1)}, u32[]{:S(2)}, u32[]{:S(2)}) collective-permute-start(f32[4,2048]{1,0:T(4,128)S(1)} %fusion.22), channel_id=1, source_target_pairs={{0,8},{8,0},{4,12},{12,4},{16,24},{24,16},{20,28},{28,20},{32,40},... | collective-permute-start | bytes 98312 | tf_op jit(solution)/shard_map/ppermute | solution.py:23
  23.4 1.9 %collective-permute-done.1 = f32[4,2048]{1,0:T(4,128)S(1)} collective-permute-done((f32[4,2048]{1,0:T(4,128)S(1)}, f32[4,2048]{1,0:T(4,128)S(1)}, u32[]{:S(2)}, u32[]{:S(2)}) %collective-permute-start.1) | collective-permute-done | bytes 32800 | tf_op jit(solution)/shard_map/ppermute | solution.py:23
  25.9 6.1 %collective-permute-start.2 = (f32[4,2048]{1,0:T(4,128)S(1)}, f32[4,2048]{1,0:T(4,128)S(1)}, u32[]{:S(2)}, u32[]{:S(2)}) collective-permute-start(f32[4,2048]{1,0:T(4,128)S(1)} %fusion.21), channel_id=1, source_target_pairs={{0,16},{16,0},{4,20},{20,4},{8,24},{24,8},{12,28},{28,12},{32,48},... | collective-permute-start | bytes 98312 | tf_op jit(solution)/shard_map/ppermute | solution.py:23
  32.0 2.0 %collective-permute-done.2 = f32[4,2048]{1,0:T(4,128)S(1)} collective-permute-done((f32[4,2048]{1,0:T(4,128)S(1)}, f32[4,2048]{1,0:T(4,128)S(1)}, u32[]{:S(2)}, u32[]{:S(2)}) %collective-permute-start.2) | collective-permute-done | bytes 32800 | tf_op jit(solution)/shard_map/ppermute | solution.py:23
  34.7 9.2 %collective-permute-start.3 = (f32[4,2048]{1,0:T(4,128)S(1)}, f32[4,2048]{1,0:T(4,128)S(1)}, u32[]{:S(2)}, u32[]{:S(2)}) collective-permute-start(f32[4,2048]{1,0:T(4,128)S(1)} %fusion.20), channel_id=1, source_target_pairs={{0,32},{32,0},{4,36},{36,4},{8,40},{40,8},{12,44},{44,12},{16,48},... | collective-permute-start | bytes 98312 | tf_op jit(solution)/shard_map/ppermute | solution.py:23
  43.9 1.8 %collective-permute-done.3 = f32[4,2048]{1,0:T(4,128)S(1)} collective-permute-done((f32[4,2048]{1,0:T(4,128)S(1)}, f32[4,2048]{1,0:T(4,128)S(1)}, u32[]{:S(2)}, u32[]{:S(2)}) %collective-permute-start.3) | collective-permute-done | bytes 32800 | tf_op jit(solution)/shard_map/ppermute | solution.py:23
  46.7 3.5 %collective-permute-start.4 = (f32[8,2048]{1,0:T(8,128)S(1)}, f32[8,2048]{1,0:T(8,128)S(1)}, u32[]{:S(2)}, u32[]{:S(2)}) collective-permute-start(f32[8,2048]{1,0:T(8,128)S(1)} %fusion.19), channel_id=1, source_target_pairs={{0,64},{64,0},{4,68},{68,4},{8,72},{72,8},{12,76},{76,12},{16,80},... | collective-permute-start | bytes 196616 | tf_op jit(solution)/shard_map/ppermute | solution.py:23
  50.2 2.7 %collective-permute-done.4 = f32[8,2048]{1,0:T(8,128)S(1)} collective-permute-done((f32[8,2048]{1,0:T(8,128)S(1)}, f32[8,2048]{1,0:T(8,128)S(1)}, u32[]{:S(2)}, u32[]{:S(2)}) %collective-permute-start.4) | collective-permute-done | bytes 65568 | tf_op jit(solution)/shard_map/ppermute | solution.py:23
  54.2 3.5 %collective-permute-start.5 = (f32[16,2048]{1,0:T(8,128)S(1)}, f32[16,2048]{1,0:T(8,128)S(1)}, u32[]{:S(2)}, u32[]{:S(2)}) collective-permute-start(f32[16,2048]{1,0:T(8,128)S(1)} %fusion.15), channel_id=1, source_target_pairs={{0,128},{128,0},{4,132},{132,4},{8,136},{136,8},{12,140},{140,12},... | collective-permute-start | bytes 393224 | tf_op jit(solution)/shard_map/ppermute | solution.py:23
  57.8 4.3 %collective-permute-done.5 = f32[16,2048]{1,0:T(8,128)S(1)} collective-permute-done((f32[16,2048]{1,0:T(8,128)S(1)}, f32[16,2048]{1,0:T(8,128)S(1)}, u32[]{:S(2)}, u32[]{:S(2)}) %collective-permute-start.5) | collective-permute-done | bytes 131104 | tf_op jit(solution)/shard_map/ppermute | solution.py:23
  64.3 7.2 %collective-permute-start.6 = (f32[32,2048]{1,0:T(8,128)S(1)}, f32[32,2048]{1,0:T(8,128)S(1)}, u32[]{:S(2)}, u32[]{:S(2)}) collective-permute-start(f32[32,2048]{1,0:T(8,128)S(1)} %fusion.13), channel_id=1, source_target_pairs={{384,0},{388,4},{392,8},{396,12},{400,16},{404,20},{408,24},{412,2... | collective-permute-start | bytes 786440 | tf_op jit(solution)/shard_map/ppermute | solution.py:27
  71.6 6.9 %collective-permute-done.6 = f32[32,2048]{1,0:T(8,128)S(1)} collective-permute-done((f32[32,2048]{1,0:T(8,128)S(1)}, f32[32,2048]{1,0:T(8,128)S(1)}, u32[]{:S(2)}, u32[]{:S(2)}) %collective-permute-start.6) | collective-permute-done | bytes 262176 | tf_op jit(solution)/shard_map/ppermute | solution.py:27
  78.8 0.4 reshape.337
  79.8 0.4 fusion
  84.7 9.8 %all_to_all.10 = f32[9,4,512]{2,0,1:T(8,128)S(1)} all-to-all(f32[9,4,512]{2,0,1:T(8,128)S(1)} %stack.5), channel_id=1, replica_groups=mesh['freq'=128,'tm'=4] {'tm'}, dimensions={1} | all-to-all | bytes 147456 | tf_op jit(solution)/shard_map/all_to_all | solution.py:179
  94.5 1.9 %collective-permute-start.7 = (f32[9,512]{1,0:T(8,128)S(1)}, f32[9,512]{1,0:T(8,128)S(1)}, u32[]{:S(2)}, u32[]{:S(2)}) collective-permute-start(f32[9,512]{1,0:T(8,128)S(1)} %reduce_max.99), channel_id=1, source_target_pairs={{0,4},{4,0},{8,12},{12,8},{16,20},{20,16},{24,28},{28,24},{32,36},... | collective-permute-start | bytes 55304 | tf_op jit(solution)/shard_map/ppermute | solution.py:23
  96.4 1.2 %collective-permute-done.7 = f32[9,512]{1,0:T(8,128)S(1)} collective-permute-done((f32[9,512]{1,0:T(8,128)S(1)}, f32[9,512]{1,0:T(8,128)S(1)}, u32[]{:S(2)}, u32[]{:S(2)}) %collective-permute-start.7) | collective-permute-done | bytes 18464 | tf_op jit(solution)/shard_map/ppermute | solution.py:23
  97.6 3.3 %collective-permute-start.8 = (f32[9,512]{1,0:T(8,128)S(1)}, f32[9,512]{1,0:T(8,128)S(1)}, u32[]{:S(2)}, u32[]{:S(2)}) collective-permute-start(f32[9,512]{1,0:T(8,128)S(1)} %max.9), channel_id=1, source_target_pairs={{0,8},{8,0},{4,12},{12,4},{16,24},{24,16},{20,28},{28,20},{32,40},... | collective-permute-start | bytes 55304 | tf_op jit(solution)/shard_map/ppermute | solution.py:23
  100.9 2.4 %collective-permute-done.8 = f32[9,512]{1,0:T(8,128)S(1)} collective-permute-done((f32[9,512]{1,0:T(8,128)S(1)}, f32[9,512]{1,0:T(8,128)S(1)}, u32[]{:S(2)}, u32[]{:S(2)}) %collective-permute-start.8) | collective-permute-done | bytes 18464 | tf_op jit(solution)/shard_map/ppermute | solution.py:23
  103.4 8.2 %collective-permute-start.9 = (f32[9,512]{1,0:T(8,128)S(1)}, f32[9,512]{1,0:T(8,128)S(1)}, u32[]{:S(2)}, u32[]{:S(2)}) collective-permute-start(f32[9,512]{1,0:T(8,128)S(1)} %max.10), channel_id=1, source_target_pairs={{56,0},{60,4},{16,8},{20,12},{8,16},{12,20},{32,24},{36,28},{24,32... | collective-permute-start | bytes 55304 | tf_op jit(solution)/shard_map/ppermute | solution.py:27
  111.6 1.9 %collective-permute-done.9 = f32[9,512]{1,0:T(8,128)S(1)} collective-permute-done((f32[9,512]{1,0:T(8,128)S(1)}, f32[9,512]{1,0:T(8,128)S(1)}, u32[]{:S(2)}, u32[]{:S(2)}) %collective-permute-start.9) | collective-permute-done | bytes 18464 | tf_op jit(solution)/shard_map/ppermute | solution.py:27
  113.4 0.6 max.11
  (159 shorter events, 15.0 us)
Async XLA Ops:
  0.0 9.5 %copy-start = (s32[4094]{0:T(1024)S(1)}, s32[4094]{0:T(1024)}, u32[]{:S(2)}) copy-start(s32[4094]{0:T(1024)} %param.8) | copy-start | bytes 49132
  1.8 4.5 %copy-start.3 = (s32[9,196]{1,0:T(8,128)S(1)}, s32[9,196]{1,0:T(8,128)}, u32[]{:S(2)}) copy-start(s32[9,196]{1,0:T(8,128)} %constant.84.clone) | copy-start | bytes 21172
  1.8 4.5 %copy-start.4 = (s32[9,196]{1,0:T(8,128)S(1)}, s32[9,196]{1,0:T(8,128)}, u32[]{:S(2)}) copy-start(s32[9,196]{1,0:T(8,128)} %constant.83.clone) | copy-start | bytes 21172
  1.8 10.4 %all-to-all-start = ((f32[4,16,512]{2,1,0:T(8,128)}), f32[4,16,512]{2,1,0:T(8,128)S(1)}, u32[]{:S(2)}, u32[]{:S(2)}) async-start(f32[4,16,512]{2,1,0:T(8,128)} %broadcast_in_dim.648), calls=%async_computation | async-start | bytes 262144 | tf_op jit(solution)/shard_map/all_to_all | solution.py:134
  6.3 0.7 copy-start.2
  7.1 0.7 copy-start.1
  15.5 3.1 %collective-permute-start = (f32[4,2048]{1,0:T(4,128)S(1)}, f32[4,2048]{1,0:T(4,128)S(1)}, u32[]{:S(2)}, u32[]{:S(2)}) collective-permute-start(f32[4,2048]{1,0:T(4,128)S(1)} %dynamic-slice_add_fusion), channel_id=1, source_target_pairs={{0,4},{4,0},{8,12},{12,8},{16,20},{20,16},{24,28},{28,24},{32,36},... | collective-permute-start | bytes 98312 | tf_op jit(solution)/shard_map/ppermute | solution.py:23
  19.1 6.2 %collective-permute-start.1 = (f32[4,2048]{1,0:T(4,128)S(1)}, f32[4,2048]{1,0:T(4,128)S(1)}, u32[]{:S(2)}, u32[]{:S(2)}) collective-permute-start(f32[4,2048]{1,0:T(4,128)S(1)} %fusion.22), channel_id=1, source_target_pairs={{0,8},{8,0},{4,12},{12,4},{16,24},{24,16},{20,28},{28,20},{32,40},... | collective-permute-start | bytes 98312 | tf_op jit(solution)/shard_map/ppermute | solution.py:23
  25.9 8.1 %collective-permute-start.2 = (f32[4,2048]{1,0:T(4,128)S(1)}, f32[4,2048]{1,0:T(4,128)S(1)}, u32[]{:S(2)}, u32[]{:S(2)}) collective-permute-start(f32[4,2048]{1,0:T(4,128)S(1)} %fusion.21), channel_id=1, source_target_pairs={{0,16},{16,0},{4,20},{20,4},{8,24},{24,8},{12,28},{28,12},{32,48},... | collective-permute-start | bytes 98312 | tf_op jit(solution)/shard_map/ppermute | solution.py:23
  34.7 11.1 %collective-permute-start.3 = (f32[4,2048]{1,0:T(4,128)S(1)}, f32[4,2048]{1,0:T(4,128)S(1)}, u32[]{:S(2)}, u32[]{:S(2)}) collective-permute-start(f32[4,2048]{1,0:T(4,128)S(1)} %fusion.20), channel_id=1, source_target_pairs={{0,32},{32,0},{4,36},{36,4},{8,40},{40,8},{12,44},{44,12},{16,48},... | collective-permute-start | bytes 98312 | tf_op jit(solution)/shard_map/ppermute | solution.py:23
  46.7 6.1 %collective-permute-start.4 = (f32[8,2048]{1,0:T(8,128)S(1)}, f32[8,2048]{1,0:T(8,128)S(1)}, u32[]{:S(2)}, u32[]{:S(2)}) collective-permute-start(f32[8,2048]{1,0:T(8,128)S(1)} %fusion.19), channel_id=1, source_target_pairs={{0,64},{64,0},{4,68},{68,4},{8,72},{72,8},{12,76},{76,12},{16,80},... | collective-permute-start | bytes 196616 | tf_op jit(solution)/shard_map/ppermute | solution.py:23
  54.2 7.9 %collective-permute-start.5 = (f32[16,2048]{1,0:T(8,128)S(1)}, f32[16,2048]{1,0:T(8,128)S(1)}, u32[]{:S(2)}, u32[]{:S(2)}) collective-permute-start(f32[16,2048]{1,0:T(8,128)S(1)} %fusion.15), channel_id=1, source_target_pairs={{0,128},{128,0},{4,132},{132,4},{8,136},{136,8},{12,140},{140,12},... | collective-permute-start | bytes 393224 | tf_op jit(solution)/shard_map/ppermute | solution.py:23
  64.3 14.2 %collective-permute-start.6 = (f32[32,2048]{1,0:T(8,128)S(1)}, f32[32,2048]{1,0:T(8,128)S(1)}, u32[]{:S(2)}, u32[]{:S(2)}) collective-permute-start(f32[32,2048]{1,0:T(8,128)S(1)} %fusion.13), channel_id=1, source_target_pairs={{384,0},{388,4},{392,8},{396,12},{400,16},{404,20},{408,24},{412,2... | collective-permute-start | bytes 786440 | tf_op jit(solution)/shard_map/ppermute | solution.py:27
  94.5 3.1 %collective-permute-start.7 = (f32[9,512]{1,0:T(8,128)S(1)}, f32[9,512]{1,0:T(8,128)S(1)}, u32[]{:S(2)}, u32[]{:S(2)}) collective-permute-start(f32[9,512]{1,0:T(8,128)S(1)} %reduce_max.99), channel_id=1, source_target_pairs={{0,4},{4,0},{8,12},{12,8},{16,20},{20,16},{24,28},{28,24},{32,36},... | collective-permute-start | bytes 55304 | tf_op jit(solution)/shard_map/ppermute | solution.py:23
  97.6 5.8 %collective-permute-start.8 = (f32[9,512]{1,0:T(8,128)S(1)}, f32[9,512]{1,0:T(8,128)S(1)}, u32[]{:S(2)}, u32[]{:S(2)}) collective-permute-start(f32[9,512]{1,0:T(8,128)S(1)} %max.9), channel_id=1, source_target_pairs={{0,8},{8,0},{4,12},{12,4},{16,24},{24,16},{20,28},{28,20},{32,40},... | collective-permute-start | bytes 55304 | tf_op jit(solution)/shard_map/ppermute | solution.py:23
  103.4 10.0 %collective-permute-start.9 = (f32[9,512]{1,0:T(8,128)S(1)}, f32[9,512]{1,0:T(8,128)S(1)}, u32[]{:S(2)}, u32[]{:S(2)}) collective-permute-start(f32[9,512]{1,0:T(8,128)S(1)} %max.10), channel_id=1, source_target_pairs={{56,0},{60,4},{16,8},{20,12},{8,16},{12,20},{32,24},{36,28},{24,32... | collective-permute-start | bytes 55304 | tf_op jit(solution)/shard_map/ppermute | solution.py:27

commit v7 on v4

--- a/solution.py
+++ b/solution.py
@@ -50,54 +50,87 @@
     return low_rows + moved
 
 
-def delay_plan(sub_dev, held, freq_bits, shared, all_trials):
-    terms = 2 + freq_bits
-    ids, rates, jits, level_rows = [], [], [], []
-    trial_count = 2
-    while trial_count <= sub_dev:
-        groups = sub_dev // trial_count
-        rows = groups * trial_count
-        trial = np.tile(np.arange(trial_count), groups)
-        group = np.repeat(np.arange(groups), trial_count)
-        one_id = np.zeros((terms, rows), np.int64)
-        one_id[0] = trial
-        one_rate = np.zeros((terms, rows), np.int64)
-        one_rate[0] = all_trials // trial_count - 1 + group
-        for bit in range(freq_bits):
-            one_rate[2 + bit] = groups << bit
-        ids.append(one_id)
-        rates.append(one_rate)
-        level_rows.append(rows)
-        trial_count = trial_count * 2
-    now = np.zeros((terms, held), np.int64)
-    now[0] = np.arange(held)
-    now[1] = held
+def shift_rows(rows, shifts, bit_count):
+    limit = 2**bit_count - 1
+    offsets = limit - shifts
+    moved = zero_front(rows, limit)
+    for bit_index in range(bit_count):
+        step_size = 2**bit_index
+        cols = moved.shape[-1]
+        selected = (offsets >> bit_index & 1)[:, None] == 1
+        moved = jnp.where(selected, moved[:, step_size:], moved[:, : cols - step_size])
+    return moved
+
+
+def delay_plan(sub_dev, held, tm_bits, freq_bits, shared, all_trials):
+    terms = 1 + tm_bits + freq_bits
+    local_bits = sub_dev.bit_length() - 1
+    held_bits = held.bit_length() - 1
+
+    def held_trial(m, right):
+        value = np.zeros(terms, np.int64)
+        for p in range(held_bits + tm_bits):
+            if p < right:
+                continue
+            if p < held_bits:
+                value[0] += (m >> p & 1) << (p - right)
+            else:
+                value[1 + p - held_bits] += 1 << (p - right)
+        return value
+
+    ids, rates, jits = [], [], []
+    slot = {}
+    for k in range(1, local_bits + 1):
+        trial_count = 2**k
+        for m in range(held):
+            trial = held_trial(m, local_bits - k)
+            for g in range(sub_dev >> k):
+                key = (k, g, tuple(trial))
+                if key in slot:
+                    continue
+                slot[key] = len(ids)
+                rate = np.zeros(terms, np.int64)
+                rate[0] = all_trials // trial_count - 1 + g
+                for bit in range(freq_bits):
+                    rate[1 + tm_bits + bit] = (sub_dev >> k) << bit
+                jit = trial.copy()
+                jit[0] += trial_count - 2
+                ids.append(trial)
+                rates.append(rate)
+                jits.append(jit)
+    paths = np.zeros((held * sub_dev, len(ids)), np.float32)
+    for m in range(held):
+        for i in range(sub_dev):
+            for k in range(1, local_bits + 1):
+                if i >> (k - 1) & 1:
+                    key = (k, i >> k, tuple(held_trial(m, local_bits - k)))
+                    paths[m * sub_dev + i, slot[key]] += 1.0
+    unique_count = len(ids)
+    level_rows = []
+    now = np.zeros((held, terms), np.int64)
+    for m in range(held):
+        now[m] = held_trial(m, 0)
     for bit_index in range(freq_bits):
         trial_count = sub_dev * 2 ** (bit_index + 1)
         if bit_index >= freq_bits - shared:
-            now = 2 * np.repeat(now, 2, axis=1)
-            now[0] = now[0] + np.tile(np.arange(2), now.shape[1] // 2)
+            now = 2 * np.repeat(now, 2, axis=0)
+            now[:, 0] = now[:, 0] + np.tile(np.arange(2), now.shape[0] // 2)
         else:
             now = 2 * now
-            now[2 + bit_index] = now[2 + bit_index] + 1
-        one_rate = np.zeros_like(now)
-        one_rate[0] = all_trials // trial_count - 1
+            now[:, 1 + tm_bits + bit_index] = now[:, 1 + tm_bits + bit_index] + 1
+        rate = np.zeros(terms, np.int64)
+        rate[0] = all_trials // trial_count - 1
         for bit in range(bit_index + 1, freq_bits):
-            one_rate[2 + bit] = 1 << (bit - bit_index - 1)
-        ids.append(now.copy())
-        rates.append(one_rate)
-        level_rows.append(now.shape[1])
-    counts = []
-    trial_count = 2
-    while trial_count <= sub_dev:
-        counts.append(trial_count)
-        trial_count = trial_count * 2
-    counts += [sub_dev * 2 ** (bit_index + 1) for bit_index in range(freq_bits)]
-    jit_rows = [one_id.copy() for one_id in ids]
-    for one_jit, trial_count in zip(jit_rows, counts):
-        one_jit[0] = one_jit[0] + trial_count - 2
-    pack = lambda parts: np.concatenate(parts, axis=1).astype(np.int32)
-    return pack(ids), pack(rates), pack(jit_rows), level_rows
+            rate[1 + tm_bits + bit] = 1 << (bit - bit_index - 1)
+        for row in now:
+            jit = row.copy()
+            jit[0] += trial_count - 2
+            ids.append(row.copy())
+            rates.append(rate)
+            jits.append(jit)
+        level_rows.append(now.shape[0])
+    pack = lambda parts: np.stack(parts, axis=1).astype(np.int32)
+    return pack(ids), pack(rates), pack(jits), paths, unique_count, level_rows
 
 
 def shards(spectrogram, low_share, jitter):
@@ -111,19 +144,25 @@
     place = lax.axis_index("tm")
     held = sub_dev // tm_count
 
-    id_terms, rate_terms, jitter_terms, level_rows = delay_plan(
-        sub_dev, held, freq_bits, shared, all_trials
+    tm_bits = tm_count.bit_length() - 1
+    id_terms, rate_terms, jitter_terms, paths, unique_count, level_rows = delay_plan(
+        sub_dev, held, tm_bits, freq_bits, shared, all_trials
     )
     factors = jnp.concatenate(
-        [jnp.ones((1,), jnp.int32), place[None].astype(jnp.int32),
+        [jnp.ones((1,), jnp.int32),
+         (place >> jnp.arange(tm_bits, dtype=jnp.int32) & 1).astype(jnp.int32),
          (device >> jnp.arange(freq_bits, dtype=jnp.int32) & 1).astype(jnp.int32)]
     )[:, None]
     ids_all = jnp.sum(factors * id_terms, axis=0)
     rates = jnp.take(low_share, jnp.sum(factors * rate_terms, axis=0))
     jitters = jnp.take(jitter, jnp.sum(factors * jitter_terms, axis=0))
     shift_table = (ids_all * rates + jitters) // 64
+    path_shift = jnp.dot(
+        paths, shift_table[:unique_count].astype(jnp.float32), precision=lax.Precision.HIGHEST
+    )
+    path_shift = jnp.round(path_shift).astype(jnp.int32)
     level_shifts = []
-    start = 0
+    start = unique_count
     for rows in level_rows:
         level_shifts.append(shift_table[start : start + rows])
         start = start + rows
@@ -133,22 +172,10 @@
     gathered = lax.all_to_all(spread, "tm", 0, 0, tiled=True)
     base = jnp.transpose(gathered, (1, 0, 2)).reshape(sub_dev, tm_count * span_time)
     full_time = base.shape[1]
-    states = base[:, None, :]
+    local_limit = sum(2**k - 1 for k in range(1, sub_dev.bit_length()))
+    moved = shift_rows(jnp.tile(base, (held, 1)), path_shift, max(local_limit.bit_length(), 1))
+    trial_rows = jnp.sum(moved.reshape(held, sub_dev, full_time), axis=1)
     level = 0
-    trial_count = 2
-    while trial_count <= sub_dev:
-        need_now = trial_count - 1
-        groups = states.shape[0] // 2
-        low_rows = jnp.repeat(states[0::2], 2, axis=1).reshape(groups * trial_count, -1)
-        high_rows = jnp.repeat(zero_front(states[1::2], need_now), 2, axis=1).reshape(
-            groups * trial_count, -1
-        )
-        states = merge_rows(low_rows, high_rows, level_shifts[level], need_now).reshape(
-            groups, trial_count, -1
-        )
-        level = level + 1
-        trial_count = trial_count * 2
-    trial_rows = lax.dynamic_slice_in_dim(states[0], place * held, held, axis=0)
     for bit_index in range(freq_bits):
         need_now = sub_dev * 2 ** (bit_index + 1) - 1
         if bit_index == freq_bits - 1 and shared >= 3 and bit_index >= 2:

time: 113 us -> 110 us (0.973)
  local copies, waits for them, and re-layouts: 8.08 us -> 5.43 us
    select_n x55 -> x49, other arithmetic: 6.01 us -> 5.41 us  [merge_rows(): jnp.where(selected, moved[:, step_size:], moved[:, :cols - step_size])]
where the time goes in v7:
time: 110 us
  starting transfers between devices  57.3 us (52%)
  waiting for transfers between devices  26.3 us (24%)
  other arithmetic  10.9 us (10%)
  blocking collectives  8.66 us (8%)
  local copies, waits for them, and re-layouts  5.43 us (5%)
    ppermute x9, starting transfers between devices, swapped(): return lax.ppermute(block, axis, route)  38.2 us
    ppermute x9, waiting for transfers between devices, swapped(): return lax.ppermute(block, axis, route)  18.2 us
    ppermute x2, starting transfers between devices, paired(): lax.ppermute(block, axis, [(partner_of(i), i) for i in range(lax.axis_siz...  14.6 us
    all_to_all x1, blocking collectives, shards(): best = jnp.max(lax.all_to_all(best, 'tm', 1, 1, tiled=True), axis=1)  8.66 us
    ppermute x2, waiting for transfers between devices, paired(): lax.ppermute(block, axis, [(partner_of(i), i) for i in range(lax.axis_siz...  6.14 us
    select_n x49, other arithmetic, merge_rows(): jnp.where(selected, moved[:, step_size:], moved[:, :cols - step_size])  5.41 us
    all_to_all x1, starting transfers between devices, shards(): gathered = lax.all_to_all(spread, 'tm', 0, 0, tiled=True)  4.42 us
  transfers between devices with their start and end apart: 12, of which 12 were waited for; matrix products, arithmetic and copies ran while one was open for 3% of the time, Pallas kernels for 0%

profile of v7, /device:TPU:16, one launch (start us, length us, event | category | flops | bytes accessed | tf_op | source)
XLA Modules:
  0.0 109.7 jit_solution(11169240156313462165)
XLA Ops:
  0.0 1.2 %convert_reduce_fusion = f32[16,512]{1,0:T(8,128)S(1)} fusion(bf16[512,512]{1,0:T(8,128)(2,1)} %param.7), kind=kLoop, calls=%fused_computation.6 | loop fusion | flops 516096 | bytes 557056 | tf_op jit(solution)/shard_map/reduce_sum | solution.py:170
  1.2 0.6 broadcast_in_dim.581
  1.8 4.4 %all-to-all-start = ((f32[4,16,512]{2,1,0:T(8,128)}), f32[4,16,512]{2,1,0:T(8,128)S(1)}, u32[]{:S(2)}, u32[]{:S(2)}) async-start(f32[4,16,512]{2,1,0:T(8,128)} %broadcast_in_dim.581), calls=%async_computation | async-start | bytes 262144 | tf_op jit(solution)/shard_map/all_to_all | solution.py:172
  6.4 0.6 copy-done.3
  7.1 0.6 copy-done.1
  7.8 1.1 %gather_fusion = s32[92]{0:T(128)S(1)} fusion(s32[2047]{0:T(1024)S(1)} %copy-done.1, s32[1024]{0:T(1024)S(1)} %pad_clamp_fusion.1), kind=kCustom, calls=%fused_computation | custom fusion | bytes 1104 | tf_op jit(solution)/shard_map/jit(_take)/gather | solution.py:157
  8.9 1.1 %gather_fusion.1 = s32[92]{0:T(128)S(1)} fusion(s32[4094]{0:T(1024)S(1)} %copy-done, s32[1024]{0:T(1024)S(1)} %pad_clamp_fusion), kind=kCustom, calls=%fused_computation.1 | custom fusion | bytes 1104 | tf_op jit(solution)/shard_map/jit(_take)/gather | solution.py:158
  10.3 1.9 %all-to-all-done = f32[4,16,512]{2,1,0:T(8,128)S(1)} async-done(((f32[4,16,512]{2,1,0:T(8,128)}), f32[4,16,512]{2,1,0:T(8,128)S(1)}, u32[]{:S(2)}, u32[]{:S(2)}) %all-to-all-start) | async-done | bytes 131104 | tf_op jit(solution)/shard_map/all_to_all | solution.py:172
  13.6 1.9 %collective-permute-start = (f32[4,2048]{1,0:T(4,128)S(1)}, f32[4,2048]{1,0:T(4,128)S(1)}, u32[]{:S(2)}, u32[]{:S(2)}) collective-permute-start(f32[4,2048]{1,0:T(4,128)S(1)} %bitcast_reduce_fusion), channel_id=1, source_target_pairs={{0,4},{4,0},{8,12},{12,8},{16,20},{20,16},{24,28},{28,24},{32,36},... | collective-permute-start | bytes 98312 | tf_op jit(solution)/shard_map/ppermute | solution.py:22
  15.6 1.1 collective-permute-done
  17.2 4.3 %collective-permute-start.1 = (f32[4,2048]{1,0:T(4,128)S(1)}, f32[4,2048]{1,0:T(4,128)S(1)}, u32[]{:S(2)}, u32[]{:S(2)}) collective-permute-start(f32[4,2048]{1,0:T(4,128)S(1)} %fusion.22), channel_id=1, source_target_pairs={{0,8},{8,0},{4,12},{12,4},{16,24},{24,16},{20,28},{28,20},{32,40},... | collective-permute-start | bytes 98312 | tf_op jit(solution)/shard_map/ppermute | solution.py:22
  21.6 1.8 %collective-permute-done.1 = f32[4,2048]{1,0:T(4,128)S(1)} collective-permute-done((f32[4,2048]{1,0:T(4,128)S(1)}, f32[4,2048]{1,0:T(4,128)S(1)}, u32[]{:S(2)}, u32[]{:S(2)}) %collective-permute-start.1) | collective-permute-done | bytes 32800 | tf_op jit(solution)/shard_map/ppermute | solution.py:22
  23.9 6.1 %collective-permute-start.2 = (f32[4,2048]{1,0:T(4,128)S(1)}, f32[4,2048]{1,0:T(4,128)S(1)}, u32[]{:S(2)}, u32[]{:S(2)}) collective-permute-start(f32[4,2048]{1,0:T(4,128)S(1)} %fusion.21), channel_id=1, source_target_pairs={{0,16},{16,0},{4,20},{20,4},{8,24},{24,8},{12,28},{28,12},{32,48},... | collective-permute-start | bytes 98312 | tf_op jit(solution)/shard_map/ppermute | solution.py:22
  30.0 2.0 %collective-permute-done.2 = f32[4,2048]{1,0:T(4,128)S(1)} collective-permute-done((f32[4,2048]{1,0:T(4,128)S(1)}, f32[4,2048]{1,0:T(4,128)S(1)}, u32[]{:S(2)}, u32[]{:S(2)}) %collective-permute-start.2) | collective-permute-done | bytes 32800 | tf_op jit(solution)/shard_map/ppermute | solution.py:22
  32.7 9.2 %collective-permute-start.3 = (f32[4,2048]{1,0:T(4,128)S(1)}, f32[4,2048]{1,0:T(4,128)S(1)}, u32[]{:S(2)}, u32[]{:S(2)}) collective-permute-start(f32[4,2048]{1,0:T(4,128)S(1)} %fusion.20), channel_id=1, source_target_pairs={{0,32},{32,0},{4,36},{36,4},{8,40},{40,8},{12,44},{44,12},{16,48},... | collective-permute-start | bytes 98312 | tf_op jit(solution)/shard_map/ppermute | solution.py:22
  41.9 1.9 %collective-permute-done.3 = f32[4,2048]{1,0:T(4,128)S(1)} collective-permute-done((f32[4,2048]{1,0:T(4,128)S(1)}, f32[4,2048]{1,0:T(4,128)S(1)}, u32[]{:S(2)}, u32[]{:S(2)}) %collective-permute-start.3) | collective-permute-done | bytes 32800 | tf_op jit(solution)/shard_map/ppermute | solution.py:22
  44.6 3.5 %collective-permute-start.4 = (f32[4,2048]{1,0:T(4,128)S(1)}, f32[4,2048]{1,0:T(4,128)S(1)}, u32[]{:S(2)}, u32[]{:S(2)}) collective-permute-start(f32[4,2048]{1,0:T(4,128)S(1)} %fusion.19), channel_id=1, source_target_pairs={{0,64},{64,0},{4,68},{68,4},{8,72},{72,8},{12,76},{76,12},{16,80},... | collective-permute-start | bytes 98312 | tf_op jit(solution)/shard_map/ppermute | solution.py:22
  48.2 2.2 %collective-permute-done.4 = f32[4,2048]{1,0:T(4,128)S(1)} collective-permute-done((f32[4,2048]{1,0:T(4,128)S(1)}, f32[4,2048]{1,0:T(4,128)S(1)}, u32[]{:S(2)}, u32[]{:S(2)}) %collective-permute-start.4) | collective-permute-done | bytes 32800 | tf_op jit(solution)/shard_map/ppermute | solution.py:22
  51.4 3.5 %collective-permute-start.5 = (f32[8,2048]{1,0:T(8,128)S(1)}, f32[8,2048]{1,0:T(8,128)S(1)}, u32[]{:S(2)}, u32[]{:S(2)}) collective-permute-start(f32[8,2048]{1,0:T(8,128)S(1)} %fusion.18), channel_id=1, source_target_pairs={{0,128},{128,0},{4,132},{132,4},{8,136},{136,8},{12,140},{140,12},... | collective-permute-start | bytes 196616 | tf_op jit(solution)/shard_map/ppermute | solution.py:22
  55.0 3.5 %collective-permute-done.5 = f32[8,2048]{1,0:T(8,128)S(1)} collective-permute-done((f32[8,2048]{1,0:T(8,128)S(1)}, f32[8,2048]{1,0:T(8,128)S(1)}, u32[]{:S(2)}, u32[]{:S(2)}) %collective-permute-start.5) | collective-permute-done | bytes 65568 | tf_op jit(solution)/shard_map/ppermute | solution.py:22
  60.0 6.3 %collective-permute-start.6 = (f32[16,2048]{1,0:T(8,128)S(1)}, f32[16,2048]{1,0:T(8,128)S(1)}, u32[]{:S(2)}, u32[]{:S(2)}) collective-permute-start(f32[16,2048]{1,0:T(8,128)S(1)} %fusion.16), channel_id=1, source_target_pairs={{384,0},{388,4},{392,8},{396,12},{400,16},{404,20},{408,24},{412,2... | collective-permute-start | bytes 393224 | tf_op jit(solution)/shard_map/ppermute | solution.py:26
  66.4 4.2 %collective-permute-done.6 = f32[16,2048]{1,0:T(8,128)S(1)} collective-permute-done((f32[16,2048]{1,0:T(8,128)S(1)}, f32[16,2048]{1,0:T(8,128)S(1)}, u32[]{:S(2)}, u32[]{:S(2)}) %collective-permute-start.6) | collective-permute-done | bytes 131104 | tf_op jit(solution)/shard_map/ppermute | solution.py:26
  74.6 8.7 %all_to_all.10 = f32[9,4,512]{2,0,1:T(8,128)S(1)} all-to-all(f32[9,4,512]{2,0,1:T(8,128)S(1)} %stack.5), channel_id=1, replica_groups=mesh['freq'=128,'tm'=4] {'tm'}, dimensions={1} | all-to-all | bytes 147456 | tf_op jit(solution)/shard_map/all_to_all | solution.py:205
  83.3 1.9 %collective-permute-start.7 = (f32[9,512]{1,0:T(8,128)S(1)}, f32[9,512]{1,0:T(8,128)S(1)}, u32[]{:S(2)}, u32[]{:S(2)}) collective-permute-start(f32[9,512]{1,0:T(8,128)S(1)} %reduce_max.99), channel_id=1, source_target_pairs={{0,4},{4,0},{8,12},{12,8},{16,20},{20,16},{24,28},{28,24},{32,36},... | collective-permute-start | bytes 55304 | tf_op jit(solution)/shard_map/ppermute | solution.py:22
  85.2 1.2 %collective-permute-done.7 = f32[9,512]{1,0:T(8,128)S(1)} collective-permute-done((f32[9,512]{1,0:T(8,128)S(1)}, f32[9,512]{1,0:T(8,128)S(1)}, u32[]{:S(2)}, u32[]{:S(2)}) %collective-permute-start.7) | collective-permute-done | bytes 18464 | tf_op jit(solution)/shard_map/ppermute | solution.py:22
  86.4 3.3 %collective-permute-start.8 = (f32[9,512]{1,0:T(8,128)S(1)}, f32[9,512]{1,0:T(8,128)S(1)}, u32[]{:S(2)}, u32[]{:S(2)}) collective-permute-start(f32[9,512]{1,0:T(8,128)S(1)} %max.12), channel_id=1, source_target_pairs={{0,8},{8,0},{4,12},{12,4},{16,24},{24,16},{20,28},{28,20},{32,40},... | collective-permute-start | bytes 55304 | tf_op jit(solution)/shard_map/ppermute | solution.py:22
  89.8 2.4 %collective-permute-done.8 = f32[9,512]{1,0:T(8,128)S(1)} collective-permute-done((f32[9,512]{1,0:T(8,128)S(1)}, f32[9,512]{1,0:T(8,128)S(1)}, u32[]{:S(2)}, u32[]{:S(2)}) %collective-permute-start.8) | collective-permute-done | bytes 18464 | tf_op jit(solution)/shard_map/ppermute | solution.py:22
  92.2 4.6 %collective-permute-start.9 = (f32[9,512]{1,0:T(8,128)S(1)}, f32[9,512]{1,0:T(8,128)S(1)}, u32[]{:S(2)}, u32[]{:S(2)}) collective-permute-start(f32[9,512]{1,0:T(8,128)S(1)} %max.13), channel_id=1, source_target_pairs={{0,16},{16,0},{4,20},{20,4},{8,24},{24,8},{12,28},{28,12},{32,48},... | collective-permute-start | bytes 55304 | tf_op jit(solution)/shard_map/ppermute | solution.py:22
  96.8 2.1 %collective-permute-done.9 = f32[9,512]{1,0:T(8,128)S(1)} collective-permute-done((f32[9,512]{1,0:T(8,128)S(1)}, f32[9,512]{1,0:T(8,128)S(1)}, u32[]{:S(2)}, u32[]{:S(2)}) %collective-permute-start.9) | collective-permute-done | bytes 18464 | tf_op jit(solution)/shard_map/ppermute | solution.py:22
  98.9 8.3 %collective-permute-start.10 = (f32[9,512]{1,0:T(8,128)S(1)}, f32[9,512]{1,0:T(8,128)S(1)}, u32[]{:S(2)}, u32[]{:S(2)}) collective-permute-start(f32[9,512]{1,0:T(8,128)S(1)} %max.14), channel_id=1, source_target_pairs={{48,0},{52,4},{56,8},{60,12},{32,16},{36,20},{40,24},{44,28},{16,3... | collective-permute-start | bytes 55304 | tf_op jit(solution)/shard_map/ppermute | solution.py:26
  107.2 1.9 %collective-permute-done.10 = f32[9,512]{1,0:T(8,128)S(1)} collective-permute-done((f32[9,512]{1,0:T(8,128)S(1)}, f32[9,512]{1,0:T(8,128)S(1)}, u32[]{:S(2)}, u32[]{:S(2)}) %collective-permute-start.10) | collective-permute-done | bytes 18464 | tf_op jit(solution)/shard_map/ppermute | solution.py:26
  109.1 0.6 max.15
  (127 shorter events, 10.6 us)
Async XLA Ops:
  0.0 8.9 %copy-start = (s32[4094]{0:T(1024)S(1)}, s32[4094]{0:T(1024)}, u32[]{:S(2)}) copy-start(s32[4094]{0:T(1024)} %param.9) | copy-start | bytes 49132
  1.8 4.5 %copy-start.4 = (s32[10,92]{1,0:T(8,128)S(1)}, s32[10,92]{1,0:T(8,128)}, u32[]{:S(2)}) copy-start(s32[10,92]{1,0:T(8,128)} %constant.80.clone) | copy-start | bytes 11044
  1.8 10.4 %all-to-all-start = ((f32[4,16,512]{2,1,0:T(8,128)}), f32[4,16,512]{2,1,0:T(8,128)S(1)}, u32[]{:S(2)}, u32[]{:S(2)}) async-start(f32[4,16,512]{2,1,0:T(8,128)} %broadcast_in_dim.581), calls=%async_computation | async-start | bytes 262144 | tf_op jit(solution)/shard_map/all_to_all | solution.py:172
  6.3 0.7 copy-start.3
  6.3 0.7 copy-start.2
  7.1 0.7 copy-start.1
  8.9 1.2 %copy-start.5 = (f32[64,20]{1,0:T(8,128)S(1)}, f32[64,20]{1,0:T(8,128)}, u32[]{:S(2)}) copy-start(f32[64,20]{1,0:T(8,128)} %constant.83.clone) | copy-start | bytes 15364
  13.6 3.1 %collective-permute-start = (f32[4,2048]{1,0:T(4,128)S(1)}, f32[4,2048]{1,0:T(4,128)S(1)}, u32[]{:S(2)}, u32[]{:S(2)}) collective-permute-start(f32[4,2048]{1,0:T(4,128)S(1)} %bitcast_reduce_fusion), channel_id=1, source_target_pairs={{0,4},{4,0},{8,12},{12,8},{16,20},{20,16},{24,28},{28,24},{32,36},... | collective-permute-start | bytes 98312 | tf_op jit(solution)/shard_map/ppermute | solution.py:22
  17.2 6.2 %collective-permute-start.1 = (f32[4,2048]{1,0:T(4,128)S(1)}, f32[4,2048]{1,0:T(4,128)S(1)}, u32[]{:S(2)}, u32[]{:S(2)}) collective-permute-start(f32[4,2048]{1,0:T(4,128)S(1)} %fusion.22), channel_id=1, source_target_pairs={{0,8},{8,0},{4,12},{12,4},{16,24},{24,16},{20,28},{28,20},{32,40},... | collective-permute-start | bytes 98312 | tf_op jit(solution)/shard_map/ppermute | solution.py:22
  23.9 8.1 %collective-permute-start.2 = (f32[4,2048]{1,0:T(4,128)S(1)}, f32[4,2048]{1,0:T(4,128)S(1)}, u32[]{:S(2)}, u32[]{:S(2)}) collective-permute-start(f32[4,2048]{1,0:T(4,128)S(1)} %fusion.21), channel_id=1, source_target_pairs={{0,16},{16,0},{4,20},{20,4},{8,24},{24,8},{12,28},{28,12},{32,48},... | collective-permute-start | bytes 98312 | tf_op jit(solution)/shard_map/ppermute | solution.py:22
  32.7 11.1 %collective-permute-start.3 = (f32[4,2048]{1,0:T(4,128)S(1)}, f32[4,2048]{1,0:T(4,128)S(1)}, u32[]{:S(2)}, u32[]{:S(2)}) collective-permute-start(f32[4,2048]{1,0:T(4,128)S(1)} %fusion.20), channel_id=1, source_target_pairs={{0,32},{32,0},{4,36},{36,4},{8,40},{40,8},{12,44},{44,12},{16,48},... | collective-permute-start | bytes 98312 | tf_op jit(solution)/shard_map/ppermute | solution.py:22
  44.6 5.8 %collective-permute-start.4 = (f32[4,2048]{1,0:T(4,128)S(1)}, f32[4,2048]{1,0:T(4,128)S(1)}, u32[]{:S(2)}, u32[]{:S(2)}) collective-permute-start(f32[4,2048]{1,0:T(4,128)S(1)} %fusion.19), channel_id=1, source_target_pairs={{0,64},{64,0},{4,68},{68,4},{8,72},{72,8},{12,76},{76,12},{16,80},... | collective-permute-start | bytes 98312 | tf_op jit(solution)/shard_map/ppermute | solution.py:22
  51.4 7.1 %collective-permute-start.5 = (f32[8,2048]{1,0:T(8,128)S(1)}, f32[8,2048]{1,0:T(8,128)S(1)}, u32[]{:S(2)}, u32[]{:S(2)}) collective-permute-start(f32[8,2048]{1,0:T(8,128)S(1)} %fusion.18), channel_id=1, source_target_pairs={{0,128},{128,0},{4,132},{132,4},{8,136},{136,8},{12,140},{140,12},... | collective-permute-start | bytes 196616 | tf_op jit(solution)/shard_map/ppermute | solution.py:22
  60.0 10.7 %collective-permute-start.6 = (f32[16,2048]{1,0:T(8,128)S(1)}, f32[16,2048]{1,0:T(8,128)S(1)}, u32[]{:S(2)}, u32[]{:S(2)}) collective-permute-start(f32[16,2048]{1,0:T(8,128)S(1)} %fusion.16), channel_id=1, source_target_pairs={{384,0},{388,4},{392,8},{396,12},{400,16},{404,20},{408,24},{412,2... | collective-permute-start | bytes 393224 | tf_op jit(solution)/shard_map/ppermute | solution.py:26
  83.3 3.1 %collective-permute-start.7 = (f32[9,512]{1,0:T(8,128)S(1)}, f32[9,512]{1,0:T(8,128)S(1)}, u32[]{:S(2)}, u32[]{:S(2)}) collective-permute-start(f32[9,512]{1,0:T(8,128)S(1)} %reduce_max.99), channel_id=1, source_target_pairs={{0,4},{4,0},{8,12},{12,8},{16,20},{20,16},{24,28},{28,24},{32,36},... | collective-permute-start | bytes 55304 | tf_op jit(solution)/shard_map/ppermute | solution.py:22
  86.4 5.8 %collective-permute-start.8 = (f32[9,512]{1,0:T(8,128)S(1)}, f32[9,512]{1,0:T(8,128)S(1)}, u32[]{:S(2)}, u32[]{:S(2)}) collective-permute-start(f32[9,512]{1,0:T(8,128)S(1)} %max.12), channel_id=1, source_target_pairs={{0,8},{8,0},{4,12},{12,4},{16,24},{24,16},{20,28},{28,20},{32,40},... | collective-permute-start | bytes 55304 | tf_op jit(solution)/shard_map/ppermute | solution.py:22
  92.2 6.7 %collective-permute-start.9 = (f32[9,512]{1,0:T(8,128)S(1)}, f32[9,512]{1,0:T(8,128)S(1)}, u32[]{:S(2)}, u32[]{:S(2)}) collective-permute-start(f32[9,512]{1,0:T(8,128)S(1)} %max.13), channel_id=1, source_target_pairs={{0,16},{16,0},{4,20},{20,4},{8,24},{24,8},{12,28},{28,12},{32,48},... | collective-permute-start | bytes 55304 | tf_op jit(solution)/shard_map/ppermute | solution.py:22
  98.9 10.2 %collective-permute-start.10 = (f32[9,512]{1,0:T(8,128)S(1)}, f32[9,512]{1,0:T(8,128)S(1)}, u32[]{:S(2)}, u32[]{:S(2)}) collective-permute-start(f32[9,512]{1,0:T(8,128)S(1)} %max.14), channel_id=1, source_target_pairs={{48,0},{52,4},{56,8},{60,12},{32,16},{36,20},{40,24},{44,28},{16,3... | collective-permute-start | bytes 55304 | tf_op jit(solution)/shard_map/ppermute | solution.py:26

commit v8 on v7

--- a/solution.py
+++ b/solution.py
@@ -60,6 +60,11 @@
         selected = (offsets >> bit_index & 1)[:, None] == 1
         moved = jnp.where(selected, moved[:, step_size:], moved[:, : cols - step_size])
     return moved
+
+
+def picked(table, index):
+    hit = index[:, None] == jnp.arange(table.shape[0], dtype=jnp.int32)[None, :]
+    return jnp.sum(jnp.where(hit, table[None, :], 0), axis=1)
 
 
 def delay_plan(sub_dev, held, tm_bits, freq_bits, shared, all_trials):
@@ -154,8 +159,8 @@
          (device >> jnp.arange(freq_bits, dtype=jnp.int32) & 1).astype(jnp.int32)]
     )[:, None]
     ids_all = jnp.sum(factors * id_terms, axis=0)
-    rates = jnp.take(low_share, jnp.sum(factors * rate_terms, axis=0))
-    jitters = jnp.take(jitter, jnp.sum(factors * jitter_terms, axis=0))
+    rates = picked(low_share, jnp.sum(factors * rate_terms, axis=0))
+    jitters = picked(jitter, jnp.sum(factors * jitter_terms, axis=0))
     shift_table = (ids_all * rates + jitters) // 64
     path_shift = jnp.dot(
         paths, shift_table[:unique_count].astype(jnp.float32), precision=lax.Precision.HIGHEST

time: 110 us -> 110 us (level)
  local copies, waits for them, and re-layouts: 5.43 us -> 1.89 us
  waiting for transfers between devices: 26.3 us -> 29.3 us
    all_to_all x1, waiting for transfers between devices: 1.93 us -> 4.94 us  [shards(): gathered = lax.all_to_all(spread, 'tm', 0, 0, tiled=True)]
    gather x2 -> x0, local copies, waits for them, and re-layouts: 2.29 us -> none  [the longest x1 1.15 us: shards(): jitters = jnp.take(jitter, jnp.sum(factors * jitter_terms, axis=0))]
    unnamed x12, local copies, waits for them, and re-layouts: 1.28 us -> 0.03 us
  transfers between devices with their start and end apart: 12 -> 12, of which waited for: 12 -> 12; matrix products, arithmetic and copies ran while one was open for 3% -> 1% of each run, Pallas kernels for 0% -> 0%
where the time goes in v8:
time: 110 us; the launch traced here: 109 us
  starting transfers between devices  57.2 us (52%)
  waiting for transfers between devices  29.3 us (27%)
  other arithmetic  11.6 us (11%)
  blocking collectives  8.36 us (8%)
  local copies, waits for them, and re-layouts  1.89 us (2%)
    ppermute x9, starting transfers between devices, swapped(): return lax.ppermute(block, axis, route)  38.2 us
    ppermute x9, waiting for transfers between devices, swapped(): return lax.ppermute(block, axis, route)  18.2 us
    ppermute x2, starting transfers between devices, paired(): lax.ppermute(block, axis, [(partner_of(i), i) for i in range(lax.axis_siz...  14.6 us
    all_to_all x1, blocking collectives, shards(): best = jnp.max(lax.all_to_all(best, 'tm', 1, 1, tiled=True), axis=1)  8.36 us
    ppermute x2, waiting for transfers between devices, paired(): lax.ppermute(block, axis, [(partner_of(i), i) for i in range(lax.axis_siz...  6.14 us
    select_n x49, other arithmetic, merge_rows(): jnp.where(selected, moved[:, step_size:], moved[:, :cols - step_size])  5.41 us
    all_to_all x1, waiting for transfers between devices, shards(): gathered = lax.all_to_all(spread, 'tm', 0, 0, tiled=True)  4.94 us
    all_to_all x1, starting transfers between devices, shards(): gathered = lax.all_to_all(spread, 'tm', 0, 0, tiled=True)  4.29 us
  transfers between devices with their start and end apart: 12, of which 12 were waited for; matrix products, arithmetic and copies ran while one was open for 1% of the time, Pallas kernels for 0%

profile of v8, /device:TPU:16, one launch (start us, length us, event | category | flops | bytes accessed | tf_op | source)
XLA Modules:
  0.0 109.4 jit_solution(5262094222727910679)
XLA Ops:
  0.0 1.2 %convert_reduce_fusion = f32[16,512]{1,0:T(8,128)S(1)} fusion(bf16[512,512]{1,0:T(8,128)(2,1)} %param.7), kind=kLoop, calls=%fused_computation.6 | loop fusion | flops 516096 | bytes 557056 | tf_op jit(solution)/shard_map/reduce_sum | solution.py:175
  1.3 0.6 broadcast_in_dim.604
  1.9 4.3 %all-to-all-start = ((f32[4,16,512]{2,1,0:T(8,128)}), f32[4,16,512]{2,1,0:T(8,128)S(1)}, u32[]{:S(2)}, u32[]{:S(2)}) async-start(f32[4,16,512]{2,1,0:T(8,128)} %broadcast_in_dim.604), calls=%async_computation | async-start | bytes 262144 | tf_op jit(solution)/shard_map/all_to_all | solution.py:177
  6.4 0.3 select_reduce_fusion.1
  6.7 0.4 select_reduce_fusion
  7.2 4.9 %all-to-all-done = f32[4,16,512]{2,1,0:T(8,128)S(1)} async-done(((f32[4,16,512]{2,1,0:T(8,128)}), f32[4,16,512]{2,1,0:T(8,128)S(1)}, u32[]{:S(2)}, u32[]{:S(2)}) %all-to-all-start) | async-done | bytes 131104 | tf_op jit(solution)/shard_map/all_to_all | solution.py:177
  12.2 0.4 slice_select_fusion.3
  13.3 0.2 bitcast_reduce_fusion
  13.5 1.9 %collective-permute-start = (f32[4,2048]{1,0:T(4,128)S(1)}, f32[4,2048]{1,0:T(4,128)S(1)}, u32[]{:S(2)}, u32[]{:S(2)}) collective-permute-start(f32[4,2048]{1,0:T(4,128)S(1)} %bitcast_reduce_fusion), channel_id=1, source_target_pairs={{0,4},{4,0},{8,12},{12,8},{16,20},{20,16},{24,28},{28,24},{32,36},... | collective-permute-start | bytes 98312 | tf_op jit(solution)/shard_map/ppermute | solution.py:22
  15.5 1.1 collective-permute-done
  17.1 4.3 %collective-permute-start.1 = (f32[4,2048]{1,0:T(4,128)S(1)}, f32[4,2048]{1,0:T(4,128)S(1)}, u32[]{:S(2)}, u32[]{:S(2)}) collective-permute-start(f32[4,2048]{1,0:T(4,128)S(1)} %fusion.22), channel_id=1, source_target_pairs={{0,8},{8,0},{4,12},{12,4},{16,24},{24,16},{20,28},{28,20},{32,40},... | collective-permute-start | bytes 98312 | tf_op jit(solution)/shard_map/ppermute | solution.py:22
  21.5 1.8 %collective-permute-done.1 = f32[4,2048]{1,0:T(4,128)S(1)} collective-permute-done((f32[4,2048]{1,0:T(4,128)S(1)}, f32[4,2048]{1,0:T(4,128)S(1)}, u32[]{:S(2)}, u32[]{:S(2)}) %collective-permute-start.1) | collective-permute-done | bytes 32800 | tf_op jit(solution)/shard_map/ppermute | solution.py:22
  23.9 6.1 %collective-permute-start.2 = (f32[4,2048]{1,0:T(4,128)S(1)}, f32[4,2048]{1,0:T(4,128)S(1)}, u32[]{:S(2)}, u32[]{:S(2)}) collective-permute-start(f32[4,2048]{1,0:T(4,128)S(1)} %fusion.21), channel_id=1, source_target_pairs={{0,16},{16,0},{4,20},{20,4},{8,24},{24,8},{12,28},{28,12},{32,48},... | collective-permute-start | bytes 98312 | tf_op jit(solution)/shard_map/ppermute | solution.py:22
  30.0 2.0 %collective-permute-done.2 = f32[4,2048]{1,0:T(4,128)S(1)} collective-permute-done((f32[4,2048]{1,0:T(4,128)S(1)}, f32[4,2048]{1,0:T(4,128)S(1)}, u32[]{:S(2)}, u32[]{:S(2)}) %collective-permute-start.2) | collective-permute-done | bytes 32800 | tf_op jit(solution)/shard_map/ppermute | solution.py:22
  32.7 9.2 %collective-permute-start.3 = (f32[4,2048]{1,0:T(4,128)S(1)}, f32[4,2048]{1,0:T(4,128)S(1)}, u32[]{:S(2)}, u32[]{:S(2)}) collective-permute-start(f32[4,2048]{1,0:T(4,128)S(1)} %fusion.20), channel_id=1, source_target_pairs={{0,32},{32,0},{4,36},{36,4},{8,40},{40,8},{12,44},{44,12},{16,48},... | collective-permute-start | bytes 98312 | tf_op jit(solution)/shard_map/ppermute | solution.py:22
  41.9 1.9 %collective-permute-done.3 = f32[4,2048]{1,0:T(4,128)S(1)} collective-permute-done((f32[4,2048]{1,0:T(4,128)S(1)}, f32[4,2048]{1,0:T(4,128)S(1)}, u32[]{:S(2)}, u32[]{:S(2)}) %collective-permute-start.3) | collective-permute-done | bytes 32800 | tf_op jit(solution)/shard_map/ppermute | solution.py:22
  44.5 3.5 %collective-permute-start.4 = (f32[4,2048]{1,0:T(4,128)S(1)}, f32[4,2048]{1,0:T(4,128)S(1)}, u32[]{:S(2)}, u32[]{:S(2)}) collective-permute-start(f32[4,2048]{1,0:T(4,128)S(1)} %fusion.19), channel_id=1, source_target_pairs={{0,64},{64,0},{4,68},{68,4},{8,72},{72,8},{12,76},{76,12},{16,80},... | collective-permute-start | bytes 98312 | tf_op jit(solution)/shard_map/ppermute | solution.py:22
  48.1 2.2 %collective-permute-done.4 = f32[4,2048]{1,0:T(4,128)S(1)} collective-permute-done((f32[4,2048]{1,0:T(4,128)S(1)}, f32[4,2048]{1,0:T(4,128)S(1)}, u32[]{:S(2)}, u32[]{:S(2)}) %collective-permute-start.4) | collective-permute-done | bytes 32800 | tf_op jit(solution)/shard_map/ppermute | solution.py:22
  51.4 3.5 %collective-permute-start.5 = (f32[8,2048]{1,0:T(8,128)S(1)}, f32[8,2048]{1,0:T(8,128)S(1)}, u32[]{:S(2)}, u32[]{:S(2)}) collective-permute-start(f32[8,2048]{1,0:T(8,128)S(1)} %fusion.18), channel_id=1, source_target_pairs={{0,128},{128,0},{4,132},{132,4},{8,136},{136,8},{12,140},{140,12},... | collective-permute-start | bytes 196616 | tf_op jit(solution)/shard_map/ppermute | solution.py:22
  54.9 3.5 %collective-permute-done.5 = f32[8,2048]{1,0:T(8,128)S(1)} collective-permute-done((f32[8,2048]{1,0:T(8,128)S(1)}, f32[8,2048]{1,0:T(8,128)S(1)}, u32[]{:S(2)}, u32[]{:S(2)}) %collective-permute-start.5) | collective-permute-done | bytes 65568 | tf_op jit(solution)/shard_map/ppermute | solution.py:22
  59.9 6.3 %collective-permute-start.6 = (f32[16,2048]{1,0:T(8,128)S(1)}, f32[16,2048]{1,0:T(8,128)S(1)}, u32[]{:S(2)}, u32[]{:S(2)}) collective-permute-start(f32[16,2048]{1,0:T(8,128)S(1)} %fusion.16), channel_id=1, source_target_pairs={{384,0},{388,4},{392,8},{396,12},{400,16},{404,20},{408,24},{412,2... | collective-permute-start | bytes 393224 | tf_op jit(solution)/shard_map/ppermute | solution.py:26
  66.4 4.2 %collective-permute-done.6 = f32[16,2048]{1,0:T(8,128)S(1)} collective-permute-done((f32[16,2048]{1,0:T(8,128)S(1)}, f32[16,2048]{1,0:T(8,128)S(1)}, u32[]{:S(2)}, u32[]{:S(2)}) %collective-permute-start.6) | collective-permute-done | bytes 131104 | tf_op jit(solution)/shard_map/ppermute | solution.py:26
  74.6 8.4 %all_to_all.10 = f32[9,4,512]{2,0,1:T(8,128)S(1)} all-to-all(f32[9,4,512]{2,0,1:T(8,128)S(1)} %stack.5), channel_id=1, replica_groups=mesh['freq'=128,'tm'=4] {'tm'}, dimensions={1} | all-to-all | bytes 147456 | tf_op jit(solution)/shard_map/all_to_all | solution.py:210
  82.9 1.9 %collective-permute-start.7 = (f32[9,512]{1,0:T(8,128)S(1)}, f32[9,512]{1,0:T(8,128)S(1)}, u32[]{:S(2)}, u32[]{:S(2)}) collective-permute-start(f32[9,512]{1,0:T(8,128)S(1)} %reduce_max.99), channel_id=1, source_target_pairs={{0,4},{4,0},{8,12},{12,8},{16,20},{20,16},{24,28},{28,24},{32,36},... | collective-permute-start | bytes 55304 | tf_op jit(solution)/shard_map/ppermute | solution.py:22
  84.9 1.2 %collective-permute-done.7 = f32[9,512]{1,0:T(8,128)S(1)} collective-permute-done((f32[9,512]{1,0:T(8,128)S(1)}, f32[9,512]{1,0:T(8,128)S(1)}, u32[]{:S(2)}, u32[]{:S(2)}) %collective-permute-start.7) | collective-permute-done | bytes 18464 | tf_op jit(solution)/shard_map/ppermute | solution.py:22
  86.0 3.3 %collective-permute-start.8 = (f32[9,512]{1,0:T(8,128)S(1)}, f32[9,512]{1,0:T(8,128)S(1)}, u32[]{:S(2)}, u32[]{:S(2)}) collective-permute-start(f32[9,512]{1,0:T(8,128)S(1)} %max.12), channel_id=1, source_target_pairs={{0,8},{8,0},{4,12},{12,4},{16,24},{24,16},{20,28},{28,20},{32,40},... | collective-permute-start | bytes 55304 | tf_op jit(solution)/shard_map/ppermute | solution.py:22
  89.4 2.4 %collective-permute-done.8 = f32[9,512]{1,0:T(8,128)S(1)} collective-permute-done((f32[9,512]{1,0:T(8,128)S(1)}, f32[9,512]{1,0:T(8,128)S(1)}, u32[]{:S(2)}, u32[]{:S(2)}) %collective-permute-start.8) | collective-permute-done | bytes 18464 | tf_op jit(solution)/shard_map/ppermute | solution.py:22
  91.8 4.6 %collective-permute-start.9 = (f32[9,512]{1,0:T(8,128)S(1)}, f32[9,512]{1,0:T(8,128)S(1)}, u32[]{:S(2)}, u32[]{:S(2)}) collective-permute-start(f32[9,512]{1,0:T(8,128)S(1)} %max.13), channel_id=1, source_target_pairs={{0,16},{16,0},{4,20},{20,4},{8,24},{24,8},{12,28},{28,12},{32,48},... | collective-permute-start | bytes 55304 | tf_op jit(solution)/shard_map/ppermute | solution.py:22
  96.4 2.1 %collective-permute-done.9 = f32[9,512]{1,0:T(8,128)S(1)} collective-permute-done((f32[9,512]{1,0:T(8,128)S(1)}, f32[9,512]{1,0:T(8,128)S(1)}, u32[]{:S(2)}, u32[]{:S(2)}) %collective-permute-start.9) | collective-permute-done | bytes 18464 | tf_op jit(solution)/shard_map/ppermute | solution.py:22
  98.5 8.3 %collective-permute-start.10 = (f32[9,512]{1,0:T(8,128)S(1)}, f32[9,512]{1,0:T(8,128)S(1)}, u32[]{:S(2)}, u32[]{:S(2)}) collective-permute-start(f32[9,512]{1,0:T(8,128)S(1)} %max.14), channel_id=1, source_target_pairs={{48,0},{52,4},{56,8},{60,12},{32,16},{36,20},{40,24},{44,28},{16,3... | collective-permute-start | bytes 55304 | tf_op jit(solution)/shard_map/ppermute | solution.py:26
  106.8 1.9 %collective-permute-done.10 = f32[9,512]{1,0:T(8,128)S(1)} collective-permute-done((f32[9,512]{1,0:T(8,128)S(1)}, f32[9,512]{1,0:T(8,128)S(1)}, u32[]{:S(2)}, u32[]{:S(2)}) %collective-permute-start.10) | collective-permute-done | bytes 18464 | tf_op jit(solution)/shard_map/ppermute | solution.py:26
  108.7 0.6 max.15
  (123 shorter events, 9.9 us)
Async XLA Ops:
  0.0 6.3 %copy-start.2 = (s32[10,92]{1,0:T(8,128)S(1)}, s32[10,92]{1,0:T(8,128)}, u32[]{:S(2)}) copy-start(s32[10,92]{1,0:T(8,128)} %constant.74.clone) | copy-start | bytes 11044
  0.0 6.3 %copy-start.3 = (s32[10,92]{1,0:T(8,128)S(1)}, s32[10,92]{1,0:T(8,128)}, u32[]{:S(2)}) copy-start(s32[10,92]{1,0:T(8,128)} %constant.73.clone) | copy-start | bytes 11044
  0.0 6.3 %copy-start.4 = (s32[10,92]{1,0:T(8,128)S(1)}, s32[10,92]{1,0:T(8,128)}, u32[]{:S(2)}) copy-start(s32[10,92]{1,0:T(8,128)} %constant.72.clone) | copy-start | bytes 11044
  0.0 7.0 %copy-start.5 = (f32[64,20]{1,0:T(8,128)S(1)}, f32[64,20]{1,0:T(8,128)}, u32[]{:S(2)}) copy-start(f32[64,20]{1,0:T(8,128)} %constant.75.clone) | copy-start | bytes 15364
  0.0 6.4 %copy-start.1 = (s32[2047]{0:T(1024)S(1)}, s32[2047]{0:T(1024)}, u32[]{:S(2)}) copy-start(s32[2047]{0:T(1024)} %param.8) | copy-start | bytes 24568
  0.0 6.6 %copy-start = (s32[4094]{0:T(1024)S(1)}, s32[4094]{0:T(1024)}, u32[]{:S(2)}) copy-start(s32[4094]{0:T(1024)} %param.9) | copy-start | bytes 49132
  1.9 10.3 %all-to-all-start = ((f32[4,16,512]{2,1,0:T(8,128)}), f32[4,16,512]{2,1,0:T(8,128)S(1)}, u32[]{:S(2)}, u32[]{:S(2)}) async-start(f32[4,16,512]{2,1,0:T(8,128)} %broadcast_in_dim.604), calls=%async_computation | async-start | bytes 262144 | tf_op jit(solution)/shard_map/all_to_all | solution.py:177
  13.5 3.1 %collective-permute-start = (f32[4,2048]{1,0:T(4,128)S(1)}, f32[4,2048]{1,0:T(4,128)S(1)}, u32[]{:S(2)}, u32[]{:S(2)}) collective-permute-start(f32[4,2048]{1,0:T(4,128)S(1)} %bitcast_reduce_fusion), channel_id=1, source_target_pairs={{0,4},{4,0},{8,12},{12,8},{16,20},{20,16},{24,28},{28,24},{32,36},... | collective-permute-start | bytes 98312 | tf_op jit(solution)/shard_map/ppermute | solution.py:22
  17.1 6.2 %collective-permute-start.1 = (f32[4,2048]{1,0:T(4,128)S(1)}, f32[4,2048]{1,0:T(4,128)S(1)}, u32[]{:S(2)}, u32[]{:S(2)}) collective-permute-start(f32[4,2048]{1,0:T(4,128)S(1)} %fusion.22), channel_id=1, source_target_pairs={{0,8},{8,0},{4,12},{12,4},{16,24},{24,16},{20,28},{28,20},{32,40},... | collective-permute-start | bytes 98312 | tf_op jit(solution)/shard_map/ppermute | solution.py:22
  23.9 8.1 %collective-permute-start.2 = (f32[4,2048]{1,0:T(4,128)S(1)}, f32[4,2048]{1,0:T(4,128)S(1)}, u32[]{:S(2)}, u32[]{:S(2)}) collective-permute-start(f32[4,2048]{1,0:T(4,128)S(1)} %fusion.21), channel_id=1, source_target_pairs={{0,16},{16,0},{4,20},{20,4},{8,24},{24,8},{12,28},{28,12},{32,48},... | collective-permute-start | bytes 98312 | tf_op jit(solution)/shard_map/ppermute | solution.py:22
  32.7 11.1 %collective-permute-start.3 = (f32[4,2048]{1,0:T(4,128)S(1)}, f32[4,2048]{1,0:T(4,128)S(1)}, u32[]{:S(2)}, u32[]{:S(2)}) collective-permute-start(f32[4,2048]{1,0:T(4,128)S(1)} %fusion.20), channel_id=1, source_target_pairs={{0,32},{32,0},{4,36},{36,4},{8,40},{40,8},{12,44},{44,12},{16,48},... | collective-permute-start | bytes 98312 | tf_op jit(solution)/shard_map/ppermute | solution.py:22
  44.5 5.8 %collective-permute-start.4 = (f32[4,2048]{1,0:T(4,128)S(1)}, f32[4,2048]{1,0:T(4,128)S(1)}, u32[]{:S(2)}, u32[]{:S(2)}) collective-permute-start(f32[4,2048]{1,0:T(4,128)S(1)} %fusion.19), channel_id=1, source_target_pairs={{0,64},{64,0},{4,68},{68,4},{8,72},{72,8},{12,76},{76,12},{16,80},... | collective-permute-start | bytes 98312 | tf_op jit(solution)/shard_map/ppermute | solution.py:22
  51.4 7.1 %collective-permute-start.5 = (f32[8,2048]{1,0:T(8,128)S(1)}, f32[8,2048]{1,0:T(8,128)S(1)}, u32[]{:S(2)}, u32[]{:S(2)}) collective-permute-start(f32[8,2048]{1,0:T(8,128)S(1)} %fusion.18), channel_id=1, source_target_pairs={{0,128},{128,0},{4,132},{132,4},{8,136},{136,8},{12,140},{140,12},... | collective-permute-start | bytes 196616 | tf_op jit(solution)/shard_map/ppermute | solution.py:22
  59.9 10.7 %collective-permute-start.6 = (f32[16,2048]{1,0:T(8,128)S(1)}, f32[16,2048]{1,0:T(8,128)S(1)}, u32[]{:S(2)}, u32[]{:S(2)}) collective-permute-start(f32[16,2048]{1,0:T(8,128)S(1)} %fusion.16), channel_id=1, source_target_pairs={{384,0},{388,4},{392,8},{396,12},{400,16},{404,20},{408,24},{412,2... | collective-permute-start | bytes 393224 | tf_op jit(solution)/shard_map/ppermute | solution.py:26
  82.9 3.1 %collective-permute-start.7 = (f32[9,512]{1,0:T(8,128)S(1)}, f32[9,512]{1,0:T(8,128)S(1)}, u32[]{:S(2)}, u32[]{:S(2)}) collective-permute-start(f32[9,512]{1,0:T(8,128)S(1)} %reduce_max.99), channel_id=1, source_target_pairs={{0,4},{4,0},{8,12},{12,8},{16,20},{20,16},{24,28},{28,24},{32,36},... | collective-permute-start | bytes 55304 | tf_op jit(solution)/shard_map/ppermute | solution.py:22
  86.0 5.8 %collective-permute-start.8 = (f32[9,512]{1,0:T(8,128)S(1)}, f32[9,512]{1,0:T(8,128)S(1)}, u32[]{:S(2)}, u32[]{:S(2)}) collective-permute-start(f32[9,512]{1,0:T(8,128)S(1)} %max.12), channel_id=1, source_target_pairs={{0,8},{8,0},{4,12},{12,4},{16,24},{24,16},{20,28},{28,20},{32,40},... | collective-permute-start | bytes 55304 | tf_op jit(solution)/shard_map/ppermute | solution.py:22
  91.8 6.7 %collective-permute-start.9 = (f32[9,512]{1,0:T(8,128)S(1)}, f32[9,512]{1,0:T(8,128)S(1)}, u32[]{:S(2)}, u32[]{:S(2)}) collective-permute-start(f32[9,512]{1,0:T(8,128)S(1)} %max.13), channel_id=1, source_target_pairs={{0,16},{16,0},{4,20},{20,4},{8,24},{24,8},{12,28},{28,12},{32,48},... | collective-permute-start | bytes 55304 | tf_op jit(solution)/shard_map/ppermute | solution.py:22
  98.5 10.2 %collective-permute-start.10 = (f32[9,512]{1,0:T(8,128)S(1)}, f32[9,512]{1,0:T(8,128)S(1)}, u32[]{:S(2)}, u32[]{:S(2)}) collective-permute-start(f32[9,512]{1,0:T(8,128)S(1)} %max.14), channel_id=1, source_target_pairs={{48,0},{52,4},{56,8},{60,12},{32,16},{36,20},{40,24},{44,28},{16,3... | collective-permute-start | bytes 55304 | tf_op jit(solution)/shard_map/ppermute | solution.py:26

commit v9 on v8

--- a/solution.py
+++ b/solution.py
@@ -87,13 +87,14 @@
     slot = {}
     for k in range(1, local_bits + 1):
         trial_count = 2**k
-        for m in range(held):
-            trial = held_trial(m, local_bits - k)
+        for d in range(sub_dev):
             for g in range(sub_dev >> k):
-                key = (k, g, tuple(trial))
+                key = (k, g, d >> (local_bits - k))
                 if key in slot:
                     continue
                 slot[key] = len(ids)
+                trial = np.zeros(terms, np.int64)
+                trial[0] = d >> (local_bits - k)
                 rate = np.zeros(terms, np.int64)
                 rate[0] = all_trials // trial_count - 1 + g
                 for bit in range(freq_bits):
@@ -103,13 +104,12 @@
                 ids.append(trial)
                 rates.append(rate)
                 jits.append(jit)
-    paths = np.zeros((held * sub_dev, len(ids)), np.float32)
-    for m in range(held):
+    paths = np.zeros((sub_dev * sub_dev, len(ids)), np.float32)
+    for d in range(sub_dev):
         for i in range(sub_dev):
             for k in range(1, local_bits + 1):
                 if i >> (k - 1) & 1:
-                    key = (k, i >> k, tuple(held_trial(m, local_bits - k)))
-                    paths[m * sub_dev + i, slot[key]] += 1.0
+                    paths[d * sub_dev + i, slot[(k, i >> k, d >> (local_bits - k))]] += 1.0
     unique_count = len(ids)
     level_rows = []
     now = np.zeros((held, terms), np.int64)
@@ -173,13 +173,16 @@
         start = start + rows
 
     base = jnp.sum(spectrogram.reshape(sub_dev, SUMMED, span_time), axis=1, dtype=jnp.float32)
-    spread = jnp.broadcast_to(base[None], (tm_count,) + base.shape)
-    gathered = lax.all_to_all(spread, "tm", 0, 0, tiled=True)
-    base = jnp.transpose(gathered, (1, 0, 2)).reshape(sub_dev, tm_count * span_time)
-    full_time = base.shape[1]
-    local_limit = sum(2**k - 1 for k in range(1, sub_dev.bit_length()))
-    moved = shift_rows(jnp.tile(base, (held, 1)), path_shift, max(local_limit.bit_length(), 1))
-    trial_rows = jnp.sum(moved.reshape(held, sub_dev, full_time), axis=1)
+    full_time = tm_count * span_time
+    halo = sum(2**k - 1 for k in range(1, sub_dev.bit_length()))
+    width = span_time + halo
+    padded = jnp.pad(base, ((0, 0), (0, halo)))
+    moved = shift_rows(jnp.tile(padded, (sub_dev, 1)), path_shift, max(halo.bit_length(), 1))
+    partial = jnp.sum(moved.reshape(sub_dev, sub_dev, width), axis=1)
+    arrived = lax.all_to_all(partial.reshape(tm_count, held, width), "tm", 0, 0, tiled=True)
+    main = jnp.transpose(arrived[:, :, :span_time], (1, 0, 2)).reshape(held, full_time)
+    spill = jnp.pad(arrived[:-1, :, span_time:], ((1, 0), (0, 0), (0, span_time - halo)))
+    trial_rows = main + jnp.transpose(spill, (1, 0, 2)).reshape(held, full_time)
     level = 0
     for bit_index in range(freq_bits):
         need_now = sub_dev * 2 ** (bit_index + 1) - 1

time: 110 us -> 113 us (1.027)
  blocking collectives: 8.36 us -> 17.9 us
  starting transfers between devices: 57.2 us -> 52.2 us
  waiting for transfers between devices: 29.3 us -> 25.1 us
  other arithmetic: 11.6 us -> 14.1 us
    all_to_all x0 -> x1, blocking collectives: none -> 9.59 us  [shards(): lax.all_to_all(partial.reshape(tm_count, held, width), 'tm', 0, 0, tiled=...]
    all_to_all x1 -> x0, waiting for transfers between devices: 4.94 us -> none  [shards(): gathered = lax.all_to_all(spread, 'tm', 0, 0, tiled=True)]
    all_to_all x1 -> x0, starting transfers between devices: 4.29 us -> none  [shards(): gathered = lax.all_to_all(spread, 'tm', 0, 0, tiled=True)]
    reduce_sum x2, other arithmetic: 0.62 us -> 2.14 us  [picked(): return jnp.sum(jnp.where(hit, table[None, :], 0), axis=1)]
  transfers between devices with their start and end apart: 12 -> 11, of which waited for: 12 -> 11; matrix products, arithmetic and copies ran while one was open for 1% -> 0% of each run, Pallas kernels for 0% -> 0%
where the time goes in v9:
time: 113 us
  starting transfers between devices  52.2 us (46%)
  waiting for transfers between devices  25.1 us (22%)
  blocking collectives  17.9 us (16%)
  other arithmetic  14.1 us (12%)
  local copies, waits for them, and re-layouts  1.24 us (1%)
    ppermute x9, starting transfers between devices, swapped(): return lax.ppermute(block, axis, route)  37.5 us
    ppermute x9, waiting for transfers between devices, swapped(): return lax.ppermute(block, axis, route)  19 us
    ppermute x2, starting transfers between devices, paired(): lax.ppermute(block, axis, [(partner_of(i), i) for i in range(lax.axis_siz...  14.6 us
    all_to_all x1, blocking collectives, shards(): lax.all_to_all(partial.reshape(tm_count, held, width), 'tm', 0, 0, tiled=...  9.59 us
    all_to_all x1, blocking collectives, shards(): best = jnp.max(lax.all_to_all(best, 'tm', 1, 1, tiled=True), axis=1)  8.36 us
    ppermute x2, waiting for transfers between devices, paired(): lax.ppermute(block, axis, [(partner_of(i), i) for i in range(lax.axis_siz...  6.14 us
    select_n x49, other arithmetic, merge_rows(): jnp.where(selected, moved[:, step_size:], moved[:, :cols - step_size])  5.41 us
  transfers between devices with their start and end apart: 11, of which 11 were waited for; matrix products, arithmetic and copies ran while one was open for 0% of the time, Pallas kernels for 0%

profile of v9, /device:TPU:16, one launch (start us, length us, event | category | flops | bytes accessed | tf_op | source)
XLA Modules:
  0.0 112.5 jit_solution(10119053807809818610)
XLA Ops:
  0.1 0.8 multiply_reduce_fusion.1
  0.9 1.2 %select_reduce_fusion = s32[136]{0:T(256)S(1)} fusion(s32[4094]{0:T(1024)} %param.9, s32[136]{0:T(256)S(1)} %get-tuple-element.8), kind=kLoop, calls=%fused_computation | loop fusion | flops 1670216 | bytes 17464 | tf_op jit(solution)/shard_map/reduce_sum | solution.py:67
  2.1 1.0 select_reduce_fusion.1
  3.1 1.1 fusion.20
  4.2 1.2 %convert_reduce_fusion = f32[16,512]{1,0:T(8,128)S(1)} fusion(bf16[512,512]{1,0:T(8,128)(2,1)} %param.7), kind=kLoop, calls=%fused_computation.4 | loop fusion | flops 516096 | bytes 557056 | tf_op jit(solution)/shard_map/reduce_sum | solution.py:175
  5.5 0.4 slice_select_fusion.4
  6.7 0.3 bitcast_reduce_fusion
  7.1 9.6 %all_to_all.10 = f32[4,4,538]{2,1,0:T(4,128)S(1)} all-to-all(f32[4,4,538]{2,1,0:T(4,128)S(1)} %reshape.277), channel_id=1, replica_groups=mesh['freq'=128,'tm'=4] {'tm'}, dimensions={0} | all-to-all | bytes 68864 | tf_op jit(solution)/shard_map/all_to_all | solution.py:182
  16.7 1.9 %collective-permute-start = (f32[4,2048]{1,0:T(4,128)S(1)}, f32[4,2048]{1,0:T(4,128)S(1)}, u32[]{:S(2)}, u32[]{:S(2)}) collective-permute-start(f32[4,2048]{1,0:T(4,128)S(1)} %bitcast.24), channel_id=1, source_target_pairs={{0,4},{4,0},{8,12},{12,8},{16,20},{20,16},{24,28},{28,24},{32,36},... | collective-permute-start | bytes 98312 | tf_op jit(solution)/shard_map/ppermute | solution.py:22
  18.7 1.1 collective-permute-done
  20.3 4.3 %collective-permute-start.1 = (f32[4,2048]{1,0:T(4,128)S(1)}, f32[4,2048]{1,0:T(4,128)S(1)}, u32[]{:S(2)}, u32[]{:S(2)}) collective-permute-start(f32[4,2048]{1,0:T(4,128)S(1)} %fusion.19), channel_id=1, source_target_pairs={{0,8},{8,0},{4,12},{12,4},{16,24},{24,16},{20,28},{28,20},{32,40},... | collective-permute-start | bytes 98312 | tf_op jit(solution)/shard_map/ppermute | solution.py:22
  24.7 1.8 %collective-permute-done.1 = f32[4,2048]{1,0:T(4,128)S(1)} collective-permute-done((f32[4,2048]{1,0:T(4,128)S(1)}, f32[4,2048]{1,0:T(4,128)S(1)}, u32[]{:S(2)}, u32[]{:S(2)}) %collective-permute-start.1) | collective-permute-done | bytes 32800 | tf_op jit(solution)/shard_map/ppermute | solution.py:22
  27.0 6.1 %collective-permute-start.2 = (f32[4,2048]{1,0:T(4,128)S(1)}, f32[4,2048]{1,0:T(4,128)S(1)}, u32[]{:S(2)}, u32[]{:S(2)}) collective-permute-start(f32[4,2048]{1,0:T(4,128)S(1)} %fusion.18), channel_id=1, source_target_pairs={{0,16},{16,0},{4,20},{20,4},{8,24},{24,8},{12,28},{28,12},{32,48},... | collective-permute-start | bytes 98312 | tf_op jit(solution)/shard_map/ppermute | solution.py:22
  33.1 2.0 %collective-permute-done.2 = f32[4,2048]{1,0:T(4,128)S(1)} collective-permute-done((f32[4,2048]{1,0:T(4,128)S(1)}, f32[4,2048]{1,0:T(4,128)S(1)}, u32[]{:S(2)}, u32[]{:S(2)}) %collective-permute-start.2) | collective-permute-done | bytes 32800 | tf_op jit(solution)/shard_map/ppermute | solution.py:22
  35.8 9.2 %collective-permute-start.3 = (f32[4,2048]{1,0:T(4,128)S(1)}, f32[4,2048]{1,0:T(4,128)S(1)}, u32[]{:S(2)}, u32[]{:S(2)}) collective-permute-start(f32[4,2048]{1,0:T(4,128)S(1)} %fusion.17), channel_id=1, source_target_pairs={{0,32},{32,0},{4,36},{36,4},{8,40},{40,8},{12,44},{44,12},{16,48},... | collective-permute-start | bytes 98312 | tf_op jit(solution)/shard_map/ppermute | solution.py:22
  45.0 1.9 %collective-permute-done.3 = f32[4,2048]{1,0:T(4,128)S(1)} collective-permute-done((f32[4,2048]{1,0:T(4,128)S(1)}, f32[4,2048]{1,0:T(4,128)S(1)}, u32[]{:S(2)}, u32[]{:S(2)}) %collective-permute-start.3) | collective-permute-done | bytes 32800 | tf_op jit(solution)/shard_map/ppermute | solution.py:22
  47.7 3.5 %collective-permute-start.4 = (f32[4,2048]{1,0:T(4,128)S(1)}, f32[4,2048]{1,0:T(4,128)S(1)}, u32[]{:S(2)}, u32[]{:S(2)}) collective-permute-start(f32[4,2048]{1,0:T(4,128)S(1)} %fusion.16), channel_id=1, source_target_pairs={{0,64},{64,0},{4,68},{68,4},{8,72},{72,8},{12,76},{76,12},{16,80},... | collective-permute-start | bytes 98312 | tf_op jit(solution)/shard_map/ppermute | solution.py:22
  51.2 2.2 %collective-permute-done.4 = f32[4,2048]{1,0:T(4,128)S(1)} collective-permute-done((f32[4,2048]{1,0:T(4,128)S(1)}, f32[4,2048]{1,0:T(4,128)S(1)}, u32[]{:S(2)}, u32[]{:S(2)}) %collective-permute-start.4) | collective-permute-done | bytes 32800 | tf_op jit(solution)/shard_map/ppermute | solution.py:22
  54.5 2.7 %collective-permute-start.5 = (f32[8,2048]{1,0:T(8,128)S(1)}, f32[8,2048]{1,0:T(8,128)S(1)}, u32[]{:S(2)}, u32[]{:S(2)}) collective-permute-start(f32[8,2048]{1,0:T(8,128)S(1)} %fusion.15), channel_id=1, source_target_pairs={{0,128},{128,0},{4,132},{132,4},{8,136},{136,8},{12,140},{140,12},... | collective-permute-start | bytes 196616 | tf_op jit(solution)/shard_map/ppermute | solution.py:22
  57.3 4.3 %collective-permute-done.5 = f32[8,2048]{1,0:T(8,128)S(1)} collective-permute-done((f32[8,2048]{1,0:T(8,128)S(1)}, f32[8,2048]{1,0:T(8,128)S(1)}, u32[]{:S(2)}, u32[]{:S(2)}) %collective-permute-start.5) | collective-permute-done | bytes 65568 | tf_op jit(solution)/shard_map/ppermute | solution.py:22
  63.1 6.3 %collective-permute-start.6 = (f32[16,2048]{1,0:T(8,128)S(1)}, f32[16,2048]{1,0:T(8,128)S(1)}, u32[]{:S(2)}, u32[]{:S(2)}) collective-permute-start(f32[16,2048]{1,0:T(8,128)S(1)} %fusion.13), channel_id=1, source_target_pairs={{384,0},{388,4},{392,8},{396,12},{400,16},{404,20},{408,24},{412,2... | collective-permute-start | bytes 393224 | tf_op jit(solution)/shard_map/ppermute | solution.py:26
  69.5 4.2 %collective-permute-done.6 = f32[16,2048]{1,0:T(8,128)S(1)} collective-permute-done((f32[16,2048]{1,0:T(8,128)S(1)}, f32[16,2048]{1,0:T(8,128)S(1)}, u32[]{:S(2)}, u32[]{:S(2)}) %collective-permute-start.6) | collective-permute-done | bytes 131104 | tf_op jit(solution)/shard_map/ppermute | solution.py:26
  77.7 8.4 %all_to_all.11 = f32[9,4,512]{2,0,1:T(8,128)S(1)} all-to-all(f32[9,4,512]{2,0,1:T(8,128)S(1)} %stack.5), channel_id=1, replica_groups=mesh['freq'=128,'tm'=4] {'tm'}, dimensions={1} | all-to-all | bytes 147456 | tf_op jit(solution)/shard_map/all_to_all | solution.py:213
  86.1 1.9 %collective-permute-start.7 = (f32[9,512]{1,0:T(8,128)S(1)}, f32[9,512]{1,0:T(8,128)S(1)}, u32[]{:S(2)}, u32[]{:S(2)}) collective-permute-start(f32[9,512]{1,0:T(8,128)S(1)} %reduce_max.99), channel_id=1, source_target_pairs={{0,4},{4,0},{8,12},{12,8},{16,20},{20,16},{24,28},{28,24},{32,36},... | collective-permute-start | bytes 55304 | tf_op jit(solution)/shard_map/ppermute | solution.py:22
  88.0 1.2 %collective-permute-done.7 = f32[9,512]{1,0:T(8,128)S(1)} collective-permute-done((f32[9,512]{1,0:T(8,128)S(1)}, f32[9,512]{1,0:T(8,128)S(1)}, u32[]{:S(2)}, u32[]{:S(2)}) %collective-permute-start.7) | collective-permute-done | bytes 18464 | tf_op jit(solution)/shard_map/ppermute | solution.py:22
  89.2 3.3 %collective-permute-start.8 = (f32[9,512]{1,0:T(8,128)S(1)}, f32[9,512]{1,0:T(8,128)S(1)}, u32[]{:S(2)}, u32[]{:S(2)}) collective-permute-start(f32[9,512]{1,0:T(8,128)S(1)} %max.12), channel_id=1, source_target_pairs={{0,8},{8,0},{4,12},{12,4},{16,24},{24,16},{20,28},{28,20},{32,40},... | collective-permute-start | bytes 55304 | tf_op jit(solution)/shard_map/ppermute | solution.py:22
  92.5 2.4 %collective-permute-done.8 = f32[9,512]{1,0:T(8,128)S(1)} collective-permute-done((f32[9,512]{1,0:T(8,128)S(1)}, f32[9,512]{1,0:T(8,128)S(1)}, u32[]{:S(2)}, u32[]{:S(2)}) %collective-permute-start.8) | collective-permute-done | bytes 18464 | tf_op jit(solution)/shard_map/ppermute | solution.py:22
  95.0 4.6 %collective-permute-start.9 = (f32[9,512]{1,0:T(8,128)S(1)}, f32[9,512]{1,0:T(8,128)S(1)}, u32[]{:S(2)}, u32[]{:S(2)}) collective-permute-start(f32[9,512]{1,0:T(8,128)S(1)} %max.13), channel_id=1, source_target_pairs={{0,16},{16,0},{4,20},{20,4},{8,24},{24,8},{12,28},{28,12},{32,48},... | collective-permute-start | bytes 55304 | tf_op jit(solution)/shard_map/ppermute | solution.py:22
  99.6 2.1 %collective-permute-done.9 = f32[9,512]{1,0:T(8,128)S(1)} collective-permute-done((f32[9,512]{1,0:T(8,128)S(1)}, f32[9,512]{1,0:T(8,128)S(1)}, u32[]{:S(2)}, u32[]{:S(2)}) %collective-permute-start.9) | collective-permute-done | bytes 18464 | tf_op jit(solution)/shard_map/ppermute | solution.py:22
  101.7 8.3 %collective-permute-start.10 = (f32[9,512]{1,0:T(8,128)S(1)}, f32[9,512]{1,0:T(8,128)S(1)}, u32[]{:S(2)}, u32[]{:S(2)}) collective-permute-start(f32[9,512]{1,0:T(8,128)S(1)} %max.14), channel_id=1, source_target_pairs={{48,0},{52,4},{56,8},{60,12},{32,16},{36,20},{40,24},{44,28},{16,3... | collective-permute-start | bytes 55304 | tf_op jit(solution)/shard_map/ppermute | solution.py:26
  110.0 1.9 %collective-permute-done.10 = f32[9,512]{1,0:T(8,128)S(1)} collective-permute-done((f32[9,512]{1,0:T(8,128)S(1)}, f32[9,512]{1,0:T(8,128)S(1)}, u32[]{:S(2)}, u32[]{:S(2)}) %collective-permute-start.10) | collective-permute-done | bytes 18464 | tf_op jit(solution)/shard_map/ppermute | solution.py:26
  111.9 0.6 max.15
  (113 shorter events, 9.9 us)
Async XLA Ops:
  16.7 3.1 %collective-permute-start = (f32[4,2048]{1,0:T(4,128)S(1)}, f32[4,2048]{1,0:T(4,128)S(1)}, u32[]{:S(2)}, u32[]{:S(2)}) collective-permute-start(f32[4,2048]{1,0:T(4,128)S(1)} %bitcast.24), channel_id=1, source_target_pairs={{0,4},{4,0},{8,12},{12,8},{16,20},{20,16},{24,28},{28,24},{32,36},... | collective-permute-start | bytes 98312 | tf_op jit(solution)/shard_map/ppermute | solution.py:22
  20.3 6.2 %collective-permute-start.1 = (f32[4,2048]{1,0:T(4,128)S(1)}, f32[4,2048]{1,0:T(4,128)S(1)}, u32[]{:S(2)}, u32[]{:S(2)}) collective-permute-start(f32[4,2048]{1,0:T(4,128)S(1)} %fusion.19), channel_id=1, source_target_pairs={{0,8},{8,0},{4,12},{12,4},{16,24},{24,16},{20,28},{28,20},{32,40},... | collective-permute-start | bytes 98312 | tf_op jit(solution)/shard_map/ppermute | solution.py:22
  27.0 8.1 %collective-permute-start.2 = (f32[4,2048]{1,0:T(4,128)S(1)}, f32[4,2048]{1,0:T(4,128)S(1)}, u32[]{:S(2)}, u32[]{:S(2)}) collective-permute-start(f32[4,2048]{1,0:T(4,128)S(1)} %fusion.18), channel_id=1, source_target_pairs={{0,16},{16,0},{4,20},{20,4},{8,24},{24,8},{12,28},{28,12},{32,48},... | collective-permute-start | bytes 98312 | tf_op jit(solution)/shard_map/ppermute | solution.py:22
  35.8 11.1 %collective-permute-start.3 = (f32[4,2048]{1,0:T(4,128)S(1)}, f32[4,2048]{1,0:T(4,128)S(1)}, u32[]{:S(2)}, u32[]{:S(2)}) collective-permute-start(f32[4,2048]{1,0:T(4,128)S(1)} %fusion.17), channel_id=1, source_target_pairs={{0,32},{32,0},{4,36},{36,4},{8,40},{40,8},{12,44},{44,12},{16,48},... | collective-permute-start | bytes 98312 | tf_op jit(solution)/shard_map/ppermute | solution.py:22
  47.7 5.8 %collective-permute-start.4 = (f32[4,2048]{1,0:T(4,128)S(1)}, f32[4,2048]{1,0:T(4,128)S(1)}, u32[]{:S(2)}, u32[]{:S(2)}) collective-permute-start(f32[4,2048]{1,0:T(4,128)S(1)} %fusion.16), channel_id=1, source_target_pairs={{0,64},{64,0},{4,68},{68,4},{8,72},{72,8},{12,76},{76,12},{16,80},... | collective-permute-start | bytes 98312 | tf_op jit(solution)/shard_map/ppermute | solution.py:22
  54.5 7.1 %collective-permute-start.5 = (f32[8,2048]{1,0:T(8,128)S(1)}, f32[8,2048]{1,0:T(8,128)S(1)}, u32[]{:S(2)}, u32[]{:S(2)}) collective-permute-start(f32[8,2048]{1,0:T(8,128)S(1)} %fusion.15), channel_id=1, source_target_pairs={{0,128},{128,0},{4,132},{132,4},{8,136},{136,8},{12,140},{140,12},... | collective-permute-start | bytes 196616 | tf_op jit(solution)/shard_map/ppermute | solution.py:22
  63.1 10.7 %collective-permute-start.6 = (f32[16,2048]{1,0:T(8,128)S(1)}, f32[16,2048]{1,0:T(8,128)S(1)}, u32[]{:S(2)}, u32[]{:S(2)}) collective-permute-start(f32[16,2048]{1,0:T(8,128)S(1)} %fusion.13), channel_id=1, source_target_pairs={{384,0},{388,4},{392,8},{396,12},{400,16},{404,20},{408,24},{412,2... | collective-permute-start | bytes 393224 | tf_op jit(solution)/shard_map/ppermute | solution.py:26
  86.1 3.1 %collective-permute-start.7 = (f32[9,512]{1,0:T(8,128)S(1)}, f32[9,512]{1,0:T(8,128)S(1)}, u32[]{:S(2)}, u32[]{:S(2)}) collective-permute-start(f32[9,512]{1,0:T(8,128)S(1)} %reduce_max.99), channel_id=1, source_target_pairs={{0,4},{4,0},{8,12},{12,8},{16,20},{20,16},{24,28},{28,24},{32,36},... | collective-permute-start | bytes 55304 | tf_op jit(solution)/shard_map/ppermute | solution.py:22
  89.2 5.8 %collective-permute-start.8 = (f32[9,512]{1,0:T(8,128)S(1)}, f32[9,512]{1,0:T(8,128)S(1)}, u32[]{:S(2)}, u32[]{:S(2)}) collective-permute-start(f32[9,512]{1,0:T(8,128)S(1)} %max.12), channel_id=1, source_target_pairs={{0,8},{8,0},{4,12},{12,4},{16,24},{24,16},{20,28},{28,20},{32,40},... | collective-permute-start | bytes 55304 | tf_op jit(solution)/shard_map/ppermute | solution.py:22
  95.0 6.7 %collective-permute-start.9 = (f32[9,512]{1,0:T(8,128)S(1)}, f32[9,512]{1,0:T(8,128)S(1)}, u32[]{:S(2)}, u32[]{:S(2)}) collective-permute-start(f32[9,512]{1,0:T(8,128)S(1)} %max.13), channel_id=1, source_target_pairs={{0,16},{16,0},{4,20},{20,4},{8,24},{24,8},{12,28},{28,12},{32,48},... | collective-permute-start | bytes 55304 | tf_op jit(solution)/shard_map/ppermute | solution.py:22
  101.7 10.2 %collective-permute-start.10 = (f32[9,512]{1,0:T(8,128)S(1)}, f32[9,512]{1,0:T(8,128)S(1)}, u32[]{:S(2)}, u32[]{:S(2)}) collective-permute-start(f32[9,512]{1,0:T(8,128)S(1)} %max.14), channel_id=1, source_target_pairs={{48,0},{52,4},{56,8},{60,12},{32,16},{36,20},{40,24},{44,28},{16,3... | collective-permute-start | bytes 55304 | tf_op jit(solution)/shard_map/ppermute | solution.py:26

commit v10 on v8

--- a/solution.py
+++ b/solution.py
@@ -1,3 +1,4 @@
+import functools
 import math
 
 import numpy as np
@@ -10,6 +11,7 @@
 WIDTHS = 9
 SHARED_LEVELS = 3
 NEAR_HALF = (6, 7, 4, 5, 2, 3, 0, 1)
+FINE_AXES = ("fy", "zh", "zl", "fc")
 
 
 def swapped(block, axis, apart):
@@ -138,14 +140,14 @@
     return pack(ids), pack(rates), pack(jits), paths, unique_count, level_rows
 
 
-def shards(spectrogram, low_share, jitter):
+def shards(freq_axis, spectrogram, low_share, jitter):
     sub_dev = spectrogram.shape[0] // SUMMED
     span_time = spectrogram.shape[1]
     all_trials = low_share.shape[0] + 1
-    freq_bits = lax.axis_size("freq").bit_length() - 1
+    freq_bits = lax.axis_size(freq_axis).bit_length() - 1
     tm_count = lax.axis_size("tm")
     shared = min(SHARED_LEVELS, freq_bits)
-    device = lax.axis_index("freq")
+    device = lax.axis_index(freq_axis)
     place = lax.axis_index("tm")
     held = sub_dev // tm_count
 
@@ -184,9 +186,9 @@
     for bit_index in range(freq_bits):
         need_now = sub_dev * 2 ** (bit_index + 1) - 1
         if bit_index == freq_bits - 1 and shared >= 3 and bit_index >= 2:
-            partner = paired(trial_rows, "freq", near_half(bit_index, bit_index - 2))
+            partner = paired(trial_rows, freq_axis, near_half(bit_index, bit_index - 2))
         else:
-            partner = swapped(trial_rows, "freq", bit_index)
+            partner = swapped(trial_rows, freq_axis, bit_index)
         upper_half = device >> bit_index & 1
         low_rows = jnp.where(upper_half == 1, partner, trial_rows)
         high_rows = jnp.where(upper_half == 1, trial_rows, partner)
@@ -209,15 +211,30 @@
     best = jnp.stack(peak_rows).reshape(WIDTHS, tm_count, span_time)
     best = jnp.max(lax.all_to_all(best, "tm", 1, 1, tiled=True), axis=1)
     for bit_index in range(freq_bits - shared):
-        if bit_index == 3:
-            best = jnp.maximum(best, paired(best, "freq", near_half(bit_index, 1)))
+        if bit_index == 1 and "zl" in freq_axis:
+            spread = jnp.broadcast_to(best[None], (4,) + best.shape)
+            best = jnp.max(lax.all_to_all(spread, "zl", 0, 0, tiled=True), axis=0)
+        elif bit_index == 2 and "zl" in freq_axis:
+            continue
+        elif bit_index == 3:
+            best = jnp.maximum(best, paired(best, freq_axis, near_half(bit_index, 1)))
         else:
-            best = jnp.maximum(best, swapped(best, "freq", bit_index))
+            best = jnp.maximum(best, swapped(best, freq_axis, bit_index))
     return best
 
 
 def solution(mesh):
-    placed = (P("freq", "tm"), P(), P())
+    count = mesh.shape["freq"]
+    if count % 16 == 0:
+        fine = jax.sharding.Mesh(
+            mesh.devices.reshape(count // 16, 2, 4, 2, mesh.shape["tm"]), FINE_AXES + ("tm",)
+        )
+        freq_axis = FINE_AXES
+    else:
+        fine = mesh
+        freq_axis = ("freq",)
+    placed = (P(freq_axis, "tm"), P(), P())
     return jax.shard_map(
-        shards, mesh=mesh, in_specs=placed, out_specs=P(None, "tm"), check_vma=False
+        functools.partial(shards, freq_axis), mesh=fine, in_specs=placed,
+        out_specs=P(None, "tm"), check_vma=False,
     )

time: 110 us -> 107 us (0.973)
  blocking collectives: 8.36 us -> 19.6 us
  starting transfers between devices: 57.2 us -> 46.7 us
  waiting for transfers between devices: 29.3 us -> 25.2 us
    all_to_all x0 -> x1, blocking collectives: none -> 11.3 us  [shards(): best = jnp.max(lax.all_to_all(spread, 'zl', 0, 0, tiled=True), axis=0)]
    ppermute x9 -> x7, starting transfers between devices: 38.2 us -> 30.3 us  [swapped(): return lax.ppermute(block, axis, route)]
    ppermute x9 -> x7, waiting for transfers between devices: 18.2 us -> 13.7 us  [swapped(): return lax.ppermute(block, axis, route)]
    ppermute x2, starting transfers between devices: 14.6 us -> 12.1 us  [paired(): lax.ppermute(block, axis, [(partner_of(i), i) for i in range(lax.axis_siz...]
  transfers between devices with their start and end apart: 12 -> 10, of which waited for: 12 -> 10; matrix products, arithmetic and copies ran while one was open for 1% -> 1% of each run, Pallas kernels for 0% -> 0%
where the time goes in v10:
time: 107 us; the launch traced here: 106 us
  starting transfers between devices  46.7 us (44%)
  waiting for transfers between devices  25.2 us (24%)
  blocking collectives  19.6 us (18%)
  other arithmetic  11.6 us (11%)
  local copies, waits for them, and re-layouts  1.9 us (2%)
    ppermute x7, starting transfers between devices, swapped(): return lax.ppermute(block, axis, route)  30.3 us
    ppermute x7, waiting for transfers between devices, swapped(): return lax.ppermute(block, axis, route)  13.7 us
    ppermute x2, starting transfers between devices, paired(): lax.ppermute(block, axis, [(partner_of(i), i) for i in range(lax.axis_siz...  12.1 us
    all_to_all x1, blocking collectives, shards(): best = jnp.max(lax.all_to_all(spread, 'zl', 0, 0, tiled=True), axis=0)  11.3 us
    all_to_all x1, blocking collectives, shards(): best = jnp.max(lax.all_to_all(best, 'tm', 1, 1, tiled=True), axis=1)  8.36 us
    ppermute x2, waiting for transfers between devices, paired(): lax.ppermute(block, axis, [(partner_of(i), i) for i in range(lax.axis_siz...  6.54 us
    select_n x49, other arithmetic, merge_rows(): jnp.where(selected, moved[:, step_size:], moved[:, :cols - step_size])  5.41 us
    all_to_all x1, waiting for transfers between devices, shards(): gathered = lax.all_to_all(spread, 'tm', 0, 0, tiled=True)  4.94 us
  transfers between devices with their start and end apart: 10, of which 10 were waited for; matrix products, arithmetic and copies ran while one was open for 1% of the time, Pallas kernels for 0%

profile of v10, /device:TPU:16, one launch (start us, length us, event | category | flops | bytes accessed | tf_op | source)
XLA Modules:
  0.0 106.0 jit_solution(12761722148067140961)
XLA Ops:
  0.0 1.2 %convert_reduce_fusion = f32[16,512]{1,0:T(8,128)S(1)} fusion(bf16[512,512]{1,0:T(8,128)(2,1)} %param.7), kind=kLoop, calls=%fused_computation.6 | loop fusion | flops 516096 | bytes 557056 | tf_op jit(solution)/shard_map/reduce_sum | solution.py:177
  1.3 0.6 broadcast_in_dim.610
  1.9 4.3 %all-to-all-start = ((f32[4,16,512]{2,1,0:T(8,128)}), f32[4,16,512]{2,1,0:T(8,128)S(1)}, u32[]{:S(2)}, u32[]{:S(2)}) async-start(f32[4,16,512]{2,1,0:T(8,128)} %broadcast_in_dim.610), calls=%async_computation | async-start | bytes 262144 | tf_op jit(solution)/shard_map/all_to_all | solution.py:179
  6.4 0.3 select_reduce_fusion.1
  6.7 0.4 select_reduce_fusion
  7.2 4.9 %all-to-all-done = f32[4,16,512]{2,1,0:T(8,128)S(1)} async-done(((f32[4,16,512]{2,1,0:T(8,128)}), f32[4,16,512]{2,1,0:T(8,128)S(1)}, u32[]{:S(2)}, u32[]{:S(2)}) %all-to-all-start) | async-done | bytes 131104 | tf_op jit(solution)/shard_map/all_to_all | solution.py:179
  12.2 0.4 slice_select_fusion.3
  12.6 0.2 slice_select_fusion.2
  12.8 0.2 slice_select_fusion.1
  13.0 0.2 slice_select_fusion
  13.3 0.2 bitcast_reduce_fusion
  13.5 1.9 %collective-permute-start = (f32[4,2048]{1,0:T(4,128)S(1)}, f32[4,2048]{1,0:T(4,128)S(1)}, u32[]{:S(2)}, u32[]{:S(2)}) collective-permute-start(f32[4,2048]{1,0:T(4,128)S(1)} %bitcast_reduce_fusion), channel_id=1, source_target_pairs={{0,4},{4,0},{8,12},{12,8},{16,20},{20,16},{24,28},{28,24},{32,36},... | collective-permute-start | bytes 98312 | tf_op jit(solution)/shard_map/ppermute | solution.py:24
  15.5 1.1 %collective-permute-done = f32[4,2048]{1,0:T(4,128)S(1)} collective-permute-done((f32[4,2048]{1,0:T(4,128)S(1)}, f32[4,2048]{1,0:T(4,128)S(1)}, u32[]{:S(2)}, u32[]{:S(2)}) %collective-permute-start) | collective-permute-done | bytes 32800 | tf_op jit(solution)/shard_map/ppermute | solution.py:24
  17.1 4.3 %collective-permute-start.1 = (f32[4,2048]{1,0:T(4,128)S(1)}, f32[4,2048]{1,0:T(4,128)S(1)}, u32[]{:S(2)}, u32[]{:S(2)}) collective-permute-start(f32[4,2048]{1,0:T(4,128)S(1)} %fusion.22), channel_id=1, source_target_pairs={{0,8},{8,0},{4,12},{12,4},{16,24},{24,16},{20,28},{28,20},{32,40},... | collective-permute-start | bytes 98312 | tf_op jit(solution)/shard_map/ppermute | solution.py:24
  21.5 1.8 %collective-permute-done.1 = f32[4,2048]{1,0:T(4,128)S(1)} collective-permute-done((f32[4,2048]{1,0:T(4,128)S(1)}, f32[4,2048]{1,0:T(4,128)S(1)}, u32[]{:S(2)}, u32[]{:S(2)}) %collective-permute-start.1) | collective-permute-done | bytes 32800 | tf_op jit(solution)/shard_map/ppermute | solution.py:24
  23.9 6.1 %collective-permute-start.2 = (f32[4,2048]{1,0:T(4,128)S(1)}, f32[4,2048]{1,0:T(4,128)S(1)}, u32[]{:S(2)}, u32[]{:S(2)}) collective-permute-start(f32[4,2048]{1,0:T(4,128)S(1)} %fusion.21), channel_id=1, source_target_pairs={{0,16},{16,0},{4,20},{20,4},{8,24},{24,8},{12,28},{28,12},{32,48},... | collective-permute-start | bytes 98312 | tf_op jit(solution)/shard_map/ppermute | solution.py:24
  30.0 2.0 %collective-permute-done.2 = f32[4,2048]{1,0:T(4,128)S(1)} collective-permute-done((f32[4,2048]{1,0:T(4,128)S(1)}, f32[4,2048]{1,0:T(4,128)S(1)}, u32[]{:S(2)}, u32[]{:S(2)}) %collective-permute-start.2) | collective-permute-done | bytes 32800 | tf_op jit(solution)/shard_map/ppermute | solution.py:24
  32.7 9.2 %collective-permute-start.3 = (f32[4,2048]{1,0:T(4,128)S(1)}, f32[4,2048]{1,0:T(4,128)S(1)}, u32[]{:S(2)}, u32[]{:S(2)}) collective-permute-start(f32[4,2048]{1,0:T(4,128)S(1)} %fusion.20), channel_id=1, source_target_pairs={{0,32},{32,0},{4,36},{36,4},{8,40},{40,8},{12,44},{44,12},{16,48},... | collective-permute-start | bytes 98312 | tf_op jit(solution)/shard_map/ppermute | solution.py:24
  41.9 1.9 %collective-permute-done.3 = f32[4,2048]{1,0:T(4,128)S(1)} collective-permute-done((f32[4,2048]{1,0:T(4,128)S(1)}, f32[4,2048]{1,0:T(4,128)S(1)}, u32[]{:S(2)}, u32[]{:S(2)}) %collective-permute-start.3) | collective-permute-done | bytes 32800 | tf_op jit(solution)/shard_map/ppermute | solution.py:24
  44.5 3.5 %collective-permute-start.4 = (f32[4,2048]{1,0:T(4,128)S(1)}, f32[4,2048]{1,0:T(4,128)S(1)}, u32[]{:S(2)}, u32[]{:S(2)}) collective-permute-start(f32[4,2048]{1,0:T(4,128)S(1)} %fusion.19), channel_id=1, source_target_pairs={{0,64},{64,0},{4,68},{68,4},{8,72},{72,8},{12,76},{76,12},{16,80},... | collective-permute-start | bytes 98312 | tf_op jit(solution)/shard_map/ppermute | solution.py:24
  48.1 2.2 %collective-permute-done.4 = f32[4,2048]{1,0:T(4,128)S(1)} collective-permute-done((f32[4,2048]{1,0:T(4,128)S(1)}, f32[4,2048]{1,0:T(4,128)S(1)}, u32[]{:S(2)}, u32[]{:S(2)}) %collective-permute-start.4) | collective-permute-done | bytes 32800 | tf_op jit(solution)/shard_map/ppermute | solution.py:24
  51.4 3.5 %collective-permute-start.5 = (f32[8,2048]{1,0:T(8,128)S(1)}, f32[8,2048]{1,0:T(8,128)S(1)}, u32[]{:S(2)}, u32[]{:S(2)}) collective-permute-start(f32[8,2048]{1,0:T(8,128)S(1)} %fusion.18), channel_id=1, source_target_pairs={{0,128},{128,0},{4,132},{132,4},{8,136},{136,8},{12,140},{140,12},... | collective-permute-start | bytes 196616 | tf_op jit(solution)/shard_map/ppermute | solution.py:24
  54.9 3.5 %collective-permute-done.5 = f32[8,2048]{1,0:T(8,128)S(1)} collective-permute-done((f32[8,2048]{1,0:T(8,128)S(1)}, f32[8,2048]{1,0:T(8,128)S(1)}, u32[]{:S(2)}, u32[]{:S(2)}) %collective-permute-start.5) | collective-permute-done | bytes 65568 | tf_op jit(solution)/shard_map/ppermute | solution.py:24
  59.9 6.3 %collective-permute-start.6 = (f32[16,2048]{1,0:T(8,128)S(1)}, f32[16,2048]{1,0:T(8,128)S(1)}, u32[]{:S(2)}, u32[]{:S(2)}) collective-permute-start(f32[16,2048]{1,0:T(8,128)S(1)} %fusion.16), channel_id=1, source_target_pairs={{384,0},{388,4},{392,8},{396,12},{400,16},{404,20},{408,24},{412,2... | collective-permute-start | bytes 393224 | tf_op jit(solution)/shard_map/ppermute | solution.py:28
  66.4 4.2 %collective-permute-done.6 = f32[16,2048]{1,0:T(8,128)S(1)} collective-permute-done((f32[16,2048]{1,0:T(8,128)S(1)}, f32[16,2048]{1,0:T(8,128)S(1)}, u32[]{:S(2)}, u32[]{:S(2)}) %collective-permute-start.6) | collective-permute-done | bytes 131104 | tf_op jit(solution)/shard_map/ppermute | solution.py:28
  74.6 8.4 %all_to_all.15 = f32[9,4,512]{2,0,1:T(8,128)S(1)} all-to-all(f32[9,4,512]{2,0,1:T(8,128)S(1)} %stack.5), channel_id=1, replica_groups=mesh['fy'=8,'zh'=2,'zl'=4,'fc'=2,'tm'=4] {'tm'}, dimensions={1} | all-to-all | bytes 147456 | tf_op jit(solution)/shard_map/all_to_all | solution.py:212
  82.9 1.9 %collective-permute-start.7 = (f32[9,512]{1,0:T(8,128)S(1)}, f32[9,512]{1,0:T(8,128)S(1)}, u32[]{:S(2)}, u32[]{:S(2)}) collective-permute-start(f32[9,512]{1,0:T(8,128)S(1)} %reduce_max.108), channel_id=1, source_target_pairs={{0,4},{4,0},{8,12},{12,8},{16,20},{20,16},{24,28},{28,24},{32,36},... | collective-permute-start | bytes 55304 | tf_op jit(solution)/shard_map/ppermute | solution.py:24
  84.9 1.2 %collective-permute-done.7 = f32[9,512]{1,0:T(8,128)S(1)} collective-permute-done((f32[9,512]{1,0:T(8,128)S(1)}, f32[9,512]{1,0:T(8,128)S(1)}, u32[]{:S(2)}, u32[]{:S(2)}) %collective-permute-start.7) | collective-permute-done | bytes 18464 | tf_op jit(solution)/shard_map/ppermute | solution.py:24
  86.1 11.3 %all_to_all.16 = f32[4,9,512]{2,1,0:T(8,128)S(1)} all-to-all(f32[4,9,512]{2,1,0:T(8,128)S(1)} %broadcast_in_dim.673), channel_id=1, replica_groups=mesh['fy'=8,'zh'=2,'zl'=4,'fc'=2,'tm'=4] {'zl'}, dimensions={0} | all-to-all | bytes 147456 | tf_op jit(solution)/shard_map/all_to_all | solution.py:216
  97.3 5.7 %collective-permute-start.8 = (f32[9,512]{1,0:T(8,128)S(1)}, f32[9,512]{1,0:T(8,128)S(1)}, u32[]{:S(2)}, u32[]{:S(2)}) collective-permute-start(f32[9,512]{1,0:T(8,128)S(1)} %reduce_max.109), channel_id=1, source_target_pairs={{48,0},{52,4},{56,8},{60,12},{32,16},{36,20},{40,24},{44,28},{16,3... | collective-permute-start | bytes 55304 | tf_op jit(solution)/shard_map/ppermute | solution.py:28
  103.1 2.3 %collective-permute-done.8 = f32[9,512]{1,0:T(8,128)S(1)} collective-permute-done((f32[9,512]{1,0:T(8,128)S(1)}, f32[9,512]{1,0:T(8,128)S(1)}, u32[]{:S(2)}, u32[]{:S(2)}) %collective-permute-start.8) | collective-permute-done | bytes 18464 | tf_op jit(solution)/shard_map/ppermute | solution.py:28
  105.4 0.6 max.7
  (120 shorter events, 9.3 us)
Async XLA Ops:
  0.0 6.3 %copy-start.2 = (s32[10,92]{1,0:T(8,128)S(1)}, s32[10,92]{1,0:T(8,128)}, u32[]{:S(2)}) copy-start(s32[10,92]{1,0:T(8,128)} %constant.82.clone) | copy-start | bytes 11044
  0.0 6.3 %copy-start.3 = (s32[10,92]{1,0:T(8,128)S(1)}, s32[10,92]{1,0:T(8,128)}, u32[]{:S(2)}) copy-start(s32[10,92]{1,0:T(8,128)} %constant.81.clone) | copy-start | bytes 11044
  0.0 6.3 %copy-start.4 = (s32[10,92]{1,0:T(8,128)S(1)}, s32[10,92]{1,0:T(8,128)}, u32[]{:S(2)}) copy-start(s32[10,92]{1,0:T(8,128)} %constant.80.clone) | copy-start | bytes 11044
  0.0 7.0 %copy-start.5 = (f32[64,20]{1,0:T(8,128)S(1)}, f32[64,20]{1,0:T(8,128)}, u32[]{:S(2)}) copy-start(f32[64,20]{1,0:T(8,128)} %constant.83.clone) | copy-start | bytes 15364
  0.0 6.4 %copy-start.1 = (s32[2047]{0:T(1024)S(1)}, s32[2047]{0:T(1024)}, u32[]{:S(2)}) copy-start(s32[2047]{0:T(1024)} %param.8) | copy-start | bytes 24568
  0.0 6.6 %copy-start = (s32[4094]{0:T(1024)S(1)}, s32[4094]{0:T(1024)}, u32[]{:S(2)}) copy-start(s32[4094]{0:T(1024)} %param.9) | copy-start | bytes 49132
  1.9 10.3 %all-to-all-start = ((f32[4,16,512]{2,1,0:T(8,128)}), f32[4,16,512]{2,1,0:T(8,128)S(1)}, u32[]{:S(2)}, u32[]{:S(2)}) async-start(f32[4,16,512]{2,1,0:T(8,128)} %broadcast_in_dim.610), calls=%async_computation | async-start | bytes 262144 | tf_op jit(solution)/shard_map/all_to_all | solution.py:179
  13.5 3.1 %collective-permute-start = (f32[4,2048]{1,0:T(4,128)S(1)}, f32[4,2048]{1,0:T(4,128)S(1)}, u32[]{:S(2)}, u32[]{:S(2)}) collective-permute-start(f32[4,2048]{1,0:T(4,128)S(1)} %bitcast_reduce_fusion), channel_id=1, source_target_pairs={{0,4},{4,0},{8,12},{12,8},{16,20},{20,16},{24,28},{28,24},{32,36},... | collective-permute-start | bytes 98312 | tf_op jit(solution)/shard_map/ppermute | solution.py:24
  17.1 6.2 %collective-permute-start.1 = (f32[4,2048]{1,0:T(4,128)S(1)}, f32[4,2048]{1,0:T(4,128)S(1)}, u32[]{:S(2)}, u32[]{:S(2)}) collective-permute-start(f32[4,2048]{1,0:T(4,128)S(1)} %fusion.22), channel_id=1, source_target_pairs={{0,8},{8,0},{4,12},{12,4},{16,24},{24,16},{20,28},{28,20},{32,40},... | collective-permute-start | bytes 98312 | tf_op jit(solution)/shard_map/ppermute | solution.py:24
  23.9 8.1 %collective-permute-start.2 = (f32[4,2048]{1,0:T(4,128)S(1)}, f32[4,2048]{1,0:T(4,128)S(1)}, u32[]{:S(2)}, u32[]{:S(2)}) collective-permute-start(f32[4,2048]{1,0:T(4,128)S(1)} %fusion.21), channel_id=1, source_target_pairs={{0,16},{16,0},{4,20},{20,4},{8,24},{24,8},{12,28},{28,12},{32,48},... | collective-permute-start | bytes 98312 | tf_op jit(solution)/shard_map/ppermute | solution.py:24
  32.7 11.1 %collective-permute-start.3 = (f32[4,2048]{1,0:T(4,128)S(1)}, f32[4,2048]{1,0:T(4,128)S(1)}, u32[]{:S(2)}, u32[]{:S(2)}) collective-permute-start(f32[4,2048]{1,0:T(4,128)S(1)} %fusion.20), channel_id=1, source_target_pairs={{0,32},{32,0},{4,36},{36,4},{8,40},{40,8},{12,44},{44,12},{16,48},... | collective-permute-start | bytes 98312 | tf_op jit(solution)/shard_map/ppermute | solution.py:24
  44.5 5.8 %collective-permute-start.4 = (f32[4,2048]{1,0:T(4,128)S(1)}, f32[4,2048]{1,0:T(4,128)S(1)}, u32[]{:S(2)}, u32[]{:S(2)}) collective-permute-start(f32[4,2048]{1,0:T(4,128)S(1)} %fusion.19), channel_id=1, source_target_pairs={{0,64},{64,0},{4,68},{68,4},{8,72},{72,8},{12,76},{76,12},{16,80},... | collective-permute-start | bytes 98312 | tf_op jit(solution)/shard_map/ppermute | solution.py:24
  51.4 7.1 %collective-permute-start.5 = (f32[8,2048]{1,0:T(8,128)S(1)}, f32[8,2048]{1,0:T(8,128)S(1)}, u32[]{:S(2)}, u32[]{:S(2)}) collective-permute-start(f32[8,2048]{1,0:T(8,128)S(1)} %fusion.18), channel_id=1, source_target_pairs={{0,128},{128,0},{4,132},{132,4},{8,136},{136,8},{12,140},{140,12},... | collective-permute-start | bytes 196616 | tf_op jit(solution)/shard_map/ppermute | solution.py:24
  59.9 10.7 %collective-permute-start.6 = (f32[16,2048]{1,0:T(8,128)S(1)}, f32[16,2048]{1,0:T(8,128)S(1)}, u32[]{:S(2)}, u32[]{:S(2)}) collective-permute-start(f32[16,2048]{1,0:T(8,128)S(1)} %fusion.16), channel_id=1, source_target_pairs={{384,0},{388,4},{392,8},{396,12},{400,16},{404,20},{408,24},{412,2... | collective-permute-start | bytes 393224 | tf_op jit(solution)/shard_map/ppermute | solution.py:28
  82.9 3.1 %collective-permute-start.7 = (f32[9,512]{1,0:T(8,128)S(1)}, f32[9,512]{1,0:T(8,128)S(1)}, u32[]{:S(2)}, u32[]{:S(2)}) collective-permute-start(f32[9,512]{1,0:T(8,128)S(1)} %reduce_max.108), channel_id=1, source_target_pairs={{0,4},{4,0},{8,12},{12,8},{16,20},{20,16},{24,28},{28,24},{32,36},... | collective-permute-start | bytes 55304 | tf_op jit(solution)/shard_map/ppermute | solution.py:24
  97.3 8.0 %collective-permute-start.8 = (f32[9,512]{1,0:T(8,128)S(1)}, f32[9,512]{1,0:T(8,128)S(1)}, u32[]{:S(2)}, u32[]{:S(2)}) collective-permute-start(f32[9,512]{1,0:T(8,128)S(1)} %reduce_max.109), channel_id=1, source_target_pairs={{48,0},{52,4},{56,8},{60,12},{32,16},{36,20},{40,24},{44,28},{16,3... | collective-permute-start | bytes 55304 | tf_op jit(solution)/shard_map/ppermute | solution.py:28

commit v11 on v10

--- a/solution.py
+++ b/solution.py
@@ -69,7 +69,7 @@
     return jnp.sum(jnp.where(hit, table[None, :], 0), axis=1)
 
 
-def delay_plan(sub_dev, held, tm_bits, freq_bits, shared, all_trials):
+def delay_plan(sub_dev, held, tm_bits, freq_bits, shared, all_trials, pair_bit):
     terms = 1 + tm_bits + freq_bits
     local_bits = sub_dev.bit_length() - 1
     held_bits = held.bit_length() - 1
@@ -129,13 +129,22 @@
         rate[0] = all_trials // trial_count - 1
         for bit in range(bit_index + 1, freq_bits):
             rate[1 + tm_bits + bit] = 1 << (bit - bit_index - 1)
-        for row in now:
-            jit = row.copy()
-            jit[0] += trial_count - 2
-            ids.append(row.copy())
-            rates.append(rate)
-            jits.append(jit)
-        level_rows.append(now.shape[0])
+        choices = [rate]
+        if bit_index == pair_bit:
+            choices = []
+            for half in range(2):
+                one = rate.copy()
+                one[1 + tm_bits + bit_index + 1] = 0
+                one[0] += half
+                choices.append(one)
+        for one in choices:
+            for row in now:
+                jit = row.copy()
+                jit[0] += trial_count - 2
+                ids.append(row.copy())
+                rates.append(one)
+                jits.append(jit)
+        level_rows.append(now.shape[0] * len(choices))
     pack = lambda parts: np.stack(parts, axis=1).astype(np.int32)
     return pack(ids), pack(rates), pack(jits), paths, unique_count, level_rows
 
@@ -152,8 +161,9 @@
     held = sub_dev // tm_count
 
     tm_bits = tm_count.bit_length() - 1
+    pair_bit = 1 if "zl" in freq_axis and freq_bits - shared > 2 else -1
     id_terms, rate_terms, jitter_terms, paths, unique_count, level_rows = delay_plan(
-        sub_dev, held, tm_bits, freq_bits, shared, all_trials
+        sub_dev, held, tm_bits, freq_bits, shared, all_trials, pair_bit
     )
     factors = jnp.concatenate(
         [jnp.ones((1,), jnp.int32),
@@ -185,6 +195,26 @@
     level = 0
     for bit_index in range(freq_bits):
         need_now = sub_dev * 2 ** (bit_index + 1) - 1
+        if bit_index == pair_bit:
+            spread = jnp.broadcast_to(trial_rows[None], (4,) + trial_rows.shape)
+            peers = lax.all_to_all(spread, "zl", 0, 0, tiled=True)
+            pairs = merge_rows(
+                jnp.concatenate([peers[0], peers[2]], axis=0),
+                zero_front(jnp.concatenate([peers[1], peers[3]], axis=0), need_now),
+                level_shifts[level],
+                need_now,
+            )
+            held_rows = trial_rows.shape[0]
+            level = level + 1
+            need_next = 2 * need_now + 1
+            trial_rows = merge_rows(
+                pairs[:held_rows], zero_front(pairs[held_rows:], need_next),
+                level_shifts[level], need_next,
+            )
+            level = level + 1
+            continue
+        if pair_bit >= 0 and bit_index == pair_bit + 1:
+            continue
         if bit_index == freq_bits - 1 and shared >= 3 and bit_index >= 2:
             partner = paired(trial_rows, freq_axis, near_half(bit_index, bit_index - 2))
         else:

time: 107 us -> 103 us (0.963)
  starting transfers between devices: 46.7 us -> 41.9 us
  waiting for transfers between devices: 25.2 us -> 28.2 us
  blocking collectives: 19.6 us -> 17.3 us
    ppermute x7 -> x5, starting transfers between devices: 30.3 us -> 17.9 us  [swapped(): return lax.ppermute(block, axis, route)]
    all_to_all x0 -> x1, starting transfers between devices: none -> 7.26 us  [shards(): peers = lax.all_to_all(spread, 'zl', 0, 0, tiled=True)]
    all_to_all x0 -> x1, waiting for transfers between devices: none -> 6.15 us  [shards(): peers = lax.all_to_all(spread, 'zl', 0, 0, tiled=True)]
    ppermute x7 -> x5, waiting for transfers between devices: 13.7 us -> 11 us  [swapped(): return lax.ppermute(block, axis, route)]
    all_to_all x1, blocking collectives: 11.3 us -> 8.92 us  [shards(): best = jnp.max(lax.all_to_all(spread, 'zl', 0, 0, tiled=True), axis=0)]
  transfers between devices with their start and end apart: 10 -> 9, of which waited for: 10 -> 9; matrix products, arithmetic and copies ran while one was open for 1% -> 1% of each run, Pallas kernels for 0% -> 0%
where the time goes in v11:
time: 103 us
  starting transfers between devices  41.9 us (41%)
  waiting for transfers between devices  28.2 us (27%)
  blocking collectives  17.3 us (17%)
  other arithmetic  11.6 us (11%)
  local copies, waits for them, and re-layouts  2.57 us (2%)
    ppermute x5, starting transfers between devices, swapped(): return lax.ppermute(block, axis, route)  17.9 us
    ppermute x2, starting transfers between devices, paired(): lax.ppermute(block, axis, [(partner_of(i), i) for i in range(lax.axis_siz...  12.4 us
    ppermute x5, waiting for transfers between devices, swapped(): return lax.ppermute(block, axis, route)  11 us
    all_to_all x1, blocking collectives, shards(): best = jnp.max(lax.all_to_all(spread, 'zl', 0, 0, tiled=True), axis=0)  8.92 us
    all_to_all x1, blocking collectives, shards(): best = jnp.max(lax.all_to_all(best, 'tm', 1, 1, tiled=True), axis=1)  8.36 us
    all_to_all x1, starting transfers between devices, shards(): peers = lax.all_to_all(spread, 'zl', 0, 0, tiled=True)  7.26 us
    all_to_all x1, waiting for transfers between devices, shards(): peers = lax.all_to_all(spread, 'zl', 0, 0, tiled=True)  6.15 us
    ppermute x2, waiting for transfers between devices, paired(): lax.ppermute(block, axis, [(partner_of(i), i) for i in range(lax.axis_siz...  6.15 us
  transfers between devices with their start and end apart: 9, of which 9 were waited for; matrix products, arithmetic and copies ran while one was open for 1% of the time, Pallas kernels for 0%

profile of v11, /device:TPU:16, one launch (start us, length us, event | category | flops | bytes accessed | tf_op | source)
XLA Modules:
  0.0 102.6 jit_solution(11390866147964682708)
XLA Ops:
  0.0 1.2 %convert_reduce_fusion = f32[16,512]{1,0:T(8,128)S(1)} fusion(bf16[512,512]{1,0:T(8,128)(2,1)} %param.7), kind=kLoop, calls=%fused_computation.6 | loop fusion | flops 516096 | bytes 557056 | tf_op jit(solution)/shard_map/reduce_sum | solution.py:187
  1.3 0.6 broadcast_in_dim.616
  1.9 4.3 %all-to-all-start = ((f32[4,16,512]{2,1,0:T(8,128)}), f32[4,16,512]{2,1,0:T(8,128)S(1)}, u32[]{:S(2)}, u32[]{:S(2)}) async-start(f32[4,16,512]{2,1,0:T(8,128)} %broadcast_in_dim.616), calls=%async_computation | async-start | bytes 262144 | tf_op jit(solution)/shard_map/all_to_all | solution.py:189
  6.4 0.3 select_reduce_fusion.1
  6.7 0.4 select_reduce_fusion
  7.3 4.8 %all-to-all-done = f32[4,16,512]{2,1,0:T(8,128)S(1)} async-done(((f32[4,16,512]{2,1,0:T(8,128)}), f32[4,16,512]{2,1,0:T(8,128)S(1)}, u32[]{:S(2)}, u32[]{:S(2)}) %all-to-all-start) | async-done | bytes 131104 | tf_op jit(solution)/shard_map/all_to_all | solution.py:189
  12.2 0.4 slice_select_fusion.3
  12.6 0.2 slice_select_fusion.2
  12.8 0.2 slice_select_fusion.1
  13.0 0.2 slice_select_fusion
  13.3 0.2 bitcast_reduce_fusion
  13.5 1.9 %collective-permute-start = (f32[4,2048]{1,0:T(4,128)S(1)}, f32[4,2048]{1,0:T(4,128)S(1)}, u32[]{:S(2)}, u32[]{:S(2)}) collective-permute-start(f32[4,2048]{1,0:T(4,128)S(1)} %bitcast_reduce_fusion), channel_id=1, source_target_pairs={{0,4},{4,0},{8,12},{12,8},{16,20},{20,16},{24,28},{28,24},{32,36},... | collective-permute-start | bytes 98312 | tf_op jit(solution)/shard_map/ppermute | solution.py:24
  15.5 1.1 %collective-permute-done = f32[4,2048]{1,0:T(4,128)S(1)} collective-permute-done((f32[4,2048]{1,0:T(4,128)S(1)}, f32[4,2048]{1,0:T(4,128)S(1)}, u32[]{:S(2)}, u32[]{:S(2)}) %collective-permute-start) | collective-permute-done | bytes 32800 | tf_op jit(solution)/shard_map/ppermute | solution.py:24
  17.1 0.7 broadcast_in_dim.622
  17.8 7.3 %all-to-all-start.1 = ((f32[4,4,2048]{2,1,0:T(4,128)}), f32[4,4,2048]{2,1,0:T(4,128)S(1)}, u32[]{:S(2)}, u32[]{:S(2)}) async-start(f32[4,4,2048]{2,1,0:T(4,128)} %broadcast_in_dim.622), calls=%async_computation.1 | async-start | bytes 262144 | tf_op jit(solution)/shard_map/all_to_all | solution.py:200
  25.1 6.1 %all-to-all-done.1 = f32[4,4,2048]{2,1,0:T(4,128)S(1)} async-done(((f32[4,4,2048]{2,1,0:T(4,128)}), f32[4,4,2048]{2,1,0:T(4,128)S(1)}, u32[]{:S(2)}, u32[]{:S(2)}) %all-to-all-start.1) | async-done | bytes 131104 | tf_op jit(solution)/shard_map/all_to_all | solution.py:200
  32.6 8.2 %collective-permute-start.1 = (f32[4,2048]{1,0:T(4,128)S(1)}, f32[4,2048]{1,0:T(4,128)S(1)}, u32[]{:S(2)}, u32[]{:S(2)}) collective-permute-start(f32[4,2048]{1,0:T(4,128)S(1)} %fusion.21), channel_id=1, source_target_pairs={{0,32},{32,0},{4,36},{36,4},{8,40},{40,8},{12,44},{44,12},{16,48},... | collective-permute-start | bytes 98312 | tf_op jit(solution)/shard_map/ppermute | solution.py:24
  40.9 1.9 %collective-permute-done.1 = f32[4,2048]{1,0:T(4,128)S(1)} collective-permute-done((f32[4,2048]{1,0:T(4,128)S(1)}, f32[4,2048]{1,0:T(4,128)S(1)}, u32[]{:S(2)}, u32[]{:S(2)}) %collective-permute-start.1) | collective-permute-done | bytes 32800 | tf_op jit(solution)/shard_map/ppermute | solution.py:24
  43.5 3.5 %collective-permute-start.2 = (f32[4,2048]{1,0:T(4,128)S(1)}, f32[4,2048]{1,0:T(4,128)S(1)}, u32[]{:S(2)}, u32[]{:S(2)}) collective-permute-start(f32[4,2048]{1,0:T(4,128)S(1)} %fusion.20), channel_id=1, source_target_pairs={{0,64},{64,0},{4,68},{68,4},{8,72},{72,8},{12,76},{76,12},{16,80},... | collective-permute-start | bytes 98312 | tf_op jit(solution)/shard_map/ppermute | solution.py:24
  47.0 2.3 %collective-permute-done.2 = f32[4,2048]{1,0:T(4,128)S(1)} collective-permute-done((f32[4,2048]{1,0:T(4,128)S(1)}, f32[4,2048]{1,0:T(4,128)S(1)}, u32[]{:S(2)}, u32[]{:S(2)}) %collective-permute-start.2) | collective-permute-done | bytes 32800 | tf_op jit(solution)/shard_map/ppermute | solution.py:24
  50.4 2.4 %collective-permute-start.3 = (f32[8,2048]{1,0:T(8,128)S(1)}, f32[8,2048]{1,0:T(8,128)S(1)}, u32[]{:S(2)}, u32[]{:S(2)}) collective-permute-start(f32[8,2048]{1,0:T(8,128)S(1)} %fusion.18), channel_id=1, source_target_pairs={{0,128},{128,0},{4,132},{132,4},{8,136},{136,8},{12,140},{140,12},... | collective-permute-start | bytes 196616 | tf_op jit(solution)/shard_map/ppermute | solution.py:24
  52.9 4.6 %collective-permute-done.3 = f32[8,2048]{1,0:T(8,128)S(1)} collective-permute-done((f32[8,2048]{1,0:T(8,128)S(1)}, f32[8,2048]{1,0:T(8,128)S(1)}, u32[]{:S(2)}, u32[]{:S(2)}) %collective-permute-start.3) | collective-permute-done | bytes 65568 | tf_op jit(solution)/shard_map/ppermute | solution.py:24
  58.9 6.3 %collective-permute-start.4 = (f32[16,2048]{1,0:T(8,128)S(1)}, f32[16,2048]{1,0:T(8,128)S(1)}, u32[]{:S(2)}, u32[]{:S(2)}) collective-permute-start(f32[16,2048]{1,0:T(8,128)S(1)} %fusion.16), channel_id=1, source_target_pairs={{384,0},{388,4},{392,8},{396,12},{400,16},{404,20},{408,24},{412,2... | collective-permute-start | bytes 393224 | tf_op jit(solution)/shard_map/ppermute | solution.py:28
  65.4 4.2 %collective-permute-done.4 = f32[16,2048]{1,0:T(8,128)S(1)} collective-permute-done((f32[16,2048]{1,0:T(8,128)S(1)}, f32[16,2048]{1,0:T(8,128)S(1)}, u32[]{:S(2)}, u32[]{:S(2)}) %collective-permute-start.4) | collective-permute-done | bytes 131104 | tf_op jit(solution)/shard_map/ppermute | solution.py:28
  70.3 0.2 fusion.3
  73.5 8.4 %all_to_all.20 = f32[9,4,512]{2,0,1:T(8,128)S(1)} all-to-all(f32[9,4,512]{2,0,1:T(8,128)S(1)} %stack.5), channel_id=1, replica_groups=mesh['fy'=8,'zh'=2,'zl'=4,'fc'=2,'tm'=4] {'tm'}, dimensions={1} | all-to-all | bytes 147456 | tf_op jit(solution)/shard_map/all_to_all | solution.py:242
  81.9 1.9 %collective-permute-start.5 = (f32[9,512]{1,0:T(8,128)S(1)}, f32[9,512]{1,0:T(8,128)S(1)}, u32[]{:S(2)}, u32[]{:S(2)}) collective-permute-start(f32[9,512]{1,0:T(8,128)S(1)} %reduce_max.108), channel_id=1, source_target_pairs={{0,4},{4,0},{8,12},{12,8},{16,20},{20,16},{24,28},{28,24},{32,36},... | collective-permute-start | bytes 55304 | tf_op jit(solution)/shard_map/ppermute | solution.py:24
  83.9 1.2 %collective-permute-done.5 = f32[9,512]{1,0:T(8,128)S(1)} collective-permute-done((f32[9,512]{1,0:T(8,128)S(1)}, f32[9,512]{1,0:T(8,128)S(1)}, u32[]{:S(2)}, u32[]{:S(2)}) %collective-permute-start.5) | collective-permute-done | bytes 18464 | tf_op jit(solution)/shard_map/ppermute | solution.py:24
  85.1 8.9 %all_to_all.21 = f32[4,9,512]{2,1,0:T(8,128)S(1)} all-to-all(f32[4,9,512]{2,1,0:T(8,128)S(1)} %broadcast_in_dim.680), channel_id=1, replica_groups=mesh['fy'=8,'zh'=2,'zl'=4,'fc'=2,'tm'=4] {'zl'}, dimensions={0} | all-to-all | bytes 147456 | tf_op jit(solution)/shard_map/all_to_all | solution.py:246
  94.0 6.1 %collective-permute-start.6 = (f32[9,512]{1,0:T(8,128)S(1)}, f32[9,512]{1,0:T(8,128)S(1)}, u32[]{:S(2)}, u32[]{:S(2)}) collective-permute-start(f32[9,512]{1,0:T(8,128)S(1)} %reduce_max.109), channel_id=1, source_target_pairs={{48,0},{52,4},{56,8},{60,12},{32,16},{36,20},{40,24},{44,28},{16,3... | collective-permute-start | bytes 55304 | tf_op jit(solution)/shard_map/ppermute | solution.py:28
  100.1 1.9 %collective-permute-done.6 = f32[9,512]{1,0:T(8,128)S(1)} collective-permute-done((f32[9,512]{1,0:T(8,128)S(1)}, f32[9,512]{1,0:T(8,128)S(1)}, u32[]{:S(2)}, u32[]{:S(2)}) %collective-permute-start.6) | collective-permute-done | bytes 18464 | tf_op jit(solution)/shard_map/ppermute | solution.py:28
  102.0 0.6 max.7
  (120 shorter events, 9.2 us)
Async XLA Ops:
  0.0 6.3 %copy-start.2 = (s32[10,96]{1,0:T(8,128)S(1)}, s32[10,96]{1,0:T(8,128)}, u32[]{:S(2)}) copy-start(s32[10,96]{1,0:T(8,128)} %constant.82.clone) | copy-start | bytes 11524
  0.0 6.3 %copy-start.3 = (s32[10,96]{1,0:T(8,128)S(1)}, s32[10,96]{1,0:T(8,128)}, u32[]{:S(2)}) copy-start(s32[10,96]{1,0:T(8,128)} %constant.81.clone) | copy-start | bytes 11524
  0.0 6.3 %copy-start.4 = (s32[10,96]{1,0:T(8,128)S(1)}, s32[10,96]{1,0:T(8,128)}, u32[]{:S(2)}) copy-start(s32[10,96]{1,0:T(8,128)} %constant.80.clone) | copy-start | bytes 11524
  0.0 7.0 %copy-start.5 = (f32[64,20]{1,0:T(8,128)S(1)}, f32[64,20]{1,0:T(8,128)}, u32[]{:S(2)}) copy-start(f32[64,20]{1,0:T(8,128)} %constant.83.clone) | copy-start | bytes 15364
  0.0 6.4 %copy-start.1 = (s32[2047]{0:T(1024)S(1)}, s32[2047]{0:T(1024)}, u32[]{:S(2)}) copy-start(s32[2047]{0:T(1024)} %param.8) | copy-start | bytes 24568
  0.0 6.6 %copy-start = (s32[4094]{0:T(1024)S(1)}, s32[4094]{0:T(1024)}, u32[]{:S(2)}) copy-start(s32[4094]{0:T(1024)} %param.9) | copy-start | bytes 49132
  1.9 10.3 %all-to-all-start = ((f32[4,16,512]{2,1,0:T(8,128)}), f32[4,16,512]{2,1,0:T(8,128)S(1)}, u32[]{:S(2)}, u32[]{:S(2)}) async-start(f32[4,16,512]{2,1,0:T(8,128)} %broadcast_in_dim.616), calls=%async_computation | async-start | bytes 262144 | tf_op jit(solution)/shard_map/all_to_all | solution.py:189
  13.5 3.1 %collective-permute-start = (f32[4,2048]{1,0:T(4,128)S(1)}, f32[4,2048]{1,0:T(4,128)S(1)}, u32[]{:S(2)}, u32[]{:S(2)}) collective-permute-start(f32[4,2048]{1,0:T(4,128)S(1)} %bitcast_reduce_fusion), channel_id=1, source_target_pairs={{0,4},{4,0},{8,12},{12,8},{16,20},{20,16},{24,28},{28,24},{32,36},... | collective-permute-start | bytes 98312 | tf_op jit(solution)/shard_map/ppermute | solution.py:24
  17.8 13.5 %all-to-all-start.1 = ((f32[4,4,2048]{2,1,0:T(4,128)}), f32[4,4,2048]{2,1,0:T(4,128)S(1)}, u32[]{:S(2)}, u32[]{:S(2)}) async-start(f32[4,4,2048]{2,1,0:T(4,128)} %broadcast_in_dim.622), calls=%async_computation.1 | async-start | bytes 262144 | tf_op jit(solution)/shard_map/all_to_all | solution.py:200
  32.6 10.1 %collective-permute-start.1 = (f32[4,2048]{1,0:T(4,128)S(1)}, f32[4,2048]{1,0:T(4,128)S(1)}, u32[]{:S(2)}, u32[]{:S(2)}) collective-permute-start(f32[4,2048]{1,0:T(4,128)S(1)} %fusion.21), channel_id=1, source_target_pairs={{0,32},{32,0},{4,36},{36,4},{8,40},{40,8},{12,44},{44,12},{16,48},... | collective-permute-start | bytes 98312 | tf_op jit(solution)/shard_map/ppermute | solution.py:24
  43.5 5.8 %collective-permute-start.2 = (f32[4,2048]{1,0:T(4,128)S(1)}, f32[4,2048]{1,0:T(4,128)S(1)}, u32[]{:S(2)}, u32[]{:S(2)}) collective-permute-start(f32[4,2048]{1,0:T(4,128)S(1)} %fusion.20), channel_id=1, source_target_pairs={{0,64},{64,0},{4,68},{68,4},{8,72},{72,8},{12,76},{76,12},{16,80},... | collective-permute-start | bytes 98312 | tf_op jit(solution)/shard_map/ppermute | solution.py:24
  50.4 7.1 %collective-permute-start.3 = (f32[8,2048]{1,0:T(8,128)S(1)}, f32[8,2048]{1,0:T(8,128)S(1)}, u32[]{:S(2)}, u32[]{:S(2)}) collective-permute-start(f32[8,2048]{1,0:T(8,128)S(1)} %fusion.18), channel_id=1, source_target_pairs={{0,128},{128,0},{4,132},{132,4},{8,136},{136,8},{12,140},{140,12},... | collective-permute-start | bytes 196616 | tf_op jit(solution)/shard_map/ppermute | solution.py:24
  58.9 10.7 %collective-permute-start.4 = (f32[16,2048]{1,0:T(8,128)S(1)}, f32[16,2048]{1,0:T(8,128)S(1)}, u32[]{:S(2)}, u32[]{:S(2)}) collective-permute-start(f32[16,2048]{1,0:T(8,128)S(1)} %fusion.16), channel_id=1, source_target_pairs={{384,0},{388,4},{392,8},{396,12},{400,16},{404,20},{408,24},{412,2... | collective-permute-start | bytes 393224 | tf_op jit(solution)/shard_map/ppermute | solution.py:28
  81.9 3.1 %collective-permute-start.5 = (f32[9,512]{1,0:T(8,128)S(1)}, f32[9,512]{1,0:T(8,128)S(1)}, u32[]{:S(2)}, u32[]{:S(2)}) collective-permute-start(f32[9,512]{1,0:T(8,128)S(1)} %reduce_max.108), channel_id=1, source_target_pairs={{0,4},{4,0},{8,12},{12,8},{16,20},{20,16},{24,28},{28,24},{32,36},... | collective-permute-start | bytes 55304 | tf_op jit(solution)/shard_map/ppermute | solution.py:24
  94.0 8.0 %collective-permute-start.6 = (f32[9,512]{1,0:T(8,128)S(1)}, f32[9,512]{1,0:T(8,128)S(1)}, u32[]{:S(2)}, u32[]{:S(2)}) collective-permute-start(f32[9,512]{1,0:T(8,128)S(1)} %reduce_max.109), channel_id=1, source_target_pairs={{48,0},{52,4},{56,8},{60,12},{32,16},{36,20},{40,24},{44,28},{16,3... | collective-permute-start | bytes 55304 | tf_op jit(solution)/shard_map/ppermute | solution.py:28

commit v12 on v11

--- a/solution.py
+++ b/solution.py
@@ -11,7 +11,6 @@
 WIDTHS = 9
 SHARED_LEVELS = 3
 NEAR_HALF = (6, 7, 4, 5, 2, 3, 0, 1)
-FINE_AXES = ("fy", "zh", "zl", "fc")
 
 
 def swapped(block, axis, apart):
@@ -69,7 +68,7 @@
     return jnp.sum(jnp.where(hit, table[None, :], 0), axis=1)
 
 
-def delay_plan(sub_dev, held, tm_bits, freq_bits, shared, all_trials, pair_bit):
+def delay_plan(sub_dev, held, tm_bits, freq_bits, shared, all_trials, pair_bits):
     terms = 1 + tm_bits + freq_bits
     local_bits = sub_dev.bit_length() - 1
     held_bits = held.bit_length() - 1
@@ -130,7 +129,7 @@
         for bit in range(bit_index + 1, freq_bits):
             rate[1 + tm_bits + bit] = 1 << (bit - bit_index - 1)
         choices = [rate]
-        if bit_index == pair_bit:
+        if bit_index in pair_bits:
             choices = []
             for half in range(2):
                 one = rate.copy()
@@ -161,9 +160,14 @@
     held = sub_dev // tm_count
 
     tm_bits = tm_count.bit_length() - 1
-    pair_bit = 1 if "zl" in freq_axis and freq_bits - shared > 2 else -1
+    pair_axes = {}
+    for bit_index, name in ((1, "zl"), (4, "yl")):
+        redundant = [bit_index + step >= freq_bits - shared for step in (0, 1)]
+        if name in freq_axis and redundant[0] == redundant[1]:
+            pair_axes[bit_index] = name
+    pair_bits = tuple(pair_axes)
     id_terms, rate_terms, jitter_terms, paths, unique_count, level_rows = delay_plan(
-        sub_dev, held, tm_bits, freq_bits, shared, all_trials, pair_bit
+        sub_dev, held, tm_bits, freq_bits, shared, all_trials, pair_bits
     )
     factors = jnp.concatenate(
         [jnp.ones((1,), jnp.int32),
@@ -195,25 +199,31 @@
     level = 0
     for bit_index in range(freq_bits):
         need_now = sub_dev * 2 ** (bit_index + 1) - 1
-        if bit_index == pair_bit:
+        if bit_index in pair_axes:
             spread = jnp.broadcast_to(trial_rows[None], (4,) + trial_rows.shape)
-            peers = lax.all_to_all(spread, "zl", 0, 0, tiled=True)
+            peers = lax.all_to_all(spread, pair_axes[bit_index], 0, 0, tiled=True)
+            doubled = bit_index >= freq_bits - shared
+            if doubled:
+                peers = jnp.repeat(peers, 2, axis=1)
             pairs = merge_rows(
                 jnp.concatenate([peers[0], peers[2]], axis=0),
                 zero_front(jnp.concatenate([peers[1], peers[3]], axis=0), need_now),
                 level_shifts[level],
                 need_now,
             )
-            held_rows = trial_rows.shape[0]
+            half = pairs.shape[0] // 2
+            low_rows, high_rows = pairs[:half], pairs[half:]
+            if doubled:
+                low_rows = jnp.repeat(low_rows, 2, axis=0)
+                high_rows = jnp.repeat(high_rows, 2, axis=0)
             level = level + 1
             need_next = 2 * need_now + 1
             trial_rows = merge_rows(
-                pairs[:held_rows], zero_front(pairs[held_rows:], need_next),
-                level_shifts[level], need_next,
+                low_rows, zero_front(high_rows, need_next), level_shifts[level], need_next
             )
             level = level + 1
             continue
-        if pair_bit >= 0 and bit_index == pair_bit + 1:
+        if bit_index - 1 in pair_axes:
             continue
         if bit_index == freq_bits - 1 and shared >= 3 and bit_index >= 2:
             partner = paired(trial_rows, freq_axis, near_half(bit_index, bit_index - 2))
@@ -255,14 +265,15 @@
 
 def solution(mesh):
     count = mesh.shape["freq"]
-    if count % 16 == 0:
-        fine = jax.sharding.Mesh(
-            mesh.devices.reshape(count // 16, 2, 4, 2, mesh.shape["tm"]), FINE_AXES + ("tm",)
-        )
-        freq_axis = FINE_AXES
+    if count == 128:
+        freq_axis, sizes = ("yh", "yl", "zh", "zl", "fc"), (2, 4, 2, 4, 2)
+    elif count == 16:
+        freq_axis, sizes = ("zh", "zl", "fc"), (2, 4, 2)
     else:
-        fine = mesh
-        freq_axis = ("freq",)
+        freq_axis, sizes = ("freq",), (count,)
+    fine = jax.sharding.Mesh(
+        mesh.devices.reshape(sizes + (mesh.shape["tm"],)), freq_axis + ("tm",)
+    )
     placed = (P(freq_axis, "tm"), P(), P())
     return jax.shard_map(
         functools.partial(shards, freq_axis), mesh=fine, in_specs=placed,

time: 103 us -> 102 us (level)
  the two profiles are of different devices: /device:TPU:16 before, /device:TPU:8 now
where the time goes in v12:
time: 102 us; the launch traced here: 101 us
  starting transfers between devices  39.5 us (39%)
  waiting for transfers between devices  27.9 us (27%)
  blocking collectives  17.3 us (17%)
  other arithmetic  11.9 us (12%)
  local copies, waits for them, and re-layouts  3.39 us (3%)
    all_to_all x2, starting transfers between devices, shards(): peers = lax.all_to_all(spread, pair_axes[bit_index], 0, 0, tiled=True)  12.6 us
    ppermute x3, starting transfers between devices, swapped(): return lax.ppermute(block, axis, route)  12.1 us
    all_to_all x2, waiting for transfers between devices, shards(): peers = lax.all_to_all(spread, pair_axes[bit_index], 0, 0, tiled=True)  11.2 us
    ppermute x2, starting transfers between devices, paired(): lax.ppermute(block, axis, [(partner_of(i), i) for i in range(lax.axis_siz...  10.6 us
    all_to_all x1, blocking collectives, shards(): best = jnp.max(lax.all_to_all(spread, 'zl', 0, 0, tiled=True), axis=0)  8.92 us
    all_to_all x1, blocking collectives, shards(): best = jnp.max(lax.all_to_all(best, 'tm', 1, 1, tiled=True), axis=1)  8.36 us
    ppermute x2, waiting for transfers between devices, paired(): lax.ppermute(block, axis, [(partner_of(i), i) for i in range(lax.axis_siz...  7.67 us
    select_n x49, other arithmetic, merge_rows(): jnp.where(selected, moved[:, step_size:], moved[:, :cols - step_size])  5.51 us
  transfers between devices with their start and end apart: 8, of which 8 were waited for; matrix products, arithmetic and copies ran while one was open for 1% of the time, Pallas kernels for 0%

profile of v12, /device:TPU:8, one launch (start us, length us, event | category | flops | bytes accessed | tf_op | source)
XLA Modules:
  0.0 100.9 jit_solution(6717053888871539004)
XLA Ops:
  0.0 1.2 %convert_reduce_fusion = f32[16,512]{1,0:T(8,128)S(1)} fusion(bf16[512,512]{1,0:T(8,128)(2,1)} %param.7), kind=kLoop, calls=%fused_computation.6 | loop fusion | flops 516096 | bytes 557056 | tf_op jit(solution)/shard_map/reduce_sum | solution.py:191
  1.3 0.6 broadcast_in_dim.633
  1.9 4.3 %all-to-all-start = ((f32[4,16,512]{2,1,0:T(8,128)}), f32[4,16,512]{2,1,0:T(8,128)S(1)}, u32[]{:S(2)}, u32[]{:S(2)}) async-start(f32[4,16,512]{2,1,0:T(8,128)} %broadcast_in_dim.633), calls=%async_computation | async-start | bytes 262144 | tf_op jit(solution)/shard_map/all_to_all | solution.py:193
  6.4 0.3 select_reduce_fusion.1
  6.7 0.4 select_reduce_fusion
  7.4 4.8 %all-to-all-done = f32[4,16,512]{2,1,0:T(8,128)S(1)} async-done(((f32[4,16,512]{2,1,0:T(8,128)}), f32[4,16,512]{2,1,0:T(8,128)S(1)}, u32[]{:S(2)}, u32[]{:S(2)}) %all-to-all-start) | async-done | bytes 131104 | tf_op jit(solution)/shard_map/all_to_all | solution.py:193
  12.2 0.4 slice_select_fusion.3
  12.6 0.2 slice_select_fusion.2
  12.8 0.2 slice_select_fusion.1
  13.0 0.2 slice_select_fusion
  13.3 0.2 bitcast_reduce_fusion
  13.5 1.9 %collective-permute-start = (f32[4,2048]{1,0:T(4,128)S(1)}, f32[4,2048]{1,0:T(4,128)S(1)}, u32[]{:S(2)}, u32[]{:S(2)}) collective-permute-start(f32[4,2048]{1,0:T(4,128)S(1)} %bitcast_reduce_fusion), channel_id=1, source_target_pairs={{0,4},{4,0},{8,12},{12,8},{16,20},{20,16},{24,28},{28,24},{32,36},... | collective-permute-start | bytes 98312 | tf_op jit(solution)/shard_map/ppermute | solution.py:23
  15.5 1.1 %collective-permute-done = f32[4,2048]{1,0:T(4,128)S(1)} collective-permute-done((f32[4,2048]{1,0:T(4,128)S(1)}, f32[4,2048]{1,0:T(4,128)S(1)}, u32[]{:S(2)}, u32[]{:S(2)}) %collective-permute-start) | collective-permute-done | bytes 32800 | tf_op jit(solution)/shard_map/ppermute | solution.py:23
  17.1 0.7 broadcast_in_dim.639
  17.8 7.3 %all-to-all-start.1 = ((f32[4,4,2048]{2,1,0:T(4,128)}), f32[4,4,2048]{2,1,0:T(4,128)S(1)}, u32[]{:S(2)}, u32[]{:S(2)}) async-start(f32[4,4,2048]{2,1,0:T(4,128)} %broadcast_in_dim.639), calls=%async_computation.1 | async-start | bytes 262144 | tf_op jit(solution)/shard_map/all_to_all | solution.py:204
  25.1 6.2 %all-to-all-done.1 = f32[4,4,2048]{2,1,0:T(4,128)S(1)} async-done(((f32[4,4,2048]{2,1,0:T(4,128)}), f32[4,4,2048]{2,1,0:T(4,128)S(1)}, u32[]{:S(2)}, u32[]{:S(2)}) %all-to-all-start.1) | async-done | bytes 131104 | tf_op jit(solution)/shard_map/all_to_all | solution.py:204
  32.6 8.2 %collective-permute-start.1 = (f32[4,2048]{1,0:T(4,128)S(1)}, f32[4,2048]{1,0:T(4,128)S(1)}, u32[]{:S(2)}, u32[]{:S(2)}) collective-permute-start(f32[4,2048]{1,0:T(4,128)S(1)} %fusion.20), channel_id=1, source_target_pairs={{0,32},{32,0},{4,36},{36,4},{8,40},{40,8},{12,44},{44,12},{16,48},... | collective-permute-start | bytes 98312 | tf_op jit(solution)/shard_map/ppermute | solution.py:23
  40.9 1.9 %collective-permute-done.1 = f32[4,2048]{1,0:T(4,128)S(1)} collective-permute-done((f32[4,2048]{1,0:T(4,128)S(1)}, f32[4,2048]{1,0:T(4,128)S(1)}, u32[]{:S(2)}, u32[]{:S(2)}) %collective-permute-start.1) | collective-permute-done | bytes 32800 | tf_op jit(solution)/shard_map/ppermute | solution.py:23
  43.5 0.7 broadcast_in_dim.661
  44.2 5.3 %all-to-all-start.2 = ((f32[4,4,2048]{2,1,0:T(4,128)}), f32[4,4,2048]{2,1,0:T(4,128)S(1)}, u32[]{:S(2)}, u32[]{:S(2)}) async-start(f32[4,4,2048]{2,1,0:T(4,128)} %broadcast_in_dim.661), calls=%async_computation.2 | async-start | bytes 262144 | tf_op jit(solution)/shard_map/all_to_all | solution.py:204
  49.6 5.1 %all-to-all-done.2 = f32[4,4,2048]{2,1,0:T(4,128)S(1)} async-done(((f32[4,4,2048]{2,1,0:T(4,128)}), f32[4,4,2048]{2,1,0:T(4,128)S(1)}, u32[]{:S(2)}, u32[]{:S(2)}) %all-to-all-start.2) | async-done | bytes 131104 | tf_op jit(solution)/shard_map/all_to_all | solution.py:204
  57.6 4.5 %collective-permute-start.2 = (f32[16,2048]{1,0:T(8,128)S(1)}, f32[16,2048]{1,0:T(8,128)S(1)}, u32[]{:S(2)}, u32[]{:S(2)}) collective-permute-start(f32[16,2048]{1,0:T(8,128)S(1)} %fusion.16), channel_id=1, source_target_pairs={{384,0},{388,4},{392,8},{396,12},{400,16},{404,20},{408,24},{412,2... | collective-permute-start | bytes 393224 | tf_op jit(solution)/shard_map/ppermute | solution.py:27
  62.2 5.8 %collective-permute-done.2 = f32[16,2048]{1,0:T(8,128)S(1)} collective-permute-done((f32[16,2048]{1,0:T(8,128)S(1)}, f32[16,2048]{1,0:T(8,128)S(1)}, u32[]{:S(2)}, u32[]{:S(2)}) %collective-permute-start.2) | collective-permute-done | bytes 131104 | tf_op jit(solution)/shard_map/ppermute | solution.py:27
  68.6 0.2 fusion.3
  69.3 0.2 slice_select_fusion.6
  71.9 8.4 %all_to_all.25 = f32[9,4,512]{2,0,1:T(8,128)S(1)} all-to-all(f32[9,4,512]{2,0,1:T(8,128)S(1)} %stack.5), channel_id=1, replica_groups=mesh['yh'=2,'yl'=4,'zh'=2,'zl'=4,'fc'=2,'tm'=4] {'tm'}, dimensions={1} | all-to-all | bytes 147456 | tf_op jit(solution)/shard_map/all_to_all | solution.py:252
  80.3 1.9 %collective-permute-start.3 = (f32[9,512]{1,0:T(8,128)S(1)}, f32[9,512]{1,0:T(8,128)S(1)}, u32[]{:S(2)}, u32[]{:S(2)}) collective-permute-start(f32[9,512]{1,0:T(8,128)S(1)} %reduce_max.108), channel_id=1, source_target_pairs={{0,4},{4,0},{8,12},{12,8},{16,20},{20,16},{24,28},{28,24},{32,36},... | collective-permute-start | bytes 55304 | tf_op jit(solution)/shard_map/ppermute | solution.py:23
  82.2 1.2 %collective-permute-done.3 = f32[9,512]{1,0:T(8,128)S(1)} collective-permute-done((f32[9,512]{1,0:T(8,128)S(1)}, f32[9,512]{1,0:T(8,128)S(1)}, u32[]{:S(2)}, u32[]{:S(2)}) %collective-permute-start.3) | collective-permute-done | bytes 18464 | tf_op jit(solution)/shard_map/ppermute | solution.py:23
  83.4 8.9 %all_to_all.26 = f32[4,9,512]{2,1,0:T(8,128)S(1)} all-to-all(f32[4,9,512]{2,1,0:T(8,128)S(1)} %broadcast_in_dim.704), channel_id=1, replica_groups=mesh['yh'=2,'yl'=4,'zh'=2,'zl'=4,'fc'=2,'tm'=4] {'zl'}, dimensions={0} | all-to-all | bytes 147456 | tf_op jit(solution)/shard_map/all_to_all | solution.py:256
  92.3 6.1 %collective-permute-start.4 = (f32[9,512]{1,0:T(8,128)S(1)}, f32[9,512]{1,0:T(8,128)S(1)}, u32[]{:S(2)}, u32[]{:S(2)}) collective-permute-start(f32[9,512]{1,0:T(8,128)S(1)} %reduce_max.109), channel_id=1, source_target_pairs={{48,0},{52,4},{56,8},{60,12},{32,16},{36,20},{40,24},{44,28},{16,3... | collective-permute-start | bytes 55304 | tf_op jit(solution)/shard_map/ppermute | solution.py:27
  98.4 1.9 %collective-permute-done.4 = f32[9,512]{1,0:T(8,128)S(1)} collective-permute-done((f32[9,512]{1,0:T(8,128)S(1)}, f32[9,512]{1,0:T(8,128)S(1)}, u32[]{:S(2)}, u32[]{:S(2)}) %collective-permute-start.4) | collective-permute-done | bytes 18464 | tf_op jit(solution)/shard_map/ppermute | solution.py:27
  100.3 0.6 max.7
  (124 shorter events, 9.3 us)
Async XLA Ops:
  0.0 6.3 %copy-start.2 = (s32[10,104]{1,0:T(8,128)S(1)}, s32[10,104]{1,0:T(8,128)}, u32[]{:S(2)}) copy-start(s32[10,104]{1,0:T(8,128)} %constant.84.clone) | copy-start | bytes 12484
  0.0 6.3 %copy-start.3 = (s32[10,104]{1,0:T(8,128)S(1)}, s32[10,104]{1,0:T(8,128)}, u32[]{:S(2)}) copy-start(s32[10,104]{1,0:T(8,128)} %constant.83.clone) | copy-start | bytes 12484
  0.0 6.3 %copy-start.4 = (s32[10,104]{1,0:T(8,128)S(1)}, s32[10,104]{1,0:T(8,128)}, u32[]{:S(2)}) copy-start(s32[10,104]{1,0:T(8,128)} %constant.82.clone) | copy-start | bytes 12484
  0.0 7.1 %copy-start.5 = (f32[64,20]{1,0:T(8,128)S(1)}, f32[64,20]{1,0:T(8,128)}, u32[]{:S(2)}) copy-start(f32[64,20]{1,0:T(8,128)} %constant.85.clone) | copy-start | bytes 15364
  0.0 6.4 %copy-start.1 = (s32[2047]{0:T(1024)S(1)}, s32[2047]{0:T(1024)}, u32[]{:S(2)}) copy-start(s32[2047]{0:T(1024)} %param.8) | copy-start | bytes 24568
  0.0 6.6 %copy-start = (s32[4094]{0:T(1024)S(1)}, s32[4094]{0:T(1024)}, u32[]{:S(2)}) copy-start(s32[4094]{0:T(1024)} %param.9) | copy-start | bytes 49132
  1.9 10.3 %all-to-all-start = ((f32[4,16,512]{2,1,0:T(8,128)}), f32[4,16,512]{2,1,0:T(8,128)S(1)}, u32[]{:S(2)}, u32[]{:S(2)}) async-start(f32[4,16,512]{2,1,0:T(8,128)} %broadcast_in_dim.633), calls=%async_computation | async-start | bytes 262144 | tf_op jit(solution)/shard_map/all_to_all | solution.py:193
  13.5 3.1 %collective-permute-start = (f32[4,2048]{1,0:T(4,128)S(1)}, f32[4,2048]{1,0:T(4,128)S(1)}, u32[]{:S(2)}, u32[]{:S(2)}) collective-permute-start(f32[4,2048]{1,0:T(4,128)S(1)} %bitcast_reduce_fusion), channel_id=1, source_target_pairs={{0,4},{4,0},{8,12},{12,8},{16,20},{20,16},{24,28},{28,24},{32,36},... | collective-permute-start | bytes 98312 | tf_op jit(solution)/shard_map/ppermute | solution.py:23
  17.8 13.5 %all-to-all-start.1 = ((f32[4,4,2048]{2,1,0:T(4,128)}), f32[4,4,2048]{2,1,0:T(4,128)S(1)}, u32[]{:S(2)}, u32[]{:S(2)}) async-start(f32[4,4,2048]{2,1,0:T(4,128)} %broadcast_in_dim.639), calls=%async_computation.1 | async-start | bytes 262144 | tf_op jit(solution)/shard_map/all_to_all | solution.py:204
  32.6 10.1 %collective-permute-start.1 = (f32[4,2048]{1,0:T(4,128)S(1)}, f32[4,2048]{1,0:T(4,128)S(1)}, u32[]{:S(2)}, u32[]{:S(2)}) collective-permute-start(f32[4,2048]{1,0:T(4,128)S(1)} %fusion.20), channel_id=1, source_target_pairs={{0,32},{32,0},{4,36},{36,4},{8,40},{40,8},{12,44},{44,12},{16,48},... | collective-permute-start | bytes 98312 | tf_op jit(solution)/shard_map/ppermute | solution.py:23
  44.2 10.5 %all-to-all-start.2 = ((f32[4,4,2048]{2,1,0:T(4,128)}), f32[4,4,2048]{2,1,0:T(4,128)S(1)}, u32[]{:S(2)}, u32[]{:S(2)}) async-start(f32[4,4,2048]{2,1,0:T(4,128)} %broadcast_in_dim.661), calls=%async_computation.2 | async-start | bytes 262144 | tf_op jit(solution)/shard_map/all_to_all | solution.py:204
  57.6 10.4 %collective-permute-start.2 = (f32[16,2048]{1,0:T(8,128)S(1)}, f32[16,2048]{1,0:T(8,128)S(1)}, u32[]{:S(2)}, u32[]{:S(2)}) collective-permute-start(f32[16,2048]{1,0:T(8,128)S(1)} %fusion.16), channel_id=1, source_target_pairs={{384,0},{388,4},{392,8},{396,12},{400,16},{404,20},{408,24},{412,2... | collective-permute-start | bytes 393224 | tf_op jit(solution)/shard_map/ppermute | solution.py:27
  80.3 3.1 %collective-permute-start.3 = (f32[9,512]{1,0:T(8,128)S(1)}, f32[9,512]{1,0:T(8,128)S(1)}, u32[]{:S(2)}, u32[]{:S(2)}) collective-permute-start(f32[9,512]{1,0:T(8,128)S(1)} %reduce_max.108), channel_id=1, source_target_pairs={{0,4},{4,0},{8,12},{12,8},{16,20},{20,16},{24,28},{28,24},{32,36},... | collective-permute-start | bytes 55304 | tf_op jit(solution)/shard_map/ppermute | solution.py:23
  92.3 8.0 %collective-permute-start.4 = (f32[9,512]{1,0:T(8,128)S(1)}, f32[9,512]{1,0:T(8,128)S(1)}, u32[]{:S(2)}, u32[]{:S(2)}) collective-permute-start(f32[9,512]{1,0:T(8,128)S(1)} %reduce_max.109), channel_id=1, source_target_pairs={{48,0},{52,4},{56,8},{60,12},{32,16},{36,20},{40,24},{44,28},{16,3... | collective-permute-start | bytes 55304 | tf_op jit(solution)/shard_map/ppermute | solution.py:27

commit v13 on v10

--- a/solution.py
+++ b/solution.py
@@ -11,7 +11,7 @@
 WIDTHS = 9
 SHARED_LEVELS = 3
 NEAR_HALF = (6, 7, 4, 5, 2, 3, 0, 1)
-FINE_AXES = ("fy", "zh", "zl", "fc")
+FINE_BITS = {"yh": 1, "yl": 2, "zh": 1, "zl": 2, "fc": 1}
 
 
 def swapped(block, axis, apart):
@@ -69,7 +69,7 @@
     return jnp.sum(jnp.where(hit, table[None, :], 0), axis=1)
 
 
-def delay_plan(sub_dev, held, tm_bits, freq_bits, shared, all_trials):
+def delay_plan(sub_dev, held, tm_bits, freq_bits, shared, all_trials, choice_bits):
     terms = 1 + tm_bits + freq_bits
     local_bits = sub_dev.bit_length() - 1
     held_bits = held.bit_length() - 1
@@ -129,13 +129,22 @@
         rate[0] = all_trials // trial_count - 1
         for bit in range(bit_index + 1, freq_bits):
             rate[1 + tm_bits + bit] = 1 << (bit - bit_index - 1)
-        for row in now:
-            jit = row.copy()
-            jit[0] += trial_count - 2
-            ids.append(row.copy())
-            rates.append(rate)
-            jits.append(jit)
-        level_rows.append(now.shape[0])
+        choices = []
+        spread_bits = choice_bits.get(bit_index, 0)
+        for value in range(2**spread_bits):
+            one = rate.copy()
+            for step in range(spread_bits):
+                one[1 + tm_bits + bit_index + 1 + step] = 0
+            one[0] += value
+            choices.append(one)
+        for one in choices:
+            for row in now:
+                jit = row.copy()
+                jit[0] += trial_count - 2
+                ids.append(row.copy())
+                rates.append(one)
+                jits.append(jit)
+        level_rows.append(now.shape[0] * len(choices))
     pack = lambda parts: np.stack(parts, axis=1).astype(np.int32)
     return pack(ids), pack(rates), pack(jits), paths, unique_count, level_rows
 
@@ -152,8 +161,18 @@
     held = sub_dev // tm_count
 
     tm_bits = tm_count.bit_length() - 1
+    groups = {}
+    for first, names in ((1, ("zh", "zl")), (4, ("yl",))):
+        width = sum(FINE_BITS[name] for name in names)
+        redundant = {first + step >= freq_bits - shared for step in range(width)}
+        if all(name in freq_axis for name in names) and len(redundant) == 1:
+            groups[first] = (names, width)
+    choice_bits = {}
+    for first, (names, width) in groups.items():
+        for step in range(width):
+            choice_bits[first + step] = width - 1 - step
     id_terms, rate_terms, jitter_terms, paths, unique_count, level_rows = delay_plan(
-        sub_dev, held, tm_bits, freq_bits, shared, all_trials
+        sub_dev, held, tm_bits, freq_bits, shared, all_trials, choice_bits
     )
     factors = jnp.concatenate(
         [jnp.ones((1,), jnp.int32),
@@ -185,6 +204,28 @@
     level = 0
     for bit_index in range(freq_bits):
         need_now = sub_dev * 2 ** (bit_index + 1) - 1
+        if bit_index in groups:
+            names, width = groups[bit_index]
+            spread = jnp.broadcast_to(trial_rows[None], (2**width,) + trial_rows.shape)
+            peers = lax.all_to_all(spread, names, 0, 0, tiled=True)
+            sets = [peers[index] for index in range(2**width)]
+            for step in range(width):
+                need_now = sub_dev * 2 ** (bit_index + step + 1) - 1
+                if bit_index + step >= freq_bits - shared:
+                    sets = [jnp.repeat(one, 2, axis=0) for one in sets]
+                rows = sets[0].shape[0]
+                merged = merge_rows(
+                    jnp.concatenate(sets[0::2], axis=0),
+                    zero_front(jnp.concatenate(sets[1::2], axis=0), need_now),
+                    level_shifts[level],
+                    need_now,
+                )
+                sets = [merged[index * rows : (index + 1) * rows] for index in range(len(sets) // 2)]
+                level = level + 1
+            trial_rows = sets[0]
+            continue
+        if any(0 < bit_index - first < groups[first][1] for first in groups):
+            continue
         if bit_index == freq_bits - 1 and shared >= 3 and bit_index >= 2:
             partner = paired(trial_rows, freq_axis, near_half(bit_index, bit_index - 2))
         else:
@@ -211,7 +252,12 @@
     best = jnp.stack(peak_rows).reshape(WIDTHS, tm_count, span_time)
     best = jnp.max(lax.all_to_all(best, "tm", 1, 1, tiled=True), axis=1)
     for bit_index in range(freq_bits - shared):
-        if bit_index == 1 and "zl" in freq_axis:
+        if bit_index == 1 and "zl" in freq_axis and freq_bits - shared >= 4:
+            spread = jnp.broadcast_to(best[None], (8,) + best.shape)
+            best = jnp.max(lax.all_to_all(spread, ("zh", "zl"), 0, 0, tiled=True), axis=0)
+        elif bit_index in (2, 3) and "zl" in freq_axis and freq_bits - shared >= 4:
+            continue
+        elif bit_index == 1 and "zl" in freq_axis:
             spread = jnp.broadcast_to(best[None], (4,) + best.shape)
             best = jnp.max(lax.all_to_all(spread, "zl", 0, 0, tiled=True), axis=0)
         elif bit_index == 2 and "zl" in freq_axis:
@@ -225,14 +271,15 @@
 
 def solution(mesh):
     count = mesh.shape["freq"]
-    if count % 16 == 0:
-        fine = jax.sharding.Mesh(
-            mesh.devices.reshape(count // 16, 2, 4, 2, mesh.shape["tm"]), FINE_AXES + ("tm",)
-        )
-        freq_axis = FINE_AXES
+    if count == 128:
+        freq_axis, sizes = ("yh", "yl", "zh", "zl", "fc"), (2, 4, 2, 4, 2)
+    elif count == 16:
+        freq_axis, sizes = ("zh", "zl", "fc"), (2, 4, 2)
     else:
-        fine = mesh
-        freq_axis = ("freq",)
+        freq_axis, sizes = ("freq",), (count,)
+    fine = jax.sharding.Mesh(
+        mesh.devices.reshape(sizes + (mesh.shape["tm"],)), freq_axis + ("tm",)
+    )
     placed = (P(freq_axis, "tm"), P(), P())
     return jax.shard_map(
         functools.partial(shards, freq_axis), mesh=fine, in_specs=placed,

time: 107 us -> 98.9 us (0.924)
  the two profiles are of different devices: /device:TPU:16 before, /device:TPU:9 now
where the time goes in v13:
time: 98.9 us; the launch traced here: 98.4 us
  starting transfers between devices  34.8 us (35%)
  waiting for transfers between devices  25 us (25%)
  blocking collectives  22 us (22%)
  other arithmetic  12.1 us (12%)
  local copies, waits for them, and re-layouts  3.5 us (4%)
    all_to_all x2, waiting for transfers between devices, shards(): peers = lax.all_to_all(spread, names, 0, 0, tiled=True)  15.3 us
    all_to_all x2, starting transfers between devices, shards(): peers = lax.all_to_all(spread, names, 0, 0, tiled=True)  14.8 us
    all_to_all x1, blocking collectives, shards(): lax.all_to_all(spread, ('zh', 'zl'), 0, 0, tiled=True)  14.8 us
    ppermute x2, starting transfers between devices, swapped(): return lax.ppermute(block, axis, route)  11.3 us
    all_to_all x1, blocking collectives, shards(): best = jnp.max(lax.all_to_all(best, 'tm', 1, 1, tiled=True), axis=1)  7.21 us
    select_n x49, other arithmetic, merge_rows(): jnp.where(selected, moved[:, step_size:], moved[:, :cols - step_size])  5.57 us
    ppermute x1, starting transfers between devices, paired(): lax.ppermute(block, axis, [(partner_of(i), i) for i in range(lax.axis_siz...  4.71 us
    ppermute x1, waiting for transfers between devices, paired(): lax.ppermute(block, axis, [(partner_of(i), i) for i in range(lax.axis_siz...  4.42 us
  transfers between devices with their start and end apart: 6, of which 6 were waited for; matrix products, arithmetic and copies ran while one was open for 1% of the time, Pallas kernels for 0%

profile of v13, /device:TPU:9, one launch (start us, length us, event | category | flops | bytes accessed | tf_op | source)
XLA Modules:
  0.0 98.4 jit_solution(16735070038771698483)
XLA Ops:
  0.0 1.2 %convert_reduce_fusion = f32[16,512]{1,0:T(8,128)S(1)} fusion(bf16[512,512]{1,0:T(8,128)(2,1)} %param.7), kind=kLoop, calls=%fused_computation.6 | loop fusion | flops 516096 | bytes 557056 | tf_op jit(solution)/shard_map/reduce_sum | solution.py:196
  1.3 0.6 broadcast_in_dim.628
  1.9 4.0 %all-to-all-start = ((f32[4,16,512]{2,1,0:T(8,128)}), f32[4,16,512]{2,1,0:T(8,128)S(1)}, u32[]{:S(2)}, u32[]{:S(2)}) async-start(f32[4,16,512]{2,1,0:T(8,128)} %broadcast_in_dim.628), calls=%async_computation | async-start | bytes 262144 | tf_op jit(solution)/shard_map/all_to_all | solution.py:198
  6.1 0.3 select_reduce_fusion.1
  6.4 0.4 select_reduce_fusion
  7.0 3.7 %all-to-all-done = f32[4,16,512]{2,1,0:T(8,128)S(1)} async-done(((f32[4,16,512]{2,1,0:T(8,128)}), f32[4,16,512]{2,1,0:T(8,128)S(1)}, u32[]{:S(2)}, u32[]{:S(2)}) %all-to-all-start) | async-done | bytes 131104 | tf_op jit(solution)/shard_map/all_to_all | solution.py:198
  10.8 0.4 slice_select_fusion.3
  11.2 0.2 slice_select_fusion.2
  11.4 0.2 slice_select_fusion.1
  11.6 0.2 slice_select_fusion
  11.8 0.2 bitcast_reduce_fusion
  12.1 4.0 %collective-permute-start = (f32[4,2048]{1,0:T(4,128)S(1)}, f32[4,2048]{1,0:T(4,128)S(1)}, u32[]{:S(2)}, u32[]{:S(2)}) collective-permute-start(f32[4,2048]{1,0:T(4,128)S(1)} %bitcast_reduce_fusion), channel_id=1, source_target_pairs={{0,4},{4,0},{8,12},{12,8},{16,20},{20,16},{24,28},{28,24},{32,36},... | collective-permute-start | bytes 98312 | tf_op jit(solution)/shard_map/ppermute | solution.py:24
  16.2 0.7 collective-permute-done
  17.5 0.7 broadcast_in_dim.634
  18.2 10.0 %all-to-all-start.1 = ((f32[8,4,2048]{2,1,0:T(4,128)}), f32[8,4,2048]{2,1,0:T(4,128)S(1)}, u32[]{:S(2)}, u32[]{:S(2)}) async-start(f32[8,4,2048]{2,1,0:T(4,128)} %broadcast_in_dim.634), calls=%async_computation.1 | async-start | bytes 524288 | tf_op jit(solution)/shard_map/all_to_all | solution.py:210
  28.5 11.0 %all-to-all-done.1 = f32[8,4,2048]{2,1,0:T(4,128)S(1)} async-done(((f32[8,4,2048]{2,1,0:T(4,128)}), f32[8,4,2048]{2,1,0:T(4,128)S(1)}, u32[]{:S(2)}, u32[]{:S(2)}) %all-to-all-start.1) | async-done | bytes 262176 | tf_op jit(solution)/shard_map/all_to_all | solution.py:210
  41.8 0.7 broadcast_in_dim.656
  42.5 4.8 %all-to-all-start.2 = ((f32[4,4,2048]{2,1,0:T(4,128)}), f32[4,4,2048]{2,1,0:T(4,128)S(1)}, u32[]{:S(2)}, u32[]{:S(2)}) async-start(f32[4,4,2048]{2,1,0:T(4,128)} %broadcast_in_dim.656), calls=%async_computation.2 | async-start | bytes 262144 | tf_op jit(solution)/shard_map/all_to_all | solution.py:210
  47.3 4.3 %all-to-all-done.2 = f32[4,4,2048]{2,1,0:T(4,128)S(1)} async-done(((f32[4,4,2048]{2,1,0:T(4,128)}), f32[4,4,2048]{2,1,0:T(4,128)S(1)}, u32[]{:S(2)}, u32[]{:S(2)}) %all-to-all-start.2) | async-done | bytes 131104 | tf_op jit(solution)/shard_map/all_to_all | solution.py:210
  54.5 4.7 %collective-permute-start.1 = (f32[16,2048]{1,0:T(8,128)S(1)}, f32[16,2048]{1,0:T(8,128)S(1)}, u32[]{:S(2)}, u32[]{:S(2)}) collective-permute-start(f32[16,2048]{1,0:T(8,128)S(1)} %fusion.16), channel_id=1, source_target_pairs={{384,0},{388,4},{392,8},{396,12},{400,16},{404,20},{408,24},{412,2... | collective-permute-start | bytes 393224 | tf_op jit(solution)/shard_map/ppermute | solution.py:28
  59.3 4.4 %collective-permute-done.1 = f32[16,2048]{1,0:T(8,128)S(1)} collective-permute-done((f32[16,2048]{1,0:T(8,128)S(1)}, f32[16,2048]{1,0:T(8,128)S(1)}, u32[]{:S(2)}, u32[]{:S(2)}) %collective-permute-start.1) | collective-permute-done | bytes 131104 | tf_op jit(solution)/shard_map/ppermute | solution.py:28
  64.4 0.2 fusion.3
  64.6 0.2 slice_select_fusion.8
  64.8 0.2 slice_select_fusion.7
  65.0 0.2 slice_select_fusion.6
  65.2 0.2 slice_select_fusion.5
  65.4 0.2 slice_select_fusion.4
  67.6 7.2 %all_to_all.25 = f32[9,4,512]{2,0,1:T(8,128)S(1)} all-to-all(f32[9,4,512]{2,0,1:T(8,128)S(1)} %stack.5), channel_id=1, replica_groups=mesh['yh'=2,'yl'=4,'zh'=2,'zl'=4,'fc'=2,'tm'=4] {'tm'}, dimensions={1} | all-to-all | bytes 147456 | tf_op jit(solution)/shard_map/all_to_all | solution.py:253
  74.8 7.3 %collective-permute-start.2 = (f32[9,512]{1,0:T(8,128)S(1)}, f32[9,512]{1,0:T(8,128)S(1)}, u32[]{:S(2)}, u32[]{:S(2)}) collective-permute-start(f32[9,512]{1,0:T(8,128)S(1)} %reduce_max.108), channel_id=1, source_target_pairs={{0,4},{4,0},{8,12},{12,8},{16,20},{20,16},{24,28},{28,24},{32,36},... | collective-permute-start | bytes 55304 | tf_op jit(solution)/shard_map/ppermute | solution.py:24
  82.1 0.8 collective-permute-done.2
  83.0 14.8 %all_to_all.26 = f32[8,9,512]{2,1,0:T(8,128)S(1)} all-to-all(f32[8,9,512]{2,1,0:T(8,128)S(1)} %broadcast_in_dim.695), channel_id=1, replica_groups=mesh['yh'=2,'yl'=4,'zh'=2,'zl'=4,'fc'=2,'tm'=4] {'zh','zl'}, dimensions={0} | all-to-all | bytes 294912 | tf_op jit(solution)/shard_map/all_to_all | solution.py:257
  97.7 0.6 reduce_max.109
  (120 shorter events, 8.8 us)
Async XLA Ops:
  0.0 6.0 %copy-start.2 = (s32[10,116]{1,0:T(8,128)S(1)}, s32[10,116]{1,0:T(8,128)}, u32[]{:S(2)}) copy-start(s32[10,116]{1,0:T(8,128)} %constant.84.clone) | copy-start | bytes 13924
  0.0 6.0 %copy-start.3 = (s32[10,116]{1,0:T(8,128)S(1)}, s32[10,116]{1,0:T(8,128)}, u32[]{:S(2)}) copy-start(s32[10,116]{1,0:T(8,128)} %constant.83.clone) | copy-start | bytes 13924
  0.0 6.0 %copy-start.4 = (s32[10,116]{1,0:T(8,128)S(1)}, s32[10,116]{1,0:T(8,128)}, u32[]{:S(2)}) copy-start(s32[10,116]{1,0:T(8,128)} %constant.82.clone) | copy-start | bytes 13924
  0.0 6.8 %copy-start.5 = (f32[64,20]{1,0:T(8,128)S(1)}, f32[64,20]{1,0:T(8,128)}, u32[]{:S(2)}) copy-start(f32[64,20]{1,0:T(8,128)} %constant.85.clone) | copy-start | bytes 15364
  0.0 6.1 %copy-start.1 = (s32[2047]{0:T(1024)S(1)}, s32[2047]{0:T(1024)}, u32[]{:S(2)}) copy-start(s32[2047]{0:T(1024)} %param.8) | copy-start | bytes 24568
  0.0 6.4 %copy-start = (s32[4094]{0:T(1024)S(1)}, s32[4094]{0:T(1024)}, u32[]{:S(2)}) copy-start(s32[4094]{0:T(1024)} %param.9) | copy-start | bytes 49132
  1.9 8.8 %all-to-all-start = ((f32[4,16,512]{2,1,0:T(8,128)}), f32[4,16,512]{2,1,0:T(8,128)S(1)}, u32[]{:S(2)}, u32[]{:S(2)}) async-start(f32[4,16,512]{2,1,0:T(8,128)} %broadcast_in_dim.628), calls=%async_computation | async-start | bytes 262144 | tf_op jit(solution)/shard_map/all_to_all | solution.py:198
  12.1 4.9 %collective-permute-start = (f32[4,2048]{1,0:T(4,128)S(1)}, f32[4,2048]{1,0:T(4,128)S(1)}, u32[]{:S(2)}, u32[]{:S(2)}) collective-permute-start(f32[4,2048]{1,0:T(4,128)S(1)} %bitcast_reduce_fusion), channel_id=1, source_target_pairs={{0,4},{4,0},{8,12},{12,8},{16,20},{20,16},{24,28},{28,24},{32,36},... | collective-permute-start | bytes 98312 | tf_op jit(solution)/shard_map/ppermute | solution.py:24
  18.2 21.3 %all-to-all-start.1 = ((f32[8,4,2048]{2,1,0:T(4,128)}), f32[8,4,2048]{2,1,0:T(4,128)S(1)}, u32[]{:S(2)}, u32[]{:S(2)}) async-start(f32[8,4,2048]{2,1,0:T(4,128)} %broadcast_in_dim.634), calls=%async_computation.1 | async-start | bytes 524288 | tf_op jit(solution)/shard_map/all_to_all | solution.py:210
  42.5 9.1 %all-to-all-start.2 = ((f32[4,4,2048]{2,1,0:T(4,128)}), f32[4,4,2048]{2,1,0:T(4,128)S(1)}, u32[]{:S(2)}, u32[]{:S(2)}) async-start(f32[4,4,2048]{2,1,0:T(4,128)} %broadcast_in_dim.656), calls=%async_computation.2 | async-start | bytes 262144 | tf_op jit(solution)/shard_map/all_to_all | solution.py:210
  54.5 9.2 %collective-permute-start.1 = (f32[16,2048]{1,0:T(8,128)S(1)}, f32[16,2048]{1,0:T(8,128)S(1)}, u32[]{:S(2)}, u32[]{:S(2)}) collective-permute-start(f32[16,2048]{1,0:T(8,128)S(1)} %fusion.16), channel_id=1, source_target_pairs={{384,0},{388,4},{392,8},{396,12},{400,16},{404,20},{408,24},{412,2... | collective-permute-start | bytes 393224 | tf_op jit(solution)/shard_map/ppermute | solution.py:28
  74.8 8.1 %collective-permute-start.2 = (f32[9,512]{1,0:T(8,128)S(1)}, f32[9,512]{1,0:T(8,128)S(1)}, u32[]{:S(2)}, u32[]{:S(2)}) collective-permute-start(f32[9,512]{1,0:T(8,128)S(1)} %reduce_max.108), channel_id=1, source_target_pairs={{0,4},{4,0},{8,12},{12,8},{16,20},{20,16},{24,28},{28,24},{32,36},... | collective-permute-start | bytes 55304 | tf_op jit(solution)/shard_map/ppermute | solution.py:24

commit v14 on v13

--- a/solution.py
+++ b/solution.py
@@ -162,7 +162,7 @@
 
     tm_bits = tm_count.bit_length() - 1
     groups = {}
-    for first, names in ((1, ("zh", "zl")), (4, ("yl",))):
+    for first, names in ((1, ("zh", "zl")), (4, ("yh", "yl"))):
         width = sum(FINE_BITS[name] for name in names)
         redundant = {first + step >= freq_bits - shared for step in range(width)}
         if all(name in freq_axis for name in names) and len(redundant) == 1:

time: 98.9 us -> 98.6 us (level)
  the two profiles are of different devices: /device:TPU:9 before, /device:TPU:1 now
where the time goes in v14:
time: 98.6 us; the launch traced here: 98 us
  starting transfers between devices  32.3 us (33%)
  waiting for transfers between devices  25.4 us (26%)
  blocking collectives  22 us (22%)
  other arithmetic  13.1 us (13%)
  local copies, waits for them, and re-layouts  4.17 us (4%)
    all_to_all x2, waiting for transfers between devices, shards(): peers = lax.all_to_all(spread, names, 0, 0, tiled=True)  20.2 us
    ppermute x2, starting transfers between devices, swapped(): return lax.ppermute(block, axis, route)  15 us
    all_to_all x1, blocking collectives, shards(): lax.all_to_all(spread, ('zh', 'zl'), 0, 0, tiled=True)  14.8 us
    all_to_all x2, starting transfers between devices, shards(): peers = lax.all_to_all(spread, names, 0, 0, tiled=True)  12.5 us
    all_to_all x1, blocking collectives, shards(): best = jnp.max(lax.all_to_all(best, 'tm', 1, 1, tiled=True), axis=1)  7.21 us
    select_n x49, other arithmetic, merge_rows(): jnp.where(selected, moved[:, step_size:], moved[:, :cols - step_size])  6.3 us
    all_to_all x1, starting transfers between devices, shards(): gathered = lax.all_to_all(spread, 'tm', 0, 0, tiled=True)  4.83 us
    all_to_all x1, waiting for transfers between devices, shards(): gathered = lax.all_to_all(spread, 'tm', 0, 0, tiled=True)  3.62 us
  transfers between devices with their start and end apart: 5, of which 5 were waited for; matrix products, arithmetic and copies ran while one was open for 2% of the time, Pallas kernels for 0%

profile of v14, /device:TPU:1, one launch (start us, length us, event | category | flops | bytes accessed | tf_op | source)
XLA Modules:
  0.0 98.0 jit_solution(18105875901406883069)
XLA Ops:
  0.0 1.2 %convert_reduce_fusion = f32[16,512]{1,0:T(8,128)S(1)} fusion(bf16[512,512]{1,0:T(8,128)(2,1)} %param.7), kind=kLoop, calls=%fused_computation.8 | loop fusion | flops 516096 | bytes 557056 | tf_op jit(solution)/shard_map/reduce_sum | solution.py:196
  1.3 0.6 broadcast_in_dim.646
  1.9 4.8 %all-to-all-start = ((f32[4,16,512]{2,1,0:T(8,128)}), f32[4,16,512]{2,1,0:T(8,128)S(1)}, u32[]{:S(2)}, u32[]{:S(2)}) async-start(f32[4,16,512]{2,1,0:T(8,128)} %broadcast_in_dim.646), calls=%async_computation | async-start | bytes 262144 | tf_op jit(solution)/shard_map/all_to_all | solution.py:198
  6.9 0.3 select_reduce_fusion.1
  7.3 0.5 select_reduce_fusion
  7.9 3.6 %all-to-all-done = f32[4,16,512]{2,1,0:T(8,128)S(1)} async-done(((f32[4,16,512]{2,1,0:T(8,128)}), f32[4,16,512]{2,1,0:T(8,128)S(1)}, u32[]{:S(2)}, u32[]{:S(2)}) %all-to-all-start) | async-done | bytes 131104 | tf_op jit(solution)/shard_map/all_to_all | solution.py:198
  11.6 0.4 slice_select_fusion.3
  12.0 0.2 slice_select_fusion.2
  12.2 0.2 slice_select_fusion.1
  12.4 0.2 slice_select_fusion
  12.7 0.2 bitcast_reduce_fusion
  12.9 8.4 %collective-permute-start = (f32[4,2048]{1,0:T(4,128)S(1)}, f32[4,2048]{1,0:T(4,128)S(1)}, u32[]{:S(2)}, u32[]{:S(2)}) collective-permute-start(f32[4,2048]{1,0:T(4,128)S(1)} %bitcast_reduce_fusion), channel_id=1, source_target_pairs={{0,4},{4,0},{8,12},{12,8},{16,20},{20,16},{24,28},{28,24},{32,36},... | collective-permute-start | bytes 98312 | tf_op jit(solution)/shard_map/ppermute | solution.py:24
  21.4 0.7 collective-permute-done
  22.6 0.7 broadcast_in_dim.652
  23.3 5.7 %all-to-all-start.1 = ((f32[8,4,2048]{2,1,0:T(4,128)}), f32[8,4,2048]{2,1,0:T(4,128)S(1)}, u32[]{:S(2)}, u32[]{:S(2)}) async-start(f32[8,4,2048]{2,1,0:T(4,128)} %broadcast_in_dim.652), calls=%async_computation.1 | async-start | bytes 524288 | tf_op jit(solution)/shard_map/all_to_all | solution.py:210
  29.2 11.1 %all-to-all-done.1 = f32[8,4,2048]{2,1,0:T(4,128)S(1)} async-done(((f32[8,4,2048]{2,1,0:T(4,128)}), f32[8,4,2048]{2,1,0:T(4,128)S(1)}, u32[]{:S(2)}, u32[]{:S(2)}) %all-to-all-start.1) | async-done | bytes 262176 | tf_op jit(solution)/shard_map/all_to_all | solution.py:210
  42.7 0.7 broadcast_in_dim.674
  43.4 6.8 %all-to-all-start.2 = ((f32[8,4,2048]{2,1,0:T(4,128)}), f32[8,4,2048]{2,1,0:T(4,128)S(1)}, u32[]{:S(2)}, u32[]{:S(2)}) async-start(f32[8,4,2048]{2,1,0:T(4,128)} %broadcast_in_dim.674), calls=%async_computation.2 | async-start | bytes 524288 | tf_op jit(solution)/shard_map/all_to_all | solution.py:210
  50.4 9.1 %all-to-all-done.2 = f32[8,4,2048]{2,1,0:T(4,128)S(1)} async-done(((f32[8,4,2048]{2,1,0:T(4,128)}), f32[8,4,2048]{2,1,0:T(4,128)S(1)}, u32[]{:S(2)}, u32[]{:S(2)}) %all-to-all-start.2) | async-done | bytes 262176 | tf_op jit(solution)/shard_map/all_to_all | solution.py:210
  64.5 0.2 reshape.311
  64.7 0.2 fusion.3
  64.9 0.2 slice_select_fusion.8
  65.1 0.2 slice_select_fusion.7
  65.3 0.2 slice_select_fusion.6
  65.5 0.2 slice_select_fusion.5
  65.7 0.2 slice_select_fusion.4
  65.9 0.2 slice_select_fusion.10
  67.9 7.2 %all_to_all.25 = f32[9,4,512]{2,0,1:T(8,128)S(1)} all-to-all(f32[9,4,512]{2,0,1:T(8,128)S(1)} %stack.5), channel_id=1, replica_groups=mesh['yh'=2,'yl'=4,'zh'=2,'zl'=4,'fc'=2,'tm'=4] {'tm'}, dimensions={1} | all-to-all | bytes 147456 | tf_op jit(solution)/shard_map/all_to_all | solution.py:253
  75.1 6.6 %collective-permute-start.1 = (f32[9,512]{1,0:T(8,128)S(1)}, f32[9,512]{1,0:T(8,128)S(1)}, u32[]{:S(2)}, u32[]{:S(2)}) collective-permute-start(f32[9,512]{1,0:T(8,128)S(1)} %reduce_max.108), channel_id=1, source_target_pairs={{0,4},{4,0},{8,12},{12,8},{16,20},{20,16},{24,28},{28,24},{32,36},... | collective-permute-start | bytes 55304 | tf_op jit(solution)/shard_map/ppermute | solution.py:24
  81.7 0.8 collective-permute-done.1
  82.6 14.8 %all_to_all.26 = f32[8,9,512]{2,1,0:T(8,128)S(1)} all-to-all(f32[8,9,512]{2,1,0:T(8,128)S(1)} %broadcast_in_dim.719), channel_id=1, replica_groups=mesh['yh'=2,'yl'=4,'zh'=2,'zl'=4,'fc'=2,'tm'=4] {'zh','zl'}, dimensions={0} | all-to-all | bytes 294912 | tf_op jit(solution)/shard_map/all_to_all | solution.py:257
  97.4 0.6 reduce_max.109
  (131 shorter events, 9.9 us)
Async XLA Ops:
  0.0 6.8 %copy-start = (s32[10,148]{1,0:T(8,128)S(1)}, s32[10,148]{1,0:T(8,128)}, u32[]{:S(2)}) copy-start(s32[10,148]{1,0:T(8,128)} %constant.33.clone) | copy-start | bytes 17764
  0.0 6.8 %copy-start.1 = (s32[10,148]{1,0:T(8,128)S(1)}, s32[10,148]{1,0:T(8,128)}, u32[]{:S(2)}) copy-start(s32[10,148]{1,0:T(8,128)} %constant.83.clone) | copy-start | bytes 17764
  0.0 6.8 %copy-start.2 = (s32[10,148]{1,0:T(8,128)S(1)}, s32[10,148]{1,0:T(8,128)}, u32[]{:S(2)}) copy-start(s32[10,148]{1,0:T(8,128)} %constant.82.clone) | copy-start | bytes 17764
  0.0 7.7 %copy-start.5 = (f32[64,20]{1,0:T(8,128)S(1)}, f32[64,20]{1,0:T(8,128)}, u32[]{:S(2)}) copy-start(f32[64,20]{1,0:T(8,128)} %constant.34.clone) | copy-start | bytes 15364
  0.0 6.9 %copy-start.4 = (s32[2047]{0:T(1024)S(1)}, s32[2047]{0:T(1024)}, u32[]{:S(2)}) copy-start(s32[2047]{0:T(1024)} %param.8) | copy-start | bytes 24568
  0.0 7.2 %copy-start.3 = (s32[4094]{0:T(1024)S(1)}, s32[4094]{0:T(1024)}, u32[]{:S(2)}) copy-start(s32[4094]{0:T(1024)} %param.9) | copy-start | bytes 49132
  1.9 9.7 %all-to-all-start = ((f32[4,16,512]{2,1,0:T(8,128)}), f32[4,16,512]{2,1,0:T(8,128)S(1)}, u32[]{:S(2)}, u32[]{:S(2)}) async-start(f32[4,16,512]{2,1,0:T(8,128)} %broadcast_in_dim.646), calls=%async_computation | async-start | bytes 262144 | tf_op jit(solution)/shard_map/all_to_all | solution.py:198
  12.9 9.2 %collective-permute-start = (f32[4,2048]{1,0:T(4,128)S(1)}, f32[4,2048]{1,0:T(4,128)S(1)}, u32[]{:S(2)}, u32[]{:S(2)}) collective-permute-start(f32[4,2048]{1,0:T(4,128)S(1)} %bitcast_reduce_fusion), channel_id=1, source_target_pairs={{0,4},{4,0},{8,12},{12,8},{16,20},{20,16},{24,28},{28,24},{32,36},... | collective-permute-start | bytes 98312 | tf_op jit(solution)/shard_map/ppermute | solution.py:24
  23.3 16.9 %all-to-all-start.1 = ((f32[8,4,2048]{2,1,0:T(4,128)}), f32[8,4,2048]{2,1,0:T(4,128)S(1)}, u32[]{:S(2)}, u32[]{:S(2)}) async-start(f32[8,4,2048]{2,1,0:T(4,128)} %broadcast_in_dim.652), calls=%async_computation.1 | async-start | bytes 524288 | tf_op jit(solution)/shard_map/all_to_all | solution.py:210
  43.4 16.1 %all-to-all-start.2 = ((f32[8,4,2048]{2,1,0:T(4,128)}), f32[8,4,2048]{2,1,0:T(4,128)S(1)}, u32[]{:S(2)}, u32[]{:S(2)}) async-start(f32[8,4,2048]{2,1,0:T(4,128)} %broadcast_in_dim.674), calls=%async_computation.2 | async-start | bytes 524288 | tf_op jit(solution)/shard_map/all_to_all | solution.py:210
  75.1 7.5 %collective-permute-start.1 = (f32[9,512]{1,0:T(8,128)S(1)}, f32[9,512]{1,0:T(8,128)S(1)}, u32[]{:S(2)}, u32[]{:S(2)}) collective-permute-start(f32[9,512]{1,0:T(8,128)S(1)} %reduce_max.108), channel_id=1, source_target_pairs={{0,4},{4,0},{8,12},{12,8},{16,20},{20,16},{24,28},{28,24},{32,36},... | collective-permute-start | bytes 55304 | tf_op jit(solution)/shard_map/ppermute | solution.py:24

commit v15 on v13

--- a/solution.py
+++ b/solution.py
@@ -250,12 +250,15 @@
             window_sum = window_sum + zero_front(window_sum, width_now)[:, :full_time]
             width_now = width_now * 2
     best = jnp.stack(peak_rows).reshape(WIDTHS, tm_count, span_time)
-    best = jnp.max(lax.all_to_all(best, "tm", 1, 1, tiled=True), axis=1)
+    joint = "zl" in freq_axis and freq_bits - shared >= 4
+    if joint:
+        blocks = jnp.transpose(best, (1, 0, 2))
+        spread = jnp.broadcast_to(blocks[None], (8,) + blocks.shape).reshape((-1,) + blocks.shape[1:])
+        best = jnp.max(lax.all_to_all(spread, ("zh", "zl", "tm"), 0, 0, tiled=True), axis=0)
+    else:
+        best = jnp.max(lax.all_to_all(best, "tm", 1, 1, tiled=True), axis=1)
     for bit_index in range(freq_bits - shared):
-        if bit_index == 1 and "zl" in freq_axis and freq_bits - shared >= 4:
-            spread = jnp.broadcast_to(best[None], (8,) + best.shape)
-            best = jnp.max(lax.all_to_all(spread, ("zh", "zl"), 0, 0, tiled=True), axis=0)
-        elif bit_index in (2, 3) and "zl" in freq_axis and freq_bits - shared >= 4:
+        if bit_index in (1, 2, 3) and joint:
             continue
         elif bit_index == 1 and "zl" in freq_axis:
             spread = jnp.broadcast_to(best[None], (4,) + best.shape)

time: 98.9 us -> 105 us (1.062)
  the two profiles are of different devices: /device:TPU:9 before, /device:TPU:43 now
where the time goes in v15:
time: 105 us
  blocking collectives  31.8 us (30%)
  starting transfers between devices  29.7 us (28%)
  waiting for transfers between devices  26.6 us (25%)
  other arithmetic  12.2 us (12%)
  local copies, waits for them, and re-layouts  3.6 us (3%)
    all_to_all x1, blocking collectives, shards(): lax.all_to_all(spread, ('zh', 'zl', 'tm'), 0, 0, tiled=True)  31.8 us
    all_to_all x2, waiting for transfers between devices, shards(): peers = lax.all_to_all(spread, names, 0, 0, tiled=True)  15.3 us
    all_to_all x2, starting transfers between devices, shards(): peers = lax.all_to_all(spread, names, 0, 0, tiled=True)  14.4 us
    ppermute x2, starting transfers between devices, swapped(): return lax.ppermute(block, axis, route)  9.07 us
    ppermute x1, waiting for transfers between devices, paired(): lax.ppermute(block, axis, [(partner_of(i), i) for i in range(lax.axis_siz...  7.21 us
    select_n x49, other arithmetic, merge_rows(): jnp.where(selected, moved[:, step_size:], moved[:, :cols - step_size])  5.57 us
    all_to_all x1, starting transfers between devices, shards(): gathered = lax.all_to_all(spread, 'tm', 0, 0, tiled=True)  4.26 us
    all_to_all x1, waiting for transfers between devices, shards(): gathered = lax.all_to_all(spread, 'tm', 0, 0, tiled=True)  2.54 us
  transfers between devices with their start and end apart: 6, of which 6 were waited for; matrix products, arithmetic and copies ran while one was open for 1% of the time, Pallas kernels for 0%

profile of v15, /device:TPU:43, one launch (start us, length us, event | category | flops | bytes accessed | tf_op | source)
XLA Modules:
  0.0 104.8 jit_solution(9072626928419441491)
XLA Ops:
  0.0 1.2 %convert_reduce_fusion = f32[16,512]{1,0:T(8,128)S(1)} fusion(bf16[512,512]{1,0:T(8,128)(2,1)} %param.7), kind=kLoop, calls=%fused_computation.6 | loop fusion | flops 516096 | bytes 557056 | tf_op jit(solution)/shard_map/reduce_sum | solution.py:196
  1.3 0.6 broadcast_in_dim.628
  1.9 4.3 %all-to-all-start = ((f32[4,16,512]{2,1,0:T(8,128)}), f32[4,16,512]{2,1,0:T(8,128)S(1)}, u32[]{:S(2)}, u32[]{:S(2)}) async-start(f32[4,16,512]{2,1,0:T(8,128)} %broadcast_in_dim.628), calls=%async_computation | async-start | bytes 262144 | tf_op jit(solution)/shard_map/all_to_all | solution.py:198
  6.4 0.3 select_reduce_fusion.1
  6.7 0.4 select_reduce_fusion
  7.3 2.5 %all-to-all-done = f32[4,16,512]{2,1,0:T(8,128)S(1)} async-done(((f32[4,16,512]{2,1,0:T(8,128)}), f32[4,16,512]{2,1,0:T(8,128)S(1)}, u32[]{:S(2)}, u32[]{:S(2)}) %all-to-all-start) | async-done | bytes 131104 | tf_op jit(solution)/shard_map/all_to_all | solution.py:198
  9.9 0.4 slice_select_fusion.3
  10.2 0.2 slice_select_fusion.2
  10.5 0.2 slice_select_fusion.1
  10.7 0.2 slice_select_fusion
  10.9 0.2 bitcast_reduce_fusion
  11.2 4.0 %collective-permute-start = (f32[4,2048]{1,0:T(4,128)S(1)}, f32[4,2048]{1,0:T(4,128)S(1)}, u32[]{:S(2)}, u32[]{:S(2)}) collective-permute-start(f32[4,2048]{1,0:T(4,128)S(1)} %bitcast_reduce_fusion), channel_id=1, source_target_pairs={{0,4},{4,0},{8,12},{12,8},{16,20},{20,16},{24,28},{28,24},{32,36},... | collective-permute-start | bytes 98312 | tf_op jit(solution)/shard_map/ppermute | solution.py:24
  15.3 0.7 collective-permute-done
  16.5 0.7 broadcast_in_dim.634
  17.3 10.0 %all-to-all-start.1 = ((f32[8,4,2048]{2,1,0:T(4,128)}), f32[8,4,2048]{2,1,0:T(4,128)S(1)}, u32[]{:S(2)}, u32[]{:S(2)}) async-start(f32[8,4,2048]{2,1,0:T(4,128)} %broadcast_in_dim.634), calls=%async_computation.1 | async-start | bytes 524288 | tf_op jit(solution)/shard_map/all_to_all | solution.py:210
  27.5 11.0 %all-to-all-done.1 = f32[8,4,2048]{2,1,0:T(4,128)S(1)} async-done(((f32[8,4,2048]{2,1,0:T(4,128)}), f32[8,4,2048]{2,1,0:T(4,128)S(1)}, u32[]{:S(2)}, u32[]{:S(2)}) %all-to-all-start.1) | async-done | bytes 262176 | tf_op jit(solution)/shard_map/all_to_all | solution.py:210
  40.9 0.7 broadcast_in_dim.656
  41.6 4.4 %all-to-all-start.2 = ((f32[4,4,2048]{2,1,0:T(4,128)}), f32[4,4,2048]{2,1,0:T(4,128)S(1)}, u32[]{:S(2)}, u32[]{:S(2)}) async-start(f32[4,4,2048]{2,1,0:T(4,128)} %broadcast_in_dim.656), calls=%async_computation.2 | async-start | bytes 262144 | tf_op jit(solution)/shard_map/all_to_all | solution.py:210
  45.9 4.3 %all-to-all-done.2 = f32[4,4,2048]{2,1,0:T(4,128)S(1)} async-done(((f32[4,4,2048]{2,1,0:T(4,128)}), f32[4,4,2048]{2,1,0:T(4,128)S(1)}, u32[]{:S(2)}, u32[]{:S(2)}) %all-to-all-start.2) | async-done | bytes 131104 | tf_op jit(solution)/shard_map/all_to_all | solution.py:210
  53.1 1.9 %collective-permute-start.1 = (f32[16,2048]{1,0:T(8,128)S(1)}, f32[16,2048]{1,0:T(8,128)S(1)}, u32[]{:S(2)}, u32[]{:S(2)}) collective-permute-start(f32[16,2048]{1,0:T(8,128)S(1)} %fusion.16), channel_id=1, source_target_pairs={{384,0},{388,4},{392,8},{396,12},{400,16},{404,20},{408,24},{412,2... | collective-permute-start | bytes 393224 | tf_op jit(solution)/shard_map/ppermute | solution.py:28
  55.2 7.2 %collective-permute-done.1 = f32[16,2048]{1,0:T(8,128)S(1)} collective-permute-done((f32[16,2048]{1,0:T(8,128)S(1)}, f32[16,2048]{1,0:T(8,128)S(1)}, u32[]{:S(2)}, u32[]{:S(2)}) %collective-permute-start.1) | collective-permute-done | bytes 131104 | tf_op jit(solution)/shard_map/ppermute | solution.py:28
  63.0 0.2 fusion.3
  63.3 0.2 slice_select_fusion.8
  63.5 0.2 slice_select_fusion.7
  63.7 0.2 slice_select_fusion.6
  63.9 0.2 slice_select_fusion.5
  64.1 0.2 slice_select_fusion.4
  64.3 0.2 slice_select_fusion.10
  66.4 31.8 %all_to_all.20 = f32[32,9,512]{2,1,0:T(8,128)S(1)} all-to-all(f32[32,9,512]{2,1,0:T(8,128)S(1)} %bitcast.58), channel_id=1, replica_groups=mesh['yh'=2,'yl'=4,'zh'=2,'zl'=4,'fc'=2,'tm'=4] {'zh','zl','tm'}, dimensions={0} | all-to-all | bytes 1179648 | tf_op jit(solution)/shard_map/all_to_all | solution.py:257
  98.3 5.1 %collective-permute-start.2 = (f32[9,512]{1,0:T(8,128)S(1)}, f32[9,512]{1,0:T(8,128)S(1)}, u32[]{:S(2)}, u32[]{:S(2)}) collective-permute-start(f32[9,512]{1,0:T(8,128)S(1)} %reduce_max.99), channel_id=1, source_target_pairs={{0,4},{4,0},{8,12},{12,8},{16,20},{20,16},{24,28},{28,24},{32,36},... | collective-permute-start | bytes 55304 | tf_op jit(solution)/shard_map/ppermute | solution.py:24
  103.4 0.8 collective-permute-done.2
  104.2 0.6 max.3
  (118 shorter events, 8.7 us)
Async XLA Ops:
  0.0 6.3 %copy-start.2 = (s32[10,116]{1,0:T(8,128)S(1)}, s32[10,116]{1,0:T(8,128)}, u32[]{:S(2)}) copy-start(s32[10,116]{1,0:T(8,128)} %constant.84.clone) | copy-start | bytes 13924
  0.0 6.3 %copy-start.3 = (s32[10,116]{1,0:T(8,128)S(1)}, s32[10,116]{1,0:T(8,128)}, u32[]{:S(2)}) copy-start(s32[10,116]{1,0:T(8,128)} %constant.83.clone) | copy-start | bytes 13924
  0.0 6.3 %copy-start.4 = (s32[10,116]{1,0:T(8,128)S(1)}, s32[10,116]{1,0:T(8,128)}, u32[]{:S(2)}) copy-start(s32[10,116]{1,0:T(8,128)} %constant.82.clone) | copy-start | bytes 13924
  0.0 7.1 %copy-start.5 = (f32[64,20]{1,0:T(8,128)S(1)}, f32[64,20]{1,0:T(8,128)}, u32[]{:S(2)}) copy-start(f32[64,20]{1,0:T(8,128)} %constant.85.clone) | copy-start | bytes 15364
  0.0 6.3 %copy-start.1 = (s32[2047]{0:T(1024)S(1)}, s32[2047]{0:T(1024)}, u32[]{:S(2)}) copy-start(s32[2047]{0:T(1024)} %param.8) | copy-start | bytes 24568
  0.0 6.6 %copy-start = (s32[4094]{0:T(1024)S(1)}, s32[4094]{0:T(1024)}, u32[]{:S(2)}) copy-start(s32[4094]{0:T(1024)} %param.9) | copy-start | bytes 49132
  1.9 7.9 %all-to-all-start = ((f32[4,16,512]{2,1,0:T(8,128)}), f32[4,16,512]{2,1,0:T(8,128)S(1)}, u32[]{:S(2)}, u32[]{:S(2)}) async-start(f32[4,16,512]{2,1,0:T(8,128)} %broadcast_in_dim.628), calls=%async_computation | async-start | bytes 262144 | tf_op jit(solution)/shard_map/all_to_all | solution.py:198
  11.2 4.9 %collective-permute-start = (f32[4,2048]{1,0:T(4,128)S(1)}, f32[4,2048]{1,0:T(4,128)S(1)}, u32[]{:S(2)}, u32[]{:S(2)}) collective-permute-start(f32[4,2048]{1,0:T(4,128)S(1)} %bitcast_reduce_fusion), channel_id=1, source_target_pairs={{0,4},{4,0},{8,12},{12,8},{16,20},{20,16},{24,28},{28,24},{32,36},... | collective-permute-start | bytes 98312 | tf_op jit(solution)/shard_map/ppermute | solution.py:24
  17.3 21.3 %all-to-all-start.1 = ((f32[8,4,2048]{2,1,0:T(4,128)}), f32[8,4,2048]{2,1,0:T(4,128)S(1)}, u32[]{:S(2)}, u32[]{:S(2)}) async-start(f32[8,4,2048]{2,1,0:T(4,128)} %broadcast_in_dim.634), calls=%async_computation.1 | async-start | bytes 524288 | tf_op jit(solution)/shard_map/all_to_all | solution.py:210
  41.6 8.7 %all-to-all-start.2 = ((f32[4,4,2048]{2,1,0:T(4,128)}), f32[4,4,2048]{2,1,0:T(4,128)S(1)}, u32[]{:S(2)}, u32[]{:S(2)}) async-start(f32[4,4,2048]{2,1,0:T(4,128)} %broadcast_in_dim.656), calls=%async_computation.2 | async-start | bytes 262144 | tf_op jit(solution)/shard_map/all_to_all | solution.py:210
  53.1 9.2 %collective-permute-start.1 = (f32[16,2048]{1,0:T(8,128)S(1)}, f32[16,2048]{1,0:T(8,128)S(1)}, u32[]{:S(2)}, u32[]{:S(2)}) collective-permute-start(f32[16,2048]{1,0:T(8,128)S(1)} %fusion.16), channel_id=1, source_target_pairs={{384,0},{388,4},{392,8},{396,12},{400,16},{404,20},{408,24},{412,2... | collective-permute-start | bytes 393224 | tf_op jit(solution)/shard_map/ppermute | solution.py:28
  98.3 5.9 %collective-permute-start.2 = (f32[9,512]{1,0:T(8,128)S(1)}, f32[9,512]{1,0:T(8,128)S(1)}, u32[]{:S(2)}, u32[]{:S(2)}) collective-permute-start(f32[9,512]{1,0:T(8,128)S(1)} %reduce_max.99), channel_id=1, source_target_pairs={{0,4},{4,0},{8,12},{12,8},{16,20},{20,16},{24,28},{28,24},{32,36},... | collective-permute-start | bytes 55304 | tf_op jit(solution)/shard_map/ppermute | solution.py:24

commit v16 on v13

--- a/solution.py
+++ b/solution.py
@@ -252,10 +252,10 @@
     best = jnp.stack(peak_rows).reshape(WIDTHS, tm_count, span_time)
     best = jnp.max(lax.all_to_all(best, "tm", 1, 1, tiled=True), axis=1)
     for bit_index in range(freq_bits - shared):
-        if bit_index == 1 and "zl" in freq_axis and freq_bits - shared >= 4:
-            spread = jnp.broadcast_to(best[None], (8,) + best.shape)
-            best = jnp.max(lax.all_to_all(spread, ("zh", "zl"), 0, 0, tiled=True), axis=0)
-        elif bit_index in (2, 3) and "zl" in freq_axis and freq_bits - shared >= 4:
+        if bit_index == 0 and "zl" in freq_axis and freq_bits - shared >= 4:
+            spread = jnp.broadcast_to(best[None], (16,) + best.shape)
+            best = jnp.max(lax.all_to_all(spread, ("zh", "zl", "fc"), 0, 0, tiled=True), axis=0)
+        elif bit_index in (1, 2, 3) and "zl" in freq_axis and freq_bits - shared >= 4:
             continue
         elif bit_index == 1 and "zl" in freq_axis:
             spread = jnp.broadcast_to(best[None], (4,) + best.shape)

time: 98.9 us -> 101 us (1.021)
  blocking collectives: 22 us -> 32.3 us
  starting transfers between devices: 34.8 us -> 27.5 us
    all_to_all x1, blocking collectives: 14.8 us -> 25.1 us  [shards(): lax.all_to_all(spread, ('zh', 'zl', 'fc'), 0, 0, tiled=True)]
    ppermute x2 -> x1, starting transfers between devices: 11.3 us -> 4.01 us  [swapped(): return lax.ppermute(block, axis, route)]
  transfers between devices with their start and end apart: 6 -> 5, of which waited for: 6 -> 5; matrix products, arithmetic and copies ran while one was open for 1% -> 1% of each run, Pallas kernels for 0% -> 0%
where the time goes in v16:
time: 101 us
  blocking collectives  32.3 us (32%)
  starting transfers between devices  27.5 us (27%)
  waiting for transfers between devices  24.1 us (24%)
  other arithmetic  12.1 us (12%)
  local copies, waits for them, and re-layouts  3.53 us (3%)
    all_to_all x1, blocking collectives, shards(): lax.all_to_all(spread, ('zh', 'zl', 'fc'), 0, 0, tiled=True)  25.1 us
    all_to_all x2, waiting for transfers between devices, shards(): peers = lax.all_to_all(spread, names, 0, 0, tiled=True)  15.3 us
    all_to_all x2, starting transfers between devices, shards(): peers = lax.all_to_all(spread, names, 0, 0, tiled=True)  14.8 us
    all_to_all x1, blocking collectives, shards(): best = jnp.max(lax.all_to_all(best, 'tm', 1, 1, tiled=True), axis=1)  7.21 us
    select_n x49, other arithmetic, merge_rows(): jnp.where(selected, moved[:, step_size:], moved[:, :cols - step_size])  5.57 us
    ppermute x1, starting transfers between devices, paired(): lax.ppermute(block, axis, [(partner_of(i), i) for i in range(lax.axis_siz...  4.71 us
    ppermute x1, waiting for transfers between devices, paired(): lax.ppermute(block, axis, [(partner_of(i), i) for i in range(lax.axis_siz...  4.42 us
    all_to_all x1, starting transfers between devices, shards(): gathered = lax.all_to_all(spread, 'tm', 0, 0, tiled=True)  4.01 us
  transfers between devices with their start and end apart: 5, of which 5 were waited for; matrix products, arithmetic and copies ran while one was open for 1% of the time, Pallas kernels for 0%

profile of v16, /device:TPU:9, one launch (start us, length us, event | category | flops | bytes accessed | tf_op | source)
XLA Modules:
  0.0 100.6 jit_solution(3596789337645798189)
XLA Ops:
  0.0 1.2 %convert_reduce_fusion = f32[16,512]{1,0:T(8,128)S(1)} fusion(bf16[512,512]{1,0:T(8,128)(2,1)} %param.7), kind=kLoop, calls=%fused_computation.6 | loop fusion | flops 516096 | bytes 557056 | tf_op jit(solution)/shard_map/reduce_sum | solution.py:196
  1.3 0.6 broadcast_in_dim.628
  1.9 4.0 %all-to-all-start = ((f32[4,16,512]{2,1,0:T(8,128)}), f32[4,16,512]{2,1,0:T(8,128)S(1)}, u32[]{:S(2)}, u32[]{:S(2)}) async-start(f32[4,16,512]{2,1,0:T(8,128)} %broadcast_in_dim.628), calls=%async_computation | async-start | bytes 262144 | tf_op jit(solution)/shard_map/all_to_all | solution.py:198
  6.1 0.3 select_reduce_fusion.1
  6.4 0.4 select_reduce_fusion
  7.0 3.7 %all-to-all-done = f32[4,16,512]{2,1,0:T(8,128)S(1)} async-done(((f32[4,16,512]{2,1,0:T(8,128)}), f32[4,16,512]{2,1,0:T(8,128)S(1)}, u32[]{:S(2)}, u32[]{:S(2)}) %all-to-all-start) | async-done | bytes 131104 | tf_op jit(solution)/shard_map/all_to_all | solution.py:198
  10.8 0.4 slice_select_fusion.3
  11.2 0.2 slice_select_fusion.2
  11.4 0.2 slice_select_fusion.1
  11.6 0.2 slice_select_fusion
  11.8 0.2 bitcast_reduce_fusion
  12.1 4.0 %collective-permute-start = (f32[4,2048]{1,0:T(4,128)S(1)}, f32[4,2048]{1,0:T(4,128)S(1)}, u32[]{:S(2)}, u32[]{:S(2)}) collective-permute-start(f32[4,2048]{1,0:T(4,128)S(1)} %bitcast_reduce_fusion), channel_id=1, source_target_pairs={{0,4},{4,0},{8,12},{12,8},{16,20},{20,16},{24,28},{28,24},{32,36},... | collective-permute-start | bytes 98312 | tf_op jit(solution)/shard_map/ppermute | solution.py:24
  16.2 0.7 collective-permute-done
  17.5 0.7 broadcast_in_dim.634
  18.2 10.0 %all-to-all-start.1 = ((f32[8,4,2048]{2,1,0:T(4,128)}), f32[8,4,2048]{2,1,0:T(4,128)S(1)}, u32[]{:S(2)}, u32[]{:S(2)}) async-start(f32[8,4,2048]{2,1,0:T(4,128)} %broadcast_in_dim.634), calls=%async_computation.1 | async-start | bytes 524288 | tf_op jit(solution)/shard_map/all_to_all | solution.py:210
  28.5 11.0 %all-to-all-done.1 = f32[8,4,2048]{2,1,0:T(4,128)S(1)} async-done(((f32[8,4,2048]{2,1,0:T(4,128)}), f32[8,4,2048]{2,1,0:T(4,128)S(1)}, u32[]{:S(2)}, u32[]{:S(2)}) %all-to-all-start.1) | async-done | bytes 262176 | tf_op jit(solution)/shard_map/all_to_all | solution.py:210
  41.8 0.7 broadcast_in_dim.656
  42.5 4.8 %all-to-all-start.2 = ((f32[4,4,2048]{2,1,0:T(4,128)}), f32[4,4,2048]{2,1,0:T(4,128)S(1)}, u32[]{:S(2)}, u32[]{:S(2)}) async-start(f32[4,4,2048]{2,1,0:T(4,128)} %broadcast_in_dim.656), calls=%async_computation.2 | async-start | bytes 262144 | tf_op jit(solution)/shard_map/all_to_all | solution.py:210
  47.3 4.3 %all-to-all-done.2 = f32[4,4,2048]{2,1,0:T(4,128)S(1)} async-done(((f32[4,4,2048]{2,1,0:T(4,128)}), f32[4,4,2048]{2,1,0:T(4,128)S(1)}, u32[]{:S(2)}, u32[]{:S(2)}) %all-to-all-start.2) | async-done | bytes 131104 | tf_op jit(solution)/shard_map/all_to_all | solution.py:210
  54.5 4.7 %collective-permute-start.1 = (f32[16,2048]{1,0:T(8,128)S(1)}, f32[16,2048]{1,0:T(8,128)S(1)}, u32[]{:S(2)}, u32[]{:S(2)}) collective-permute-start(f32[16,2048]{1,0:T(8,128)S(1)} %fusion.16), channel_id=1, source_target_pairs={{384,0},{388,4},{392,8},{396,12},{400,16},{404,20},{408,24},{412,2... | collective-permute-start | bytes 393224 | tf_op jit(solution)/shard_map/ppermute | solution.py:28
  59.3 4.4 %collective-permute-done.1 = f32[16,2048]{1,0:T(8,128)S(1)} collective-permute-done((f32[16,2048]{1,0:T(8,128)S(1)}, f32[16,2048]{1,0:T(8,128)S(1)}, u32[]{:S(2)}, u32[]{:S(2)}) %collective-permute-start.1) | collective-permute-done | bytes 131104 | tf_op jit(solution)/shard_map/ppermute | solution.py:28
  64.2 0.2 reshape.287
  64.4 0.2 fusion.3
  64.6 0.2 slice_select_fusion.8
  64.8 0.2 slice_select_fusion.7
  65.0 0.2 slice_select_fusion.6
  65.2 0.2 slice_select_fusion.5
  65.4 0.2 slice_select_fusion.4
  65.6 0.2 slice_select_fusion.10
  67.6 7.2 %all_to_all.25 = f32[9,4,512]{2,0,1:T(8,128)S(1)} all-to-all(f32[9,4,512]{2,0,1:T(8,128)S(1)} %stack.5), channel_id=1, replica_groups=mesh['yh'=2,'yl'=4,'zh'=2,'zl'=4,'fc'=2,'tm'=4] {'tm'}, dimensions={1} | all-to-all | bytes 147456 | tf_op jit(solution)/shard_map/all_to_all | solution.py:253
  74.9 25.1 %all_to_all.26 = f32[16,9,512]{2,1,0:T(8,128)S(1)} all-to-all(f32[16,9,512]{2,1,0:T(8,128)S(1)} %broadcast_in_dim.695), channel_id=1, replica_groups=mesh['yh'=2,'yl'=4,'zh'=2,'zl'=4,'fc'=2,'tm'=4] {'zh','zl','fc'}, dimensions={0} | all-to-all | bytes 589824 | tf_op jit(solution)/shard_map/all_to_all | solution.py:257
  100.0 0.7 reduce_max.109
  (117 shorter events, 8.4 us)
Async XLA Ops:
  0.0 6.0 %copy-start.2 = (s32[10,116]{1,0:T(8,128)S(1)}, s32[10,116]{1,0:T(8,128)}, u32[]{:S(2)}) copy-start(s32[10,116]{1,0:T(8,128)} %constant.84.clone) | copy-start | bytes 13924
  0.0 6.0 %copy-start.3 = (s32[10,116]{1,0:T(8,128)S(1)}, s32[10,116]{1,0:T(8,128)}, u32[]{:S(2)}) copy-start(s32[10,116]{1,0:T(8,128)} %constant.83.clone) | copy-start | bytes 13924
  0.0 6.0 %copy-start.4 = (s32[10,116]{1,0:T(8,128)S(1)}, s32[10,116]{1,0:T(8,128)}, u32[]{:S(2)}) copy-start(s32[10,116]{1,0:T(8,128)} %constant.82.clone) | copy-start | bytes 13924
  0.0 6.8 %copy-start.5 = (f32[64,20]{1,0:T(8,128)S(1)}, f32[64,20]{1,0:T(8,128)}, u32[]{:S(2)}) copy-start(f32[64,20]{1,0:T(8,128)} %constant.85.clone) | copy-start | bytes 15364
  0.0 6.1 %copy-start.1 = (s32[2047]{0:T(1024)S(1)}, s32[2047]{0:T(1024)}, u32[]{:S(2)}) copy-start(s32[2047]{0:T(1024)} %param.8) | copy-start | bytes 24568
  0.0 6.4 %copy-start = (s32[4094]{0:T(1024)S(1)}, s32[4094]{0:T(1024)}, u32[]{:S(2)}) copy-start(s32[4094]{0:T(1024)} %param.9) | copy-start | bytes 49132
  1.9 8.8 %all-to-all-start = ((f32[4,16,512]{2,1,0:T(8,128)}), f32[4,16,512]{2,1,0:T(8,128)S(1)}, u32[]{:S(2)}, u32[]{:S(2)}) async-start(f32[4,16,512]{2,1,0:T(8,128)} %broadcast_in_dim.628), calls=%async_computation | async-start | bytes 262144 | tf_op jit(solution)/shard_map/all_to_all | solution.py:198
  12.1 4.9 %collective-permute-start = (f32[4,2048]{1,0:T(4,128)S(1)}, f32[4,2048]{1,0:T(4,128)S(1)}, u32[]{:S(2)}, u32[]{:S(2)}) collective-permute-start(f32[4,2048]{1,0:T(4,128)S(1)} %bitcast_reduce_fusion), channel_id=1, source_target_pairs={{0,4},{4,0},{8,12},{12,8},{16,20},{20,16},{24,28},{28,24},{32,36},... | collective-permute-start | bytes 98312 | tf_op jit(solution)/shard_map/ppermute | solution.py:24
  18.2 21.3 %all-to-all-start.1 = ((f32[8,4,2048]{2,1,0:T(4,128)}), f32[8,4,2048]{2,1,0:T(4,128)S(1)}, u32[]{:S(2)}, u32[]{:S(2)}) async-start(f32[8,4,2048]{2,1,0:T(4,128)} %broadcast_in_dim.634), calls=%async_computation.1 | async-start | bytes 524288 | tf_op jit(solution)/shard_map/all_to_all | solution.py:210
  42.5 9.1 %all-to-all-start.2 = ((f32[4,4,2048]{2,1,0:T(4,128)}), f32[4,4,2048]{2,1,0:T(4,128)S(1)}, u32[]{:S(2)}, u32[]{:S(2)}) async-start(f32[4,4,2048]{2,1,0:T(4,128)} %broadcast_in_dim.656), calls=%async_computation.2 | async-start | bytes 262144 | tf_op jit(solution)/shard_map/all_to_all | solution.py:210
  54.5 9.2 %collective-permute-start.1 = (f32[16,2048]{1,0:T(8,128)S(1)}, f32[16,2048]{1,0:T(8,128)S(1)}, u32[]{:S(2)}, u32[]{:S(2)}) collective-permute-start(f32[16,2048]{1,0:T(8,128)S(1)} %fusion.16), channel_id=1, source_target_pairs={{384,0},{388,4},{392,8},{396,12},{400,16},{404,20},{408,24},{412,2... | collective-permute-start | bytes 393224 | tf_op jit(solution)/shard_map/ppermute | solution.py:28

commit v17 on v13

--- a/solution.py
+++ b/solution.py
@@ -40,7 +40,7 @@
     return jnp.pad(rows, [(0, 0)] * (rows.ndim - 1) + [(width, 0)])
 
 
-def merge_rows(low_rows, high_rows, shifts, need_now):
+def merge_rows(low_rows, high_rows, shifts, need_now, copies=0):
     offsets = need_now - shifts
     bit_count = max(need_now.bit_length(), 1)
     moved = high_rows
@@ -49,6 +49,10 @@
         cols = moved.shape[-1]
         selected = (offsets >> bit_index & 1)[:, None] == 1
         moved = jnp.where(selected, moved[:, step_size:], moved[:, : cols - step_size])
+    if copies:
+        return jnp.broadcast_to(low_rows[None], (copies,) + low_rows.shape) + jnp.broadcast_to(
+            moved[None], (copies,) + moved.shape
+        )
     return low_rows + moved
 
 
@@ -202,11 +206,17 @@
     moved = shift_rows(jnp.tile(base, (held, 1)), path_shift, max(local_limit.bit_length(), 1))
     trial_rows = jnp.sum(moved.reshape(held, sub_dev, full_time), axis=1)
     level = 0
+    ready = None
     for bit_index in range(freq_bits):
         need_now = sub_dev * 2 ** (bit_index + 1) - 1
         if bit_index in groups:
             names, width = groups[bit_index]
-            spread = jnp.broadcast_to(trial_rows[None], (2**width,) + trial_rows.shape)
+            if ready is None:
+                spread = jnp.broadcast_to(trial_rows[None], (2**width,) + trial_rows.shape)
+            else:
+                spread = ready
+            ready = None
+            later = groups.get(bit_index + width)
             peers = lax.all_to_all(spread, names, 0, 0, tiled=True)
             sets = [peers[index] for index in range(2**width)]
             for step in range(width):
@@ -214,12 +224,17 @@
                 if bit_index + step >= freq_bits - shared:
                     sets = [jnp.repeat(one, 2, axis=0) for one in sets]
                 rows = sets[0].shape[0]
+                last = step == width - 1 and later is not None
                 merged = merge_rows(
                     jnp.concatenate(sets[0::2], axis=0),
                     zero_front(jnp.concatenate(sets[1::2], axis=0), need_now),
                     level_shifts[level],
                     need_now,
+                    2 ** later[1] if last else 0,
                 )
+                if last:
+                    ready = merged
+                    merged = merged[0]
                 sets = [merged[index * rows : (index + 1) * rows] for index in range(len(sets) // 2)]
                 level = level + 1
             trial_rows = sets[0]
@@ -236,9 +251,14 @@
         if bit_index >= freq_bits - shared:
             low_rows = jnp.repeat(low_rows, 2, axis=0)
             high_rows = jnp.repeat(high_rows, 2, axis=0)
+        later = groups.get(bit_index + 1)
         trial_rows = merge_rows(
-            low_rows, zero_front(high_rows, need_now), level_shifts[level], need_now
+            low_rows, zero_front(high_rows, need_now), level_shifts[level], need_now,
+            2 ** later[1] if later is not None else 0,
         )
+        if later is not None:
+            ready = trial_rows
+            trial_rows = trial_rows[0]
         level = level + 1
     signal = trial_rows / math.sqrt(all_trials * SUMMED)
     peak_rows = []
@@ -251,9 +271,15 @@
             width_now = width_now * 2
     best = jnp.stack(peak_rows).reshape(WIDTHS, tm_count, span_time)
     best = jnp.max(lax.all_to_all(best, "tm", 1, 1, tiled=True), axis=1)
+    ready = None
     for bit_index in range(freq_bits - shared):
-        if bit_index == 1 and "zl" in freq_axis and freq_bits - shared >= 4:
-            spread = jnp.broadcast_to(best[None], (8,) + best.shape)
+        if bit_index == 0 and "zl" in freq_axis and freq_bits - shared >= 4:
+            partner = swapped(best, freq_axis, bit_index)
+            stretch = lambda one: jnp.broadcast_to(one[None], (8,) + one.shape)
+            ready = jnp.maximum(stretch(best), stretch(partner))
+            best = ready[0]
+        elif bit_index == 1 and "zl" in freq_axis and freq_bits - shared >= 4:
+            spread = jnp.broadcast_to(best[None], (8,) + best.shape) if ready is None else ready
             best = jnp.max(lax.all_to_all(spread, ("zh", "zl"), 0, 0, tiled=True), axis=0)
         elif bit_index in (2, 3) and "zl" in freq_axis and freq_bits - shared >= 4:
             continue

time: 98.9 us -> 98.9 us (level)
  no operation moved by 1% of the time
where the time goes in v17:
time: 98.9 us; the launch traced here: 98.4 us
  starting transfers between devices  34.8 us (35%)
  waiting for transfers between devices  25 us (25%)
  blocking collectives  22 us (22%)
  other arithmetic  12.1 us (12%)
  local copies, waits for them, and re-layouts  3.5 us (4%)
    all_to_all x2, waiting for transfers between devices, shards(): peers = lax.all_to_all(spread, names, 0, 0, tiled=True)  15.3 us
    all_to_all x2, starting transfers between devices, shards(): peers = lax.all_to_all(spread, names, 0, 0, tiled=True)  14.8 us
    all_to_all x1, blocking collectives, shards(): lax.all_to_all(spread, ('zh', 'zl'), 0, 0, tiled=True)  14.8 us
    ppermute x2, starting transfers between devices, swapped(): return lax.ppermute(block, axis, route)  11.3 us
    all_to_all x1, blocking collectives, shards(): best = jnp.max(lax.all_to_all(best, 'tm', 1, 1, tiled=True), axis=1)  7.21 us
    select_n x49, other arithmetic, merge_rows(): jnp.where(selected, moved[:, step_size:], moved[:, :cols - step_size])  5.57 us
    ppermute x1, starting transfers between devices, paired(): lax.ppermute(block, axis, [(partner_of(i), i) for i in range(lax.axis_siz...  4.71 us
    ppermute x1, waiting for transfers between devices, paired(): lax.ppermute(block, axis, [(partner_of(i), i) for i in range(lax.axis_siz...  4.42 us
  transfers between devices with their start and end apart: 6, of which 6 were waited for; matrix products, arithmetic and copies ran while one was open for 1% of the time, Pallas kernels for 0%

profile of v17, /device:TPU:9, one launch (start us, length us, event | category | flops | bytes accessed | tf_op | source)
XLA Modules:
  0.0 98.4 jit_solution(16735070038771698483)
XLA Ops:
  0.0 1.2 %convert_reduce_fusion = f32[16,512]{1,0:T(8,128)S(1)} fusion(bf16[512,512]{1,0:T(8,128)(2,1)} %param.7), kind=kLoop, calls=%fused_computation.6 | loop fusion | flops 516096 | bytes 557056 | tf_op jit(solution)/shard_map/reduce_sum | solution.py:200
  1.3 0.6 broadcast_in_dim.640
  1.9 4.0 %all-to-all-start = ((f32[4,16,512]{2,1,0:T(8,128)}), f32[4,16,512]{2,1,0:T(8,128)S(1)}, u32[]{:S(2)}, u32[]{:S(2)}) async-start(f32[4,16,512]{2,1,0:T(8,128)} %broadcast_in_dim.640), calls=%async_computation | async-start | bytes 262144 | tf_op jit(solution)/shard_map/all_to_all | solution.py:202
  6.1 0.3 select_reduce_fusion.1
  6.4 0.4 select_reduce_fusion
  7.0 3.7 %all-to-all-done = f32[4,16,512]{2,1,0:T(8,128)S(1)} async-done(((f32[4,16,512]{2,1,0:T(8,128)}), f32[4,16,512]{2,1,0:T(8,128)S(1)}, u32[]{:S(2)}, u32[]{:S(2)}) %all-to-all-start) | async-done | bytes 131104 | tf_op jit(solution)/shard_map/all_to_all | solution.py:202
  10.8 0.4 slice_select_fusion.3
  11.2 0.2 slice_select_fusion.2
  11.4 0.2 slice_select_fusion.1
  11.6 0.2 slice_select_fusion
  11.8 0.2 bitcast_reduce_fusion
  12.1 4.0 %collective-permute-start = (f32[4,2048]{1,0:T(4,128)S(1)}, f32[4,2048]{1,0:T(4,128)S(1)}, u32[]{:S(2)}, u32[]{:S(2)}) collective-permute-start(f32[4,2048]{1,0:T(4,128)S(1)} %bitcast_reduce_fusion), channel_id=1, source_target_pairs={{0,4},{4,0},{8,12},{12,8},{16,20},{20,16},{24,28},{28,24},{32,36},... | collective-permute-start | bytes 98312 | tf_op jit(solution)/shard_map/ppermute | solution.py:24
  16.2 0.7 collective-permute-done
  17.5 0.7 broadcast_in_dim.646
  18.2 10.0 %all-to-all-start.1 = ((f32[8,4,2048]{2,1,0:T(4,128)}), f32[8,4,2048]{2,1,0:T(4,128)S(1)}, u32[]{:S(2)}, u32[]{:S(2)}) async-start(f32[8,4,2048]{2,1,0:T(4,128)} %broadcast_in_dim.646), calls=%async_computation.1 | async-start | bytes 524288 | tf_op jit(solution)/shard_map/all_to_all | solution.py:220
  28.5 11.0 %all-to-all-done.1 = f32[8,4,2048]{2,1,0:T(4,128)S(1)} async-done(((f32[8,4,2048]{2,1,0:T(4,128)}), f32[8,4,2048]{2,1,0:T(4,128)S(1)}, u32[]{:S(2)}, u32[]{:S(2)}) %all-to-all-start.1) | async-done | bytes 262176 | tf_op jit(solution)/shard_map/all_to_all | solution.py:220
  41.8 0.7 broadcast_in_dim.668
  42.5 4.8 %all-to-all-start.2 = ((f32[4,4,2048]{2,1,0:T(4,128)}), f32[4,4,2048]{2,1,0:T(4,128)S(1)}, u32[]{:S(2)}, u32[]{:S(2)}) async-start(f32[4,4,2048]{2,1,0:T(4,128)} %broadcast_in_dim.668), calls=%async_computation.2 | async-start | bytes 262144 | tf_op jit(solution)/shard_map/all_to_all | solution.py:220
  47.3 4.3 %all-to-all-done.2 = f32[4,4,2048]{2,1,0:T(4,128)S(1)} async-done(((f32[4,4,2048]{2,1,0:T(4,128)}), f32[4,4,2048]{2,1,0:T(4,128)S(1)}, u32[]{:S(2)}, u32[]{:S(2)}) %all-to-all-start.2) | async-done | bytes 131104 | tf_op jit(solution)/shard_map/all_to_all | solution.py:220
  54.5 4.7 %collective-permute-start.1 = (f32[16,2048]{1,0:T(8,128)S(1)}, f32[16,2048]{1,0:T(8,128)S(1)}, u32[]{:S(2)}, u32[]{:S(2)}) collective-permute-start(f32[16,2048]{1,0:T(8,128)S(1)} %fusion.16), channel_id=1, source_target_pairs={{384,0},{388,4},{392,8},{396,12},{400,16},{404,20},{408,24},{412,2... | collective-permute-start | bytes 393224 | tf_op jit(solution)/shard_map/ppermute | solution.py:28
  59.3 4.4 %collective-permute-done.1 = f32[16,2048]{1,0:T(8,128)S(1)} collective-permute-done((f32[16,2048]{1,0:T(8,128)S(1)}, f32[16,2048]{1,0:T(8,128)S(1)}, u32[]{:S(2)}, u32[]{:S(2)}) %collective-permute-start.1) | collective-permute-done | bytes 131104 | tf_op jit(solution)/shard_map/ppermute | solution.py:28
  64.4 0.2 fusion.3
  64.6 0.2 slice_select_fusion.8
  64.8 0.2 slice_select_fusion.7
  65.0 0.2 slice_select_fusion.6
  65.2 0.2 slice_select_fusion.5
  65.4 0.2 slice_select_fusion.4
  67.6 7.2 %all_to_all.25 = f32[9,4,512]{2,0,1:T(8,128)S(1)} all-to-all(f32[9,4,512]{2,0,1:T(8,128)S(1)} %stack.5), channel_id=1, replica_groups=mesh['yh'=2,'yl'=4,'zh'=2,'zl'=4,'fc'=2,'tm'=4] {'tm'}, dimensions={1} | all-to-all | bytes 147456 | tf_op jit(solution)/shard_map/all_to_all | solution.py:273
  74.8 7.3 %collective-permute-start.2 = (f32[9,512]{1,0:T(8,128)S(1)}, f32[9,512]{1,0:T(8,128)S(1)}, u32[]{:S(2)}, u32[]{:S(2)}) collective-permute-start(f32[9,512]{1,0:T(8,128)S(1)} %reduce_max.108), channel_id=1, source_target_pairs={{0,4},{4,0},{8,12},{12,8},{16,20},{20,16},{24,28},{28,24},{32,36},... | collective-permute-start | bytes 55304 | tf_op jit(solution)/shard_map/ppermute | solution.py:24
  82.1 0.8 collective-permute-done.2
  83.0 14.8 %all_to_all.26 = f32[8,9,512]{2,1,0:T(8,128)S(1)} all-to-all(f32[8,9,512]{2,1,0:T(8,128)S(1)} %broadcast_in_dim.707), channel_id=1, replica_groups=mesh['yh'=2,'yl'=4,'zh'=2,'zl'=4,'fc'=2,'tm'=4] {'zh','zl'}, dimensions={0} | all-to-all | bytes 294912 | tf_op jit(solution)/shard_map/all_to_all | solution.py:283
  97.7 0.6 reduce_max.109
  (120 shorter events, 8.8 us)
Async XLA Ops:
  0.0 6.0 %copy-start.2 = (s32[10,116]{1,0:T(8,128)S(1)}, s32[10,116]{1,0:T(8,128)}, u32[]{:S(2)}) copy-start(s32[10,116]{1,0:T(8,128)} %constant.84.clone) | copy-start | bytes 13924
  0.0 6.0 %copy-start.3 = (s32[10,116]{1,0:T(8,128)S(1)}, s32[10,116]{1,0:T(8,128)}, u32[]{:S(2)}) copy-start(s32[10,116]{1,0:T(8,128)} %constant.83.clone) | copy-start | bytes 13924
  0.0 6.0 %copy-start.4 = (s32[10,116]{1,0:T(8,128)S(1)}, s32[10,116]{1,0:T(8,128)}, u32[]{:S(2)}) copy-start(s32[10,116]{1,0:T(8,128)} %constant.82.clone) | copy-start | bytes 13924
  0.0 6.8 %copy-start.5 = (f32[64,20]{1,0:T(8,128)S(1)}, f32[64,20]{1,0:T(8,128)}, u32[]{:S(2)}) copy-start(f32[64,20]{1,0:T(8,128)} %constant.85.clone) | copy-start | bytes 15364
  0.0 6.1 %copy-start.1 = (s32[2047]{0:T(1024)S(1)}, s32[2047]{0:T(1024)}, u32[]{:S(2)}) copy-start(s32[2047]{0:T(1024)} %param.8) | copy-start | bytes 24568
  0.0 6.4 %copy-start = (s32[4094]{0:T(1024)S(1)}, s32[4094]{0:T(1024)}, u32[]{:S(2)}) copy-start(s32[4094]{0:T(1024)} %param.9) | copy-start | bytes 49132
  1.9 8.8 %all-to-all-start = ((f32[4,16,512]{2,1,0:T(8,128)}), f32[4,16,512]{2,1,0:T(8,128)S(1)}, u32[]{:S(2)}, u32[]{:S(2)}) async-start(f32[4,16,512]{2,1,0:T(8,128)} %broadcast_in_dim.640), calls=%async_computation | async-start | bytes 262144 | tf_op jit(solution)/shard_map/all_to_all | solution.py:202
  12.1 4.9 %collective-permute-start = (f32[4,2048]{1,0:T(4,128)S(1)}, f32[4,2048]{1,0:T(4,128)S(1)}, u32[]{:S(2)}, u32[]{:S(2)}) collective-permute-start(f32[4,2048]{1,0:T(4,128)S(1)} %bitcast_reduce_fusion), channel_id=1, source_target_pairs={{0,4},{4,0},{8,12},{12,8},{16,20},{20,16},{24,28},{28,24},{32,36},... | collective-permute-start | bytes 98312 | tf_op jit(solution)/shard_map/ppermute | solution.py:24
  18.2 21.3 %all-to-all-start.1 = ((f32[8,4,2048]{2,1,0:T(4,128)}), f32[8,4,2048]{2,1,0:T(4,128)S(1)}, u32[]{:S(2)}, u32[]{:S(2)}) async-start(f32[8,4,2048]{2,1,0:T(4,128)} %broadcast_in_dim.646), calls=%async_computation.1 | async-start | bytes 524288 | tf_op jit(solution)/shard_map/all_to_all | solution.py:220
  42.5 9.1 %all-to-all-start.2 = ((f32[4,4,2048]{2,1,0:T(4,128)}), f32[4,4,2048]{2,1,0:T(4,128)S(1)}, u32[]{:S(2)}, u32[]{:S(2)}) async-start(f32[4,4,2048]{2,1,0:T(4,128)} %broadcast_in_dim.668), calls=%async_computation.2 | async-start | bytes 262144 | tf_op jit(solution)/shard_map/all_to_all | solution.py:220
  54.5 9.2 %collective-permute-start.1 = (f32[16,2048]{1,0:T(8,128)S(1)}, f32[16,2048]{1,0:T(8,128)S(1)}, u32[]{:S(2)}, u32[]{:S(2)}) collective-permute-start(f32[16,2048]{1,0:T(8,128)S(1)} %fusion.16), channel_id=1, source_target_pairs={{384,0},{388,4},{392,8},{396,12},{400,16},{404,20},{408,24},{412,2... | collective-permute-start | bytes 393224 | tf_op jit(solution)/shard_map/ppermute | solution.py:28
  74.8 8.1 %collective-permute-start.2 = (f32[9,512]{1,0:T(8,128)S(1)}, f32[9,512]{1,0:T(8,128)S(1)}, u32[]{:S(2)}, u32[]{:S(2)}) collective-permute-start(f32[9,512]{1,0:T(8,128)S(1)} %reduce_max.108), channel_id=1, source_target_pairs={{0,4},{4,0},{8,12},{12,8},{16,20},{20,16},{24,28},{28,24},{32,36},... | collective-permute-start | bytes 55304 | tf_op jit(solution)/shard_map/ppermute | solution.py:24

commit v18 on v17

--- a/solution.py
+++ b/solution.py
@@ -197,7 +197,10 @@
         level_shifts.append(shift_table[start : start + rows])
         start = start + rows
 
-    base = jnp.sum(spectrogram.reshape(sub_dev, SUMMED, span_time), axis=1, dtype=jnp.float32)
+    members = np.arange(sub_dev * SUMMED) // SUMMED == np.arange(sub_dev)[:, None]
+    base = jnp.dot(
+        jnp.asarray(members, jnp.bfloat16), spectrogram, preferred_element_type=jnp.float32
+    )
     spread = jnp.broadcast_to(base[None], (tm_count,) + base.shape)
     gathered = lax.all_to_all(spread, "tm", 0, 0, tiled=True)
     base = jnp.transpose(gathered, (1, 0, 2)).reshape(sub_dev, tm_count * span_time)

time: 98.9 us -> 99.7 us (level)
  other arithmetic: 12.1 us -> 10.9 us
  local copies, waits for them, and re-layouts: 3.5 us -> 4.53 us
    reduce_sum x1 -> x0, other arithmetic: 1.22 us -> none  [shards(): jnp.sum(spectrogram.reshape(sub_dev, SUMMED, span_time), axis=1, dtype=jn...]
    unnamed x12 -> x14, local copies, waits for them, and re-layouts: 0.03 us -> 1.04 us
where the time goes in v18:
time: 99.7 us; the launch traced here: 99.1 us
  starting transfers between devices  34.8 us (35%)
  waiting for transfers between devices  25 us (25%)
  blocking collectives  22 us (22%)
  other arithmetic  10.9 us (11%)
  local copies, waits for them, and re-layouts  4.53 us (5%)
  matrix products  1.08 us (1%)
    all_to_all x2, waiting for transfers between devices, shards(): peers = lax.all_to_all(spread, names, 0, 0, tiled=True)  15.3 us
    all_to_all x2, starting transfers between devices, shards(): peers = lax.all_to_all(spread, names, 0, 0, tiled=True)  14.8 us
    all_to_all x1, blocking collectives, shards(): lax.all_to_all(spread, ('zh', 'zl'), 0, 0, tiled=True)  14.8 us
    ppermute x2, starting transfers between devices, swapped(): return lax.ppermute(block, axis, route)  11.3 us
    all_to_all x1, blocking collectives, shards(): best = jnp.max(lax.all_to_all(best, 'tm', 1, 1, tiled=True), axis=1)  7.21 us
    select_n x49, other arithmetic, merge_rows(): jnp.where(selected, moved[:, step_size:], moved[:, :cols - step_size])  5.57 us
    ppermute x1, starting transfers between devices, paired(): lax.ppermute(block, axis, [(partner_of(i), i) for i in range(lax.axis_siz...  4.71 us
    ppermute x1, waiting for transfers between devices, paired(): lax.ppermute(block, axis, [(partner_of(i), i) for i in range(lax.axis_siz...  4.42 us
  transfers between devices with their start and end apart: 6, of which 6 were waited for; matrix products, arithmetic and copies ran while one was open for 1% of the time, Pallas kernels for 0%

profile of v18, /device:TPU:9, one launch (start us, length us, event | category | flops | bytes accessed | tf_op | source)
XLA Modules:
  0.0 99.1 jit_solution(16827656628563060298)
XLA Ops:
  0.0 1.0 %copy-done = bf16[512,512]{1,0:T(8,128)(2,1)S(1)} copy-done((bf16[512,512]{1,0:T(8,128)(2,1)S(1)}, bf16[512,512]{1,0:T(8,128)(2,1)}, u32[]{:S(2)}) %copy-start) | copy-done | bytes 524312
  1.1 0.9 fusion.39
  2.0 0.7 broadcast_in_dim.640
  2.6 4.0 %all-to-all-start = ((f32[4,16,512]{2,1,0:T(8,128)}), f32[4,16,512]{2,1,0:T(8,128)S(1)}, u32[]{:S(2)}, u32[]{:S(2)}) async-start(f32[4,16,512]{2,1,0:T(8,128)} %broadcast_in_dim.640), calls=%async_computation | async-start | bytes 262144 | tf_op jit(solution)/shard_map/all_to_all | solution.py:205
  6.8 0.3 select_reduce_fusion.1
  7.1 0.4 select_reduce_fusion
  7.7 3.7 %all-to-all-done = f32[4,16,512]{2,1,0:T(8,128)S(1)} async-done(((f32[4,16,512]{2,1,0:T(8,128)}), f32[4,16,512]{2,1,0:T(8,128)S(1)}, u32[]{:S(2)}, u32[]{:S(2)}) %all-to-all-start) | async-done | bytes 131104 | tf_op jit(solution)/shard_map/all_to_all | solution.py:205
  11.5 0.4 slice_select_fusion.3
  11.9 0.2 slice_select_fusion.2
  12.1 0.2 slice_select_fusion.1
  12.3 0.2 slice_select_fusion
  12.6 0.2 bitcast_reduce_fusion
  12.8 4.0 %collective-permute-start = (f32[4,2048]{1,0:T(4,128)S(1)}, f32[4,2048]{1,0:T(4,128)S(1)}, u32[]{:S(2)}, u32[]{:S(2)}) collective-permute-start(f32[4,2048]{1,0:T(4,128)S(1)} %bitcast_reduce_fusion), channel_id=1, source_target_pairs={{0,4},{4,0},{8,12},{12,8},{16,20},{20,16},{24,28},{28,24},{32,36},... | collective-permute-start | bytes 98312 | tf_op jit(solution)/shard_map/ppermute | solution.py:24
  16.9 0.7 collective-permute-done
  18.2 0.7 broadcast_in_dim.646
  18.9 10.0 %all-to-all-start.1 = ((f32[8,4,2048]{2,1,0:T(4,128)}), f32[8,4,2048]{2,1,0:T(4,128)S(1)}, u32[]{:S(2)}, u32[]{:S(2)}) async-start(f32[8,4,2048]{2,1,0:T(4,128)} %broadcast_in_dim.646), calls=%async_computation.1 | async-start | bytes 524288 | tf_op jit(solution)/shard_map/all_to_all | solution.py:223
  29.2 11.0 %all-to-all-done.1 = f32[8,4,2048]{2,1,0:T(4,128)S(1)} async-done(((f32[8,4,2048]{2,1,0:T(4,128)}), f32[8,4,2048]{2,1,0:T(4,128)S(1)}, u32[]{:S(2)}, u32[]{:S(2)}) %all-to-all-start.1) | async-done | bytes 262176 | tf_op jit(solution)/shard_map/all_to_all | solution.py:223
  42.6 0.7 broadcast_in_dim.668
  43.2 4.8 %all-to-all-start.2 = ((f32[4,4,2048]{2,1,0:T(4,128)}), f32[4,4,2048]{2,1,0:T(4,128)S(1)}, u32[]{:S(2)}, u32[]{:S(2)}) async-start(f32[4,4,2048]{2,1,0:T(4,128)} %broadcast_in_dim.668), calls=%async_computation.2 | async-start | bytes 262144 | tf_op jit(solution)/shard_map/all_to_all | solution.py:223
  48.0 4.3 %all-to-all-done.2 = f32[4,4,2048]{2,1,0:T(4,128)S(1)} async-done(((f32[4,4,2048]{2,1,0:T(4,128)}), f32[4,4,2048]{2,1,0:T(4,128)S(1)}, u32[]{:S(2)}, u32[]{:S(2)}) %all-to-all-start.2) | async-done | bytes 131104 | tf_op jit(solution)/shard_map/all_to_all | solution.py:223
  55.2 4.7 %collective-permute-start.1 = (f32[16,2048]{1,0:T(8,128)S(1)}, f32[16,2048]{1,0:T(8,128)S(1)}, u32[]{:S(2)}, u32[]{:S(2)}) collective-permute-start(f32[16,2048]{1,0:T(8,128)S(1)} %fusion.16), channel_id=1, source_target_pairs={{384,0},{388,4},{392,8},{396,12},{400,16},{404,20},{408,24},{412,2... | collective-permute-start | bytes 393224 | tf_op jit(solution)/shard_map/ppermute | solution.py:28
  60.0 4.4 %collective-permute-done.1 = f32[16,2048]{1,0:T(8,128)S(1)} collective-permute-done((f32[16,2048]{1,0:T(8,128)S(1)}, f32[16,2048]{1,0:T(8,128)S(1)}, u32[]{:S(2)}, u32[]{:S(2)}) %collective-permute-start.1) | collective-permute-done | bytes 131104 | tf_op jit(solution)/shard_map/ppermute | solution.py:28
  65.1 0.2 fusion.3
  65.3 0.2 slice_select_fusion.8
  65.5 0.2 slice_select_fusion.7
  65.7 0.2 slice_select_fusion.6
  65.9 0.2 slice_select_fusion.5
  68.3 7.2 %all_to_all.25 = f32[9,4,512]{2,0,1:T(8,128)S(1)} all-to-all(f32[9,4,512]{2,0,1:T(8,128)S(1)} %stack.5), channel_id=1, replica_groups=mesh['yh'=2,'yl'=4,'zh'=2,'zl'=4,'fc'=2,'tm'=4] {'tm'}, dimensions={1} | all-to-all | bytes 147456 | tf_op jit(solution)/shard_map/all_to_all | solution.py:276
  75.6 7.3 %collective-permute-start.2 = (f32[9,512]{1,0:T(8,128)S(1)}, f32[9,512]{1,0:T(8,128)S(1)}, u32[]{:S(2)}, u32[]{:S(2)}) collective-permute-start(f32[9,512]{1,0:T(8,128)S(1)} %reduce_max.108), channel_id=1, source_target_pairs={{0,4},{4,0},{8,12},{12,8},{16,20},{20,16},{24,28},{28,24},{32,36},... | collective-permute-start | bytes 55304 | tf_op jit(solution)/shard_map/ppermute | solution.py:24
  82.8 0.8 collective-permute-done.2
  83.7 14.8 %all_to_all.26 = f32[8,9,512]{2,1,0:T(8,128)S(1)} all-to-all(f32[8,9,512]{2,1,0:T(8,128)S(1)} %broadcast_in_dim.707), channel_id=1, replica_groups=mesh['yh'=2,'yl'=4,'zh'=2,'zl'=4,'fc'=2,'tm'=4] {'zh','zl'}, dimensions={0} | all-to-all | bytes 294912 | tf_op jit(solution)/shard_map/all_to_all | solution.py:286
  98.4 0.6 reduce_max.109
  (122 shorter events, 9.0 us)
Async XLA Ops:
  0.0 1.1 %copy-start = (bf16[512,512]{1,0:T(8,128)(2,1)S(1)}, bf16[512,512]{1,0:T(8,128)(2,1)}, u32[]{:S(2)}) copy-start(bf16[512,512]{1,0:T(8,128)(2,1)} %param.8) | copy-start | bytes 1572868
  0.0 6.7 %copy-start.3 = (s32[10,116]{1,0:T(8,128)S(1)}, s32[10,116]{1,0:T(8,128)}, u32[]{:S(2)}) copy-start(s32[10,116]{1,0:T(8,128)} %constant.85.clone) | copy-start | bytes 13924
  0.0 6.7 %copy-start.4 = (s32[10,116]{1,0:T(8,128)S(1)}, s32[10,116]{1,0:T(8,128)}, u32[]{:S(2)}) copy-start(s32[10,116]{1,0:T(8,128)} %constant.84.clone) | copy-start | bytes 13924
  0.0 6.7 %copy-start.5 = (s32[10,116]{1,0:T(8,128)S(1)}, s32[10,116]{1,0:T(8,128)}, u32[]{:S(2)}) copy-start(s32[10,116]{1,0:T(8,128)} %constant.83.clone) | copy-start | bytes 13924
  0.0 7.5 %copy-start.6 = (f32[64,20]{1,0:T(8,128)S(1)}, f32[64,20]{1,0:T(8,128)}, u32[]{:S(2)}) copy-start(f32[64,20]{1,0:T(8,128)} %constant.86.clone) | copy-start | bytes 15364
  0.0 6.8 %copy-start.2 = (s32[2047]{0:T(1024)S(1)}, s32[2047]{0:T(1024)}, u32[]{:S(2)}) copy-start(s32[2047]{0:T(1024)} %param.9) | copy-start | bytes 24568
  1.1 6.1 %copy-start.1 = (s32[4094]{0:T(1024)S(1)}, s32[4094]{0:T(1024)}, u32[]{:S(2)}) copy-start(s32[4094]{0:T(1024)} %param.10) | copy-start | bytes 49132
  2.6 8.8 %all-to-all-start = ((f32[4,16,512]{2,1,0:T(8,128)}), f32[4,16,512]{2,1,0:T(8,128)S(1)}, u32[]{:S(2)}, u32[]{:S(2)}) async-start(f32[4,16,512]{2,1,0:T(8,128)} %broadcast_in_dim.640), calls=%async_computation | async-start | bytes 262144 | tf_op jit(solution)/shard_map/all_to_all | solution.py:205
  12.8 4.9 %collective-permute-start = (f32[4,2048]{1,0:T(4,128)S(1)}, f32[4,2048]{1,0:T(4,128)S(1)}, u32[]{:S(2)}, u32[]{:S(2)}) collective-permute-start(f32[4,2048]{1,0:T(4,128)S(1)} %bitcast_reduce_fusion), channel_id=1, source_target_pairs={{0,4},{4,0},{8,12},{12,8},{16,20},{20,16},{24,28},{28,24},{32,36},... | collective-permute-start | bytes 98312 | tf_op jit(solution)/shard_map/ppermute | solution.py:24
  18.9 21.3 %all-to-all-start.1 = ((f32[8,4,2048]{2,1,0:T(4,128)}), f32[8,4,2048]{2,1,0:T(4,128)S(1)}, u32[]{:S(2)}, u32[]{:S(2)}) async-start(f32[8,4,2048]{2,1,0:T(4,128)} %broadcast_in_dim.646), calls=%async_computation.1 | async-start | bytes 524288 | tf_op jit(solution)/shard_map/all_to_all | solution.py:223
  43.2 9.1 %all-to-all-start.2 = ((f32[4,4,2048]{2,1,0:T(4,128)}), f32[4,4,2048]{2,1,0:T(4,128)S(1)}, u32[]{:S(2)}, u32[]{:S(2)}) async-start(f32[4,4,2048]{2,1,0:T(4,128)} %broadcast_in_dim.668), calls=%async_computation.2 | async-start | bytes 262144 | tf_op jit(solution)/shard_map/all_to_all | solution.py:223
  55.2 9.2 %collective-permute-start.1 = (f32[16,2048]{1,0:T(8,128)S(1)}, f32[16,2048]{1,0:T(8,128)S(1)}, u32[]{:S(2)}, u32[]{:S(2)}) collective-permute-start(f32[16,2048]{1,0:T(8,128)S(1)} %fusion.16), channel_id=1, source_target_pairs={{384,0},{388,4},{392,8},{396,12},{400,16},{404,20},{408,24},{412,2... | collective-permute-start | bytes 393224 | tf_op jit(solution)/shard_map/ppermute | solution.py:28
  75.6 8.1 %collective-permute-start.2 = (f32[9,512]{1,0:T(8,128)S(1)}, f32[9,512]{1,0:T(8,128)S(1)}, u32[]{:S(2)}, u32[]{:S(2)}) collective-permute-start(f32[9,512]{1,0:T(8,128)S(1)} %reduce_max.108), channel_id=1, source_target_pairs={{0,4},{4,0},{8,12},{12,8},{16,20},{20,16},{24,28},{28,24},{32,36},... | collective-permute-start | bytes 55304 | tf_op jit(solution)/shard_map/ppermute | solution.py:24

commit v19 on v17

--- a/solution.py
+++ b/solution.py
@@ -260,12 +260,12 @@
             ready = trial_rows
             trial_rows = trial_rows[0]
         level = level + 1
-    signal = trial_rows / math.sqrt(all_trials * SUMMED)
+    signal = trial_rows
     peak_rows = []
     window_sum = signal
     width_now = 1
     for level_index in range(WIDTHS):
-        peak_rows.append(jnp.max(window_sum, axis=0) / math.sqrt(width_now))
+        peak_rows.append(jnp.max(window_sum, axis=0) / math.sqrt(all_trials * SUMMED) / math.sqrt(width_now))
         if level_index + 1 < WIDTHS:
             window_sum = window_sum + zero_front(window_sum, width_now)[:, :full_time]
             width_now = width_now * 2

time: 98.9 us -> 98.9 us (level)
  no operation moved by 1% of the time
where the time goes in v19:
time: 98.9 us; the launch traced here: 98.4 us
  starting transfers between devices  34.8 us (35%)
  waiting for transfers between devices  25 us (25%)
  blocking collectives  22 us (22%)
  other arithmetic  12.1 us (12%)
  local copies, waits for them, and re-layouts  3.5 us (4%)
    all_to_all x2, waiting for transfers between devices, shards(): peers = lax.all_to_all(spread, names, 0, 0, tiled=True)  15.3 us
    all_to_all x2, starting transfers between devices, shards(): peers = lax.all_to_all(spread, names, 0, 0, tiled=True)  14.8 us
    all_to_all x1, blocking collectives, shards(): lax.all_to_all(spread, ('zh', 'zl'), 0, 0, tiled=True)  14.8 us
    ppermute x2, starting transfers between devices, swapped(): return lax.ppermute(block, axis, route)  11.3 us
    all_to_all x1, blocking collectives, shards(): best = jnp.max(lax.all_to_all(best, 'tm', 1, 1, tiled=True), axis=1)  7.21 us
    select_n x49, other arithmetic, merge_rows(): jnp.where(selected, moved[:, step_size:], moved[:, :cols - step_size])  5.57 us
    ppermute x1, starting transfers between devices, paired(): lax.ppermute(block, axis, [(partner_of(i), i) for i in range(lax.axis_siz...  4.71 us
    ppermute x1, waiting for transfers between devices, paired(): lax.ppermute(block, axis, [(partner_of(i), i) for i in range(lax.axis_siz...  4.42 us
  transfers between devices with their start and end apart: 6, of which 6 were waited for; matrix products, arithmetic and copies ran while one was open for 1% of the time, Pallas kernels for 0%

profile of v19, /device:TPU:9, one launch (start us, length us, event | category | flops | bytes accessed | tf_op | source)
XLA Modules:
  0.0 98.4 jit_solution(10746237400553238737)
XLA Ops:
  0.0 1.2 %convert_reduce_fusion = f32[16,512]{1,0:T(8,128)S(1)} fusion(bf16[512,512]{1,0:T(8,128)(2,1)} %param.7), kind=kLoop, calls=%fused_computation.6 | loop fusion | flops 516096 | bytes 557056 | tf_op jit(solution)/shard_map/reduce_sum | solution.py:200
  1.3 0.6 broadcast_in_dim.640
  1.9 4.0 %all-to-all-start = ((f32[4,16,512]{2,1,0:T(8,128)}), f32[4,16,512]{2,1,0:T(8,128)S(1)}, u32[]{:S(2)}, u32[]{:S(2)}) async-start(f32[4,16,512]{2,1,0:T(8,128)} %broadcast_in_dim.640), calls=%async_computation | async-start | bytes 262144 | tf_op jit(solution)/shard_map/all_to_all | solution.py:202
  6.1 0.3 select_reduce_fusion.1
  6.4 0.4 select_reduce_fusion
  7.0 3.7 %all-to-all-done = f32[4,16,512]{2,1,0:T(8,128)S(1)} async-done(((f32[4,16,512]{2,1,0:T(8,128)}), f32[4,16,512]{2,1,0:T(8,128)S(1)}, u32[]{:S(2)}, u32[]{:S(2)}) %all-to-all-start) | async-done | bytes 131104 | tf_op jit(solution)/shard_map/all_to_all | solution.py:202
  10.8 0.4 slice_select_fusion.3
  11.2 0.2 slice_select_fusion.2
  11.4 0.2 slice_select_fusion.1
  11.6 0.2 slice_select_fusion
  11.8 0.2 bitcast_reduce_fusion
  12.1 4.0 %collective-permute-start = (f32[4,2048]{1,0:T(4,128)S(1)}, f32[4,2048]{1,0:T(4,128)S(1)}, u32[]{:S(2)}, u32[]{:S(2)}) collective-permute-start(f32[4,2048]{1,0:T(4,128)S(1)} %bitcast_reduce_fusion), channel_id=1, source_target_pairs={{0,4},{4,0},{8,12},{12,8},{16,20},{20,16},{24,28},{28,24},{32,36},... | collective-permute-start | bytes 98312 | tf_op jit(solution)/shard_map/ppermute | solution.py:24
  16.2 0.7 collective-permute-done
  17.5 0.7 broadcast_in_dim.646
  18.2 10.0 %all-to-all-start.1 = ((f32[8,4,2048]{2,1,0:T(4,128)}), f32[8,4,2048]{2,1,0:T(4,128)S(1)}, u32[]{:S(2)}, u32[]{:S(2)}) async-start(f32[8,4,2048]{2,1,0:T(4,128)} %broadcast_in_dim.646), calls=%async_computation.1 | async-start | bytes 524288 | tf_op jit(solution)/shard_map/all_to_all | solution.py:220
  28.5 11.0 %all-to-all-done.1 = f32[8,4,2048]{2,1,0:T(4,128)S(1)} async-done(((f32[8,4,2048]{2,1,0:T(4,128)}), f32[8,4,2048]{2,1,0:T(4,128)S(1)}, u32[]{:S(2)}, u32[]{:S(2)}) %all-to-all-start.1) | async-done | bytes 262176 | tf_op jit(solution)/shard_map/all_to_all | solution.py:220
  41.8 0.7 broadcast_in_dim.668
  42.5 4.8 %all-to-all-start.2 = ((f32[4,4,2048]{2,1,0:T(4,128)}), f32[4,4,2048]{2,1,0:T(4,128)S(1)}, u32[]{:S(2)}, u32[]{:S(2)}) async-start(f32[4,4,2048]{2,1,0:T(4,128)} %broadcast_in_dim.668), calls=%async_computation.2 | async-start | bytes 262144 | tf_op jit(solution)/shard_map/all_to_all | solution.py:220
  47.3 4.3 %all-to-all-done.2 = f32[4,4,2048]{2,1,0:T(4,128)S(1)} async-done(((f32[4,4,2048]{2,1,0:T(4,128)}), f32[4,4,2048]{2,1,0:T(4,128)S(1)}, u32[]{:S(2)}, u32[]{:S(2)}) %all-to-all-start.2) | async-done | bytes 131104 | tf_op jit(solution)/shard_map/all_to_all | solution.py:220
  54.5 4.7 %collective-permute-start.1 = (f32[16,2048]{1,0:T(8,128)S(1)}, f32[16,2048]{1,0:T(8,128)S(1)}, u32[]{:S(2)}, u32[]{:S(2)}) collective-permute-start(f32[16,2048]{1,0:T(8,128)S(1)} %fusion.15), channel_id=1, source_target_pairs={{384,0},{388,4},{392,8},{396,12},{400,16},{404,20},{408,24},{412,2... | collective-permute-start | bytes 393224 | tf_op jit(solution)/shard_map/ppermute | solution.py:28
  59.3 4.4 %collective-permute-done.1 = f32[16,2048]{1,0:T(8,128)S(1)} collective-permute-done((f32[16,2048]{1,0:T(8,128)S(1)}, f32[16,2048]{1,0:T(8,128)S(1)}, u32[]{:S(2)}, u32[]{:S(2)}) %collective-permute-start.1) | collective-permute-done | bytes 131104 | tf_op jit(solution)/shard_map/ppermute | solution.py:28
  64.4 0.2 fusion.3
  64.6 0.2 slice_select_fusion.8
  64.8 0.2 slice_select_fusion.7
  65.0 0.2 slice_select_fusion.6
  65.2 0.2 slice_select_fusion.5
  65.4 0.2 slice_select_fusion.4
  67.6 7.2 %all_to_all.25 = f32[9,4,512]{2,0,1:T(8,128)S(1)} all-to-all(f32[9,4,512]{2,0,1:T(8,128)S(1)} %stack.2), channel_id=1, replica_groups=mesh['yh'=2,'yl'=4,'zh'=2,'zl'=4,'fc'=2,'tm'=4] {'tm'}, dimensions={1} | all-to-all | bytes 147456 | tf_op jit(solution)/shard_map/all_to_all | solution.py:273
  74.9 7.3 %collective-permute-start.2 = (f32[9,512]{1,0:T(8,128)S(1)}, f32[9,512]{1,0:T(8,128)S(1)}, u32[]{:S(2)}, u32[]{:S(2)}) collective-permute-start(f32[9,512]{1,0:T(8,128)S(1)} %reduce_max.108), channel_id=1, source_target_pairs={{0,4},{4,0},{8,12},{12,8},{16,20},{20,16},{24,28},{28,24},{32,36},... | collective-permute-start | bytes 55304 | tf_op jit(solution)/shard_map/ppermute | solution.py:24
  82.1 0.8 collective-permute-done.2
  83.0 14.8 %all_to_all.26 = f32[8,9,512]{2,1,0:T(8,128)S(1)} all-to-all(f32[8,9,512]{2,1,0:T(8,128)S(1)} %broadcast_in_dim.707), channel_id=1, replica_groups=mesh['yh'=2,'yl'=4,'zh'=2,'zl'=4,'fc'=2,'tm'=4] {'zh','zl'}, dimensions={0} | all-to-all | bytes 294912 | tf_op jit(solution)/shard_map/all_to_all | solution.py:283
  97.7 0.6 reduce_max.109
  (121 shorter events, 8.8 us)
Async XLA Ops:
  0.0 6.0 %copy-start.2 = (s32[10,116]{1,0:T(8,128)S(1)}, s32[10,116]{1,0:T(8,128)}, u32[]{:S(2)}) copy-start(s32[10,116]{1,0:T(8,128)} %constant.179.clone) | copy-start | bytes 13924
  0.0 6.0 %copy-start.3 = (s32[10,116]{1,0:T(8,128)S(1)}, s32[10,116]{1,0:T(8,128)}, u32[]{:S(2)}) copy-start(s32[10,116]{1,0:T(8,128)} %constant.178.clone) | copy-start | bytes 13924
  0.0 6.0 %copy-start.4 = (s32[10,116]{1,0:T(8,128)S(1)}, s32[10,116]{1,0:T(8,128)}, u32[]{:S(2)}) copy-start(s32[10,116]{1,0:T(8,128)} %constant.88.clone) | copy-start | bytes 13924
  0.0 6.8 %copy-start.5 = (f32[64,20]{1,0:T(8,128)S(1)}, f32[64,20]{1,0:T(8,128)}, u32[]{:S(2)}) copy-start(f32[64,20]{1,0:T(8,128)} %constant.180.clone) | copy-start | bytes 15364
  0.0 6.1 %copy-start.1 = (s32[2047]{0:T(1024)S(1)}, s32[2047]{0:T(1024)}, u32[]{:S(2)}) copy-start(s32[2047]{0:T(1024)} %param.8) | copy-start | bytes 24568
  0.0 6.4 %copy-start = (s32[4094]{0:T(1024)S(1)}, s32[4094]{0:T(1024)}, u32[]{:S(2)}) copy-start(s32[4094]{0:T(1024)} %param.9) | copy-start | bytes 49132
  1.9 8.8 %all-to-all-start = ((f32[4,16,512]{2,1,0:T(8,128)}), f32[4,16,512]{2,1,0:T(8,128)S(1)}, u32[]{:S(2)}, u32[]{:S(2)}) async-start(f32[4,16,512]{2,1,0:T(8,128)} %broadcast_in_dim.640), calls=%async_computation | async-start | bytes 262144 | tf_op jit(solution)/shard_map/all_to_all | solution.py:202
  12.1 4.9 %collective-permute-start = (f32[4,2048]{1,0:T(4,128)S(1)}, f32[4,2048]{1,0:T(4,128)S(1)}, u32[]{:S(2)}, u32[]{:S(2)}) collective-permute-start(f32[4,2048]{1,0:T(4,128)S(1)} %bitcast_reduce_fusion), channel_id=1, source_target_pairs={{0,4},{4,0},{8,12},{12,8},{16,20},{20,16},{24,28},{28,24},{32,36},... | collective-permute-start | bytes 98312 | tf_op jit(solution)/shard_map/ppermute | solution.py:24
  18.2 21.3 %all-to-all-start.1 = ((f32[8,4,2048]{2,1,0:T(4,128)}), f32[8,4,2048]{2,1,0:T(4,128)S(1)}, u32[]{:S(2)}, u32[]{:S(2)}) async-start(f32[8,4,2048]{2,1,0:T(4,128)} %broadcast_in_dim.646), calls=%async_computation.1 | async-start | bytes 524288 | tf_op jit(solution)/shard_map/all_to_all | solution.py:220
  42.5 9.1 %all-to-all-start.2 = ((f32[4,4,2048]{2,1,0:T(4,128)}), f32[4,4,2048]{2,1,0:T(4,128)S(1)}, u32[]{:S(2)}, u32[]{:S(2)}) async-start(f32[4,4,2048]{2,1,0:T(4,128)} %broadcast_in_dim.668), calls=%async_computation.2 | async-start | bytes 262144 | tf_op jit(solution)/shard_map/all_to_all | solution.py:220
  54.5 9.2 %collective-permute-start.1 = (f32[16,2048]{1,0:T(8,128)S(1)}, f32[16,2048]{1,0:T(8,128)S(1)}, u32[]{:S(2)}, u32[]{:S(2)}) collective-permute-start(f32[16,2048]{1,0:T(8,128)S(1)} %fusion.15), channel_id=1, source_target_pairs={{384,0},{388,4},{392,8},{396,12},{400,16},{404,20},{408,24},{412,2... | collective-permute-start | bytes 393224 | tf_op jit(solution)/shard_map/ppermute | solution.py:28
  74.9 8.1 %collective-permute-start.2 = (f32[9,512]{1,0:T(8,128)S(1)}, f32[9,512]{1,0:T(8,128)S(1)}, u32[]{:S(2)}, u32[]{:S(2)}) collective-permute-start(f32[9,512]{1,0:T(8,128)S(1)} %reduce_max.108), channel_id=1, source_target_pairs={{0,4},{4,0},{8,12},{12,8},{16,20},{20,16},{24,28},{28,24},{32,36},... | collective-permute-start | bytes 55304 | tf_op jit(solution)/shard_map/ppermute | solution.py:24
